TPU v7x, 256 devices: a whole 4x4x8 slice. The times are simulated.
256 devices in a mesh: req: 64 (over x, z, core), mlp: 4 (over y).
Axes of the slice: x: 4, y: 4, z: 8, core: 2. Of those that a mesh axis runs over, the one named last changes fastest.
Arguments:
- drafts: bfloat16 [512, 16, 2048], P('req', None, 'mlp'), may hold values from -60 to 60
- slot_of: int32 [512], replicated, may hold values from 0 to 511, as said below
- lengths: int32 [512], P('req'), may hold values from 2 to 256, as said below
- parents: int32 [512, 16], P('req'), may hold values from 0 to 14, as said below
- accepted_tokens: int32 [512, 8], P('req'), may hold values from 0 to 15, as said below
- cached_key_value: bfloat16 [512, 256, 4, 128], P('req', None, 'mlp'), may hold values from -2000 to 2000
- attn_gain: float32 [2048], replicated, may hold values from 0.1 to 1.9
- query_weight: bfloat16 [2048, 768], P(None, 'mlp'), may hold values from -0.125 to 0.125
- key_value_weight: bfloat16 [2048, 512], P(None, 'mlp'), may hold values from -0.125 to 0.125
- w_out: bfloat16 [768, 2048], P('mlp'), may hold values from -0.21875 to 0.21875
- mlp_gain: float32 [2048], replicated, may hold values from 0.1 to 1.9
- w_gate: bfloat16 [2048, 2560], P(None, 'mlp'), may hold values from -0.125 to 0.125
- w_up: bfloat16 [2048, 2560], P(None, 'mlp'), may hold values from -0.125 to 0.125
- w_down: bfloat16 [2560, 2048], P('mlp'), may hold values from -0.125 to 0.125
Outputs:
- layer_output: bfloat16 [512, 16, 2048], P('req', None, 'mlp')
- accepted_kv: bfloat16 [512, 8, 4, 128], P('req', None, 'mlp')
Inputs may be any that keep to these rules, and one draw needn't show every extreme that they name: `slot_of`: A permutation of the 512 slots; the cache of slot s is held by index s // 8 of req. Of the 8 requests that arrive on one index of req, at most 1 have their caches on any one index, and that many do for some. `lengths`: some slot holds exactly 256 cached positions. parents[s, 0] = 0 and parents[s, j] < j for j >= 1. accepted_tokens[s, 0] = 0, the entries rise, and each entry is the parent of the next.
All inputs are finite; a program needn't handle non-finite values.
Results may differ from a plain program's by a relative error of at most 0.0095.
Values may be sent and summed in bfloat16 or wider, within the bound.
No kernel may reach another device: no remote copies, remote signals or barrier semaphores. Data moves between devices by JAX's collectives and lax.ppermute only.
A program may use at most 64 MiB of HBM per device.

v0:
```python
import math

import jax
import jax.numpy as jnp
from jax import lax
from jax.sharding import PartitionSpec as P

HEAD_DIM = 64


EPS = 1e-06
HIGH = lax.Precision.HIGHEST


def route_tables(slot_of, per_owner_rows, sources, groups, my_index):
    owners = slot_of // per_owner_rows
    owner_grid = owners.reshape(sources, per_owner_rows)
    request_ids = jnp.arange(per_owner_rows)
    earlier = request_ids[None, :] < request_ids[:, None]
    position = jnp.sum((owner_grid[:, :, None] == owner_grid[:, None, :]) & earlier[None], axis=2)
    column = (jnp.arange(sources, dtype=jnp.int32)[:, None] * groups + position).reshape(-1)
    slot_count = sources * groups
    my_owners = lax.dynamic_index_in_dim(owner_grid, my_index, 0, keepdims=False)
    my_position = lax.dynamic_index_in_dim(position, my_index, 0, keepdims=False)
    target = my_owners * groups + my_position
    sender = (jnp.arange(slot_count)[:, None] == target[None, :]).astype(jnp.bfloat16)
    arrive = (slot_of[None, :] == my_index * per_owner_rows + request_ids[:, None]).astype(
        jnp.bfloat16
    )
    places = (column[:, None] == jnp.arange(slot_count)[None, :]).astype(jnp.bfloat16)
    receiver = jnp.dot(arrive, places, preferred_element_type=jnp.float32).astype(jnp.bfloat16)
    return (sender, receiver)


def ancestry(tree_links, tokens):
    parent_link = (
        tree_links[:, :, None] == jnp.arange(tokens, dtype=jnp.int32)[None, None, :]
    ).astype(jnp.float32)
    reachable = jnp.maximum(parent_link, jnp.eye(tokens, dtype=jnp.float32)[None])
    for squaring in range(max(tokens - 1, 1).bit_length()):
        reachable = jnp.minimum(
            jnp.einsum("rij,rjk->rik", reachable, reachable, precision=HIGH), 1.0
        )
    return reachable > 0.5


def cache_scores(query_rows, cache_block, cache_len, score_scale, head_size):
    key_rows = cache_block[..., :head_size].astype(jnp.float32)
    scores = jnp.einsum("rtkgd,rckd->rkgtc", query_rows, key_rows, precision=HIGH) * score_scale
    row_ids = jnp.arange(cache_block.shape[1])
    live_rows = row_ids[None, :] < cache_len[:, None]
    return jnp.where(live_rows[:, None, None, None, :], scores, -jnp.inf)


def weighted(weights, cache_block, head_size):
    return jnp.einsum(
        "rkgtc,rckd->rtkgd",
        weights,
        cache_block[..., head_size:],
        preferred_element_type=jnp.float32,
    )


def per_device(
    drafts,
    slot_of,
    lengths,
    parents,
    accepted_tokens,
    cached_key_value,
    attn_gain,
    query_weight,
    key_value_weight,
    w_out,
    mlp_gain,
    w_gate,
    w_up,
    w_down,
):
    req_count = lax.axis_size("req")
    my_index = lax.axis_index("req")
    part_index = lax.axis_index("mlp")
    per_owner_rows, tokens, quarter = drafts.shape
    sends = max(1, per_owner_rows // req_count)
    sender, receiver = route_tables(slot_of, per_owner_rows, req_count, sends, my_index)
    flat_rows = drafts.reshape(per_owner_rows, tokens * quarter)
    outgoing = jnp.dot(sender, flat_rows, preferred_element_type=jnp.float32).astype(jnp.bfloat16)
    outgoing = outgoing.reshape(req_count, sends, tokens * quarter)
    incoming = lax.all_to_all(outgoing, "req", split_axis=0, concat_axis=0, tiled=True)
    local_rows = jnp.dot(
        receiver,
        incoming.reshape(req_count * sends, tokens * quarter),
        preferred_element_type=jnp.float32,
    ).astype(jnp.bfloat16)
    local_rows = local_rows.reshape(per_owner_rows * tokens, quarter)
    full_rows = lax.all_gather(local_rows, "mlp", axis=1, tiled=True)
    wide_rows = full_rows.astype(jnp.float32)
    normalized_rows = (
        wide_rows
        * lax.rsqrt(jnp.mean(wide_rows * wide_rows, axis=1, keepdims=True) + EPS)
        * attn_gain
    ).astype(jnp.bfloat16)
    kv_heads = key_value_weight.shape[1] // (2 * HEAD_DIM)
    group_heads = query_weight.shape[1] // (kv_heads * HEAD_DIM)
    query_rows = jnp.dot(normalized_rows, query_weight, preferred_element_type=jnp.float32).reshape(
        per_owner_rows, tokens, kv_heads, group_heads, HEAD_DIM
    )
    new_key_value = (
        jnp.dot(normalized_rows, key_value_weight, preferred_element_type=jnp.float32)
        .astype(jnp.bfloat16)
        .reshape(per_owner_rows, tokens, kv_heads, 2 * HEAD_DIM)
    )
    picker = (
        accepted_tokens[:, :, None] == jnp.arange(tokens, dtype=jnp.int32)[None, None, :]
    ).astype(jnp.bfloat16)
    accepted_rows = jnp.einsum(
        "rat,rtkd->rakd", picker, new_key_value, preferred_element_type=jnp.float32
    ).astype(jnp.bfloat16)
    score_scale = 1.0 / math.sqrt(HEAD_DIM)
    draft_keys = new_key_value[..., :HEAD_DIM].astype(jnp.float32)
    draft_scores = (
        jnp.einsum("rtkgd,rjkd->rkgtj", query_rows, draft_keys, precision=HIGH) * score_scale
    )
    draft_scores = jnp.where(ancestry(parents, tokens)[:, None, None], draft_scores, -jnp.inf)
    draft_top = jnp.max(draft_scores, axis=-1)
    scores = cache_scores(query_rows, cached_key_value, lengths, score_scale, HEAD_DIM)
    row_top = jnp.maximum(draft_top, jnp.max(scores, axis=-1))
    weights = jnp.exp(scores - row_top[..., None]).astype(jnp.bfloat16)
    numerator = weighted(weights, cached_key_value, HEAD_DIM)
    denominator = jnp.sum(weights.astype(jnp.float32), axis=-1)
    draft_weights = jnp.exp(draft_scores - row_top[..., None]).astype(jnp.bfloat16)
    numerator = numerator + jnp.einsum(
        "rkgtj,rjkd->rtkgd",
        draft_weights,
        new_key_value[..., HEAD_DIM:],
        preferred_element_type=jnp.float32,
    )
    denominator = denominator + jnp.sum(draft_weights.astype(jnp.float32), axis=-1)
    attended = (numerator / jnp.transpose(denominator, (0, 3, 1, 2))[..., None]).astype(
        jnp.bfloat16
    )
    attended = attended.reshape(per_owner_rows * tokens, kv_heads * group_heads * HEAD_DIM)
    head_part = jnp.dot(attended, w_out, preferred_element_type=jnp.float32)
    attn_sum = lax.psum(head_part.astype(jnp.bfloat16), "mlp").astype(jnp.float32)
    residual = wide_rows + attn_sum
    normed_two = (
        residual * lax.rsqrt(jnp.mean(residual * residual, axis=1, keepdims=True) + EPS) * mlp_gain
    ).astype(jnp.bfloat16)
    gate_out = jnp.dot(normed_two, w_gate, preferred_element_type=jnp.float32)
    up_out = jnp.dot(normed_two, w_up, preferred_element_type=jnp.float32)
    residual_share = lax.dynamic_slice_in_dim(residual, part_index * quarter, quarter, 1)
    hidden = (jax.nn.silu(gate_out) * up_out).astype(jnp.bfloat16)
    unit_part = jnp.dot(hidden, w_down, preferred_element_type=jnp.float32)
    unit_share = lax.psum_scatter(
        unit_part.astype(jnp.bfloat16), "mlp", scatter_dimension=1, tiled=True
    ).astype(jnp.float32)
    result = (residual_share + unit_share).astype(jnp.bfloat16)
    result_rows = result.reshape(per_owner_rows, tokens * quarter)
    returning = jnp.dot(receiver.T, result_rows, preferred_element_type=jnp.float32).astype(
        jnp.bfloat16
    )
    returning = returning.reshape(req_count, sends, tokens * quarter)
    arrived = lax.all_to_all(returning, "req", split_axis=0, concat_axis=0, tiled=True)
    back_rows = jnp.dot(
        sender.T,
        arrived.reshape(req_count * sends, tokens * quarter),
        preferred_element_type=jnp.float32,
    ).astype(jnp.bfloat16)
    return (back_rows.reshape(per_owner_rows, tokens, quarter), accepted_rows)


def solution(mesh):
    placed = (
        P("req", None, "mlp"),
        P(),
        P("req"),
        P("req", None),
        P("req", None),
        P("req", None, "mlp", None),
        P(),
        P(None, "mlp"),
        P(None, "mlp"),
        P("mlp", None),
        P(),
        P(None, "mlp"),
        P(None, "mlp"),
        P("mlp", None),
    )
    return jax.shard_map(
        per_device,
        mesh=mesh,
        in_specs=placed,
        out_specs=(P("req", None, "mlp"), P("req", None, "mlp", None)),
        check_vma=False,
    )
```

profile of v0, /device:TPU:1, one launch (start us, length us, event | category | flops | bytes accessed | tf_op | source)
XLA Modules:
  0.0 239.9 jit_solution(3685939278999989164)
XLA Ops:
  12.0 3.4 %reduce.6 = bf16[64,8192]{1,0:T(8,128)(2,1)} reduce(bf16[64,1,8192]{2,0,1:T(8,128)(2,1)} %fusion, bf16[]{:T(256)} %broadcast.99), dimensions={1}, to_apply=%copy.78.reduce_sub_computation | reduce | bytes 2097154 | tf_op jit(solution)/shard_map/reshape | solution.py:88
  15.4 2.7 %reshape.219 = bf16[64,2,4096]{2,1,0:T(2,128)(2,1)} reshape(bf16[64,8192]{1,0:T(8,128)(2,1)} %reduce.6) | data formatting | bytes 2097152
  18.1 13.2 %all-to-all-start = ((bf16[64,2,4096]{2,1,0:T(2,128)(2,1)}), bf16[64,2,4096]{2,1,0:T(2,128)(2,1)}, u32[]{:S(2)}, u32[]{:S(2)}) async-start(bf16[64,2,4096]{2,1,0:T(2,128)(2,1)} %reshape.219), calls=%async_computation | async-start | bytes 2097152 | tf_op jit(solution)/shard_map/all_to_all | solution.py:89
  33.4 26.3 %all-to-all-done = bf16[64,2,4096]{2,1,0:T(2,128)(2,1)} async-done(((bf16[64,2,4096]{2,1,0:T(2,128)(2,1)}), bf16[64,2,4096]{2,1,0:T(2,128)(2,1)}, u32[]{:S(2)}, u32[]{:S(2)}) %all-to-all-start) | async-done | bytes 1048608 | tf_op jit(solution)/shard_map/all_to_all | solution.py:89
  59.7 7.5 %reshape.220 = bf16[64,1,8192]{2,1,0:T(2,128)(2,1)} reshape(bf16[64,2,4096]{2,1,0:T(2,128)(2,1)} %all-to-all-done) | data formatting | bytes 2097152
  67.2 2.8 %convolution_convert_fusion.3 = bf16[8,8192]{1,0:T(8,128)(2,1)S(1)} fusion(bf16[8,64]{1,0:T(8,128)(2,1)S(1)} %convolution_convert_fusion.8, bf16[64,1,8192]{2,1,0:T(2,128)(2,1)} %reshape.220), kind=kOutput, calls=%fused_computation.5 | convolution fusion | flops 8454144 | bytes 1180672 | tf_op jit(solution)/shard_map/dot_general | solution.py:90
  70.1 11.4 %all_gather.3 = bf16[128,2048]{1,0:T(8,128)(2,1)S(1)} all-gather(bf16[128,512]{1,0:T(8,128)(2,1)S(1)} %reshape.199), channel_id=1, replica_groups=mesh['req'=64,'mlp'=4] {'mlp'}, dimensions={1}, use_global_device_ids=true | all-gather | bytes 655360 | tf_op jit(solution)/shard_map/all_gather | solution.py:96
  81.6 2.0 convolution_convert_fusion.6
  83.7 1.6 fusion.34
  85.4 1.5 fusion.53
  86.9 1.8 fusion.54
  91.0 2.2 convolution_convert_fusion.5
  93.3 44.9 %all-reduce.2.cloned.1.call-done = bf16[128,2048]{1,0:T(8,128)(2,1)} async-done(((bf16[128,2048]{1,0:T(8,128)(2,1)}), bf16[128,2048]{1,0:T(8,128)(2,1)}) %all-reduce.2.cloned.1.call-update) | async-done | bytes 524304 | tf_op jit(solution)/shard_map/psum | solution.py:144
  138.2 2.2 convert_add_fusion
  140.4 2.5 %fusion.52 = f32[128,640]{1,0:T(8,128)S(1)} fusion(bf16[2048,640]{1,0:T(8,128)(2,1)} %param.25, f32[2048]{0:T(1024)S(1)} %copy-done.2, f32[128]{0:T(128)S(1)} %add_rsqrt_fusion, bf16[128,2048]{1,0:T(8,128)(2,1)S(1)} %all_gather.3, bf16[128,2048]{1,0:T(8,128)(2,1)} %all-reduce.2.cloned.1.call-done), kind=kOutput, calls=%fused_computation.99 | convolution fusion | flops 337117184 | bytes 4006400 | tf_op jit(solution)/shard_map/dot_general | solution.py:149
  143.0 3.8 %convolution_convert_fusion.4 = bf16[128,2048]{1,0:T(8,128)(2,1)} fusion(bf16[640,2048]{1,0:T(8,128)(2,1)S(1)} %copy-done, bf16[2048,640]{1,0:T(8,128)(2,1)} %param.26, f32[128,640]{1,0:T(8,128)S(1)} %fusion.52, f32[2048]{0:T(1024)S(1)} %copy-done.2, f32[128]{0:T(128)S(1)} %add_rsqrt_fusion, bf16[128,2048]{1,0:T(8,128)(2,1)S(1)} %all_gather.3, ...), kind=kOutput, calls=%fused_computation.6 | convolution fusion | flops 673415168 | bytes 7152128 | tf_op jit(solution)/shard_map/dot_general | solution.py:153
  146.8 24.9 %reduce-scatter.2.cloned.1.call-done = bf16[128,512]{1,0:T(8,128)(2,1)} async-done(((bf16[128,2048]{1,0:T(8,128)(2,1)}), bf16[128,512]{1,0:T(8,128)(2,1)}) %reduce-scatter.2.cloned.1.call-update) | async-done | bytes 131088 | tf_op jit(solution)/shard_map/reduce_scatter | solution.py:154
  172.8 1.5 fusion.1
  174.3 3.4 %reduce.7 = bf16[64,8192]{1,0:T(8,128)(2,1)} reduce(bf16[64,1,8192]{2,0,1:T(8,128)(2,1)} %fusion.1, bf16[]{:T(256)} %broadcast.99), dimensions={1}, to_apply=%copy.87.reduce_sub_computation | reduce | bytes 2097154 | tf_op jit(solution)/shard_map/reshape | solution.py:162
  177.7 2.6 %reshape.221 = bf16[64,2,4096]{2,1,0:T(2,128)(2,1)} reshape(bf16[64,8192]{1,0:T(8,128)(2,1)} %reduce.7) | data formatting | bytes 2097152
  180.3 13.3 %all-to-all-start.1 = ((bf16[64,2,4096]{2,1,0:T(2,128)(2,1)}), bf16[64,2,4096]{2,1,0:T(2,128)(2,1)}, u32[]{:S(2)}, u32[]{:S(2)}) async-start(bf16[64,2,4096]{2,1,0:T(2,128)(2,1)} %reshape.221), calls=%async_computation.2 | async-start | bytes 2097152 | tf_op jit(solution)/shard_map/all_to_all | solution.py:163
  194.5 27.6 %all-to-all-done.1 = bf16[64,2,4096]{2,1,0:T(2,128)(2,1)} async-done(((bf16[64,2,4096]{2,1,0:T(2,128)(2,1)}), bf16[64,2,4096]{2,1,0:T(2,128)(2,1)}, u32[]{:S(2)}, u32[]{:S(2)}) %all-to-all-start.1) | async-done | bytes 1048608 | tf_op jit(solution)/shard_map/all_to_all | solution.py:163
  222.1 7.5 %reshape.222 = bf16[64,1,8192]{2,1,0:T(2,128)(2,1)} reshape(bf16[64,2,4096]{2,1,0:T(2,128)(2,1)} %all-to-all-done.1) | data formatting | bytes 2097152
  229.6 2.8 %convolution_convert_fusion.2 = bf16[8,8192]{1,0:T(8,128)(2,1)S(1)} fusion(bf16[64,1,8192]{2,1,0:T(2,128)(2,1)} %reshape.222, s32[8]{0:T(128)S(1)} %copy-done.6), kind=kOutput, calls=%fused_computation.4 | convolution fusion | flops 8454656 | bytes 1179680 | tf_op jit(solution)/shard_map/dot_general | solution.py:164
  (66 shorter events, 12.2 us)
Async XLA Ops:
  7.2 135.8 %copy-start = (bf16[640,2048]{1,0:T(8,128)(2,1)S(1)}, bf16[640,2048]{1,0:T(8,128)(2,1)}, u32[]{:S(2)}) copy-start(bf16[640,2048]{1,0:T(8,128)(2,1)} %param.27) | copy-start | bytes 7864324
  9.5 0.5 copy-start.5
  15.4 16.1 %copy-start.7 = (s32[8,16]{1,0:T(8,128)S(1)}, s32[8,16]{1,0:T(8,128)}, u32[]{:S(2)}) copy-start(s32[8,16]{1,0:T(8,128)} %param.17) | copy-start | bytes 1540
  15.4 17.1 %copy-start.9 = (s32[8]{0:T(128)S(1)}, s32[8]{0:T(128)}, u32[]{:S(2)}) copy-start(s32[8]{0:T(128)} %param.16) | copy-start | bytes 100
  15.4 17.7 %copy-start.8 = (s32[512]{0:T(512)S(1)}, s32[512]{0:T(512)}, u32[]{:S(2)}) copy-start(s32[512]{0:T(512)} %param.15) | copy-start | bytes 6148
  18.1 41.6 %all-to-all-start = ((bf16[64,2,4096]{2,1,0:T(2,128)(2,1)}), bf16[64,2,4096]{2,1,0:T(2,128)(2,1)}, u32[]{:S(2)}, u32[]{:S(2)}) async-start(bf16[64,2,4096]{2,1,0:T(2,128)(2,1)} %reshape.219), calls=%async_computation | async-start | bytes 2097152 | tf_op jit(solution)/shard_map/all_to_all | solution.py:89
  31.3 106.9 %all-reduce.2.cloned.1.call-start = ((), (), s32[]{:S(2)}) async-start(), calls=%async_computation.3 | async-start | bytes 1048576 | tf_op jit(solution)/shard_map/psum | solution.py:144
  33.4 36.6 %copy-start.3 = (bf16[8,64]{1,0:T(8,128)(2,1)}, bf16[8,64]{1,0:T(8,128)(2,1)S(1)}, u32[]{:S(2)}) copy-start(bf16[8,64]{1,0:T(8,128)(2,1)S(1)} %convolution_convert_fusion.8) | copy-start | bytes 3076
  33.4 48.2 %copy-start.10 = (f32[2048]{0:T(1024)S(1)}, f32[2048]{0:T(1024)}, u32[]{:S(2)}) copy-start(f32[2048]{0:T(1024)} %param.20) | copy-start | bytes 24580
  85.4 5.1 %copy-start.1 = (bf16[128,128]{1,0:T(8,128)(2,1)S(1)}, bf16[128,128]{1,0:T(8,128)(2,1)}, u32[]{:S(2)}) copy-start(bf16[128,128]{1,0:T(8,128)(2,1)} %convolution_convert_fusion.6) | copy-start | bytes 98308
  90.5 49.9 %copy-start.2 = (f32[2048]{0:T(1024)S(1)}, f32[2048]{0:T(1024)}, u32[]{:S(2)}) copy-start(f32[2048]{0:T(1024)} %param.24) | copy-start | bytes 24580
  93.2 78.4 %reduce-scatter.2.cloned.1.call-start = ((), (), s32[]{:S(2)}) async-start(), calls=%async_computation.4 | async-start | bytes 655360 | tf_op jit(solution)/shard_map/reduce_scatter | solution.py:154
  142.9 29.8 %copy-start.4 = (bf16[8,64]{1,0:T(8,128)(2,1)S(1)}, bf16[8,64]{1,0:T(8,128)(2,1)}, u32[]{:S(2)}) copy-start(bf16[8,64]{1,0:T(8,128)(2,1)} %copy-done.3) | copy-start | bytes 3076
  177.7 16.0 %copy-start.11 = (s32[8,8]{1,0:T(8,128)S(1)}, s32[8,8]{1,0:T(8,128)}, u32[]{:S(2)}) copy-start(s32[8,8]{1,0:T(8,128)} %param.18) | copy-start | bytes 772
  180.3 49.3 %copy-start.6 = (s32[8]{0:T(128)S(1)}, s32[8]{0:T(128)}, u32[]{:S(2)}) copy-start(s32[8]{0:T(128)} %copy-done.5) | copy-start | bytes 100
  180.3 41.8 %all-to-all-start.1 = ((bf16[64,2,4096]{2,1,0:T(2,128)(2,1)}), bf16[64,2,4096]{2,1,0:T(2,128)(2,1)}, u32[]{:S(2)}, u32[]{:S(2)}) async-start(bf16[64,2,4096]{2,1,0:T(2,128)(2,1)} %reshape.221), calls=%async_computation.2 | async-start | bytes 2097152 | tf_op jit(solution)/shard_map/all_to_all | solution.py:163
Sparse Core Ops, SparseCore 0:
  93.3 44.7 all-reduce.1
  146.9 24.6 reduce-scatter.1
where the time goes:
time: 241 us; the launch traced here: 240 us
  waiting for transfers between devices  124 us (51%)
  matrix products  27.5 us (11%)
  starting transfers between devices  26.6 us (11%)
  local copies, waits for them, and re-layouts  24 us (10%)
  between operations  14.3 us (6%)
  other arithmetic  12.4 us (5%)
  blocking collectives  11.4 us (5%)
    psum x1, waiting for transfers between devices, per_device(): lax.psum(head_part.astype(jnp.bfloat16), 'mlp').astype(jnp.float32)  44.9 us
    all_to_all x1, waiting for transfers between devices, per_device(): lax.all_to_all(returning, 'req', split_axis=0, concat_axis=0, tiled=True)  27.6 us
    all_to_all x1, waiting for transfers between devices, per_device(): lax.all_to_all(outgoing, 'req', split_axis=0, concat_axis=0, tiled=True)  26.3 us
    reduce_scatter x1, waiting for transfers between devices, per_device(): lax.psum_scatter(unit_part.astype(jnp.bfloat16), 'mlp', scatter_dimension...  24.9 us
    unnamed x30, local copies, waits for them, and re-layouts  22.6 us
    all_to_all x1, starting transfers between devices, per_device(): lax.all_to_all(returning, 'req', split_axis=0, concat_axis=0, tiled=True)  13.3 us
    all_to_all x1, starting transfers between devices, per_device(): lax.all_to_all(outgoing, 'req', split_axis=0, concat_axis=0, tiled=True)  13.2 us
    all_gather x1, blocking collectives, per_device(): full_rows = lax.all_gather(local_rows, 'mlp', axis=1, tiled=True)  11.4 us
  transfers between devices with their start and end apart: 4, of which 4 were waited for; matrix products, arithmetic and copies ran while one was open for 1% of the time, Pallas kernels for 0%

commit v1 on v0

v1 whole, which is shorter than its diff:
```python
import math

import jax
import jax.numpy as jnp
from jax import lax
from jax.sharding import PartitionSpec as P

HEAD_DIM = 64


EPS = 1e-06
HIGH = lax.Precision.HIGHEST


def ancestry(tree_links, tokens):
    parent_link = (
        tree_links[:, :, None] == jnp.arange(tokens, dtype=jnp.int32)[None, None, :]
    ).astype(jnp.float32)
    reachable = jnp.maximum(parent_link, jnp.eye(tokens, dtype=jnp.float32)[None])
    for squaring in range(max(tokens - 1, 1).bit_length()):
        reachable = jnp.minimum(
            jnp.einsum("rij,rjk->rik", reachable, reachable, precision=HIGH), 1.0
        )
    return reachable > 0.5


def shift_mlp(value, shift, count):
    return lax.ppermute(value, "mlp", [(i, (i + shift) % count) for i in range(count)])


def gather_mlp(value, count, part_index):
    pieces = [value] + [shift_mlp(value, k, count) for k in range(1, count)]
    stacked = jnp.stack(pieces)
    order = (part_index - jnp.arange(count, dtype=jnp.int32)) % count
    return jnp.take(stacked, order, axis=0, mode="clip")


def per_device(
    drafts,
    slot_of,
    lengths,
    parents,
    accepted_tokens,
    cached_key_value,
    attn_gain,
    query_weight,
    key_value_weight,
    w_out,
    mlp_gain,
    w_gate,
    w_up,
    w_down,
):
    req_count = lax.axis_size("req")
    mlp_count = lax.axis_size("mlp")
    my_index = lax.axis_index("req")
    part_index = lax.axis_index("mlp")
    per_owner_rows, tokens, quarter = drafts.shape
    model_dim = quarter * mlp_count

    w_out_all = gather_mlp(w_out, mlp_count, part_index)

    local_ids = jnp.arange(per_owner_rows, dtype=jnp.int32)
    devices = jnp.arange(req_count, dtype=jnp.int32)
    my_slots = lax.dynamic_slice_in_dim(slot_of, my_index * per_owner_rows, per_owner_rows)
    my_owners = my_slots // per_owner_rows
    send_pick = jnp.sum(
        jnp.where(my_owners[None, :] == devices[:, None], local_ids[None, :], 0), axis=1
    )
    owned_slots = my_index * per_owner_rows + local_ids
    requests = jnp.arange(slot_of.shape[0], dtype=jnp.int32)
    request_of = jnp.sum(
        jnp.where(slot_of[None, :] == owned_slots[:, None], requests[None, :], 0), axis=1
    )
    source_of = request_of // per_owner_rows
    return_pick = jnp.sum(
        jnp.where(source_of[None, :] == devices[:, None], local_ids[None, :], 0), axis=1
    )

    outgoing = jnp.take(drafts, send_pick, axis=0, mode="clip")
    incoming = lax.all_to_all(outgoing, "req", 0, 0, tiled=True)
    local_rows = jnp.take(incoming, source_of, axis=0, mode="clip")

    rows = per_owner_rows * tokens
    full_rows = gather_mlp(local_rows.reshape(rows, quarter), mlp_count, part_index)
    wide_rows = full_rows.astype(jnp.float32)
    square_mean = jnp.sum(wide_rows * wide_rows, axis=(0, 2)) / model_dim
    attn_scale = lax.rsqrt(square_mean + EPS)
    normalized_rows = (
        wide_rows * attn_scale[None, :, None] * attn_gain.reshape(mlp_count, 1, quarter)
    ).astype(jnp.bfloat16)
    kv_heads = key_value_weight.shape[1] // (2 * HEAD_DIM)
    group_heads = query_weight.shape[1] // (kv_heads * HEAD_DIM)
    query_rows = jnp.einsum(
        "jtf,jfc->tc",
        normalized_rows,
        query_weight.reshape(mlp_count, quarter, -1),
        preferred_element_type=jnp.float32,
    ).reshape(per_owner_rows, tokens, kv_heads, group_heads, HEAD_DIM)
    new_key_value = (
        jnp.einsum(
            "jtf,jfc->tc",
            normalized_rows,
            key_value_weight.reshape(mlp_count, quarter, -1),
            preferred_element_type=jnp.float32,
        )
        .astype(jnp.bfloat16)
        .reshape(per_owner_rows, tokens, kv_heads, 2 * HEAD_DIM)
    )
    picker = (
        accepted_tokens[:, :, None] == jnp.arange(tokens, dtype=jnp.int32)[None, None, :]
    ).astype(jnp.bfloat16)
    accepted_rows = jnp.einsum(
        "rat,rtkd->rakd", picker, new_key_value, preferred_element_type=jnp.float32
    ).astype(jnp.bfloat16)

    score_scale = 1.0 / math.sqrt(HEAD_DIM)
    draft_keys = new_key_value[..., :HEAD_DIM].astype(jnp.float32)
    draft_scores = (
        jnp.einsum("rtkgd,rjkd->rkgtj", query_rows, draft_keys, precision=HIGH) * score_scale
    )
    draft_scores = jnp.where(ancestry(parents, tokens)[:, None, None], draft_scores, -jnp.inf)
    draft_top = jnp.max(draft_scores, axis=-1)
    cache_keys = cached_key_value[..., :HEAD_DIM].astype(jnp.float32)
    scores = (
        jnp.einsum("rtkgd,rckd->rkgtc", query_rows, cache_keys, precision=HIGH) * score_scale
    )
    live_rows = jnp.arange(cached_key_value.shape[1])[None, :] < lengths[:, None]
    scores = jnp.where(live_rows[:, None, None, None, :], scores, -jnp.inf)
    row_top = jnp.maximum(draft_top, jnp.max(scores, axis=-1))
    weights = jnp.exp(scores - row_top[..., None]).astype(jnp.bfloat16)
    numerator = jnp.einsum(
        "rkgtc,rckd->rtkgd",
        weights,
        cached_key_value[..., HEAD_DIM:],
        preferred_element_type=jnp.float32,
    )
    denominator = jnp.sum(weights.astype(jnp.float32), axis=-1)
    draft_weights = jnp.exp(draft_scores - row_top[..., None]).astype(jnp.bfloat16)
    numerator = numerator + jnp.einsum(
        "rkgtj,rjkd->rtkgd",
        draft_weights,
        new_key_value[..., HEAD_DIM:],
        preferred_element_type=jnp.float32,
    )
    denominator = denominator + jnp.sum(draft_weights.astype(jnp.float32), axis=-1)
    attended = (numerator / jnp.transpose(denominator, (0, 3, 1, 2))[..., None]).astype(
        jnp.bfloat16
    )
    head_width = kv_heads * group_heads * HEAD_DIM
    attended = attended.reshape(per_owner_rows, tokens, head_width)

    returning = jnp.take(attended, return_pick, axis=0, mode="clip")
    arrived = lax.all_to_all(returning, "req", 0, 0, tiled=True)
    back_rows = jnp.take(arrived, my_owners, axis=0, mode="clip")

    packed = jnp.concatenate(
        [back_rows.reshape(rows, head_width), drafts.reshape(rows, quarter)], axis=1
    )
    gathered = gather_mlp(packed, mlp_count, part_index)
    heads_all = gathered[:, :, :head_width]
    owned_all = gathered[:, :, head_width:].astype(jnp.float32)

    group_products = jnp.einsum(
        "jtc,jcd->jtd", heads_all, w_out_all, preferred_element_type=jnp.float32
    )
    attn_sum = jnp.sum(group_products.astype(jnp.bfloat16).astype(jnp.float32), axis=0)
    residual = jnp.transpose(owned_all, (1, 0, 2)).reshape(rows, model_dim) + attn_sum
    normed_two = (
        residual * lax.rsqrt(jnp.mean(residual * residual, axis=1, keepdims=True) + EPS) * mlp_gain
    ).astype(jnp.bfloat16)
    gate_out = jnp.dot(normed_two, w_gate, preferred_element_type=jnp.float32)
    up_out = jnp.dot(normed_two, w_up, preferred_element_type=jnp.float32)
    hidden = (jax.nn.silu(gate_out) * up_out).astype(jnp.bfloat16)
    unit_part = (
        jnp.dot(hidden, w_down, preferred_element_type=jnp.float32)
        .astype(jnp.bfloat16)
        .reshape(rows, mlp_count, quarter)
    )

    unit_share = lax.dynamic_index_in_dim(unit_part, part_index, 1, keepdims=False).astype(
        jnp.float32
    )
    for k in range(1, mlp_count):
        target = (part_index + k) % mlp_count
        piece = lax.dynamic_index_in_dim(unit_part, target, 1, keepdims=False)
        unit_share = unit_share + shift_mlp(piece, k, mlp_count).astype(jnp.float32)
    residual_share = lax.dynamic_slice_in_dim(residual, part_index * quarter, quarter, 1)
    result = (residual_share + unit_share).astype(jnp.bfloat16)
    return (result.reshape(per_owner_rows, tokens, quarter), accepted_rows)


def solution(mesh):
    placed = (
        P("req", None, "mlp"),
        P(),
        P("req"),
        P("req", None),
        P("req", None),
        P("req", None, "mlp", None),
        P(),
        P(None, "mlp"),
        P(None, "mlp"),
        P("mlp", None),
        P(),
        P(None, "mlp"),
        P(None, "mlp"),
        P("mlp", None),
    )
    return jax.shard_map(
        per_device,
        mesh=mesh,
        in_specs=placed,
        out_specs=(P("req", None, "mlp"), P("req", None, "mlp", None)),
        check_vma=False,
    )
```

time: 241 us -> 163 us (0.68)
  waiting for transfers between devices: 124 us -> 54.5 us
  between operations: 14.3 us -> 1.01 us
  starting transfers between devices: 26.6 us -> 38.7 us
  matrix products: 27.5 us -> 15.8 us
  blocking collectives: 11.4 us -> 0 us
  other arithmetic: 12.4 us -> 21.9 us
  local copies, waits for them, and re-layouts: 24 us -> 28.7 us
    psum x1 -> x0, waiting for transfers between devices: 44.9 us -> none  [per_device(): lax.psum(head_part.astype(jnp.bfloat16), 'mlp').astype(jnp.float32)]
    reduce_scatter x1 -> x0, waiting for transfers between devices: 24.9 us -> none  [per_device(): lax.psum_scatter(unit_part.astype(jnp.bfloat16), 'mlp', scatter_dimension...]
    unnamed x30 -> x35, local copies, waits for them, and re-layouts: 22.6 us -> 1.66 us
    ppermute x0 -> x12, starting transfers between devices: none -> 18.8 us  [shift_mlp(): lax.ppermute(value, 'mlp', [(i, (i + shift) % count) for i in range(count)])]
    ppermute x0 -> x12, waiting for transfers between devices: none -> 17.4 us  [shift_mlp(): lax.ppermute(value, 'mlp', [(i, (i + shift) % count) for i in range(count)])]
    all_to_all x2, waiting for transfers between devices: 53.9 us -> 37 us  [the longest x1 25.1 us: per_device(): incoming = lax.all_to_all(outgoing, 'req', 0, 0, tiled=True)]
    gather x0 -> x7, local copies, waits for them, and re-layouts: none -> 15.5 us  [the longest x3 8.11 us: gather_mlp(): return jnp.take(stacked, order, axis=0, mode='clip')]
    all_gather x1 -> x0, blocking collectives: 11.4 us -> none  [per_device(): full_rows = lax.all_gather(local_rows, 'mlp', axis=1, tiled=True)]
  transfers between devices with their start and end apart: 4 -> 14, of which waited for: 4 -> 6; matrix products, arithmetic and copies ran while one was open for 1% -> 13% of each run, Pallas kernels for 0% -> 0%
where the time goes in v1:
time: 163 us; the launch traced here: 161 us
  waiting for transfers between devices  54.5 us (33%)
  starting transfers between devices  38.7 us (24%)
  local copies, waits for them, and re-layouts  28.7 us (18%)
  other arithmetic  21.9 us (13%)
  matrix products  15.8 us (10%)
    all_to_all x1, waiting for transfers between devices, per_device(): incoming = lax.all_to_all(outgoing, 'req', 0, 0, tiled=True)  25.1 us
    ppermute x12, starting transfers between devices, shift_mlp(): lax.ppermute(value, 'mlp', [(i, (i + shift) % count) for i in range(count)])  18.8 us
    ppermute x12, waiting for transfers between devices, shift_mlp(): lax.ppermute(value, 'mlp', [(i, (i + shift) % count) for i in range(count)])  17.4 us
    all_to_all x1, starting transfers between devices, per_device(): incoming = lax.all_to_all(outgoing, 'req', 0, 0, tiled=True)  13.2 us
    all_to_all x1, waiting for transfers between devices, per_device(): arrived = lax.all_to_all(returning, 'req', 0, 0, tiled=True)  12 us
    another operation x4, other arithmetic, gather_mlp(): stacked = jnp.stack(pieces)  8.73 us
    gather x3, local copies, waits for them, and re-layouts, gather_mlp(): return jnp.take(stacked, order, axis=0, mode='clip')  8.11 us
    all_to_all x1, starting transfers between devices, per_device(): arrived = lax.all_to_all(returning, 'req', 0, 0, tiled=True)  6.75 us
  transfers between devices with their start and end apart: 14, of which 6 were waited for; matrix products, arithmetic and copies ran while one was open for 13% of the time, Pallas kernels for 0%

profile of v1, /device:TPU:1, one launch (start us, length us, event | category | flops | bytes accessed | tf_op | source)
XLA Modules:
  0.0 160.6 jit_solution(16533896376836472005)
XLA Ops:
  3.1 2.5 %gather_fusion = bf16[64,16,512]{2,1,0:T(8,128)(2,1)} fusion(bf16[8,16,512]{2,1,0:T(8,128)(2,1)} %param.14, s32[1024]{0:T(1024)S(1)} %pad_clamp_fusion.4), kind=kCustom, calls=%fused_computation | custom fusion | bytes 2097408 | tf_op jit(solution)/shard_map/jit(_take)/gather | solution.py:80
  5.7 13.2 %all-to-all-start = ((bf16[64,16,512]{2,1,0:T(8,128)(2,1)}), bf16[64,16,512]{2,1,0:T(8,128)(2,1)}, u32[]{:S(2)}, u32[]{:S(2)}) async-start(bf16[64,16,512]{2,1,0:T(8,128)(2,1)} %gather_fusion), calls=%async_computation | async-start | bytes 2097152 | tf_op jit(solution)/shard_map/all_to_all | solution.py:81
  22.2 25.1 %all-to-all-done = bf16[64,16,512]{2,1,0:T(8,128)(2,1)} async-done(((bf16[64,16,512]{2,1,0:T(8,128)(2,1)}), bf16[64,16,512]{2,1,0:T(8,128)(2,1)}, u32[]{:S(2)}, u32[]{:S(2)}) %all-to-all-start) | async-done | bytes 1048608 | tf_op jit(solution)/shard_map/all_to_all | solution.py:81
  47.3 1.9 %gather_fusion.1 = bf16[8,16,512]{2,1,0:T(8,128)(2,1)S(1)} fusion(bf16[64,16,512]{2,1,0:T(8,128)(2,1)} %all-to-all-done, s32[1024]{0:T(1024)} %pad_clamp_fusion.3), kind=kCustom, calls=%fused_computation.1 | custom fusion | bytes 262176 | tf_op jit(solution)/shard_map/jit(_take)/gather | solution.py:82
  50.6 2.6 %collective-permute-start.1 = (bf16[128,512]{1,0:T(8,128)(2,1)S(1)}, bf16[128,512]{1,0:T(8,128)(2,1)}, u32[]{:S(2)}, u32[]{:S(2)}) collective-permute-start(bf16[128,512]{1,0:T(8,128)(2,1)S(1)} %bitcast.178), channel_id=1, source_target_pairs={{0,2},{1,3},{2,0},{3,1},{4,6},{5,7},{6,4},{7,5},{8,10},{9,11},{10,... | collective-permute-start | bytes 393224 | tf_op jit(solution)/shard_map/ppermute | solution.py:28
  59.6 1.9 %pad_maximum_fusion.2 = bf16[4,128,512]{2,1,0:T(8,128)(2,1)} fusion(bf16[1,128,512]{2,1,0:T(8,128)(2,1)} %bitcast.6, bf16[1,128,512]{2,1,0:T(8,128)(2,1)} %bitcast.5, bf16[1,128,512]{2,1,0:T(8,128)(2,1)} %bitcast.4, bf16[1,128,512]{2,1,0:T(8,128)(2,1)S(1)} %bitcast.180), kind=kLoop, calls=%fused_computation.51 | loop fusion | flops 786432 | bytes 1048576 | tf_op jit(solution)/shard_map/stack | solution.py:33
  70.9 6.8 %all-to-all-start.1 = ((bf16[64,16,192]{2,1,0:T(8,128)(2,1)}), bf16[64,16,192]{2,1,0:T(8,128)(2,1)}, u32[]{:S(2)}, u32[]{:S(2)}) async-start(bf16[64,16,192]{2,1,0:T(8,128)(2,1)} %gather_fusion.3), calls=%async_computation.1 | async-start | bytes 1048576 | tf_op jit(solution)/shard_map/all_to_all | solution.py:154
  78.7 2.1 %collective-permute-start.7 = (bf16[192,2048]{1,0:T(8,128)(2,1)}, bf16[192,2048]{1,0:T(8,128)(2,1)}, u32[]{:S(2)}, u32[]{:S(2)}) collective-permute-start(bf16[192,2048]{1,0:T(8,128)(2,1)} %param.23), channel_id=1, source_target_pairs={{0,2},{1,3},{2,0},{3,1},{4,6},{5,7},{6,4},{7,5},{8,10},{9,11},{10,... | collective-permute-start | bytes 2359304 | tf_op jit(solution)/shard_map/ppermute | solution.py:28
  82.9 12.0 %all-to-all-done.1 = bf16[64,16,192]{2,1,0:T(8,128)(2,1)} async-done(((bf16[64,16,192]{2,1,0:T(8,128)(2,1)}), bf16[64,16,192]{2,1,0:T(8,128)(2,1)}, u32[]{:S(2)}, u32[]{:S(2)}) %all-to-all-start.1) | async-done | bytes 393248 | tf_op jit(solution)/shard_map/all_to_all | solution.py:154
  99.2 2.1 %collective-permute-start.4 = (bf16[128,704]{0,1:T(8,128)(2,1)}, bf16[128,704]{0,1:T(8,128)(2,1)}, u32[]{:S(2)}, u32[]{:S(2)}) collective-permute-start(bf16[128,704]{0,1:T(8,128)(2,1)} %get-tuple-element.15), channel_id=1, source_target_pairs={{0,2},{1,3},{2,0},{3,1},{4,6},{5,7},{6,4},{7,5},{8,10},{9,11},{10,... | collective-permute-start | bytes 540680 | tf_op jit(solution)/shard_map/ppermute | solution.py:28
  102.7 12.5 %collective-permute-done.7 = bf16[192,2048]{1,0:T(8,128)(2,1)} collective-permute-done((bf16[192,2048]{1,0:T(8,128)(2,1)}, bf16[192,2048]{1,0:T(8,128)(2,1)}, u32[]{:S(2)}, u32[]{:S(2)}) %collective-permute-start.7) | collective-permute-done | bytes 786464 | tf_op jit(solution)/shard_map/ppermute | solution.py:28
  115.8 3.1 %pad_maximum_fusion = bf16[4,192,2048]{2,1,0:T(8,128)(2,1)} fusion(bf16[1,192,2048]{2,1,0:T(8,128)(2,1)} %bitcast.56, bf16[1,192,2048]{2,1,0:T(8,128)(2,1)} %bitcast.55, bf16[1,192,2048]{2,1,0:T(8,128)(2,1)S(1)} %bitcast.174, bf16[1,192,2048]{2,1,0:T(8,128)(2,1)} %bitcast.173), kind=kLoop, calls=%fused_computation.8 | loop fusion | flops 4718592 | bytes 6291456 | tf_op jit(solution)/shard_map/stack | solution.py:33
  118.9 4.4 %gather_fusion.6 = bf16[4,192,2048]{2,1,0:T(8,128)(2,1)} fusion(bf16[4,192,2048]{2,1,0:T(8,128)(2,1)} %pad_maximum_fusion, s32[1024]{0:T(1024)} %pad_clamp_fusion.2), kind=kCustom, calls=%fused_computation.6 | custom fusion | bytes 6291472 | tf_op jit(solution)/shard_map/jit(_take)/gather | solution.py:35
  123.4 2.0 %pad_maximum_fusion.1 = bf16[4,128,704]{1,2,0:T(8,128)(2,1)} fusion(bf16[1,128,704]{1,2,0:T(8,128)(2,1)} %bitcast.50, bf16[1,128,704]{1,2,0:T(8,128)(2,1)} %bitcast.49, bf16[1,128,704]{1,2,0:T(8,128)(2,1)} %bitcast.48, bf16[1,128,704]{1,2,0:T(8,128)(2,1)S(1)} %copy-done.6), kind=kLoop, calls=%fused_computation.49 | loop fusion | flops 1081344 | bytes 1441792 | tf_op jit(solution)/shard_map/stack | solution.py:33
  125.4 1.9 %gather_fusion.5 = bf16[4,128,704]{1,2,0:T(8,128)(2,1)S(1)} fusion(bf16[4,128,704]{1,2,0:T(8,128)(2,1)} %pad_maximum_fusion.1, s32[1024]{0:T(1024)} %pad_clamp_fusion.2), kind=kCustom, calls=%fused_computation.5 | custom fusion | bytes 1441808 | tf_op jit(solution)/shard_map/jit(_take)/gather | solution.py:35
  128.4 3.7 %convert_reduce_fusion = f32[128,2048]{1,0:T(8,128)} fusion(bf16[4,192,2048]{2,1,0:T(8,128)(2,1)} %gather_fusion.6, bf16[4,128,704]{1,2,0:T(8,128)(2,1)S(1)} %gather_fusion.5), kind=kOutput, calls=%fused_computation.7 | convolution fusion | flops 405536768 | bytes 4390912 | tf_op jit(solution)/shard_map/jtc,jcd->jtd/dot_general | solution.py:164
  132.1 2.5 %copy.67 = f32[128,2048]{0,1:T(8,128)} copy(f32[128,2048]{1,0:T(8,128)} %convert_reduce_fusion) | data formatting | bytes 2097152 | tf_op jit(solution)/shard_map/reduce_sum | solution.py:167
  136.1 2.5 %copy.66 = f32[128,2048]{1,0:T(8,128)} copy(f32[128,2048]{0,1:T(8,128)} %bitcast.172) | data formatting | bytes 2097152 | tf_op jit(solution)/shard_map/reshape | solution.py:168
  138.7 1.8 %add.153 = f32[128,2048]{1,0:T(8,128)S(1)} add(f32[128,2048]{1,0:T(8,128)} %copy.66, f32[128,2048]{1,0:T(8,128)} %convert_reduce_fusion) | non-fusion elementwise | flops 262144 | bytes 3145728 | tf_op jit(solution)/shard_map/add | solution.py:168
  142.1 4.0 %convolution_convert_fusion.1 = bf16[128,2048]{1,0:T(8,128)(2,1)} fusion(bf16[640,2048]{1,0:T(8,128)(2,1)S(1)} %copy-done, bf16[2048,640]{1,0:T(8,128)(2,1)} %param.26, f32[128,640]{1,0:T(8,128)S(1)} %fusion.54, f32[128,2048]{1,0:T(8,128)} %copy-done.1, f32[2048]{0:T(1024)S(1)} %copy-done.9, f32[128]{0:T(128)S(1)} %add_rsqrt_fusion), kind=kOutput, calls=%fused_computation.10 | convolution fusion | flops 672628736 | bytes 7152128 | tf_op jit(solution)/shard_map/dot_general | solution.py:176
  148.6 1.9 %collective-permute-start.10 = (bf16[128,512]{1,0:T(8,128)(2,1)S(1)}, bf16[128,512]{1,0:T(8,128)(2,1)S(1)}, u32[]{:S(2)}, u32[]{:S(2)}) collective-permute-start(bf16[128,512]{1,0:T(8,128)(2,1)S(1)} %bitcast.182), channel_id=1, source_target_pairs={{0,2},{1,3},{2,0},{3,1},{4,6},{5,7},{6,4},{7,5},{8,10},{9,11},{10,... | collective-permute-start | bytes 393224 | tf_op jit(solution)/shard_map/ppermute | solution.py:28
  150.5 2.9 %collective-permute-start.11 = (bf16[128,512]{1,0:T(8,128)(2,1)S(1)}, bf16[128,512]{1,0:T(8,128)(2,1)S(1)}, u32[]{:S(2)}, u32[]{:S(2)}) collective-permute-start(bf16[128,512]{1,0:T(8,128)(2,1)S(1)} %bitcast.183), channel_id=1, source_target_pairs={{0,3},{1,0},{2,1},{3,2},{4,7},{5,4},{6,5},{7,6},{8,11},{9,8},{10,9... | collective-permute-start | bytes 393224 | tf_op jit(solution)/shard_map/ppermute | solution.py:28
  155.2 3.7 %collective-permute-done.11 = bf16[128,512]{1,0:T(8,128)(2,1)S(1)} collective-permute-done((bf16[128,512]{1,0:T(8,128)(2,1)S(1)}, bf16[128,512]{1,0:T(8,128)(2,1)S(1)}, u32[]{:S(2)}, u32[]{:S(2)}) %collective-permute-start.11) | collective-permute-done | bytes 131104 | tf_op jit(solution)/shard_map/ppermute | solution.py:28
  158.9 1.8 %fusion.38 = bf16[128,512]{1,0:T(8,128)(2,1)} fusion(bf16[128,512]{1,0:T(8,128)(2,1)S(1)} %collective-permute-done.11, bf16[128,512]{1,0:T(8,128)(2,1)S(1)} %collective-permute-done.10, bf16[128,512]{1,0:T(8,128)(2,1)} %collective-permute-done.9, f32[128,2048]{1,0:T(8,128)} %copy-done.1, s32[]{:T(128)S(6)} %select_n.105, ...), kind=kLoop, calls=%fused_computation.70 | loop fusion | flops 589824 | bytes 917508 | tf_op jit(solution)/shard_map/convert_element_type | solution.py:189
  (101 shorter events, 40.7 us)
Async XLA Ops:
  0.6 141.5 %copy-start = (bf16[640,2048]{1,0:T(8,128)(2,1)S(1)}, bf16[640,2048]{1,0:T(8,128)(2,1)}, u32[]{:S(2)}) copy-start(bf16[640,2048]{1,0:T(8,128)(2,1)} %param.27) | copy-start | bytes 7864324
  0.6 20.1 %copy-start.14 = (s32[8]{0:T(128)S(1)}, s32[8]{0:T(128)}, u32[]{:S(2)}) copy-start(s32[8]{0:T(128)} %param.16) | copy-start | bytes 100
  0.7 20.7 %copy-start.11 = (s32[8,16]{1,0:T(8,128)S(1)}, s32[8,16]{1,0:T(8,128)}, u32[]{:S(2)}) copy-start(s32[8,16]{1,0:T(8,128)} %param.17) | copy-start | bytes 1540
  0.7 56.2 %copy-start.5 = (bf16[2048,192]{0,1:T(8,128)(2,1)S(1)}, bf16[2048,192]{0,1:T(8,128)(2,1)}, u32[]{:S(2)}) copy-start(bf16[2048,192]{0,1:T(8,128)(2,1)} %param.21) | copy-start | bytes 2359300
  5.7 41.6 %all-to-all-start = ((bf16[64,16,512]{2,1,0:T(8,128)(2,1)}), bf16[64,16,512]{2,1,0:T(8,128)(2,1)}, u32[]{:S(2)}, u32[]{:S(2)}) async-start(bf16[64,16,512]{2,1,0:T(8,128)(2,1)} %gather_fusion), calls=%async_computation | async-start | bytes 2097152 | tf_op jit(solution)/shard_map/all_to_all | solution.py:81
  49.2 9.9 %collective-permute-start = (bf16[128,512]{1,0:T(8,128)(2,1)S(1)}, bf16[128,512]{1,0:T(8,128)(2,1)}, u32[]{:S(2)}, u32[]{:S(2)}) collective-permute-start(bf16[128,512]{1,0:T(8,128)(2,1)S(1)} %bitcast.177), channel_id=1, source_target_pairs={{0,1},{1,2},{2,3},{3,0},{4,5},{5,6},{6,7},{7,4},{8,9},{9,10},{10,1... | collective-permute-start | bytes 393224 | tf_op jit(solution)/shard_map/ppermute | solution.py:28
  50.6 9.0 %collective-permute-start.1 = (bf16[128,512]{1,0:T(8,128)(2,1)S(1)}, bf16[128,512]{1,0:T(8,128)(2,1)}, u32[]{:S(2)}, u32[]{:S(2)}) collective-permute-start(bf16[128,512]{1,0:T(8,128)(2,1)S(1)} %bitcast.178), channel_id=1, source_target_pairs={{0,2},{1,3},{2,0},{3,1},{4,6},{5,7},{6,4},{7,5},{8,10},{9,11},{10,... | collective-permute-start | bytes 393224 | tf_op jit(solution)/shard_map/ppermute | solution.py:28
  53.2 6.4 %collective-permute-start.2 = (bf16[128,512]{1,0:T(8,128)(2,1)S(1)}, bf16[128,512]{1,0:T(8,128)(2,1)}, u32[]{:S(2)}, u32[]{:S(2)}) collective-permute-start(bf16[128,512]{1,0:T(8,128)(2,1)S(1)} %bitcast.179), channel_id=1, source_target_pairs={{0,3},{1,0},{2,1},{3,2},{4,7},{5,4},{6,5},{7,6},{8,11},{9,8},{10,9... | collective-permute-start | bytes 393224 | tf_op jit(solution)/shard_map/ppermute | solution.py:28
  58.3 6.7 %copy-start.7 = (f32[4,512]{1,0:T(4,128)S(1)}, f32[4,512]{1,0:T(4,128)}, u32[]{:S(2)}) copy-start(f32[4,512]{1,0:T(4,128)} %mul.96) | copy-start | bytes 24580
  61.5 6.0 %copy-start.10 = (pred[8,256]{1,0:T(8,128)(4,1)S(1)}, pred[8,256]{1,0:T(8,128)(4,1)}, u32[]{:S(2)}) copy-start(pred[8,256]{1,0:T(8,128)(4,1)} %iota_compare_fusion.5) | copy-start | bytes 6148
  67.5 14.6 %copy-start.2 = (bf16[8,16,512]{2,1,0:T(8,128)(2,1)S(1)}, bf16[8,16,512]{2,1,0:T(8,128)(2,1)}, u32[]{:S(2)}) copy-start(bf16[8,16,512]{2,1,0:T(8,128)(2,1)} %param.14) | copy-start | bytes 393220
  68.3 14.6 %copy-start.13 = (s32[8]{0:T(128)S(1)}, s32[8]{0:T(128)}, u32[]{:S(2)}) copy-start(s32[8]{0:T(128)} %copy-done.12) | copy-start | bytes 100
  70.9 24.0 %all-to-all-start.1 = ((bf16[64,16,192]{2,1,0:T(8,128)(2,1)}), bf16[64,16,192]{2,1,0:T(8,128)(2,1)}, u32[]{:S(2)}, u32[]{:S(2)}) async-start(bf16[64,16,192]{2,1,0:T(8,128)(2,1)} %gather_fusion.3), calls=%async_computation.1 | async-start | bytes 1048576 | tf_op jit(solution)/shard_map/all_to_all | solution.py:154
  77.7 23.7 %collective-permute-start.6 = (bf16[192,2048]{1,0:T(8,128)(2,1)}, bf16[192,2048]{1,0:T(8,128)(2,1)S(1)}, u32[]{:S(2)}, u32[]{:S(2)}) collective-permute-start(bf16[192,2048]{1,0:T(8,128)(2,1)} %param.23), channel_id=1, source_target_pairs={{0,1},{1,2},{2,3},{3,0},{4,5},{5,6},{6,7},{7,4},{8,9},{9,10},{10,1... | collective-permute-start | bytes 2359304 | tf_op jit(solution)/shard_map/ppermute | solution.py:28
  78.7 36.4 %collective-permute-start.7 = (bf16[192,2048]{1,0:T(8,128)(2,1)}, bf16[192,2048]{1,0:T(8,128)(2,1)}, u32[]{:S(2)}, u32[]{:S(2)}) collective-permute-start(bf16[192,2048]{1,0:T(8,128)(2,1)} %param.23), channel_id=1, source_target_pairs={{0,2},{1,3},{2,0},{3,1},{4,6},{5,7},{6,4},{7,5},{8,10},{9,11},{10,... | collective-permute-start | bytes 2359304 | tf_op jit(solution)/shard_map/ppermute | solution.py:28
  80.8 35.0 %collective-permute-start.8 = (bf16[192,2048]{1,0:T(8,128)(2,1)}, bf16[192,2048]{1,0:T(8,128)(2,1)}, u32[]{:S(2)}, u32[]{:S(2)}) collective-permute-start(bf16[192,2048]{1,0:T(8,128)(2,1)} %param.23), channel_id=1, source_target_pairs={{0,3},{1,0},{2,1},{3,2},{4,7},{5,4},{6,5},{7,6},{8,11},{9,8},{10,9... | collective-permute-start | bytes 2359304 | tf_op jit(solution)/shard_map/ppermute | solution.py:28
  98.3 25.1 %collective-permute-start.3 = (bf16[128,704]{0,1:T(8,128)(2,1)}, bf16[128,704]{0,1:T(8,128)(2,1)}, u32[]{:S(2)}, u32[]{:S(2)}) collective-permute-start(bf16[128,704]{0,1:T(8,128)(2,1)} %get-tuple-element.15), channel_id=1, source_target_pairs={{0,1},{1,2},{2,3},{3,0},{4,5},{5,6},{6,7},{7,4},{8,9},{9,10},{10,1... | collective-permute-start | bytes 540680 | tf_op jit(solution)/shard_map/ppermute | solution.py:28
  99.2 24.1 %collective-permute-start.4 = (bf16[128,704]{0,1:T(8,128)(2,1)}, bf16[128,704]{0,1:T(8,128)(2,1)}, u32[]{:S(2)}, u32[]{:S(2)}) collective-permute-start(bf16[128,704]{0,1:T(8,128)(2,1)} %get-tuple-element.15), channel_id=1, source_target_pairs={{0,2},{1,3},{2,0},{3,1},{4,6},{5,7},{6,4},{7,5},{8,10},{9,11},{10,... | collective-permute-start | bytes 540680 | tf_op jit(solution)/shard_map/ppermute | solution.py:28
  101.4 22.0 %collective-permute-start.5 = (bf16[128,704]{0,1:T(8,128)(2,1)}, bf16[128,704]{0,1:T(8,128)(2,1)}, u32[]{:S(2)}, u32[]{:S(2)}) collective-permute-start(bf16[128,704]{0,1:T(8,128)(2,1)} %get-tuple-element.15), channel_id=1, source_target_pairs={{0,3},{1,0},{2,1},{3,2},{4,7},{5,4},{6,5},{7,6},{8,11},{9,8},{10,9... | collective-permute-start | bytes 540680 | tf_op jit(solution)/shard_map/ppermute | solution.py:28
  134.6 6.8 %copy-start.9 = (f32[2048]{0:T(1024)S(1)}, f32[2048]{0:T(1024)}, u32[]{:S(2)}) copy-start(f32[2048]{0:T(1024)} %param.24) | copy-start | bytes 24580
  146.1 7.5 %copy-start.15 = (s32[8,8]{1,0:T(8,128)S(1)}, s32[8,8]{1,0:T(8,128)}, u32[]{:S(2)}) copy-start(s32[8,8]{1,0:T(8,128)} %param.18) | copy-start | bytes 772
  148.6 6.5 %collective-permute-start.10 = (bf16[128,512]{1,0:T(8,128)(2,1)S(1)}, bf16[128,512]{1,0:T(8,128)(2,1)S(1)}, u32[]{:S(2)}, u32[]{:S(2)}) collective-permute-start(bf16[128,512]{1,0:T(8,128)(2,1)S(1)} %bitcast.182), channel_id=1, source_target_pairs={{0,2},{1,3},{2,0},{3,1},{4,6},{5,7},{6,4},{7,5},{8,10},{9,11},{10,... | collective-permute-start | bytes 393224 | tf_op jit(solution)/shard_map/ppermute | solution.py:28
  150.5 8.3 %collective-permute-start.11 = (bf16[128,512]{1,0:T(8,128)(2,1)S(1)}, bf16[128,512]{1,0:T(8,128)(2,1)S(1)}, u32[]{:S(2)}, u32[]{:S(2)}) collective-permute-start(bf16[128,512]{1,0:T(8,128)(2,1)S(1)} %bitcast.183), channel_id=1, source_target_pairs={{0,3},{1,0},{2,1},{3,2},{4,7},{5,4},{6,5},{7,6},{8,11},{9,8},{10,9... | collective-permute-start | bytes 393224 | tf_op jit(solution)/shard_map/ppermute | solution.py:28
  153.5 5.4 %collective-permute-start.9 = (bf16[128,512]{1,0:T(8,128)(2,1)S(1)}, bf16[128,512]{1,0:T(8,128)(2,1)}, u32[]{:S(2)}, u32[]{:S(2)}) collective-permute-start(bf16[128,512]{1,0:T(8,128)(2,1)S(1)} %bitcast.184), channel_id=1, source_target_pairs={{0,1},{1,2},{2,3},{3,0},{4,5},{5,6},{6,7},{7,4},{8,9},{9,10},{10,1... | collective-permute-start | bytes 393224 | tf_op jit(solution)/shard_map/ppermute | solution.py:28
  (6 other events, 17.1 us)

commit v2 on v1

--- a/solution.py
+++ b/solution.py
@@ -4,6 +4,7 @@
 import jax.numpy as jnp
 from jax import lax
 from jax.sharding import PartitionSpec as P
+
 
 HEAD_DIM = 64
 
@@ -17,7 +18,7 @@
         tree_links[:, :, None] == jnp.arange(tokens, dtype=jnp.int32)[None, None, :]
     ).astype(jnp.float32)
     reachable = jnp.maximum(parent_link, jnp.eye(tokens, dtype=jnp.float32)[None])
-    for squaring in range(max(tokens - 1, 1).bit_length()):
+    for _ in range(max(tokens - 1, 1).bit_length()):
         reachable = jnp.minimum(
             jnp.einsum("rij,rjk->rik", reachable, reachable, precision=HIGH), 1.0
         )
@@ -28,11 +29,17 @@
     return lax.ppermute(value, "mlp", [(i, (i + shift) % count) for i in range(count)])
 
 
-def gather_mlp(value, count, part_index):
-    pieces = [value] + [shift_mlp(value, k, count) for k in range(1, count)]
-    stacked = jnp.stack(pieces)
-    order = (part_index - jnp.arange(count, dtype=jnp.int32)) % count
-    return jnp.take(stacked, order, axis=0, mode="clip")
+def stack_mlp(value, count):
+    return jnp.stack([value] + [shift_mlp(value, k, count) for k in range(1, count)])
+
+
+def place_blocks(stacked, count, part_index):
+    width = stacked.shape[-1]
+    full = jnp.zeros(stacked.shape[1:-1] + (width * count,), stacked.dtype)
+    for k in range(count):
+        offset = ((part_index - k) % count) * width
+        full = lax.dynamic_update_slice_in_dim(full, stacked[k], offset, full.ndim - 1)
+    return full
 
 
 def per_device(
@@ -56,9 +63,8 @@
     my_index = lax.axis_index("req")
     part_index = lax.axis_index("mlp")
     per_owner_rows, tokens, quarter = drafts.shape
-    model_dim = quarter * mlp_count
-
-    w_out_all = gather_mlp(w_out, mlp_count, part_index)
+
+    w_out_all = stack_mlp(w_out, mlp_count)
 
     local_ids = jnp.arange(per_owner_rows, dtype=jnp.int32)
     devices = jnp.arange(req_count, dtype=jnp.int32)
@@ -82,28 +88,22 @@
     local_rows = jnp.take(incoming, source_of, axis=0, mode="clip")
 
     rows = per_owner_rows * tokens
-    full_rows = gather_mlp(local_rows.reshape(rows, quarter), mlp_count, part_index)
+    full_rows = place_blocks(
+        stack_mlp(local_rows.reshape(rows, quarter), mlp_count), mlp_count, part_index
+    )
     wide_rows = full_rows.astype(jnp.float32)
-    square_mean = jnp.sum(wide_rows * wide_rows, axis=(0, 2)) / model_dim
-    attn_scale = lax.rsqrt(square_mean + EPS)
     normalized_rows = (
-        wide_rows * attn_scale[None, :, None] * attn_gain.reshape(mlp_count, 1, quarter)
+        wide_rows
+        * lax.rsqrt(jnp.mean(wide_rows * wide_rows, axis=1, keepdims=True) + EPS)
+        * attn_gain
     ).astype(jnp.bfloat16)
     kv_heads = key_value_weight.shape[1] // (2 * HEAD_DIM)
     group_heads = query_weight.shape[1] // (kv_heads * HEAD_DIM)
-    query_rows = jnp.einsum(
-        "jtf,jfc->tc",
-        normalized_rows,
-        query_weight.reshape(mlp_count, quarter, -1),
-        preferred_element_type=jnp.float32,
-    ).reshape(per_owner_rows, tokens, kv_heads, group_heads, HEAD_DIM)
+    query_rows = jnp.dot(normalized_rows, query_weight, preferred_element_type=jnp.float32).reshape(
+        per_owner_rows, tokens, kv_heads, group_heads, HEAD_DIM
+    )
     new_key_value = (
-        jnp.einsum(
-            "jtf,jfc->tc",
-            normalized_rows,
-            key_value_weight.reshape(mlp_count, quarter, -1),
-            preferred_element_type=jnp.float32,
-        )
+        jnp.dot(normalized_rows, key_value_weight, preferred_element_type=jnp.float32)
         .astype(jnp.bfloat16)
         .reshape(per_owner_rows, tokens, kv_heads, 2 * HEAD_DIM)
     )
@@ -157,33 +157,34 @@
     packed = jnp.concatenate(
         [back_rows.reshape(rows, head_width), drafts.reshape(rows, quarter)], axis=1
     )
-    gathered = gather_mlp(packed, mlp_count, part_index)
+    gathered = stack_mlp(packed, mlp_count)
     heads_all = gathered[:, :, :head_width]
-    owned_all = gathered[:, :, head_width:].astype(jnp.float32)
+    owned_all = place_blocks(gathered[:, :, head_width:], mlp_count, part_index)
 
     group_products = jnp.einsum(
         "jtc,jcd->jtd", heads_all, w_out_all, preferred_element_type=jnp.float32
     )
     attn_sum = jnp.sum(group_products.astype(jnp.bfloat16).astype(jnp.float32), axis=0)
-    residual = jnp.transpose(owned_all, (1, 0, 2)).reshape(rows, model_dim) + attn_sum
+    residual = owned_all.astype(jnp.float32) + attn_sum
     normed_two = (
         residual * lax.rsqrt(jnp.mean(residual * residual, axis=1, keepdims=True) + EPS) * mlp_gain
     ).astype(jnp.bfloat16)
     gate_out = jnp.dot(normed_two, w_gate, preferred_element_type=jnp.float32)
     up_out = jnp.dot(normed_two, w_up, preferred_element_type=jnp.float32)
     hidden = (jax.nn.silu(gate_out) * up_out).astype(jnp.bfloat16)
-    unit_part = (
-        jnp.dot(hidden, w_down, preferred_element_type=jnp.float32)
-        .astype(jnp.bfloat16)
-        .reshape(rows, mlp_count, quarter)
-    )
-
-    unit_share = lax.dynamic_index_in_dim(unit_part, part_index, 1, keepdims=False).astype(
+    unit_part = jnp.einsum(
+        "tu,ujd->jtd",
+        hidden,
+        w_down.reshape(w_down.shape[0], mlp_count, quarter),
+        preferred_element_type=jnp.float32,
+    ).astype(jnp.bfloat16)
+
+    unit_share = lax.dynamic_index_in_dim(unit_part, part_index, 0, keepdims=False).astype(
         jnp.float32
     )
     for k in range(1, mlp_count):
         target = (part_index + k) % mlp_count
-        piece = lax.dynamic_index_in_dim(unit_part, target, 1, keepdims=False)
+        piece = lax.dynamic_index_in_dim(unit_part, target, 0, keepdims=False)
         unit_share = unit_share + shift_mlp(piece, k, mlp_count).astype(jnp.float32)
     residual_share = lax.dynamic_slice_in_dim(residual, part_index * quarter, quarter, 1)
     result = (residual_share + unit_share).astype(jnp.bfloat16)

time: 163 us -> 152 us (0.933)
  other arithmetic: 21.9 us -> 6.55 us
  waiting for transfers between devices: 54.5 us -> 68.7 us
  local copies, waits for them, and re-layouts: 28.7 us -> 21.3 us
    ppermute x12, waiting for transfers between devices: 17.4 us -> 29.9 us  [shift_mlp(): lax.ppermute(value, 'mlp', [(i, (i + shift) % count) for i in range(count)])]
    squeeze x0 -> x9, local copies, waits for them, and re-layouts: none -> 9.85 us  [the longest x8 9.15 us: place_blocks(): stacked[k]]
    gather x3 -> x0, local copies, waits for them, and re-layouts: 8.11 us -> none  [gather_mlp(): return jnp.take(stacked, order, axis=0, mode='clip')]
    another operation x4 -> x1, other arithmetic: 8.73 us -> 0.72 us  [stack_mlp(): jnp.stack([value] + [shift_mlp(value, k, count) for k in range(1, count)])]
    reshape x3 -> x0, local copies, waits for them, and re-layouts: 5.43 us -> none  [the longest x1 2.53 us: per_device(): jnp.transpose(owned_all, (1, 0, 2)).reshape(rows, model_dim) + attn_sum]
    reduce_sum x1 -> x0, local copies, waits for them, and re-layouts: 2.53 us -> none  [per_device(): jnp.sum(group_products.astype(jnp.bfloat16).astype(jnp.float32), axis=0)]
    dynamic_update_slice x0 -> x8, local copies, waits for them, and re-layouts: none -> 1.93 us  [place_blocks(): lax.dynamic_update_slice_in_dim(full, stacked[k], offset, full.ndim - 1)]
    add x1 -> x0, other arithmetic: 1.8 us -> none  [per_device(): jnp.transpose(owned_all, (1, 0, 2)).reshape(rows, model_dim) + attn_sum]
  transfers between devices with their start and end apart: 14 -> 14, of which waited for: 6 -> 8; matrix products, arithmetic and copies ran while one was open for 13% -> 11% of each run, Pallas kernels for 0% -> 0%
where the time goes in v2:
time: 152 us; the launch traced here: 150 us
  waiting for transfers between devices  68.7 us (45%)
  starting transfers between devices  37.7 us (25%)
  local copies, waits for them, and re-layouts  21.3 us (14%)
  matrix products  15 us (10%)
  other arithmetic  6.55 us (4%)
    ppermute x12, waiting for transfers between devices, shift_mlp(): lax.ppermute(value, 'mlp', [(i, (i + shift) % count) for i in range(count)])  29.9 us
    all_to_all x1, waiting for transfers between devices, per_device(): incoming = lax.all_to_all(outgoing, 'req', 0, 0, tiled=True)  26.8 us
    ppermute x12, starting transfers between devices, shift_mlp(): lax.ppermute(value, 'mlp', [(i, (i + shift) % count) for i in range(count)])  17.6 us
    all_to_all x1, starting transfers between devices, per_device(): incoming = lax.all_to_all(outgoing, 'req', 0, 0, tiled=True)  13.3 us
    all_to_all x1, waiting for transfers between devices, per_device(): arrived = lax.all_to_all(returning, 'req', 0, 0, tiled=True)  12.1 us
    squeeze x8, local copies, waits for them, and re-layouts, place_blocks(): stacked[k]  9.15 us
    all_to_all x1, starting transfers between devices, per_device(): arrived = lax.all_to_all(returning, 'req', 0, 0, tiled=True)  6.75 us
    dot_general x1, matrix products, per_device(): jnp.einsum('tu,ujd->jtd', hidden, w_down.reshape(w_down.shape[0], mlp_cou...  3.16 us
  transfers between devices with their start and end apart: 14, of which 8 were waited for; matrix products, arithmetic and copies ran while one was open for 11% of the time, Pallas kernels for 0%

profile of v2, /device:TPU:1, one launch (start us, length us, event | category | flops | bytes accessed | tf_op | source)
XLA Modules:
  0.0 150.4 jit_solution(726367455371044458)
XLA Ops:
  3.1 2.6 %gather_fusion = bf16[64,16,512]{2,1,0:T(8,128)(2,1)} fusion(bf16[8,16,512]{2,1,0:T(8,128)(2,1)} %param.14, s32[1024]{0:T(1024)S(1)} %pad_clamp_fusion.3), kind=kCustom, calls=%fused_computation | custom fusion | bytes 2097408 | tf_op jit(solution)/shard_map/jit(_take)/gather | solution.py:86
  5.6 13.3 %all-to-all-start = ((bf16[64,16,512]{2,1,0:T(8,128)(2,1)}), bf16[64,16,512]{2,1,0:T(8,128)(2,1)}, u32[]{:S(2)}, u32[]{:S(2)}) async-start(bf16[64,16,512]{2,1,0:T(8,128)(2,1)} %gather_fusion), calls=%async_computation | async-start | bytes 2097152 | tf_op jit(solution)/shard_map/all_to_all | solution.py:87
  20.6 26.8 %all-to-all-done = bf16[64,16,512]{2,1,0:T(8,128)(2,1)} async-done(((bf16[64,16,512]{2,1,0:T(8,128)(2,1)}), bf16[64,16,512]{2,1,0:T(8,128)(2,1)}, u32[]{:S(2)}, u32[]{:S(2)}) %all-to-all-start) | async-done | bytes 1048608 | tf_op jit(solution)/shard_map/all_to_all | solution.py:87
  47.4 1.8 %gather_fusion.1 = bf16[8,16,512]{2,1,0:T(8,128)(2,1)S(1)} fusion(bf16[64,16,512]{2,1,0:T(8,128)(2,1)} %all-to-all-done, s32[1024]{0:T(1024)S(1)} %pad_clamp_fusion.2), kind=kCustom, calls=%fused_computation.1 | custom fusion | bytes 262176 | tf_op jit(solution)/shard_map/jit(_take)/gather | solution.py:88
  51.3 2.7 %collective-permute-start.1 = (bf16[128,512]{1,0:T(8,128)(2,1)S(1)}, bf16[128,512]{1,0:T(8,128)(2,1)S(1)}, u32[]{:S(2)}, u32[]{:S(2)}) collective-permute-start(bf16[128,512]{1,0:T(8,128)(2,1)S(1)} %bitcast.141), channel_id=1, source_target_pairs={{0,2},{1,3},{2,0},{3,1},{4,6},{5,7},{6,4},{7,5},{8,10},{9,11},{10,... | collective-permute-start | bytes 393224 | tf_op jit(solution)/shard_map/ppermute | solution.py:29
  55.6 3.9 %collective-permute-done.1 = bf16[128,512]{1,0:T(8,128)(2,1)S(1)} collective-permute-done((bf16[128,512]{1,0:T(8,128)(2,1)S(1)}, bf16[128,512]{1,0:T(8,128)(2,1)S(1)}, u32[]{:S(2)}, u32[]{:S(2)}) %collective-permute-start.1) | collective-permute-done | bytes 131104 | tf_op jit(solution)/shard_map/ppermute | solution.py:29
  59.7 2.0 %convolution_convert_fusion = bf16[128,128]{1,0:T(8,128)(2,1)} fusion(bf16[2048,128]{1,0:T(8,128)(2,1)} %param.22, bf16[128,2048]{1,0:T(8,128)(2,1)S(1)} %constant_dynamic-update-slice_fusion.4, f32[2048]{0:T(1024)S(1)} %copy-done.12, f32[128]{0:T(128)S(1)} %add_rsqrt_fusion.1), kind=kOutput, calls=%fused_computation.37 | convolution fusion | flops 68173824 | bytes 1090048 | tf_op jit(solution)/shard_map/dot_general | solution.py:106
  68.0 6.7 %all-to-all-start.1 = ((bf16[64,16,192]{2,1,0:T(8,128)(2,1)}), bf16[64,16,192]{2,1,0:T(8,128)(2,1)S(1)}, u32[]{:S(2)}, u32[]{:S(2)}) async-start(bf16[64,16,192]{2,1,0:T(8,128)(2,1)} %gather_fusion.2), calls=%async_computation.1 | async-start | bytes 1048576 | tf_op jit(solution)/shard_map/all_to_all | solution.py:154
  76.4 2.1 %collective-permute-start.7 = (bf16[192,2048]{1,0:T(8,128)(2,1)}, bf16[192,2048]{1,0:T(8,128)(2,1)}, u32[]{:S(2)}, u32[]{:S(2)}) collective-permute-start(bf16[192,2048]{1,0:T(8,128)(2,1)} %param.23), channel_id=1, source_target_pairs={{0,2},{1,3},{2,0},{3,1},{4,6},{5,7},{6,4},{7,5},{8,10},{9,11},{10,... | collective-permute-start | bytes 2359304 | tf_op jit(solution)/shard_map/ppermute | solution.py:29
  80.0 12.1 %all-to-all-done.1 = bf16[64,16,192]{2,1,0:T(8,128)(2,1)S(1)} async-done(((bf16[64,16,192]{2,1,0:T(8,128)(2,1)}), bf16[64,16,192]{2,1,0:T(8,128)(2,1)S(1)}, u32[]{:S(2)}, u32[]{:S(2)}) %all-to-all-start.1) | async-done | bytes 393248 | tf_op jit(solution)/shard_map/all_to_all | solution.py:154
  94.9 2.1 %collective-permute-start.4 = (bf16[128,704]{0,1:T(8,128)(2,1)}, bf16[128,704]{0,1:T(8,128)(2,1)}, u32[]{:S(2)}, u32[]{:S(2)}) collective-permute-start(bf16[128,704]{0,1:T(8,128)(2,1)} %get-tuple-element.14), channel_id=1, source_target_pairs={{0,2},{1,3},{2,0},{3,1},{4,6},{5,7},{6,4},{7,5},{8,10},{9,11},{10,... | collective-permute-start | bytes 540680 | tf_op jit(solution)/shard_map/ppermute | solution.py:29
  97.3 20.8 %collective-permute-done.3 = bf16[128,704]{0,1:T(8,128)(2,1)} collective-permute-done((bf16[128,704]{0,1:T(8,128)(2,1)}, bf16[128,704]{0,1:T(8,128)(2,1)}, u32[]{:S(2)}, u32[]{:S(2)}) %collective-permute-start.3) | collective-permute-done | bytes 180256 | tf_op jit(solution)/shard_map/ppermute | solution.py:29
  118.1 1.6 %slice_bitcast_fusion.2 = bf16[128,512]{0,1:T(8,128)(2,1)} fusion(bf16[1,128,704]{1,2,0:T(8,128)(2,1)} %bitcast.33), kind=kLoop, calls=%fused_computation.79 | loop fusion | bytes 262144 | tf_op jit(solution)/shard_map/squeeze | solution.py:41
  120.7 1.6 %slice_bitcast_fusion.1 = bf16[128,512]{0,1:T(8,128)(2,1)} fusion(bf16[1,128,704]{1,2,0:T(8,128)(2,1)} %bitcast.35), kind=kLoop, calls=%fused_computation.78 | loop fusion | bytes 262144 | tf_op jit(solution)/shard_map/squeeze | solution.py:41
  122.3 1.7 %copy.57 = bf16[128,512]{1,0:T(8,128)(2,1)} copy(bf16[128,512]{0,1:T(8,128)(2,1)} %slice_bitcast_fusion.1) | data formatting | bytes 262144 | tf_op jit(solution)/shard_map/squeeze | solution.py:41
  123.9 1.6 %slice_bitcast_fusion = bf16[128,512]{0,1:T(8,128)(2,1)} fusion(bf16[1,128,704]{1,2,0:T(8,128)(2,1)} %bitcast.37), kind=kLoop, calls=%fused_computation.77 | loop fusion | bytes 262144 | tf_op jit(solution)/shard_map/squeeze | solution.py:41
  125.5 1.7 %copy.58 = bf16[128,512]{1,0:T(8,128)(2,1)} copy(bf16[128,512]{0,1:T(8,128)(2,1)} %slice_bitcast_fusion) | data formatting | bytes 262144 | tf_op jit(solution)/shard_map/squeeze | solution.py:41
  129.1 2.8 %convert_reduce_fusion = f32[128,2048]{1,0:T(8,128)S(1)} fusion(bf16[1,192,2048]{2,1,0:T(8,128)(2,1)} %bitcast.42, bf16[1,192,2048]{2,1,0:T(8,128)(2,1)} %bitcast.41, bf16[1,192,2048]{2,1,0:T(8,128)(2,1)} %bitcast.40, bf16[1,192,2048]{2,1,0:T(8,128)(2,1)} %bitcast.150, bf16[1,128,704]{1,2,0:T(8,128)(2,1)} %bitcast.37, bf16[1,128,704]{1,2,0:T(8,128)(2,1)} %bitcast.35, ...), kind=kOutput, calls=%fused_computation.4 | convolution fusion | flops 411041792 | bytes 4915200 | tf_op jit(solution)/shard_map/jtc,jcd->jtd/dot_general | solution.py:164
  134.6 3.2 %fusion.14 = bf16[128,4,512]{2,0,1:T(8,128)(2,1)S(1)} fusion(bf16[80,4,8,512]{3,2,1,0:T(8,128)(2,1)} %bitcast.149, bf16[2048,640]{1,0:T(8,128)(2,1)S(1)} %copy-done, f32[128,640]{1,0:T(8,128)S(1)} %fusion.66, f32[128,2048]{1,0:T(8,128)} %copy-done.2, f32[2048]{0:T(1024)S(1)} %copy-done.6, f32[128]{0:T(128)S(1)} %add_rsqrt_fusion), kind=kOutput, calls=%fused_computation.19 | convolution fusion | flops 672628736 | bytes 7152128 | tf_op jit(solution)/shard_map/tu,ujd->jtd/dot_general | solution.py:175
  139.6 2.7 %collective-permute-start.11 = (bf16[128,512]{1,0:T(8,128)(2,1)S(1)}, bf16[128,512]{1,0:T(8,128)(2,1)}, u32[]{:S(2)}, u32[]{:S(2)}) collective-permute-start(bf16[128,512]{1,0:T(8,128)(2,1)S(1)} %get-tuple-element.11), channel_id=1, source_target_pairs={{0,3},{1,0},{2,1},{3,2},{4,7},{5,4},{6,5},{7,6},{8,11},{9,8},{10,9... | collective-permute-start | bytes 393224 | tf_op jit(solution)/shard_map/ppermute | solution.py:29
  142.3 1.6 %fusion.26 = bf16[8,8,1,128]{3,1,2,0:T(8,128)(2,1)} fusion(bf16[8,16,128]{2,1,0:T(8,128)(2,1)} %bitcast.147, s32[8,8]{1,0:T(8,128)S(1)} %copy-done.13), kind=kOutput, calls=%fused_computation.40 | convolution fusion | flops 271360 | bytes 49408 | tf_op jit(solution)/shard_map/rat,rtkd->rakd/dot_general | solution.py:113
  144.0 1.9 %collective-permute-done.11 = bf16[128,512]{1,0:T(8,128)(2,1)} collective-permute-done((bf16[128,512]{1,0:T(8,128)(2,1)S(1)}, bf16[128,512]{1,0:T(8,128)(2,1)}, u32[]{:S(2)}, u32[]{:S(2)}) %collective-permute-start.11) | collective-permute-done | bytes 131104 | tf_op jit(solution)/shard_map/ppermute | solution.py:29
  145.9 2.6 %collective-permute-done.9 = bf16[128,512]{1,0:T(8,128)(2,1)} collective-permute-done((bf16[128,512]{1,0:T(8,128)(2,1)S(1)}, bf16[128,512]{1,0:T(8,128)(2,1)}, u32[]{:S(2)}, u32[]{:S(2)}) %collective-permute-start.9) | collective-permute-done | bytes 131104 | tf_op jit(solution)/shard_map/ppermute | solution.py:29
  148.6 1.8 %fusion.46 = bf16[128,512]{1,0:T(8,128)(2,1)} fusion(bf16[128,512]{1,0:T(8,128)(2,1)} %collective-permute-done.11, bf16[128,512]{1,0:T(8,128)(2,1)S(1)} %collective-permute-done.10, bf16[128,512]{1,0:T(8,128)(2,1)} %collective-permute-done.9, f32[128,2048]{1,0:T(8,128)} %copy-done.2, s32[]{:T(128)S(6)} %select_n.135, bf16[128,4,512]{2,0,1:T(8,128)(2,1)S(1)} %fusion.14, ...), kind=kLoop, calls=%fused_computation.64 | loop fusion | flops 589824 | bytes 917512 | tf_op jit(solution)/shard_map/convert_element_type | solution.py:190
  (97 shorter events, 27.7 us)
Async XLA Ops:
  0.6 134.0 %copy-start = (bf16[2048,640]{1,0:T(8,128)(2,1)S(1)}, bf16[2048,640]{1,0:T(8,128)(2,1)}, u32[]{:S(2)}) copy-start(bf16[2048,640]{1,0:T(8,128)(2,1)} %param.26) | copy-start | bytes 7864324
  0.6 18.4 %copy-start.10 = (s32[8]{0:T(128)S(1)}, s32[8]{0:T(128)}, u32[]{:S(2)}) copy-start(s32[8]{0:T(128)} %param.16) | copy-start | bytes 100
  0.7 19.1 %copy-start.7 = (s32[8,16]{1,0:T(8,128)S(1)}, s32[8,16]{1,0:T(8,128)}, u32[]{:S(2)}) copy-start(s32[8,16]{1,0:T(8,128)} %param.17) | copy-start | bytes 1540
  5.6 54.1 %copy-start.12 = (f32[2048]{0:T(1024)S(1)}, f32[2048]{0:T(1024)}, u32[]{:S(2)}) copy-start(f32[2048]{0:T(1024)} %param.20) | copy-start | bytes 24580
  5.6 41.7 %all-to-all-start = ((bf16[64,16,512]{2,1,0:T(8,128)(2,1)}), bf16[64,16,512]{2,1,0:T(8,128)(2,1)}, u32[]{:S(2)}, u32[]{:S(2)}) async-start(bf16[64,16,512]{2,1,0:T(8,128)(2,1)} %gather_fusion), calls=%async_computation | async-start | bytes 2097152 | tf_op jit(solution)/shard_map/all_to_all | solution.py:87
  49.2 6.4 %collective-permute-start = (bf16[128,512]{1,0:T(8,128)(2,1)S(1)}, bf16[128,512]{1,0:T(8,128)(2,1)S(1)}, u32[]{:S(2)}, u32[]{:S(2)}) collective-permute-start(bf16[128,512]{1,0:T(8,128)(2,1)S(1)} %bitcast.140), channel_id=1, source_target_pairs={{0,1},{1,2},{2,3},{3,0},{4,5},{5,6},{6,7},{7,4},{8,9},{9,10},{10,1... | collective-permute-start | bytes 393224 | tf_op jit(solution)/shard_map/ppermute | solution.py:29
  51.3 10.5 %copy-start.11 = (bf16[2048,192]{0,1:T(8,128)(2,1)S(1)}, bf16[2048,192]{0,1:T(8,128)(2,1)}, u32[]{:S(2)}) copy-start(bf16[2048,192]{0,1:T(8,128)(2,1)} %param.21) | copy-start | bytes 2359300
  51.3 8.2 %collective-permute-start.1 = (bf16[128,512]{1,0:T(8,128)(2,1)S(1)}, bf16[128,512]{1,0:T(8,128)(2,1)S(1)}, u32[]{:S(2)}, u32[]{:S(2)}) collective-permute-start(bf16[128,512]{1,0:T(8,128)(2,1)S(1)} %bitcast.141), channel_id=1, source_target_pairs={{0,2},{1,3},{2,0},{3,1},{4,6},{5,7},{6,4},{7,5},{8,10},{9,11},{10,... | collective-permute-start | bytes 393224 | tf_op jit(solution)/shard_map/ppermute | solution.py:29
  54.0 5.5 %collective-permute-start.2 = (bf16[128,512]{1,0:T(8,128)(2,1)S(1)}, bf16[128,512]{1,0:T(8,128)(2,1)S(1)}, u32[]{:S(2)}, u32[]{:S(2)}) collective-permute-start(bf16[128,512]{1,0:T(8,128)(2,1)S(1)} %bitcast.142), channel_id=1, source_target_pairs={{0,3},{1,0},{2,1},{3,2},{4,7},{5,4},{6,5},{7,6},{8,11},{9,8},{10,9... | collective-permute-start | bytes 393224 | tf_op jit(solution)/shard_map/ppermute | solution.py:29
  55.1 8.7 %copy-start.4 = (bf16[8,256,1,128]{3,1,2,0:T(8,128)(2,1)S(1)}, bf16[8,256,1,128]{3,1,2,0:T(8,128)(2,1)}, u32[]{:S(2)}) copy-start(bf16[8,256,1,128]{3,1,2,0:T(8,128)(2,1)} %param.19) | copy-start | bytes 1572868
  65.3 14.6 %copy-start.1 = (bf16[8,16,512]{2,1,0:T(8,128)(2,1)S(1)}, bf16[8,16,512]{2,1,0:T(8,128)(2,1)}, u32[]{:S(2)}) copy-start(bf16[8,16,512]{2,1,0:T(8,128)(2,1)} %param.14) | copy-start | bytes 393220
  65.5 14.5 %copy-start.9 = (s32[8]{0:T(128)S(1)}, s32[8]{0:T(128)}, u32[]{:S(2)}) copy-start(s32[8]{0:T(128)} %copy-done.8) | copy-start | bytes 100
  68.0 24.0 %all-to-all-start.1 = ((bf16[64,16,192]{2,1,0:T(8,128)(2,1)}), bf16[64,16,192]{2,1,0:T(8,128)(2,1)S(1)}, u32[]{:S(2)}, u32[]{:S(2)}) async-start(bf16[64,16,192]{2,1,0:T(8,128)(2,1)} %gather_fusion.2), calls=%async_computation.1 | async-start | bytes 1048576 | tf_op jit(solution)/shard_map/all_to_all | solution.py:154
  74.8 54.2 %collective-permute-start.6 = (bf16[192,2048]{1,0:T(8,128)(2,1)}, bf16[192,2048]{1,0:T(8,128)(2,1)}, u32[]{:S(2)}, u32[]{:S(2)}) collective-permute-start(bf16[192,2048]{1,0:T(8,128)(2,1)} %param.23), channel_id=1, source_target_pairs={{0,1},{1,2},{2,3},{3,0},{4,5},{5,6},{6,7},{7,4},{8,9},{9,10},{10,1... | collective-permute-start | bytes 2359304 | tf_op jit(solution)/shard_map/ppermute | solution.py:29
  76.4 52.7 %collective-permute-start.7 = (bf16[192,2048]{1,0:T(8,128)(2,1)}, bf16[192,2048]{1,0:T(8,128)(2,1)}, u32[]{:S(2)}, u32[]{:S(2)}) collective-permute-start(bf16[192,2048]{1,0:T(8,128)(2,1)} %param.23), channel_id=1, source_target_pairs={{0,2},{1,3},{2,0},{3,1},{4,6},{5,7},{6,4},{7,5},{8,10},{9,11},{10,... | collective-permute-start | bytes 2359304 | tf_op jit(solution)/shard_map/ppermute | solution.py:29
  78.5 50.6 %collective-permute-start.8 = (bf16[192,2048]{1,0:T(8,128)(2,1)}, bf16[192,2048]{1,0:T(8,128)(2,1)}, u32[]{:S(2)}, u32[]{:S(2)}) collective-permute-start(bf16[192,2048]{1,0:T(8,128)(2,1)} %param.23), channel_id=1, source_target_pairs={{0,3},{1,0},{2,1},{3,2},{4,7},{5,4},{6,5},{7,6},{8,11},{9,8},{10,9... | collective-permute-start | bytes 2359304 | tf_op jit(solution)/shard_map/ppermute | solution.py:29
  93.5 24.6 %collective-permute-start.3 = (bf16[128,704]{0,1:T(8,128)(2,1)}, bf16[128,704]{0,1:T(8,128)(2,1)}, u32[]{:S(2)}, u32[]{:S(2)}) collective-permute-start(bf16[128,704]{0,1:T(8,128)(2,1)} %get-tuple-element.14), channel_id=1, source_target_pairs={{0,1},{1,2},{2,3},{3,0},{4,5},{5,6},{6,7},{7,4},{8,9},{9,10},{10,1... | collective-permute-start | bytes 540680 | tf_op jit(solution)/shard_map/ppermute | solution.py:29
  94.9 25.7 %collective-permute-start.4 = (bf16[128,704]{0,1:T(8,128)(2,1)}, bf16[128,704]{0,1:T(8,128)(2,1)}, u32[]{:S(2)}, u32[]{:S(2)}) collective-permute-start(bf16[128,704]{0,1:T(8,128)(2,1)} %get-tuple-element.14), channel_id=1, source_target_pairs={{0,2},{1,3},{2,0},{3,1},{4,6},{5,7},{6,4},{7,5},{8,10},{9,11},{10,... | collective-permute-start | bytes 540680 | tf_op jit(solution)/shard_map/ppermute | solution.py:29
  118.1 5.8 %collective-permute-start.5 = (bf16[128,704]{0,1:T(8,128)(2,1)}, bf16[128,704]{0,1:T(8,128)(2,1)}, u32[]{:S(2)}, u32[]{:S(2)}) collective-permute-start(bf16[128,704]{0,1:T(8,128)(2,1)} %get-tuple-element.14), channel_id=1, source_target_pairs={{0,3},{1,0},{2,1},{3,2},{4,7},{5,4},{6,5},{7,6},{8,11},{9,8},{10,9... | collective-permute-start | bytes 540680 | tf_op jit(solution)/shard_map/ppermute | solution.py:29
  129.1 4.0 %copy-start.6 = (f32[2048]{0:T(1024)S(1)}, f32[2048]{0:T(1024)}, u32[]{:S(2)}) copy-start(f32[2048]{0:T(1024)} %param.24) | copy-start | bytes 24580
  134.6 7.7 %copy-start.13 = (s32[8,8]{1,0:T(8,128)S(1)}, s32[8,8]{1,0:T(8,128)}, u32[]{:S(2)}) copy-start(s32[8,8]{1,0:T(8,128)} %param.18) | copy-start | bytes 772
  138.5 5.5 %collective-permute-start.10 = (bf16[128,512]{1,0:T(8,128)(2,1)}, bf16[128,512]{1,0:T(8,128)(2,1)S(1)}, u32[]{:S(2)}, u32[]{:S(2)}) collective-permute-start(bf16[128,512]{1,0:T(8,128)(2,1)} %get-tuple-element.12), channel_id=1, source_target_pairs={{0,2},{1,3},{2,0},{3,1},{4,6},{5,7},{6,4},{7,5},{8,10},{9,11},{10,... | collective-permute-start | bytes 393224 | tf_op jit(solution)/shard_map/ppermute | solution.py:29
  139.6 6.3 %collective-permute-start.11 = (bf16[128,512]{1,0:T(8,128)(2,1)S(1)}, bf16[128,512]{1,0:T(8,128)(2,1)}, u32[]{:S(2)}, u32[]{:S(2)}) collective-permute-start(bf16[128,512]{1,0:T(8,128)(2,1)S(1)} %get-tuple-element.11), channel_id=1, source_target_pairs={{0,3},{1,0},{2,1},{3,2},{4,7},{5,4},{6,5},{7,6},{8,11},{9,8},{10,9... | collective-permute-start | bytes 393224 | tf_op jit(solution)/shard_map/ppermute | solution.py:29
  142.3 6.2 %collective-permute-start.9 = (bf16[128,512]{1,0:T(8,128)(2,1)S(1)}, bf16[128,512]{1,0:T(8,128)(2,1)}, u32[]{:S(2)}, u32[]{:S(2)}) collective-permute-start(bf16[128,512]{1,0:T(8,128)(2,1)S(1)} %get-tuple-element.10), channel_id=1, source_target_pairs={{0,1},{1,2},{2,3},{3,0},{4,5},{5,6},{6,7},{7,4},{8,9},{9,10},{10,1... | collective-permute-start | bytes 393224 | tf_op jit(solution)/shard_map/ppermute | solution.py:29
  (4 other events, 7.3 us)

commit v3 on v2

--- a/solution.py
+++ b/solution.py
@@ -29,16 +29,16 @@
     return lax.ppermute(value, "mlp", [(i, (i + shift) % count) for i in range(count)])
 
 
-def stack_mlp(value, count):
-    return jnp.stack([value] + [shift_mlp(value, k, count) for k in range(1, count)])
-
-
-def place_blocks(stacked, count, part_index):
-    width = stacked.shape[-1]
-    full = jnp.zeros(stacked.shape[1:-1] + (width * count,), stacked.dtype)
-    for k in range(count):
+def pieces_mlp(value, count):
+    return [value] + [shift_mlp(value, k, count) for k in range(1, count)]
+
+
+def place_blocks(pieces, count, part_index):
+    width = pieces[0].shape[-1]
+    full = jnp.zeros(pieces[0].shape[:-1] + (width * count,), pieces[0].dtype)
+    for k, piece in enumerate(pieces):
         offset = ((part_index - k) % count) * width
-        full = lax.dynamic_update_slice_in_dim(full, stacked[k], offset, full.ndim - 1)
+        full = lax.dynamic_update_slice_in_dim(full, piece, offset, full.ndim - 1)
     return full
 
 
@@ -64,7 +64,7 @@
     part_index = lax.axis_index("mlp")
     per_owner_rows, tokens, quarter = drafts.shape
 
-    w_out_all = stack_mlp(w_out, mlp_count)
+    w_out_all = pieces_mlp(w_out, mlp_count)
 
     local_ids = jnp.arange(per_owner_rows, dtype=jnp.int32)
     devices = jnp.arange(req_count, dtype=jnp.int32)
@@ -89,7 +89,7 @@
 
     rows = per_owner_rows * tokens
     full_rows = place_blocks(
-        stack_mlp(local_rows.reshape(rows, quarter), mlp_count), mlp_count, part_index
+        pieces_mlp(local_rows.reshape(rows, quarter), mlp_count), mlp_count, part_index
     )
     wide_rows = full_rows.astype(jnp.float32)
     normalized_rows = (
@@ -155,17 +155,17 @@
     back_rows = jnp.take(arrived, my_owners, axis=0, mode="clip")
 
     packed = jnp.concatenate(
-        [back_rows.reshape(rows, head_width), drafts.reshape(rows, quarter)], axis=1
-    )
-    gathered = stack_mlp(packed, mlp_count)
-    heads_all = gathered[:, :, :head_width]
-    owned_all = place_blocks(gathered[:, :, head_width:], mlp_count, part_index)
-
-    group_products = jnp.einsum(
-        "jtc,jcd->jtd", heads_all, w_out_all, preferred_element_type=jnp.float32
-    )
-    attn_sum = jnp.sum(group_products.astype(jnp.bfloat16).astype(jnp.float32), axis=0)
-    residual = owned_all.astype(jnp.float32) + attn_sum
+        [drafts.reshape(rows, quarter), back_rows.reshape(rows, head_width)], axis=1
+    )
+    gathered = pieces_mlp(packed, mlp_count)
+    owned_all = place_blocks([piece[:, :quarter] for piece in gathered], mlp_count, part_index)
+
+    residual = owned_all.astype(jnp.float32)
+    for piece, rows_of_group in zip(gathered, w_out_all):
+        group_product = jnp.dot(
+            piece[:, quarter:], rows_of_group, preferred_element_type=jnp.float32
+        )
+        residual = residual + group_product.astype(jnp.bfloat16).astype(jnp.float32)
     normed_two = (
         residual * lax.rsqrt(jnp.mean(residual * residual, axis=1, keepdims=True) + EPS) * mlp_gain
     ).astype(jnp.bfloat16)

time: 152 us -> 147 us (0.967)
  local copies, waits for them, and re-layouts: 21.3 us -> 10.3 us
  waiting for transfers between devices: 68.7 us -> 72.6 us
  matrix products: 15 us -> 18.2 us
    squeeze x8 -> x0, local copies, waits for them, and re-layouts: 9.15 us -> none  [place_blocks(): stacked[k]]
    ppermute x12, waiting for transfers between devices: 29.9 us -> 34.3 us  [shift_mlp(): lax.ppermute(value, 'mlp', [(i, (i + shift) % count) for i in range(count)])]
    dot_general x1 -> x4, matrix products: 2.76 us -> 6.04 us  [per_device(): jnp.dot(piece[:, quarter:], rows_of_group, preferred_element_type=jnp.flo...]
    dynamic_update_slice x8, local copies, waits for them, and re-layouts: 1.93 us -> 0.11 us  [place_blocks(): full = lax.dynamic_update_slice_in_dim(full, piece, offset, full.ndim - 1)]
  transfers between devices with their start and end apart: 14 -> 14, of which waited for: 8 -> 10; matrix products, arithmetic and copies ran while one was open for 11% -> 7% of each run, Pallas kernels for 0% -> 0%
where the time goes in v3:
time: 147 us; the launch traced here: 144 us
  waiting for transfers between devices  72.6 us (49%)
  starting transfers between devices  36.4 us (25%)
  matrix products  18.2 us (12%)
  local copies, waits for them, and re-layouts  10.3 us (7%)
  other arithmetic  5.61 us (4%)
    ppermute x12, waiting for transfers between devices, shift_mlp(): lax.ppermute(value, 'mlp', [(i, (i + shift) % count) for i in range(count)])  34.3 us
    all_to_all x1, waiting for transfers between devices, per_device(): incoming = lax.all_to_all(outgoing, 'req', 0, 0, tiled=True)  26.8 us
    ppermute x12, starting transfers between devices, shift_mlp(): lax.ppermute(value, 'mlp', [(i, (i + shift) % count) for i in range(count)])  16.1 us
    all_to_all x1, starting transfers between devices, per_device(): incoming = lax.all_to_all(outgoing, 'req', 0, 0, tiled=True)  13.3 us
    all_to_all x1, waiting for transfers between devices, per_device(): arrived = lax.all_to_all(returning, 'req', 0, 0, tiled=True)  11.4 us
    all_to_all x1, starting transfers between devices, per_device(): arrived = lax.all_to_all(returning, 'req', 0, 0, tiled=True)  6.94 us
    dot_general x4, matrix products, per_device(): jnp.dot(piece[:, quarter:], rows_of_group, preferred_element_type=jnp.flo...  6.04 us
    dot_general x1, matrix products, per_device(): jnp.einsum('tu,ujd->jtd', hidden, w_down.reshape(w_down.shape[0], mlp_cou...  3.14 us
  transfers between devices with their start and end apart: 14, of which 10 were waited for; matrix products, arithmetic and copies ran while one was open for 7% of the time, Pallas kernels for 0%

profile of v3, /device:TPU:1, one launch (start us, length us, event | category | flops | bytes accessed | tf_op | source)
XLA Modules:
  0.0 144.2 jit_solution(12762006515886222731)
XLA Ops:
  3.1 2.5 %gather_fusion = bf16[64,16,512]{2,1,0:T(8,128)(2,1)} fusion(bf16[8,16,512]{2,1,0:T(8,128)(2,1)} %param.14, s32[1024]{0:T(1024)S(1)} %pad_clamp_fusion.3), kind=kCustom, calls=%fused_computation | custom fusion | bytes 2097408 | tf_op jit(solution)/shard_map/jit(_take)/gather | solution.py:86
  5.6 13.3 %all-to-all-start = ((bf16[64,16,512]{2,1,0:T(8,128)(2,1)}), bf16[64,16,512]{2,1,0:T(8,128)(2,1)}, u32[]{:S(2)}, u32[]{:S(2)}) async-start(bf16[64,16,512]{2,1,0:T(8,128)(2,1)} %gather_fusion), calls=%async_computation | async-start | bytes 2097152 | tf_op jit(solution)/shard_map/all_to_all | solution.py:87
  20.6 26.8 %all-to-all-done = bf16[64,16,512]{2,1,0:T(8,128)(2,1)} async-done(((bf16[64,16,512]{2,1,0:T(8,128)(2,1)}), bf16[64,16,512]{2,1,0:T(8,128)(2,1)}, u32[]{:S(2)}, u32[]{:S(2)}) %all-to-all-start) | async-done | bytes 1048608 | tf_op jit(solution)/shard_map/all_to_all | solution.py:87
  47.4 1.8 %gather_fusion.1 = bf16[8,16,512]{2,1,0:T(8,128)(2,1)S(1)} fusion(bf16[64,16,512]{2,1,0:T(8,128)(2,1)} %all-to-all-done, s32[1024]{0:T(1024)S(1)} %pad_clamp_fusion.2), kind=kCustom, calls=%fused_computation.1 | custom fusion | bytes 262176 | tf_op jit(solution)/shard_map/jit(_take)/gather | solution.py:88
  51.3 2.7 %collective-permute-start.1 = (bf16[128,512]{1,0:T(8,128)(2,1)S(1)}, bf16[128,512]{1,0:T(8,128)(2,1)S(1)}, u32[]{:S(2)}, u32[]{:S(2)}) collective-permute-start(bf16[128,512]{1,0:T(8,128)(2,1)S(1)} %bitcast.132), channel_id=1, source_target_pairs={{0,2},{1,3},{2,0},{3,1},{4,6},{5,7},{6,4},{7,5},{8,10},{9,11},{10,... | collective-permute-start | bytes 393224 | tf_op jit(solution)/shard_map/ppermute | solution.py:29
  55.6 3.9 %collective-permute-done.1 = bf16[128,512]{1,0:T(8,128)(2,1)S(1)} collective-permute-done((bf16[128,512]{1,0:T(8,128)(2,1)S(1)}, bf16[128,512]{1,0:T(8,128)(2,1)S(1)}, u32[]{:S(2)}, u32[]{:S(2)}) %collective-permute-start.1) | collective-permute-done | bytes 131104 | tf_op jit(solution)/shard_map/ppermute | solution.py:29
  59.7 2.0 %convolution_convert_fusion.4 = bf16[128,128]{1,0:T(8,128)(2,1)} fusion(bf16[2048,128]{1,0:T(8,128)(2,1)} %param.22, bf16[128,2048]{1,0:T(8,128)(2,1)S(1)} %constant_dynamic-update-slice_fusion, f32[2048]{0:T(1024)S(1)} %copy-done.12, f32[128]{0:T(128)S(1)} %add_rsqrt_fusion.1), kind=kOutput, calls=%fused_computation.35 | convolution fusion | flops 68173824 | bytes 1090048 | tf_op jit(solution)/shard_map/dot_general | solution.py:106
  68.1 6.9 %all-to-all-start.1 = ((bf16[64,16,192]{2,1,0:T(8,128)(2,1)}), bf16[64,16,192]{2,1,0:T(8,128)(2,1)}, u32[]{:S(2)}, u32[]{:S(2)}) async-start(bf16[64,16,192]{2,1,0:T(8,128)(2,1)} %gather_fusion.2), calls=%async_computation.1 | async-start | bytes 1048576 | tf_op jit(solution)/shard_map/all_to_all | solution.py:154
  75.0 3.0 %collective-permute-start.7 = (bf16[192,2048]{1,0:T(8,128)(2,1)}, bf16[192,2048]{1,0:T(8,128)(2,1)}, u32[]{:S(2)}, u32[]{:S(2)}) collective-permute-start(bf16[192,2048]{1,0:T(8,128)(2,1)} %param.23), channel_id=1, source_target_pairs={{0,2},{1,3},{2,0},{3,1},{4,6},{5,7},{6,4},{7,5},{8,10},{9,11},{10,... | collective-permute-start | bytes 2359304 | tf_op jit(solution)/shard_map/ppermute | solution.py:29
  78.1 2.6 %collective-permute-start.8 = (bf16[192,2048]{1,0:T(8,128)(2,1)}, bf16[192,2048]{1,0:T(8,128)(2,1)}, u32[]{:S(2)}, u32[]{:S(2)}) collective-permute-start(bf16[192,2048]{1,0:T(8,128)(2,1)} %param.23), channel_id=1, source_target_pairs={{0,3},{1,0},{2,1},{3,2},{4,7},{5,4},{6,5},{7,6},{8,11},{9,8},{10,9... | collective-permute-start | bytes 2359304 | tf_op jit(solution)/shard_map/ppermute | solution.py:29
  80.8 11.4 %all-to-all-done.1 = bf16[64,16,192]{2,1,0:T(8,128)(2,1)} async-done(((bf16[64,16,192]{2,1,0:T(8,128)(2,1)}), bf16[64,16,192]{2,1,0:T(8,128)(2,1)}, u32[]{:S(2)}, u32[]{:S(2)}) %all-to-all-start.1) | async-done | bytes 393248 | tf_op jit(solution)/shard_map/all_to_all | solution.py:154
  92.2 1.6 %gather_fusion.3 = bf16[8,16,192]{2,1,0:T(8,128)(2,1)S(1)} fusion(bf16[64,16,192]{2,1,0:T(8,128)(2,1)} %all-to-all-done.1, s32[1024]{0:T(1024)S(1)} %pad_clamp_fusion), kind=kCustom, calls=%fused_computation.3 | custom fusion | bytes 98336 | tf_op jit(solution)/shard_map/jit(_take)/gather | solution.py:155
  93.8 1.5 %collective-permute-start.3 = (bf16[128,704]{1,0:T(8,128)(2,1)S(1)}, bf16[128,704]{1,0:T(8,128)(2,1)S(1)}, u32[]{:S(2)}, u32[]{:S(2)}) collective-permute-start(bf16[128,704]{1,0:T(8,128)(2,1)S(1)} %pad_maximum_fusion), channel_id=1, source_target_pairs={{0,1},{1,2},{2,3},{3,0},{4,5},{5,6},{6,7},{7,4},{8,9},{9,10},{10,1... | collective-permute-start | bytes 540680 | tf_op jit(solution)/shard_map/ppermute | solution.py:29
  95.4 2.1 %collective-permute-start.4 = (bf16[128,704]{1,0:T(8,128)(2,1)S(1)}, bf16[128,704]{1,0:T(8,128)(2,1)S(1)}, u32[]{:S(2)}, u32[]{:S(2)}) collective-permute-start(bf16[128,704]{1,0:T(8,128)(2,1)S(1)} %pad_maximum_fusion), channel_id=1, source_target_pairs={{0,2},{1,3},{2,0},{3,1},{4,6},{5,7},{6,4},{7,5},{8,10},{9,11},{10,... | collective-permute-start | bytes 540680 | tf_op jit(solution)/shard_map/ppermute | solution.py:29
  98.9 19.3 %collective-permute-done.3 = bf16[128,704]{1,0:T(8,128)(2,1)S(1)} collective-permute-done((bf16[128,704]{1,0:T(8,128)(2,1)S(1)}, bf16[128,704]{1,0:T(8,128)(2,1)S(1)}, u32[]{:S(2)}, u32[]{:S(2)}) %collective-permute-start.3) | collective-permute-done | bytes 180256 | tf_op jit(solution)/shard_map/ppermute | solution.py:29
  118.2 2.5 %collective-permute-done.4 = bf16[128,704]{1,0:T(8,128)(2,1)S(1)} collective-permute-done((bf16[128,704]{1,0:T(8,128)(2,1)S(1)}, bf16[128,704]{1,0:T(8,128)(2,1)S(1)}, u32[]{:S(2)}, u32[]{:S(2)}) %collective-permute-start.4) | collective-permute-done | bytes 180256 | tf_op jit(solution)/shard_map/ppermute | solution.py:29
  120.7 3.3 %collective-permute-done.5 = bf16[128,704]{1,0:T(8,128)(2,1)S(1)} collective-permute-done((bf16[128,704]{1,0:T(8,128)(2,1)S(1)}, bf16[128,704]{1,0:T(8,128)(2,1)S(1)}, u32[]{:S(2)}, u32[]{:S(2)}) %collective-permute-start.5) | collective-permute-done | bytes 180256 | tf_op jit(solution)/shard_map/ppermute | solution.py:29
  127.0 1.7 %multiply_reduce_fusion = (f32[128]{0:T(128)S(1)}, f32[128,2048]{1,0:T(8,128)S(1)}) fusion(bf16[192,2048]{1,0:T(8,128)(2,1)} %collective-permute-done.8, bf16[128,704]{1,0:T(8,128)(2,1)S(1)} %collective-permute-done.5, f32[128,2048]{1,0:T(8,128)S(1)} %fusion.4, f32[128,2048]{1,0:T(8,128)S(1)} %fusion.5, f32[128,2048]{1,0:T(8,128)S(1)} %fusion.6, ...), kind=kOutput, calls=%fused_computation.45 | convolution fusion | flops 103022464 | bytes 5571072 | tf_op jit(solution)/shard_map/dot_general | solution.py:165
  130.4 3.1 %fusion.7 = bf16[128,4,512]{2,0,1:T(8,128)(2,1)S(1)} fusion(bf16[80,4,8,512]{3,2,1,0:T(8,128)(2,1)} %bitcast.139, bf16[2048,640]{1,0:T(8,128)(2,1)S(1)} %copy-done, f32[128,640]{1,0:T(8,128)S(1)} %fusion.59, f32[128,2048]{1,0:T(8,128)} %copy-done.2, f32[2048]{0:T(1024)S(1)} %copy-done.6, f32[128]{0:T(128)S(1)} %add_rsqrt_fusion), kind=kOutput, calls=%fused_computation.17 | convolution fusion | flops 672628736 | bytes 7152128 | tf_op jit(solution)/shard_map/tu,ujd->jtd/dot_general | solution.py:175
  134.2 1.7 %collective-permute-start.11 = (bf16[128,512]{1,0:T(8,128)(2,1)S(1)}, bf16[128,512]{1,0:T(8,128)(2,1)}, u32[]{:S(2)}, u32[]{:S(2)}) collective-permute-start(bf16[128,512]{1,0:T(8,128)(2,1)S(1)} %get-tuple-element.9), channel_id=1, source_target_pairs={{0,3},{1,0},{2,1},{3,2},{4,7},{5,4},{6,5},{7,6},{8,11},{9,8},{10,9... | collective-permute-start | bytes 393224 | tf_op jit(solution)/shard_map/ppermute | solution.py:29
  135.9 1.6 %fusion.19 = bf16[8,8,1,128]{3,1,2,0:T(8,128)(2,1)} fusion(bf16[8,16,128]{2,1,0:T(8,128)(2,1)} %bitcast.137, s32[8,8]{1,0:T(8,128)S(1)} %copy-done.13), kind=kOutput, calls=%fused_computation.38 | convolution fusion | flops 271360 | bytes 49408 | tf_op jit(solution)/shard_map/rat,rtkd->rakd/dot_general | solution.py:113
  137.5 2.3 %collective-permute-done.10 = bf16[128,512]{1,0:T(8,128)(2,1)S(1)} collective-permute-done((bf16[128,512]{1,0:T(8,128)(2,1)}, bf16[128,512]{1,0:T(8,128)(2,1)S(1)}, u32[]{:S(2)}, u32[]{:S(2)}) %collective-permute-start.10) | collective-permute-done | bytes 131104 | tf_op jit(solution)/shard_map/ppermute | solution.py:29
  140.3 2.1 %collective-permute-done.9 = bf16[128,512]{1,0:T(8,128)(2,1)} collective-permute-done((bf16[128,512]{1,0:T(8,128)(2,1)S(1)}, bf16[128,512]{1,0:T(8,128)(2,1)}, u32[]{:S(2)}, u32[]{:S(2)}) %collective-permute-start.9) | collective-permute-done | bytes 131104 | tf_op jit(solution)/shard_map/ppermute | solution.py:29
  142.4 1.8 %fusion.37 = bf16[128,512]{1,0:T(8,128)(2,1)} fusion(bf16[128,512]{1,0:T(8,128)(2,1)} %collective-permute-done.11, bf16[128,512]{1,0:T(8,128)(2,1)S(1)} %collective-permute-done.10, bf16[128,512]{1,0:T(8,128)(2,1)} %collective-permute-done.9, f32[128,2048]{1,0:T(8,128)} %copy-done.2, s32[]{:T(128)S(6)} %select_n.135, bf16[128,4,512]{2,0,1:T(8,128)(2,1)S(1)} %fusion.7, ...), kind=kLoop, calls=%fused_computation.62 | loop fusion | flops 589824 | bytes 917512 | tf_op jit(solution)/shard_map/convert_element_type | solution.py:190
  (89 shorter events, 21.4 us)
Async XLA Ops:
  0.6 129.7 %copy-start = (bf16[2048,640]{1,0:T(8,128)(2,1)S(1)}, bf16[2048,640]{1,0:T(8,128)(2,1)}, u32[]{:S(2)}) copy-start(bf16[2048,640]{1,0:T(8,128)(2,1)} %param.26) | copy-start | bytes 7864324
  0.6 18.4 %copy-start.10 = (s32[8]{0:T(128)S(1)}, s32[8]{0:T(128)}, u32[]{:S(2)}) copy-start(s32[8]{0:T(128)} %param.16) | copy-start | bytes 100
  0.7 19.1 %copy-start.7 = (s32[8,16]{1,0:T(8,128)S(1)}, s32[8,16]{1,0:T(8,128)}, u32[]{:S(2)}) copy-start(s32[8,16]{1,0:T(8,128)} %param.17) | copy-start | bytes 1540
  5.6 54.1 %copy-start.12 = (f32[2048]{0:T(1024)S(1)}, f32[2048]{0:T(1024)}, u32[]{:S(2)}) copy-start(f32[2048]{0:T(1024)} %param.20) | copy-start | bytes 24580
  5.6 41.7 %all-to-all-start = ((bf16[64,16,512]{2,1,0:T(8,128)(2,1)}), bf16[64,16,512]{2,1,0:T(8,128)(2,1)}, u32[]{:S(2)}, u32[]{:S(2)}) async-start(bf16[64,16,512]{2,1,0:T(8,128)(2,1)} %gather_fusion), calls=%async_computation | async-start | bytes 2097152 | tf_op jit(solution)/shard_map/all_to_all | solution.py:87
  49.2 6.4 %collective-permute-start = (bf16[128,512]{1,0:T(8,128)(2,1)S(1)}, bf16[128,512]{1,0:T(8,128)(2,1)S(1)}, u32[]{:S(2)}, u32[]{:S(2)}) collective-permute-start(bf16[128,512]{1,0:T(8,128)(2,1)S(1)} %bitcast.131), channel_id=1, source_target_pairs={{0,1},{1,2},{2,3},{3,0},{4,5},{5,6},{6,7},{7,4},{8,9},{9,10},{10,1... | collective-permute-start | bytes 393224 | tf_op jit(solution)/shard_map/ppermute | solution.py:29
  51.3 10.5 %copy-start.11 = (bf16[2048,192]{0,1:T(8,128)(2,1)S(1)}, bf16[2048,192]{0,1:T(8,128)(2,1)}, u32[]{:S(2)}) copy-start(bf16[2048,192]{0,1:T(8,128)(2,1)} %param.21) | copy-start | bytes 2359300
  51.3 8.2 %collective-permute-start.1 = (bf16[128,512]{1,0:T(8,128)(2,1)S(1)}, bf16[128,512]{1,0:T(8,128)(2,1)S(1)}, u32[]{:S(2)}, u32[]{:S(2)}) collective-permute-start(bf16[128,512]{1,0:T(8,128)(2,1)S(1)} %bitcast.132), channel_id=1, source_target_pairs={{0,2},{1,3},{2,0},{3,1},{4,6},{5,7},{6,4},{7,5},{8,10},{9,11},{10,... | collective-permute-start | bytes 393224 | tf_op jit(solution)/shard_map/ppermute | solution.py:29
  54.0 5.5 %collective-permute-start.2 = (bf16[128,512]{1,0:T(8,128)(2,1)S(1)}, bf16[128,512]{1,0:T(8,128)(2,1)S(1)}, u32[]{:S(2)}, u32[]{:S(2)}) collective-permute-start(bf16[128,512]{1,0:T(8,128)(2,1)S(1)} %bitcast.133), channel_id=1, source_target_pairs={{0,3},{1,0},{2,1},{3,2},{4,7},{5,4},{6,5},{7,6},{8,11},{9,8},{10,9... | collective-permute-start | bytes 393224 | tf_op jit(solution)/shard_map/ppermute | solution.py:29
  55.1 8.7 %copy-start.4 = (bf16[8,256,1,128]{3,1,2,0:T(8,128)(2,1)S(1)}, bf16[8,256,1,128]{3,1,2,0:T(8,128)(2,1)}, u32[]{:S(2)}) copy-start(bf16[8,256,1,128]{3,1,2,0:T(8,128)(2,1)} %param.19) | copy-start | bytes 1572868
  62.3 3.7 %copy-start.5 = (bf16[128,128]{1,0:T(8,128)(2,1)S(1)}, bf16[128,128]{1,0:T(8,128)(2,1)}, u32[]{:S(2)}) copy-start(bf16[128,128]{1,0:T(8,128)(2,1)} %convolution_convert_fusion.4) | copy-start | bytes 98308
  65.3 15.4 %copy-start.9 = (s32[8]{0:T(128)S(1)}, s32[8]{0:T(128)}, u32[]{:S(2)}) copy-start(s32[8]{0:T(128)} %copy-done.8) | copy-start | bytes 100
  65.5 15.2 %copy-start.1 = (bf16[8,16,512]{2,1,0:T(8,128)(2,1)S(1)}, bf16[8,16,512]{2,1,0:T(8,128)(2,1)}, u32[]{:S(2)}) copy-start(bf16[8,16,512]{2,1,0:T(8,128)(2,1)} %param.14) | copy-start | bytes 393220
  68.1 24.1 %all-to-all-start.1 = ((bf16[64,16,192]{2,1,0:T(8,128)(2,1)}), bf16[64,16,192]{2,1,0:T(8,128)(2,1)}, u32[]{:S(2)}, u32[]{:S(2)}) async-start(bf16[64,16,192]{2,1,0:T(8,128)(2,1)} %gather_fusion.2), calls=%async_computation.1 | async-start | bytes 1048576 | tf_op jit(solution)/shard_map/all_to_all | solution.py:154
  75.0 49.1 %collective-permute-start.7 = (bf16[192,2048]{1,0:T(8,128)(2,1)}, bf16[192,2048]{1,0:T(8,128)(2,1)}, u32[]{:S(2)}, u32[]{:S(2)}) collective-permute-start(bf16[192,2048]{1,0:T(8,128)(2,1)} %param.23), channel_id=1, source_target_pairs={{0,2},{1,3},{2,0},{3,1},{4,6},{5,7},{6,4},{7,5},{8,10},{9,11},{10,... | collective-permute-start | bytes 2359304 | tf_op jit(solution)/shard_map/ppermute | solution.py:29
  78.0 47.5 %collective-permute-start.6 = (bf16[192,2048]{1,0:T(8,128)(2,1)}, bf16[192,2048]{1,0:T(8,128)(2,1)}, u32[]{:S(2)}, u32[]{:S(2)}) collective-permute-start(bf16[192,2048]{1,0:T(8,128)(2,1)} %param.23), channel_id=1, source_target_pairs={{0,1},{1,2},{2,3},{3,0},{4,5},{5,6},{6,7},{7,4},{8,9},{9,10},{10,1... | collective-permute-start | bytes 2359304 | tf_op jit(solution)/shard_map/ppermute | solution.py:29
  78.1 48.9 %collective-permute-start.8 = (bf16[192,2048]{1,0:T(8,128)(2,1)}, bf16[192,2048]{1,0:T(8,128)(2,1)}, u32[]{:S(2)}, u32[]{:S(2)}) collective-permute-start(bf16[192,2048]{1,0:T(8,128)(2,1)} %param.23), channel_id=1, source_target_pairs={{0,3},{1,0},{2,1},{3,2},{4,7},{5,4},{6,5},{7,6},{8,11},{9,8},{10,9... | collective-permute-start | bytes 2359304 | tf_op jit(solution)/shard_map/ppermute | solution.py:29
  93.8 24.3 %collective-permute-start.3 = (bf16[128,704]{1,0:T(8,128)(2,1)S(1)}, bf16[128,704]{1,0:T(8,128)(2,1)S(1)}, u32[]{:S(2)}, u32[]{:S(2)}) collective-permute-start(bf16[128,704]{1,0:T(8,128)(2,1)S(1)} %pad_maximum_fusion), channel_id=1, source_target_pairs={{0,1},{1,2},{2,3},{3,0},{4,5},{5,6},{6,7},{7,4},{8,9},{9,10},{10,1... | collective-permute-start | bytes 540680 | tf_op jit(solution)/shard_map/ppermute | solution.py:29
  95.4 25.3 %collective-permute-start.4 = (bf16[128,704]{1,0:T(8,128)(2,1)S(1)}, bf16[128,704]{1,0:T(8,128)(2,1)S(1)}, u32[]{:S(2)}, u32[]{:S(2)}) collective-permute-start(bf16[128,704]{1,0:T(8,128)(2,1)S(1)} %pad_maximum_fusion), channel_id=1, source_target_pairs={{0,2},{1,3},{2,0},{3,1},{4,6},{5,7},{6,4},{7,5},{8,10},{9,11},{10,... | collective-permute-start | bytes 540680 | tf_op jit(solution)/shard_map/ppermute | solution.py:29
  118.2 5.9 %collective-permute-start.5 = (bf16[128,704]{1,0:T(8,128)(2,1)S(1)}, bf16[128,704]{1,0:T(8,128)(2,1)S(1)}, u32[]{:S(2)}, u32[]{:S(2)}) collective-permute-start(bf16[128,704]{1,0:T(8,128)(2,1)S(1)} %pad_maximum_fusion), channel_id=1, source_target_pairs={{0,3},{1,0},{2,1},{3,2},{4,7},{5,4},{6,5},{7,6},{8,11},{9,8},{10,9... | collective-permute-start | bytes 540680 | tf_op jit(solution)/shard_map/ppermute | solution.py:29
  130.4 5.5 %copy-start.13 = (s32[8,8]{1,0:T(8,128)S(1)}, s32[8,8]{1,0:T(8,128)}, u32[]{:S(2)}) copy-start(s32[8,8]{1,0:T(8,128)} %param.18) | copy-start | bytes 772
  134.2 5.6 %collective-permute-start.10 = (bf16[128,512]{1,0:T(8,128)(2,1)}, bf16[128,512]{1,0:T(8,128)(2,1)S(1)}, u32[]{:S(2)}, u32[]{:S(2)}) collective-permute-start(bf16[128,512]{1,0:T(8,128)(2,1)} %get-tuple-element.10), channel_id=1, source_target_pairs={{0,2},{1,3},{2,0},{3,1},{4,6},{5,7},{6,4},{7,5},{8,10},{9,11},{10,... | collective-permute-start | bytes 393224 | tf_op jit(solution)/shard_map/ppermute | solution.py:29
  134.2 6.1 %collective-permute-start.11 = (bf16[128,512]{1,0:T(8,128)(2,1)S(1)}, bf16[128,512]{1,0:T(8,128)(2,1)}, u32[]{:S(2)}, u32[]{:S(2)}) collective-permute-start(bf16[128,512]{1,0:T(8,128)(2,1)S(1)} %get-tuple-element.9), channel_id=1, source_target_pairs={{0,3},{1,0},{2,1},{3,2},{4,7},{5,4},{6,5},{7,6},{8,11},{9,8},{10,9... | collective-permute-start | bytes 393224 | tf_op jit(solution)/shard_map/ppermute | solution.py:29
  135.9 6.4 %collective-permute-start.9 = (bf16[128,512]{1,0:T(8,128)(2,1)S(1)}, bf16[128,512]{1,0:T(8,128)(2,1)}, u32[]{:S(2)}, u32[]{:S(2)}) collective-permute-start(bf16[128,512]{1,0:T(8,128)(2,1)S(1)} %get-tuple-element.8), channel_id=1, source_target_pairs={{0,1},{1,2},{2,3},{3,0},{4,5},{5,6},{6,7},{7,4},{8,9},{9,10},{10,1... | collective-permute-start | bytes 393224 | tf_op jit(solution)/shard_map/ppermute | solution.py:29
  (4 other events, 7.0 us)

commit v4 on v3

--- a/solution.py
+++ b/solution.py
@@ -88,9 +88,8 @@
     local_rows = jnp.take(incoming, source_of, axis=0, mode="clip")
 
     rows = per_owner_rows * tokens
-    full_rows = place_blocks(
-        pieces_mlp(local_rows.reshape(rows, quarter), mlp_count), mlp_count, part_index
-    )
+    owner_pieces = pieces_mlp(local_rows.reshape(rows, quarter), mlp_count)
+    full_rows = place_blocks(owner_pieces, mlp_count, part_index)
     wide_rows = full_rows.astype(jnp.float32)
     normalized_rows = (
         wide_rows

time: 147 us -> 147 us (level)
  no operation moved by 1% of the time
where the time goes in v4:
time: 147 us; the launch traced here: 144 us
  waiting for transfers between devices  72.6 us (49%)
  starting transfers between devices  36.4 us (25%)
  matrix products  18.2 us (12%)
  local copies, waits for them, and re-layouts  10.3 us (7%)
  other arithmetic  5.61 us (4%)
    ppermute x12, waiting for transfers between devices, shift_mlp(): lax.ppermute(value, 'mlp', [(i, (i + shift) % count) for i in range(count)])  34.3 us
    all_to_all x1, waiting for transfers between devices, per_device(): incoming = lax.all_to_all(outgoing, 'req', 0, 0, tiled=True)  26.8 us
    ppermute x12, starting transfers between devices, shift_mlp(): lax.ppermute(value, 'mlp', [(i, (i + shift) % count) for i in range(count)])  16.1 us
    all_to_all x1, starting transfers between devices, per_device(): incoming = lax.all_to_all(outgoing, 'req', 0, 0, tiled=True)  13.3 us
    all_to_all x1, waiting for transfers between devices, per_device(): arrived = lax.all_to_all(returning, 'req', 0, 0, tiled=True)  11.4 us
    all_to_all x1, starting transfers between devices, per_device(): arrived = lax.all_to_all(returning, 'req', 0, 0, tiled=True)  6.94 us
    dot_general x4, matrix products, per_device(): jnp.dot(piece[:, quarter:], rows_of_group, preferred_element_type=jnp.flo...  6.04 us
    dot_general x1, matrix products, per_device(): jnp.einsum('tu,ujd->jtd', hidden, w_down.reshape(w_down.shape[0], mlp_cou...  3.14 us
  transfers between devices with their start and end apart: 14, of which 10 were waited for; matrix products, arithmetic and copies ran while one was open for 7% of the time, Pallas kernels for 0%

profile of v4, /device:TPU:1, one launch (start us, length us, event | category | flops | bytes accessed | tf_op | source)
XLA Modules:
  0.0 144.2 jit_solution(12762006515886222731)
XLA Ops:
  3.1 2.5 %gather_fusion = bf16[64,16,512]{2,1,0:T(8,128)(2,1)} fusion(bf16[8,16,512]{2,1,0:T(8,128)(2,1)} %param.14, s32[1024]{0:T(1024)S(1)} %pad_clamp_fusion.3), kind=kCustom, calls=%fused_computation | custom fusion | bytes 2097408 | tf_op jit(solution)/shard_map/jit(_take)/gather | solution.py:86
  5.6 13.3 %all-to-all-start = ((bf16[64,16,512]{2,1,0:T(8,128)(2,1)}), bf16[64,16,512]{2,1,0:T(8,128)(2,1)}, u32[]{:S(2)}, u32[]{:S(2)}) async-start(bf16[64,16,512]{2,1,0:T(8,128)(2,1)} %gather_fusion), calls=%async_computation | async-start | bytes 2097152 | tf_op jit(solution)/shard_map/all_to_all | solution.py:87
  20.6 26.8 %all-to-all-done = bf16[64,16,512]{2,1,0:T(8,128)(2,1)} async-done(((bf16[64,16,512]{2,1,0:T(8,128)(2,1)}), bf16[64,16,512]{2,1,0:T(8,128)(2,1)}, u32[]{:S(2)}, u32[]{:S(2)}) %all-to-all-start) | async-done | bytes 1048608 | tf_op jit(solution)/shard_map/all_to_all | solution.py:87
  47.4 1.8 %gather_fusion.1 = bf16[8,16,512]{2,1,0:T(8,128)(2,1)S(1)} fusion(bf16[64,16,512]{2,1,0:T(8,128)(2,1)} %all-to-all-done, s32[1024]{0:T(1024)S(1)} %pad_clamp_fusion.2), kind=kCustom, calls=%fused_computation.1 | custom fusion | bytes 262176 | tf_op jit(solution)/shard_map/jit(_take)/gather | solution.py:88
  51.3 2.7 %collective-permute-start.1 = (bf16[128,512]{1,0:T(8,128)(2,1)S(1)}, bf16[128,512]{1,0:T(8,128)(2,1)S(1)}, u32[]{:S(2)}, u32[]{:S(2)}) collective-permute-start(bf16[128,512]{1,0:T(8,128)(2,1)S(1)} %bitcast.132), channel_id=1, source_target_pairs={{0,2},{1,3},{2,0},{3,1},{4,6},{5,7},{6,4},{7,5},{8,10},{9,11},{10,... | collective-permute-start | bytes 393224 | tf_op jit(solution)/shard_map/ppermute | solution.py:29
  55.6 3.9 %collective-permute-done.1 = bf16[128,512]{1,0:T(8,128)(2,1)S(1)} collective-permute-done((bf16[128,512]{1,0:T(8,128)(2,1)S(1)}, bf16[128,512]{1,0:T(8,128)(2,1)S(1)}, u32[]{:S(2)}, u32[]{:S(2)}) %collective-permute-start.1) | collective-permute-done | bytes 131104 | tf_op jit(solution)/shard_map/ppermute | solution.py:29
  59.7 2.0 %convolution_convert_fusion.4 = bf16[128,128]{1,0:T(8,128)(2,1)} fusion(bf16[2048,128]{1,0:T(8,128)(2,1)} %param.22, bf16[128,2048]{1,0:T(8,128)(2,1)S(1)} %constant_dynamic-update-slice_fusion, f32[2048]{0:T(1024)S(1)} %copy-done.12, f32[128]{0:T(128)S(1)} %add_rsqrt_fusion.1), kind=kOutput, calls=%fused_computation.35 | convolution fusion | flops 68173824 | bytes 1090048 | tf_op jit(solution)/shard_map/dot_general | solution.py:105
  68.1 6.9 %all-to-all-start.1 = ((bf16[64,16,192]{2,1,0:T(8,128)(2,1)}), bf16[64,16,192]{2,1,0:T(8,128)(2,1)}, u32[]{:S(2)}, u32[]{:S(2)}) async-start(bf16[64,16,192]{2,1,0:T(8,128)(2,1)} %gather_fusion.2), calls=%async_computation.1 | async-start | bytes 1048576 | tf_op jit(solution)/shard_map/all_to_all | solution.py:153
  75.0 3.0 %collective-permute-start.7 = (bf16[192,2048]{1,0:T(8,128)(2,1)}, bf16[192,2048]{1,0:T(8,128)(2,1)}, u32[]{:S(2)}, u32[]{:S(2)}) collective-permute-start(bf16[192,2048]{1,0:T(8,128)(2,1)} %param.23), channel_id=1, source_target_pairs={{0,2},{1,3},{2,0},{3,1},{4,6},{5,7},{6,4},{7,5},{8,10},{9,11},{10,... | collective-permute-start | bytes 2359304 | tf_op jit(solution)/shard_map/ppermute | solution.py:29
  78.1 2.6 %collective-permute-start.8 = (bf16[192,2048]{1,0:T(8,128)(2,1)}, bf16[192,2048]{1,0:T(8,128)(2,1)}, u32[]{:S(2)}, u32[]{:S(2)}) collective-permute-start(bf16[192,2048]{1,0:T(8,128)(2,1)} %param.23), channel_id=1, source_target_pairs={{0,3},{1,0},{2,1},{3,2},{4,7},{5,4},{6,5},{7,6},{8,11},{9,8},{10,9... | collective-permute-start | bytes 2359304 | tf_op jit(solution)/shard_map/ppermute | solution.py:29
  80.8 11.4 %all-to-all-done.1 = bf16[64,16,192]{2,1,0:T(8,128)(2,1)} async-done(((bf16[64,16,192]{2,1,0:T(8,128)(2,1)}), bf16[64,16,192]{2,1,0:T(8,128)(2,1)}, u32[]{:S(2)}, u32[]{:S(2)}) %all-to-all-start.1) | async-done | bytes 393248 | tf_op jit(solution)/shard_map/all_to_all | solution.py:153
  92.2 1.6 %gather_fusion.3 = bf16[8,16,192]{2,1,0:T(8,128)(2,1)S(1)} fusion(bf16[64,16,192]{2,1,0:T(8,128)(2,1)} %all-to-all-done.1, s32[1024]{0:T(1024)S(1)} %pad_clamp_fusion), kind=kCustom, calls=%fused_computation.3 | custom fusion | bytes 98336 | tf_op jit(solution)/shard_map/jit(_take)/gather | solution.py:154
  93.8 1.5 %collective-permute-start.3 = (bf16[128,704]{1,0:T(8,128)(2,1)S(1)}, bf16[128,704]{1,0:T(8,128)(2,1)S(1)}, u32[]{:S(2)}, u32[]{:S(2)}) collective-permute-start(bf16[128,704]{1,0:T(8,128)(2,1)S(1)} %pad_maximum_fusion), channel_id=1, source_target_pairs={{0,1},{1,2},{2,3},{3,0},{4,5},{5,6},{6,7},{7,4},{8,9},{9,10},{10,1... | collective-permute-start | bytes 540680 | tf_op jit(solution)/shard_map/ppermute | solution.py:29
  95.4 2.1 %collective-permute-start.4 = (bf16[128,704]{1,0:T(8,128)(2,1)S(1)}, bf16[128,704]{1,0:T(8,128)(2,1)S(1)}, u32[]{:S(2)}, u32[]{:S(2)}) collective-permute-start(bf16[128,704]{1,0:T(8,128)(2,1)S(1)} %pad_maximum_fusion), channel_id=1, source_target_pairs={{0,2},{1,3},{2,0},{3,1},{4,6},{5,7},{6,4},{7,5},{8,10},{9,11},{10,... | collective-permute-start | bytes 540680 | tf_op jit(solution)/shard_map/ppermute | solution.py:29
  98.9 19.3 %collective-permute-done.3 = bf16[128,704]{1,0:T(8,128)(2,1)S(1)} collective-permute-done((bf16[128,704]{1,0:T(8,128)(2,1)S(1)}, bf16[128,704]{1,0:T(8,128)(2,1)S(1)}, u32[]{:S(2)}, u32[]{:S(2)}) %collective-permute-start.3) | collective-permute-done | bytes 180256 | tf_op jit(solution)/shard_map/ppermute | solution.py:29
  118.2 2.5 %collective-permute-done.4 = bf16[128,704]{1,0:T(8,128)(2,1)S(1)} collective-permute-done((bf16[128,704]{1,0:T(8,128)(2,1)S(1)}, bf16[128,704]{1,0:T(8,128)(2,1)S(1)}, u32[]{:S(2)}, u32[]{:S(2)}) %collective-permute-start.4) | collective-permute-done | bytes 180256 | tf_op jit(solution)/shard_map/ppermute | solution.py:29
  120.7 3.3 %collective-permute-done.5 = bf16[128,704]{1,0:T(8,128)(2,1)S(1)} collective-permute-done((bf16[128,704]{1,0:T(8,128)(2,1)S(1)}, bf16[128,704]{1,0:T(8,128)(2,1)S(1)}, u32[]{:S(2)}, u32[]{:S(2)}) %collective-permute-start.5) | collective-permute-done | bytes 180256 | tf_op jit(solution)/shard_map/ppermute | solution.py:29
  127.0 1.7 %multiply_reduce_fusion = (f32[128]{0:T(128)S(1)}, f32[128,2048]{1,0:T(8,128)S(1)}) fusion(bf16[192,2048]{1,0:T(8,128)(2,1)} %collective-permute-done.8, bf16[128,704]{1,0:T(8,128)(2,1)S(1)} %collective-permute-done.5, f32[128,2048]{1,0:T(8,128)S(1)} %fusion.4, f32[128,2048]{1,0:T(8,128)S(1)} %fusion.5, f32[128,2048]{1,0:T(8,128)S(1)} %fusion.6, ...), kind=kOutput, calls=%fused_computation.45 | convolution fusion | flops 103022464 | bytes 5571072 | tf_op jit(solution)/shard_map/dot_general | solution.py:164
  130.4 3.1 %fusion.7 = bf16[128,4,512]{2,0,1:T(8,128)(2,1)S(1)} fusion(bf16[80,4,8,512]{3,2,1,0:T(8,128)(2,1)} %bitcast.139, bf16[2048,640]{1,0:T(8,128)(2,1)S(1)} %copy-done, f32[128,640]{1,0:T(8,128)S(1)} %fusion.59, f32[128,2048]{1,0:T(8,128)} %copy-done.2, f32[2048]{0:T(1024)S(1)} %copy-done.6, f32[128]{0:T(128)S(1)} %add_rsqrt_fusion), kind=kOutput, calls=%fused_computation.17 | convolution fusion | flops 672628736 | bytes 7152128 | tf_op jit(solution)/shard_map/tu,ujd->jtd/dot_general | solution.py:174
  134.2 1.7 %collective-permute-start.11 = (bf16[128,512]{1,0:T(8,128)(2,1)S(1)}, bf16[128,512]{1,0:T(8,128)(2,1)}, u32[]{:S(2)}, u32[]{:S(2)}) collective-permute-start(bf16[128,512]{1,0:T(8,128)(2,1)S(1)} %get-tuple-element.9), channel_id=1, source_target_pairs={{0,3},{1,0},{2,1},{3,2},{4,7},{5,4},{6,5},{7,6},{8,11},{9,8},{10,9... | collective-permute-start | bytes 393224 | tf_op jit(solution)/shard_map/ppermute | solution.py:29
  135.9 1.6 %fusion.19 = bf16[8,8,1,128]{3,1,2,0:T(8,128)(2,1)} fusion(bf16[8,16,128]{2,1,0:T(8,128)(2,1)} %bitcast.137, s32[8,8]{1,0:T(8,128)S(1)} %copy-done.13), kind=kOutput, calls=%fused_computation.38 | convolution fusion | flops 271360 | bytes 49408 | tf_op jit(solution)/shard_map/rat,rtkd->rakd/dot_general | solution.py:112
  137.5 2.3 %collective-permute-done.10 = bf16[128,512]{1,0:T(8,128)(2,1)S(1)} collective-permute-done((bf16[128,512]{1,0:T(8,128)(2,1)}, bf16[128,512]{1,0:T(8,128)(2,1)S(1)}, u32[]{:S(2)}, u32[]{:S(2)}) %collective-permute-start.10) | collective-permute-done | bytes 131104 | tf_op jit(solution)/shard_map/ppermute | solution.py:29
  140.3 2.1 %collective-permute-done.9 = bf16[128,512]{1,0:T(8,128)(2,1)} collective-permute-done((bf16[128,512]{1,0:T(8,128)(2,1)S(1)}, bf16[128,512]{1,0:T(8,128)(2,1)}, u32[]{:S(2)}, u32[]{:S(2)}) %collective-permute-start.9) | collective-permute-done | bytes 131104 | tf_op jit(solution)/shard_map/ppermute | solution.py:29
  142.4 1.8 %fusion.37 = bf16[128,512]{1,0:T(8,128)(2,1)} fusion(bf16[128,512]{1,0:T(8,128)(2,1)} %collective-permute-done.11, bf16[128,512]{1,0:T(8,128)(2,1)S(1)} %collective-permute-done.10, bf16[128,512]{1,0:T(8,128)(2,1)} %collective-permute-done.9, f32[128,2048]{1,0:T(8,128)} %copy-done.2, s32[]{:T(128)S(6)} %select_n.135, bf16[128,4,512]{2,0,1:T(8,128)(2,1)S(1)} %fusion.7, ...), kind=kLoop, calls=%fused_computation.62 | loop fusion | flops 589824 | bytes 917512 | tf_op jit(solution)/shard_map/convert_element_type | solution.py:189
  (89 shorter events, 21.4 us)
Async XLA Ops:
  0.6 129.7 %copy-start = (bf16[2048,640]{1,0:T(8,128)(2,1)S(1)}, bf16[2048,640]{1,0:T(8,128)(2,1)}, u32[]{:S(2)}) copy-start(bf16[2048,640]{1,0:T(8,128)(2,1)} %param.26) | copy-start | bytes 7864324
  0.6 18.4 %copy-start.10 = (s32[8]{0:T(128)S(1)}, s32[8]{0:T(128)}, u32[]{:S(2)}) copy-start(s32[8]{0:T(128)} %param.16) | copy-start | bytes 100
  0.7 19.1 %copy-start.7 = (s32[8,16]{1,0:T(8,128)S(1)}, s32[8,16]{1,0:T(8,128)}, u32[]{:S(2)}) copy-start(s32[8,16]{1,0:T(8,128)} %param.17) | copy-start | bytes 1540
  5.6 54.1 %copy-start.12 = (f32[2048]{0:T(1024)S(1)}, f32[2048]{0:T(1024)}, u32[]{:S(2)}) copy-start(f32[2048]{0:T(1024)} %param.20) | copy-start | bytes 24580
  5.6 41.7 %all-to-all-start = ((bf16[64,16,512]{2,1,0:T(8,128)(2,1)}), bf16[64,16,512]{2,1,0:T(8,128)(2,1)}, u32[]{:S(2)}, u32[]{:S(2)}) async-start(bf16[64,16,512]{2,1,0:T(8,128)(2,1)} %gather_fusion), calls=%async_computation | async-start | bytes 2097152 | tf_op jit(solution)/shard_map/all_to_all | solution.py:87
  49.2 6.4 %collective-permute-start = (bf16[128,512]{1,0:T(8,128)(2,1)S(1)}, bf16[128,512]{1,0:T(8,128)(2,1)S(1)}, u32[]{:S(2)}, u32[]{:S(2)}) collective-permute-start(bf16[128,512]{1,0:T(8,128)(2,1)S(1)} %bitcast.131), channel_id=1, source_target_pairs={{0,1},{1,2},{2,3},{3,0},{4,5},{5,6},{6,7},{7,4},{8,9},{9,10},{10,1... | collective-permute-start | bytes 393224 | tf_op jit(solution)/shard_map/ppermute | solution.py:29
  51.3 10.5 %copy-start.11 = (bf16[2048,192]{0,1:T(8,128)(2,1)S(1)}, bf16[2048,192]{0,1:T(8,128)(2,1)}, u32[]{:S(2)}) copy-start(bf16[2048,192]{0,1:T(8,128)(2,1)} %param.21) | copy-start | bytes 2359300
  51.3 8.2 %collective-permute-start.1 = (bf16[128,512]{1,0:T(8,128)(2,1)S(1)}, bf16[128,512]{1,0:T(8,128)(2,1)S(1)}, u32[]{:S(2)}, u32[]{:S(2)}) collective-permute-start(bf16[128,512]{1,0:T(8,128)(2,1)S(1)} %bitcast.132), channel_id=1, source_target_pairs={{0,2},{1,3},{2,0},{3,1},{4,6},{5,7},{6,4},{7,5},{8,10},{9,11},{10,... | collective-permute-start | bytes 393224 | tf_op jit(solution)/shard_map/ppermute | solution.py:29
  54.0 5.5 %collective-permute-start.2 = (bf16[128,512]{1,0:T(8,128)(2,1)S(1)}, bf16[128,512]{1,0:T(8,128)(2,1)S(1)}, u32[]{:S(2)}, u32[]{:S(2)}) collective-permute-start(bf16[128,512]{1,0:T(8,128)(2,1)S(1)} %bitcast.133), channel_id=1, source_target_pairs={{0,3},{1,0},{2,1},{3,2},{4,7},{5,4},{6,5},{7,6},{8,11},{9,8},{10,9... | collective-permute-start | bytes 393224 | tf_op jit(solution)/shard_map/ppermute | solution.py:29
  55.1 8.7 %copy-start.4 = (bf16[8,256,1,128]{3,1,2,0:T(8,128)(2,1)S(1)}, bf16[8,256,1,128]{3,1,2,0:T(8,128)(2,1)}, u32[]{:S(2)}) copy-start(bf16[8,256,1,128]{3,1,2,0:T(8,128)(2,1)} %param.19) | copy-start | bytes 1572868
  62.3 3.7 %copy-start.5 = (bf16[128,128]{1,0:T(8,128)(2,1)S(1)}, bf16[128,128]{1,0:T(8,128)(2,1)}, u32[]{:S(2)}) copy-start(bf16[128,128]{1,0:T(8,128)(2,1)} %convolution_convert_fusion.4) | copy-start | bytes 98308
  65.3 15.4 %copy-start.9 = (s32[8]{0:T(128)S(1)}, s32[8]{0:T(128)}, u32[]{:S(2)}) copy-start(s32[8]{0:T(128)} %copy-done.8) | copy-start | bytes 100
  65.5 15.2 %copy-start.1 = (bf16[8,16,512]{2,1,0:T(8,128)(2,1)S(1)}, bf16[8,16,512]{2,1,0:T(8,128)(2,1)}, u32[]{:S(2)}) copy-start(bf16[8,16,512]{2,1,0:T(8,128)(2,1)} %param.14) | copy-start | bytes 393220
  68.1 24.1 %all-to-all-start.1 = ((bf16[64,16,192]{2,1,0:T(8,128)(2,1)}), bf16[64,16,192]{2,1,0:T(8,128)(2,1)}, u32[]{:S(2)}, u32[]{:S(2)}) async-start(bf16[64,16,192]{2,1,0:T(8,128)(2,1)} %gather_fusion.2), calls=%async_computation.1 | async-start | bytes 1048576 | tf_op jit(solution)/shard_map/all_to_all | solution.py:153
  75.0 49.1 %collective-permute-start.7 = (bf16[192,2048]{1,0:T(8,128)(2,1)}, bf16[192,2048]{1,0:T(8,128)(2,1)}, u32[]{:S(2)}, u32[]{:S(2)}) collective-permute-start(bf16[192,2048]{1,0:T(8,128)(2,1)} %param.23), channel_id=1, source_target_pairs={{0,2},{1,3},{2,0},{3,1},{4,6},{5,7},{6,4},{7,5},{8,10},{9,11},{10,... | collective-permute-start | bytes 2359304 | tf_op jit(solution)/shard_map/ppermute | solution.py:29
  78.0 47.5 %collective-permute-start.6 = (bf16[192,2048]{1,0:T(8,128)(2,1)}, bf16[192,2048]{1,0:T(8,128)(2,1)}, u32[]{:S(2)}, u32[]{:S(2)}) collective-permute-start(bf16[192,2048]{1,0:T(8,128)(2,1)} %param.23), channel_id=1, source_target_pairs={{0,1},{1,2},{2,3},{3,0},{4,5},{5,6},{6,7},{7,4},{8,9},{9,10},{10,1... | collective-permute-start | bytes 2359304 | tf_op jit(solution)/shard_map/ppermute | solution.py:29
  78.1 48.9 %collective-permute-start.8 = (bf16[192,2048]{1,0:T(8,128)(2,1)}, bf16[192,2048]{1,0:T(8,128)(2,1)}, u32[]{:S(2)}, u32[]{:S(2)}) collective-permute-start(bf16[192,2048]{1,0:T(8,128)(2,1)} %param.23), channel_id=1, source_target_pairs={{0,3},{1,0},{2,1},{3,2},{4,7},{5,4},{6,5},{7,6},{8,11},{9,8},{10,9... | collective-permute-start | bytes 2359304 | tf_op jit(solution)/shard_map/ppermute | solution.py:29
  93.8 24.3 %collective-permute-start.3 = (bf16[128,704]{1,0:T(8,128)(2,1)S(1)}, bf16[128,704]{1,0:T(8,128)(2,1)S(1)}, u32[]{:S(2)}, u32[]{:S(2)}) collective-permute-start(bf16[128,704]{1,0:T(8,128)(2,1)S(1)} %pad_maximum_fusion), channel_id=1, source_target_pairs={{0,1},{1,2},{2,3},{3,0},{4,5},{5,6},{6,7},{7,4},{8,9},{9,10},{10,1... | collective-permute-start | bytes 540680 | tf_op jit(solution)/shard_map/ppermute | solution.py:29
  95.4 25.3 %collective-permute-start.4 = (bf16[128,704]{1,0:T(8,128)(2,1)S(1)}, bf16[128,704]{1,0:T(8,128)(2,1)S(1)}, u32[]{:S(2)}, u32[]{:S(2)}) collective-permute-start(bf16[128,704]{1,0:T(8,128)(2,1)S(1)} %pad_maximum_fusion), channel_id=1, source_target_pairs={{0,2},{1,3},{2,0},{3,1},{4,6},{5,7},{6,4},{7,5},{8,10},{9,11},{10,... | collective-permute-start | bytes 540680 | tf_op jit(solution)/shard_map/ppermute | solution.py:29
  118.2 5.9 %collective-permute-start.5 = (bf16[128,704]{1,0:T(8,128)(2,1)S(1)}, bf16[128,704]{1,0:T(8,128)(2,1)S(1)}, u32[]{:S(2)}, u32[]{:S(2)}) collective-permute-start(bf16[128,704]{1,0:T(8,128)(2,1)S(1)} %pad_maximum_fusion), channel_id=1, source_target_pairs={{0,3},{1,0},{2,1},{3,2},{4,7},{5,4},{6,5},{7,6},{8,11},{9,8},{10,9... | collective-permute-start | bytes 540680 | tf_op jit(solution)/shard_map/ppermute | solution.py:29
  130.4 5.5 %copy-start.13 = (s32[8,8]{1,0:T(8,128)S(1)}, s32[8,8]{1,0:T(8,128)}, u32[]{:S(2)}) copy-start(s32[8,8]{1,0:T(8,128)} %param.18) | copy-start | bytes 772
  134.2 5.6 %collective-permute-start.10 = (bf16[128,512]{1,0:T(8,128)(2,1)}, bf16[128,512]{1,0:T(8,128)(2,1)S(1)}, u32[]{:S(2)}, u32[]{:S(2)}) collective-permute-start(bf16[128,512]{1,0:T(8,128)(2,1)} %get-tuple-element.10), channel_id=1, source_target_pairs={{0,2},{1,3},{2,0},{3,1},{4,6},{5,7},{6,4},{7,5},{8,10},{9,11},{10,... | collective-permute-start | bytes 393224 | tf_op jit(solution)/shard_map/ppermute | solution.py:29
  134.2 6.1 %collective-permute-start.11 = (bf16[128,512]{1,0:T(8,128)(2,1)S(1)}, bf16[128,512]{1,0:T(8,128)(2,1)}, u32[]{:S(2)}, u32[]{:S(2)}) collective-permute-start(bf16[128,512]{1,0:T(8,128)(2,1)S(1)} %get-tuple-element.9), channel_id=1, source_target_pairs={{0,3},{1,0},{2,1},{3,2},{4,7},{5,4},{6,5},{7,6},{8,11},{9,8},{10,9... | collective-permute-start | bytes 393224 | tf_op jit(solution)/shard_map/ppermute | solution.py:29
  135.9 6.4 %collective-permute-start.9 = (bf16[128,512]{1,0:T(8,128)(2,1)S(1)}, bf16[128,512]{1,0:T(8,128)(2,1)}, u32[]{:S(2)}, u32[]{:S(2)}) collective-permute-start(bf16[128,512]{1,0:T(8,128)(2,1)S(1)} %get-tuple-element.8), channel_id=1, source_target_pairs={{0,1},{1,2},{2,3},{3,0},{4,5},{5,6},{6,7},{7,4},{8,9},{9,10},{10,1... | collective-permute-start | bytes 393224 | tf_op jit(solution)/shard_map/ppermute | solution.py:29
  (4 other events, 7.0 us)

commit v5 on v4

--- a/solution.py
+++ b/solution.py
@@ -168,25 +168,30 @@
     normed_two = (
         residual * lax.rsqrt(jnp.mean(residual * residual, axis=1, keepdims=True) + EPS) * mlp_gain
     ).astype(jnp.bfloat16)
-    gate_out = jnp.dot(normed_two, w_gate, preferred_element_type=jnp.float32)
-    up_out = jnp.dot(normed_two, w_up, preferred_element_type=jnp.float32)
-    hidden = (jax.nn.silu(gate_out) * up_out).astype(jnp.bfloat16)
-    unit_part = jnp.einsum(
-        "tu,ujd->jtd",
-        hidden,
-        w_down.reshape(w_down.shape[0], mlp_count, quarter),
-        preferred_element_type=jnp.float32,
-    ).astype(jnp.bfloat16)
-
-    unit_share = lax.dynamic_index_in_dim(unit_part, part_index, 0, keepdims=False).astype(
-        jnp.float32
-    )
-    for k in range(1, mlp_count):
-        target = (part_index + k) % mlp_count
-        piece = lax.dynamic_index_in_dim(unit_part, target, 0, keepdims=False)
-        unit_share = unit_share + shift_mlp(piece, k, mlp_count).astype(jnp.float32)
     residual_share = lax.dynamic_slice_in_dim(residual, part_index * quarter, quarter, 1)
-    result = (residual_share + unit_share).astype(jnp.bfloat16)
+    halves = []
+    half = rows // 2
+    for lower in (0, half):
+        normed_half = normed_two[lower : lower + half]
+        gate_out = jnp.dot(normed_half, w_gate, preferred_element_type=jnp.float32)
+        up_out = jnp.dot(normed_half, w_up, preferred_element_type=jnp.float32)
+        hidden = (jax.nn.silu(gate_out) * up_out).astype(jnp.bfloat16)
+        unit_part = jnp.einsum(
+            "tu,ujd->jtd",
+            hidden,
+            w_down.reshape(w_down.shape[0], mlp_count, quarter),
+            preferred_element_type=jnp.float32,
+        ).astype(jnp.bfloat16)
+
+        unit_share = lax.dynamic_index_in_dim(unit_part, part_index, 0, keepdims=False).astype(
+            jnp.float32
+        )
+        for k in range(1, mlp_count):
+            target = (part_index + k) % mlp_count
+            piece = lax.dynamic_index_in_dim(unit_part, target, 0, keepdims=False)
+            unit_share = unit_share + shift_mlp(piece, k, mlp_count).astype(jnp.float32)
+        halves.append((residual_share[lower : lower + half] + unit_share).astype(jnp.bfloat16))
+    result = jnp.concatenate(halves, axis=0)
     return (result.reshape(per_owner_rows, tokens, quarter), accepted_rows)
 
 

time: 147 us -> 155 us (1.054)
  the two profiles are of different devices: /device:TPU:1 before, /device:TPU:6 now
where the time goes in v5:
time: 155 us
  waiting for transfers between devices  68.6 us (44%)
  starting transfers between devices  45.6 us (29%)
  matrix products  23.3 us (15%)
  local copies, waits for them, and re-layouts  10.2 us (7%)
  other arithmetic  5.75 us (4%)
    ppermute x15, waiting for transfers between devices, shift_mlp(): lax.ppermute(value, 'mlp', [(i, (i + shift) % count) for i in range(count)])  33.7 us
    ppermute x15, starting transfers between devices, shift_mlp(): lax.ppermute(value, 'mlp', [(i, (i + shift) % count) for i in range(count)])  25.6 us
    all_to_all x1, waiting for transfers between devices, per_device(): incoming = lax.all_to_all(outgoing, 'req', 0, 0, tiled=True)  24.9 us
    all_to_all x1, starting transfers between devices, per_device(): incoming = lax.all_to_all(outgoing, 'req', 0, 0, tiled=True)  12.5 us
    all_to_all x1, waiting for transfers between devices, per_device(): arrived = lax.all_to_all(returning, 'req', 0, 0, tiled=True)  10 us
    all_to_all x1, starting transfers between devices, per_device(): arrived = lax.all_to_all(returning, 'req', 0, 0, tiled=True)  7.45 us
    dot_general x2, matrix products, per_device(): jnp.einsum('tu,ujd->jtd', hidden, w_down.reshape(w_down.shape[0], mlp_cou...  6.46 us
    dot_general x4, matrix products, per_device(): jnp.dot(piece[:, quarter:], rows_of_group, preferred_element_type=jnp.flo...  6.04 us
  transfers between devices with their start and end apart: 17, of which 9 were waited for; matrix products, arithmetic and copies ran while one was open for 9% of the time, Pallas kernels for 0%

profile of v5, /device:TPU:6, one launch (start us, length us, event | category | flops | bytes accessed | tf_op | source)
XLA Modules:
  0.0 154.5 jit_solution(17327400430209627852)
XLA Ops:
  3.1 2.5 %gather_fusion = bf16[64,16,512]{2,1,0:T(8,128)(2,1)} fusion(bf16[8,16,512]{2,1,0:T(8,128)(2,1)} %param.14, s32[1024]{0:T(1024)S(1)} %pad_clamp_fusion.3), kind=kCustom, calls=%fused_computation | custom fusion | bytes 2097408 | tf_op jit(solution)/shard_map/jit(_take)/gather | solution.py:86
  5.6 12.5 %all-to-all-start = ((bf16[64,16,512]{2,1,0:T(8,128)(2,1)}), bf16[64,16,512]{2,1,0:T(8,128)(2,1)}, u32[]{:S(2)}, u32[]{:S(2)}) async-start(bf16[64,16,512]{2,1,0:T(8,128)(2,1)} %gather_fusion), calls=%async_computation | async-start | bytes 2097152 | tf_op jit(solution)/shard_map/all_to_all | solution.py:87
  19.7 24.9 %all-to-all-done = bf16[64,16,512]{2,1,0:T(8,128)(2,1)} async-done(((bf16[64,16,512]{2,1,0:T(8,128)(2,1)}), bf16[64,16,512]{2,1,0:T(8,128)(2,1)}, u32[]{:S(2)}, u32[]{:S(2)}) %all-to-all-start) | async-done | bytes 1048608 | tf_op jit(solution)/shard_map/all_to_all | solution.py:87
  44.6 1.8 %gather_fusion.1 = bf16[8,16,512]{2,1,0:T(8,128)(2,1)S(1)} fusion(bf16[64,16,512]{2,1,0:T(8,128)(2,1)} %all-to-all-done, s32[1024]{0:T(1024)S(1)} %pad_clamp_fusion.2), kind=kCustom, calls=%fused_computation.1 | custom fusion | bytes 262176 | tf_op jit(solution)/shard_map/jit(_take)/gather | solution.py:88
  46.4 1.7 %collective-permute-start = (bf16[128,512]{1,0:T(8,128)(2,1)S(1)}, bf16[128,512]{1,0:T(8,128)(2,1)S(1)}, u32[]{:S(2)}, u32[]{:S(2)}) collective-permute-start(bf16[128,512]{1,0:T(8,128)(2,1)S(1)} %bitcast.150), channel_id=1, source_target_pairs={{0,1},{1,2},{2,3},{3,0},{4,5},{5,6},{6,7},{7,4},{8,9},{9,10},{10,1... | collective-permute-start | bytes 393224 | tf_op jit(solution)/shard_map/ppermute | solution.py:29
  48.8 3.0 %collective-permute-start.1 = (bf16[128,512]{1,0:T(8,128)(2,1)S(1)}, bf16[128,512]{1,0:T(8,128)(2,1)S(1)}, u32[]{:S(2)}, u32[]{:S(2)}) collective-permute-start(bf16[128,512]{1,0:T(8,128)(2,1)S(1)} %bitcast.151), channel_id=1, source_target_pairs={{0,2},{1,3},{2,0},{3,1},{4,6},{5,7},{6,4},{7,5},{8,10},{9,11},{10,... | collective-permute-start | bytes 393224 | tf_op jit(solution)/shard_map/ppermute | solution.py:29
  53.3 3.9 %collective-permute-done.1 = bf16[128,512]{1,0:T(8,128)(2,1)S(1)} collective-permute-done((bf16[128,512]{1,0:T(8,128)(2,1)S(1)}, bf16[128,512]{1,0:T(8,128)(2,1)S(1)}, u32[]{:S(2)}, u32[]{:S(2)}) %collective-permute-start.1) | collective-permute-done | bytes 131104 | tf_op jit(solution)/shard_map/ppermute | solution.py:29
  58.4 2.0 %convolution_convert_fusion.4 = bf16[128,128]{1,0:T(8,128)(2,1)} fusion(bf16[2048,128]{1,0:T(8,128)(2,1)} %param.22, bf16[128,2048]{1,0:T(8,128)(2,1)S(1)} %constant_dynamic-update-slice_fusion, f32[2048]{0:T(1024)S(1)} %copy-done.12, f32[128]{0:T(128)S(1)} %add_rsqrt_fusion.1), kind=kOutput, calls=%fused_computation.42 | convolution fusion | flops 68173824 | bytes 1090048 | tf_op jit(solution)/shard_map/dot_general | solution.py:105
  66.7 7.4 %all-to-all-start.1 = ((bf16[64,16,192]{2,1,0:T(8,128)(2,1)}), bf16[64,16,192]{2,1,0:T(8,128)(2,1)}, u32[]{:S(2)}, u32[]{:S(2)}) async-start(bf16[64,16,192]{2,1,0:T(8,128)(2,1)} %gather_fusion.2), calls=%async_computation.1 | async-start | bytes 1048576 | tf_op jit(solution)/shard_map/all_to_all | solution.py:153
  74.1 3.3 %collective-permute-start.7 = (bf16[192,2048]{1,0:T(8,128)(2,1)}, bf16[192,2048]{1,0:T(8,128)(2,1)}, u32[]{:S(2)}, u32[]{:S(2)}) collective-permute-start(bf16[192,2048]{1,0:T(8,128)(2,1)} %param.23), channel_id=1, source_target_pairs={{0,2},{1,3},{2,0},{3,1},{4,6},{5,7},{6,4},{7,5},{8,10},{9,11},{10,... | collective-permute-start | bytes 2359304 | tf_op jit(solution)/shard_map/ppermute | solution.py:29
  77.8 2.9 %collective-permute-start.8 = (bf16[192,2048]{1,0:T(8,128)(2,1)}, bf16[192,2048]{1,0:T(8,128)(2,1)}, u32[]{:S(2)}, u32[]{:S(2)}) collective-permute-start(bf16[192,2048]{1,0:T(8,128)(2,1)} %param.23), channel_id=1, source_target_pairs={{0,3},{1,0},{2,1},{3,2},{4,7},{5,4},{6,5},{7,6},{8,11},{9,8},{10,9... | collective-permute-start | bytes 2359304 | tf_op jit(solution)/shard_map/ppermute | solution.py:29
  80.7 10.0 %all-to-all-done.1 = bf16[64,16,192]{2,1,0:T(8,128)(2,1)} async-done(((bf16[64,16,192]{2,1,0:T(8,128)(2,1)}), bf16[64,16,192]{2,1,0:T(8,128)(2,1)}, u32[]{:S(2)}, u32[]{:S(2)}) %all-to-all-start.1) | async-done | bytes 393248 | tf_op jit(solution)/shard_map/all_to_all | solution.py:153
  90.7 1.6 %gather_fusion.3 = bf16[8,16,192]{2,1,0:T(8,128)(2,1)S(1)} fusion(bf16[64,16,192]{2,1,0:T(8,128)(2,1)} %all-to-all-done.1, s32[1024]{0:T(1024)S(1)} %pad_clamp_fusion), kind=kCustom, calls=%fused_computation.3 | custom fusion | bytes 98336 | tf_op jit(solution)/shard_map/jit(_take)/gather | solution.py:154
  92.4 1.8 %collective-permute-start.3 = (bf16[128,704]{1,0:T(8,128)(2,1)S(1)}, bf16[128,704]{1,0:T(8,128)(2,1)S(1)}, u32[]{:S(2)}, u32[]{:S(2)}) collective-permute-start(bf16[128,704]{1,0:T(8,128)(2,1)S(1)} %pad_maximum_fusion), channel_id=1, source_target_pairs={{0,1},{1,2},{2,3},{3,0},{4,5},{5,6},{6,7},{7,4},{8,9},{9,10},{10,1... | collective-permute-start | bytes 540680 | tf_op jit(solution)/shard_map/ppermute | solution.py:29
  94.2 2.4 %collective-permute-start.4 = (bf16[128,704]{1,0:T(8,128)(2,1)S(1)}, bf16[128,704]{1,0:T(8,128)(2,1)S(1)}, u32[]{:S(2)}, u32[]{:S(2)}) collective-permute-start(bf16[128,704]{1,0:T(8,128)(2,1)S(1)} %pad_maximum_fusion), channel_id=1, source_target_pairs={{0,2},{1,3},{2,0},{3,1},{4,6},{5,7},{6,4},{7,5},{8,10},{9,11},{10,... | collective-permute-start | bytes 540680 | tf_op jit(solution)/shard_map/ppermute | solution.py:29
  98.0 19.4 %collective-permute-done.3 = bf16[128,704]{1,0:T(8,128)(2,1)S(1)} collective-permute-done((bf16[128,704]{1,0:T(8,128)(2,1)S(1)}, bf16[128,704]{1,0:T(8,128)(2,1)S(1)}, u32[]{:S(2)}, u32[]{:S(2)}) %collective-permute-start.3) | collective-permute-done | bytes 180256 | tf_op jit(solution)/shard_map/ppermute | solution.py:29
  118.1 2.8 %collective-permute-done.4 = bf16[128,704]{1,0:T(8,128)(2,1)S(1)} collective-permute-done((bf16[128,704]{1,0:T(8,128)(2,1)S(1)}, bf16[128,704]{1,0:T(8,128)(2,1)S(1)}, u32[]{:S(2)}, u32[]{:S(2)}) %collective-permute-start.4) | collective-permute-done | bytes 180256 | tf_op jit(solution)/shard_map/ppermute | solution.py:29
  120.9 3.3 %collective-permute-done.5 = bf16[128,704]{1,0:T(8,128)(2,1)S(1)} collective-permute-done((bf16[128,704]{1,0:T(8,128)(2,1)S(1)}, bf16[128,704]{1,0:T(8,128)(2,1)S(1)}, u32[]{:S(2)}, u32[]{:S(2)}) %collective-permute-start.5) | collective-permute-done | bytes 180256 | tf_op jit(solution)/shard_map/ppermute | solution.py:29
  127.1 1.8 %multiply_reduce_fusion = (f32[128]{0:T(128)S(1)}, f32[128,2048]{1,0:T(8,128)S(1)}) fusion(bf16[192,2048]{1,0:T(8,128)(2,1)} %collective-permute-done.8, bf16[128,704]{1,0:T(8,128)(2,1)S(1)} %collective-permute-done.5, f32[128,2048]{1,0:T(8,128)S(1)} %fusion.5, f32[128,2048]{1,0:T(8,128)S(1)} %fusion.6, f32[128,2048]{1,0:T(8,128)S(1)} %fusion.7, ...), kind=kOutput, calls=%fused_computation.52 | convolution fusion | flops 103022464 | bytes 5571072 | tf_op jit(solution)/shard_map/dot_general | solution.py:164
  131.4 2.9 %fusion.13 = bf16[64,4,512]{2,0,1:T(8,128)(2,1)S(1)} fusion(bf16[80,4,8,512]{3,2,1,0:T(8,128)(2,1)} %bitcast.158, bf16[2048,640]{1,0:T(8,128)(2,1)S(1)} %copy-done, bf16[128,2048]{1,0:T(8,128)(2,1)S(1)} %multiply_convert_fusion, f32[64,640]{1,0:T(8,128)} %fusion.39), kind=kOutput, calls=%fused_computation.21 | convolution fusion | flops 335921152 | bytes 5931008 | tf_op jit(solution)/shard_map/tu,ujd->jtd/dot_general | solution.py:179
  135.7 2.3 %collective-permute-start.13 = (bf16[64,512]{1,0:T(8,128)(2,1)S(1)}, bf16[64,512]{1,0:T(8,128)(2,1)}, u32[]{:S(2)}, u32[]{:S(2)}) collective-permute-start(bf16[64,512]{1,0:T(8,128)(2,1)S(1)} %get-tuple-element.15), channel_id=1, source_target_pairs={{0,2},{1,3},{2,0},{3,1},{4,6},{5,7},{6,4},{7,5},{8,10},{9,11},{10,... | collective-permute-start | bytes 196616 | tf_op jit(solution)/shard_map/ppermute | solution.py:29
  138.3 3.6 %fusion.10 = bf16[64,4,512]{2,0,1:T(8,128)(2,1)} fusion(bf16[80,4,8,512]{3,2,1,0:T(8,128)(2,1)} %bitcast.159, bf16[2048,640]{1,0:T(8,128)(2,1)S(1)} %copy-done, bf16[128,2048]{1,0:T(8,128)(2,1)S(1)} %multiply_convert_fusion, f32[64,640]{1,0:T(8,128)} %fusion.43), kind=kOutput, calls=%fused_computation.20 | convolution fusion | flops 335921152 | bytes 5931008 | tf_op jit(solution)/shard_map/tu,ujd->jtd/dot_general | solution.py:179
  142.8 2.9 %collective-permute-start.10 = (bf16[64,512]{1,0:T(8,128)(2,1)S(1)}, bf16[64,512]{1,0:T(8,128)(2,1)S(1)}, u32[]{:S(2)}, u32[]{:S(2)}) collective-permute-start(bf16[64,512]{1,0:T(8,128)(2,1)S(1)} %get-tuple-element.12), channel_id=1, source_target_pairs={{0,2},{1,3},{2,0},{3,1},{4,6},{5,7},{6,4},{7,5},{8,10},{9,11},{10,... | collective-permute-start | bytes 196616 | tf_op jit(solution)/shard_map/ppermute | solution.py:29
  150.0 2.7 %collective-permute-done.9 = bf16[64,512]{1,0:T(8,128)(2,1)S(1)} collective-permute-done((bf16[64,512]{1,0:T(8,128)(2,1)S(1)}, bf16[64,512]{1,0:T(8,128)(2,1)S(1)}, u32[]{:S(2)}, u32[]{:S(2)}) %collective-permute-start.9) | collective-permute-done | bytes 65568 | tf_op jit(solution)/shard_map/ppermute | solution.py:29
  (100 shorter events, 30.3 us)
Async XLA Ops:
  0.6 130.8 %copy-start = (bf16[2048,640]{1,0:T(8,128)(2,1)S(1)}, bf16[2048,640]{1,0:T(8,128)(2,1)}, u32[]{:S(2)}) copy-start(bf16[2048,640]{1,0:T(8,128)(2,1)} %param.26) | copy-start | bytes 7864324
  0.6 17.6 %copy-start.10 = (s32[8]{0:T(128)S(1)}, s32[8]{0:T(128)}, u32[]{:S(2)}) copy-start(s32[8]{0:T(128)} %param.16) | copy-start | bytes 100
  0.7 18.2 %copy-start.7 = (s32[8,16]{1,0:T(8,128)S(1)}, s32[8,16]{1,0:T(8,128)}, u32[]{:S(2)}) copy-start(s32[8,16]{1,0:T(8,128)} %param.17) | copy-start | bytes 1540
  5.6 52.8 %copy-start.12 = (f32[2048]{0:T(1024)S(1)}, f32[2048]{0:T(1024)}, u32[]{:S(2)}) copy-start(f32[2048]{0:T(1024)} %param.20) | copy-start | bytes 24580
  5.6 39.0 %all-to-all-start = ((bf16[64,16,512]{2,1,0:T(8,128)(2,1)}), bf16[64,16,512]{2,1,0:T(8,128)(2,1)}, u32[]{:S(2)}, u32[]{:S(2)}) async-start(bf16[64,16,512]{2,1,0:T(8,128)(2,1)} %gather_fusion), calls=%async_computation | async-start | bytes 2097152 | tf_op jit(solution)/shard_map/all_to_all | solution.py:87
  46.4 6.8 %collective-permute-start = (bf16[128,512]{1,0:T(8,128)(2,1)S(1)}, bf16[128,512]{1,0:T(8,128)(2,1)S(1)}, u32[]{:S(2)}, u32[]{:S(2)}) collective-permute-start(bf16[128,512]{1,0:T(8,128)(2,1)S(1)} %bitcast.150), channel_id=1, source_target_pairs={{0,1},{1,2},{2,3},{3,0},{4,5},{5,6},{6,7},{7,4},{8,9},{9,10},{10,1... | collective-permute-start | bytes 393224 | tf_op jit(solution)/shard_map/ppermute | solution.py:29
  48.8 11.6 %copy-start.11 = (bf16[2048,192]{0,1:T(8,128)(2,1)S(1)}, bf16[2048,192]{0,1:T(8,128)(2,1)}, u32[]{:S(2)}) copy-start(bf16[2048,192]{0,1:T(8,128)(2,1)} %param.21) | copy-start | bytes 2359300
  48.8 8.4 %collective-permute-start.1 = (bf16[128,512]{1,0:T(8,128)(2,1)S(1)}, bf16[128,512]{1,0:T(8,128)(2,1)S(1)}, u32[]{:S(2)}, u32[]{:S(2)}) collective-permute-start(bf16[128,512]{1,0:T(8,128)(2,1)S(1)} %bitcast.151), channel_id=1, source_target_pairs={{0,2},{1,3},{2,0},{3,1},{4,6},{5,7},{6,4},{7,5},{8,10},{9,11},{10,... | collective-permute-start | bytes 393224 | tf_op jit(solution)/shard_map/ppermute | solution.py:29
  51.8 6.4 %collective-permute-start.2 = (bf16[128,512]{1,0:T(8,128)(2,1)S(1)}, bf16[128,512]{1,0:T(8,128)(2,1)S(1)}, u32[]{:S(2)}, u32[]{:S(2)}) collective-permute-start(bf16[128,512]{1,0:T(8,128)(2,1)S(1)} %bitcast.152), channel_id=1, source_target_pairs={{0,3},{1,0},{2,1},{3,2},{4,7},{5,4},{6,5},{7,6},{8,11},{9,8},{10,9... | collective-permute-start | bytes 393224 | tf_op jit(solution)/shard_map/ppermute | solution.py:29
  63.9 16.7 %copy-start.9 = (s32[8]{0:T(128)S(1)}, s32[8]{0:T(128)}, u32[]{:S(2)}) copy-start(s32[8]{0:T(128)} %copy-done.8) | copy-start | bytes 100
  64.2 16.5 %copy-start.1 = (bf16[8,16,512]{2,1,0:T(8,128)(2,1)S(1)}, bf16[8,16,512]{2,1,0:T(8,128)(2,1)}, u32[]{:S(2)}) copy-start(bf16[8,16,512]{2,1,0:T(8,128)(2,1)} %param.14) | copy-start | bytes 393220
  66.7 24.1 %all-to-all-start.1 = ((bf16[64,16,192]{2,1,0:T(8,128)(2,1)}), bf16[64,16,192]{2,1,0:T(8,128)(2,1)}, u32[]{:S(2)}, u32[]{:S(2)}) async-start(bf16[64,16,192]{2,1,0:T(8,128)(2,1)} %gather_fusion.2), calls=%async_computation.1 | async-start | bytes 1048576 | tf_op jit(solution)/shard_map/all_to_all | solution.py:153
  74.1 50.0 %collective-permute-start.7 = (bf16[192,2048]{1,0:T(8,128)(2,1)}, bf16[192,2048]{1,0:T(8,128)(2,1)}, u32[]{:S(2)}, u32[]{:S(2)}) collective-permute-start(bf16[192,2048]{1,0:T(8,128)(2,1)} %param.23), channel_id=1, source_target_pairs={{0,2},{1,3},{2,0},{3,1},{4,6},{5,7},{6,4},{7,5},{8,10},{9,11},{10,... | collective-permute-start | bytes 2359304 | tf_op jit(solution)/shard_map/ppermute | solution.py:29
  77.4 48.2 %collective-permute-start.6 = (bf16[192,2048]{1,0:T(8,128)(2,1)}, bf16[192,2048]{1,0:T(8,128)(2,1)}, u32[]{:S(2)}, u32[]{:S(2)}) collective-permute-start(bf16[192,2048]{1,0:T(8,128)(2,1)} %param.23), channel_id=1, source_target_pairs={{0,1},{1,2},{2,3},{3,0},{4,5},{5,6},{6,7},{7,4},{8,9},{9,10},{10,1... | collective-permute-start | bytes 2359304 | tf_op jit(solution)/shard_map/ppermute | solution.py:29
  77.8 49.3 %collective-permute-start.8 = (bf16[192,2048]{1,0:T(8,128)(2,1)}, bf16[192,2048]{1,0:T(8,128)(2,1)}, u32[]{:S(2)}, u32[]{:S(2)}) collective-permute-start(bf16[192,2048]{1,0:T(8,128)(2,1)} %param.23), channel_id=1, source_target_pairs={{0,3},{1,0},{2,1},{3,2},{4,7},{5,4},{6,5},{7,6},{8,11},{9,8},{10,9... | collective-permute-start | bytes 2359304 | tf_op jit(solution)/shard_map/ppermute | solution.py:29
  92.4 25.0 %collective-permute-start.3 = (bf16[128,704]{1,0:T(8,128)(2,1)S(1)}, bf16[128,704]{1,0:T(8,128)(2,1)S(1)}, u32[]{:S(2)}, u32[]{:S(2)}) collective-permute-start(bf16[128,704]{1,0:T(8,128)(2,1)S(1)} %pad_maximum_fusion), channel_id=1, source_target_pairs={{0,1},{1,2},{2,3},{3,0},{4,5},{5,6},{6,7},{7,4},{8,9},{9,10},{10,1... | collective-permute-start | bytes 540680 | tf_op jit(solution)/shard_map/ppermute | solution.py:29
  94.2 26.6 %collective-permute-start.4 = (bf16[128,704]{1,0:T(8,128)(2,1)S(1)}, bf16[128,704]{1,0:T(8,128)(2,1)S(1)}, u32[]{:S(2)}, u32[]{:S(2)}) collective-permute-start(bf16[128,704]{1,0:T(8,128)(2,1)S(1)} %pad_maximum_fusion), channel_id=1, source_target_pairs={{0,2},{1,3},{2,0},{3,1},{4,6},{5,7},{6,4},{7,5},{8,10},{9,11},{10,... | collective-permute-start | bytes 540680 | tf_op jit(solution)/shard_map/ppermute | solution.py:29
  117.4 6.7 %collective-permute-start.5 = (bf16[128,704]{1,0:T(8,128)(2,1)S(1)}, bf16[128,704]{1,0:T(8,128)(2,1)S(1)}, u32[]{:S(2)}, u32[]{:S(2)}) collective-permute-start(bf16[128,704]{1,0:T(8,128)(2,1)S(1)} %pad_maximum_fusion), channel_id=1, source_target_pairs={{0,3},{1,0},{2,1},{3,2},{4,7},{5,4},{6,5},{7,6},{8,11},{9,8},{10,9... | collective-permute-start | bytes 540680 | tf_op jit(solution)/shard_map/ppermute | solution.py:29
  135.0 12.3 %collective-permute-start.12 = (bf16[64,512]{1,0:T(8,128)(2,1)}, bf16[64,512]{1,0:T(8,128)(2,1)}, u32[]{:S(2)}, u32[]{:S(2)}) collective-permute-start(bf16[64,512]{1,0:T(8,128)(2,1)} %get-tuple-element.13), channel_id=1, source_target_pairs={{0,1},{1,2},{2,3},{3,0},{4,5},{5,6},{6,7},{7,4},{8,9},{9,10},{10,1... | collective-permute-start | bytes 196616 | tf_op jit(solution)/shard_map/ppermute | solution.py:29
  135.7 13.7 %collective-permute-start.13 = (bf16[64,512]{1,0:T(8,128)(2,1)S(1)}, bf16[64,512]{1,0:T(8,128)(2,1)}, u32[]{:S(2)}, u32[]{:S(2)}) collective-permute-start(bf16[64,512]{1,0:T(8,128)(2,1)S(1)} %get-tuple-element.15), channel_id=1, source_target_pairs={{0,2},{1,3},{2,0},{3,1},{4,6},{5,7},{6,4},{7,5},{8,10},{9,11},{10,... | collective-permute-start | bytes 196616 | tf_op jit(solution)/shard_map/ppermute | solution.py:29
  137.9 11.4 %collective-permute-start.14 = (bf16[64,512]{1,0:T(8,128)(2,1)S(1)}, bf16[64,512]{1,0:T(8,128)(2,1)}, u32[]{:S(2)}, u32[]{:S(2)}) collective-permute-start(bf16[64,512]{1,0:T(8,128)(2,1)S(1)} %get-tuple-element.14), channel_id=1, source_target_pairs={{0,3},{1,0},{2,1},{3,2},{4,7},{5,4},{6,5},{7,6},{8,11},{9,8},{10,9... | collective-permute-start | bytes 196616 | tf_op jit(solution)/shard_map/ppermute | solution.py:29
  142.8 6.5 %collective-permute-start.10 = (bf16[64,512]{1,0:T(8,128)(2,1)S(1)}, bf16[64,512]{1,0:T(8,128)(2,1)S(1)}, u32[]{:S(2)}, u32[]{:S(2)}) collective-permute-start(bf16[64,512]{1,0:T(8,128)(2,1)S(1)} %get-tuple-element.12), channel_id=1, source_target_pairs={{0,2},{1,3},{2,0},{3,1},{4,6},{5,7},{6,4},{7,5},{8,10},{9,11},{10,... | collective-permute-start | bytes 196616 | tf_op jit(solution)/shard_map/ppermute | solution.py:29
  145.7 4.3 %collective-permute-start.11 = (bf16[64,512]{1,0:T(8,128)(2,1)S(1)}, bf16[64,512]{1,0:T(8,128)(2,1)S(1)}, u32[]{:S(2)}, u32[]{:S(2)}) collective-permute-start(bf16[64,512]{1,0:T(8,128)(2,1)S(1)} %get-tuple-element.11), channel_id=1, source_target_pairs={{0,3},{1,0},{2,1},{3,2},{4,7},{5,4},{6,5},{7,6},{8,11},{9,8},{10,9... | collective-permute-start | bytes 196616 | tf_op jit(solution)/shard_map/ppermute | solution.py:29
  147.2 5.5 %collective-permute-start.9 = (bf16[64,512]{1,0:T(8,128)(2,1)S(1)}, bf16[64,512]{1,0:T(8,128)(2,1)S(1)}, u32[]{:S(2)}, u32[]{:S(2)}) collective-permute-start(bf16[64,512]{1,0:T(8,128)(2,1)S(1)} %get-tuple-element.10), channel_id=1, source_target_pairs={{0,1},{1,2},{2,3},{3,0},{4,5},{5,6},{6,7},{7,4},{8,9},{9,10},{10,1... | collective-permute-start | bytes 196616 | tf_op jit(solution)/shard_map/ppermute | solution.py:29
  (7 other events, 29.7 us)

commit v6 on v4

--- a/solution.py
+++ b/solution.py
@@ -64,30 +64,28 @@
     part_index = lax.axis_index("mlp")
     per_owner_rows, tokens, quarter = drafts.shape
 
+    rows = per_owner_rows * tokens
     w_out_all = pieces_mlp(w_out, mlp_count)
+    owned_pieces = pieces_mlp(drafts.reshape(rows, quarter), mlp_count)
 
     local_ids = jnp.arange(per_owner_rows, dtype=jnp.int32)
-    devices = jnp.arange(req_count, dtype=jnp.int32)
     my_slots = lax.dynamic_slice_in_dim(slot_of, my_index * per_owner_rows, per_owner_rows)
     my_owners = my_slots // per_owner_rows
-    send_pick = jnp.sum(
-        jnp.where(my_owners[None, :] == devices[:, None], local_ids[None, :], 0), axis=1
-    )
     owned_slots = my_index * per_owner_rows + local_ids
     requests = jnp.arange(slot_of.shape[0], dtype=jnp.int32)
     request_of = jnp.sum(
         jnp.where(slot_of[None, :] == owned_slots[:, None], requests[None, :], 0), axis=1
     )
     source_of = request_of // per_owner_rows
-    return_pick = jnp.sum(
-        jnp.where(source_of[None, :] == devices[:, None], local_ids[None, :], 0), axis=1
-    )
-
-    outgoing = jnp.take(drafts, send_pick, axis=0, mode="clip")
+
+    outgoing = (
+        jnp.zeros((req_count,) + drafts.shape[1:], drafts.dtype)
+        .at[my_owners]
+        .set(drafts, unique_indices=True, mode="promise_in_bounds")
+    )
     incoming = lax.all_to_all(outgoing, "req", 0, 0, tiled=True)
     local_rows = jnp.take(incoming, source_of, axis=0, mode="clip")
 
-    rows = per_owner_rows * tokens
     owner_pieces = pieces_mlp(local_rows.reshape(rows, quarter), mlp_count)
     full_rows = place_blocks(owner_pieces, mlp_count, part_index)
     wide_rows = full_rows.astype(jnp.float32)
@@ -149,20 +147,21 @@
     head_width = kv_heads * group_heads * HEAD_DIM
     attended = attended.reshape(per_owner_rows, tokens, head_width)
 
-    returning = jnp.take(attended, return_pick, axis=0, mode="clip")
+    returning = (
+        jnp.zeros((req_count,) + attended.shape[1:], attended.dtype)
+        .at[source_of]
+        .set(attended, unique_indices=True, mode="promise_in_bounds")
+    )
     arrived = lax.all_to_all(returning, "req", 0, 0, tiled=True)
     back_rows = jnp.take(arrived, my_owners, axis=0, mode="clip")
 
-    packed = jnp.concatenate(
-        [drafts.reshape(rows, quarter), back_rows.reshape(rows, head_width)], axis=1
-    )
-    gathered = pieces_mlp(packed, mlp_count)
-    owned_all = place_blocks([piece[:, :quarter] for piece in gathered], mlp_count, part_index)
+    gathered = pieces_mlp(back_rows.reshape(rows, head_width), mlp_count)
+    owned_all = place_blocks(owned_pieces, mlp_count, part_index)
 
     residual = owned_all.astype(jnp.float32)
     for piece, rows_of_group in zip(gathered, w_out_all):
         group_product = jnp.dot(
-            piece[:, quarter:], rows_of_group, preferred_element_type=jnp.float32
+            piece, rows_of_group, preferred_element_type=jnp.float32
         )
         residual = residual + group_product.astype(jnp.bfloat16).astype(jnp.float32)
     normed_two = (

time: 147 us -> 162 us (1.10)
  starting transfers between devices: 36.4 us -> 43.6 us
  waiting for transfers between devices: 72.6 us -> 77.4 us
  local copies, waits for them, and re-layouts: 10.3 us -> 12.9 us
    ppermute x12 -> x15, waiting for transfers between devices: 34.3 us -> 50.5 us  [shift_mlp(): lax.ppermute(value, 'mlp', [(i, (i + shift) % count) for i in range(count)])]
    all_to_all x1, waiting for transfers between devices: 11.4 us -> 0.01 us  [per_device(): arrived = lax.all_to_all(returning, 'req', 0, 0, tiled=True)]
    ppermute x12 -> x15, starting transfers between devices: 16.1 us -> 23.4 us  [shift_mlp(): lax.ppermute(value, 'mlp', [(i, (i + shift) % count) for i in range(count)])]
    scatter x0 -> x2, local copies, waits for them, and re-layouts: none -> 4.27 us  [the longest x1 2.27 us: per_device(): outgoing = jnp.zeros((req_count,) + drafts.shape[1:], drafts.dtype).at[my...]
    gather x2 -> x0, local copies, waits for them, and re-layouts: 4.06 us -> none  [the longest x1 2.54 us: per_device(): outgoing = jnp.take(drafts, send_pick, axis=0, mode='clip')]
    broadcast_in_dim x0 -> x2, local copies, waits for them, and re-layouts: none -> 1.95 us  [the longest x1 1.12 us: per_device(): jnp.zeros((req_count,) + drafts.shape[1:], drafts.dtype).at[my_owners]]
  transfers between devices with their start and end apart: 14 -> 17, of which waited for: 10 -> 10; matrix products, arithmetic and copies ran while one was open for 7% -> 7% of each run, Pallas kernels for 0% -> 0%
where the time goes in v6:
time: 162 us; the launch traced here: 159 us
  waiting for transfers between devices  77.4 us (48%)
  starting transfers between devices  43.6 us (27%)
  matrix products  18.8 us (12%)
  local copies, waits for them, and re-layouts  12.9 us (8%)
  other arithmetic  5.15 us (3%)
    ppermute x15, waiting for transfers between devices, shift_mlp(): lax.ppermute(value, 'mlp', [(i, (i + shift) % count) for i in range(count)])  50.5 us
    all_to_all x1, waiting for transfers between devices, per_device(): incoming = lax.all_to_all(outgoing, 'req', 0, 0, tiled=True)  26.8 us
    ppermute x15, starting transfers between devices, shift_mlp(): lax.ppermute(value, 'mlp', [(i, (i + shift) % count) for i in range(count)])  23.4 us
    all_to_all x1, starting transfers between devices, per_device(): incoming = lax.all_to_all(outgoing, 'req', 0, 0, tiled=True)  13.3 us
    all_to_all x1, starting transfers between devices, per_device(): arrived = lax.all_to_all(returning, 'req', 0, 0, tiled=True)  6.95 us
    dot_general x4, matrix products, per_device(): jnp.dot(piece, rows_of_group, preferred_element_type=jnp.float32)  5.88 us
  transfers between devices with their start and end apart: 17, of which 10 were waited for; matrix products, arithmetic and copies ran while one was open for 7% of the time, Pallas kernels for 0%

profile of v6, /device:TPU:1, one launch (start us, length us, event | category | flops | bytes accessed | tf_op | source)
XLA Modules:
  0.0 158.9 jit_solution(6123111374259521919)
XLA Ops:
  3.2 2.3 %scatter_fusion = bf16[64,16,512]{2,1,0:T(8,128)(2,1)} fusion(bf16[64,16,512]{2,1,0:T(8,128)(2,1)} %broadcast_in_dim.75, s32[8]{0:T(128)S(1)} %get-tuple-element.10, bf16[8,16,512]{2,1,0:T(8,128)(2,1)} %param.14), kind=kCustom, calls=%fused_computation.2 | custom fusion | bytes 393248 | tf_op jit(solution)/shard_map/scatter | solution.py:84
  5.5 13.3 %all-to-all-start = ((bf16[64,16,512]{2,1,0:T(8,128)(2,1)}), bf16[64,16,512]{2,1,0:T(8,128)(2,1)}, u32[]{:S(2)}, u32[]{:S(2)}) async-start(bf16[64,16,512]{2,1,0:T(8,128)(2,1)} %scatter_fusion), calls=%async_computation | async-start | bytes 2097152 | tf_op jit(solution)/shard_map/all_to_all | solution.py:86
  20.4 26.8 %all-to-all-done = bf16[64,16,512]{2,1,0:T(8,128)(2,1)} async-done(((bf16[64,16,512]{2,1,0:T(8,128)(2,1)}), bf16[64,16,512]{2,1,0:T(8,128)(2,1)}, u32[]{:S(2)}, u32[]{:S(2)}) %all-to-all-start) | async-done | bytes 1048608 | tf_op jit(solution)/shard_map/all_to_all | solution.py:86
  47.2 1.8 %gather_fusion = bf16[8,16,512]{2,1,0:T(8,128)(2,1)S(1)} fusion(bf16[64,16,512]{2,1,0:T(8,128)(2,1)} %all-to-all-done, s32[1024]{0:T(1024)S(1)} %pad_clamp_fusion.1), kind=kCustom, calls=%fused_computation | custom fusion | bytes 262176 | tf_op jit(solution)/shard_map/jit(_take)/gather | solution.py:87
  51.2 2.7 %collective-permute-start.4 = (bf16[128,512]{1,0:T(8,128)(2,1)S(1)}, bf16[128,512]{1,0:T(8,128)(2,1)S(1)}, u32[]{:S(2)}, u32[]{:S(2)}) collective-permute-start(bf16[128,512]{1,0:T(8,128)(2,1)S(1)} %bitcast.139), channel_id=1, source_target_pairs={{0,2},{1,3},{2,0},{3,1},{4,6},{5,7},{6,4},{7,5},{8,10},{9,11},{10,... | collective-permute-start | bytes 393224 | tf_op jit(solution)/shard_map/ppermute | solution.py:29
  55.4 3.9 %collective-permute-done.4 = bf16[128,512]{1,0:T(8,128)(2,1)S(1)} collective-permute-done((bf16[128,512]{1,0:T(8,128)(2,1)S(1)}, bf16[128,512]{1,0:T(8,128)(2,1)S(1)}, u32[]{:S(2)}, u32[]{:S(2)}) %collective-permute-start.4) | collective-permute-done | bytes 131104 | tf_op jit(solution)/shard_map/ppermute | solution.py:29
  59.7 2.0 %convolution_convert_fusion.4 = bf16[128,128]{1,0:T(8,128)(2,1)} fusion(bf16[2048,128]{1,0:T(8,128)(2,1)} %param.22, bf16[128,2048]{1,0:T(8,128)(2,1)S(1)} %constant_dynamic-update-slice_fusion, f32[2048]{0:T(1024)S(1)} %copy-done.13, f32[128]{0:T(128)S(1)} %add_rsqrt_fusion.1), kind=kOutput, calls=%fused_computation.35 | convolution fusion | flops 68173824 | bytes 1090048 | tf_op jit(solution)/shard_map/dot_general | solution.py:103
  63.0 1.5 fusion.56
  68.0 2.0 %scatter_fusion.1 = bf16[64,16,192]{2,1,0:T(8,128)(2,1)} fusion(bf16[64,16,192]{2,1,0:T(8,128)(2,1)} %broadcast_in_dim.47, s32[8]{0:T(128)S(1)} %copy-done.10, bf16[8,16,192]{2,1,0:T(8,128)(2,1)S(1)} %reshape.273), kind=kCustom, calls=%fused_computation.3 | custom fusion | bytes 147488 | tf_op jit(solution)/shard_map/scatter | solution.py:153
  70.0 7.0 %all-to-all-start.1 = ((bf16[64,16,192]{2,1,0:T(8,128)(2,1)}), bf16[64,16,192]{2,1,0:T(8,128)(2,1)}, u32[]{:S(2)}, u32[]{:S(2)}) async-start(bf16[64,16,192]{2,1,0:T(8,128)(2,1)} %scatter_fusion.1), calls=%async_computation.1 | async-start | bytes 1048576 | tf_op jit(solution)/shard_map/all_to_all | solution.py:155
  76.9 3.0 %collective-permute-start.9 = (bf16[192,2048]{1,0:T(8,128)(2,1)}, bf16[192,2048]{1,0:T(8,128)(2,1)}, u32[]{:S(2)}, u32[]{:S(2)}) collective-permute-start(bf16[192,2048]{1,0:T(8,128)(2,1)} %param.23), channel_id=1, source_target_pairs={{0,2},{1,3},{2,0},{3,1},{4,6},{5,7},{6,4},{7,5},{8,10},{9,11},{10,... | collective-permute-start | bytes 2359304 | tf_op jit(solution)/shard_map/ppermute | solution.py:29
  80.0 3.8 %collective-permute-start.1 = (bf16[128,512]{1,0:T(8,128)(2,1)S(1)}, bf16[128,512]{1,0:T(8,128)(2,1)S(1)}, u32[]{:S(2)}, u32[]{:S(2)}) collective-permute-start(bf16[128,512]{1,0:T(8,128)(2,1)S(1)} %bitcast.135), channel_id=1, source_target_pairs={{0,2},{1,3},{2,0},{3,1},{4,6},{5,7},{6,4},{7,5},{8,10},{9,11},{10,... | collective-permute-start | bytes 393224 | tf_op jit(solution)/shard_map/ppermute | solution.py:29
  84.3 34.5 %collective-permute-done = bf16[128,512]{1,0:T(8,128)(2,1)} collective-permute-done((bf16[128,512]{1,0:T(8,128)(2,1)S(1)}, bf16[128,512]{1,0:T(8,128)(2,1)}, u32[]{:S(2)}, u32[]{:S(2)}) %collective-permute-start) | collective-permute-done | bytes 131104 | tf_op jit(solution)/shard_map/ppermute | solution.py:29
  119.9 1.6 %gather_fusion.1 = bf16[8,16,192]{2,1,0:T(8,128)(2,1)S(1)} fusion(bf16[64,16,192]{2,1,0:T(8,128)(2,1)} %all-to-all-done.1, s32[1024]{0:T(1024)S(1)} %pad_clamp_fusion), kind=kCustom, calls=%fused_computation.1 | custom fusion | bytes 98336 | tf_op jit(solution)/shard_map/jit(_take)/gather | solution.py:156
  121.5 3.0 %collective-permute-start.8 = (bf16[128,192]{1,0:T(8,128)(2,1)S(1)}, bf16[128,192]{1,0:T(8,128)(2,1)S(1)}, u32[]{:S(2)}, u32[]{:S(2)}) collective-permute-start(bf16[128,192]{1,0:T(8,128)(2,1)S(1)} %bitcast.142), channel_id=1, source_target_pairs={{0,2},{1,3},{2,0},{3,1},{4,6},{5,7},{6,4},{7,5},{8,10},{9,11},{10,... | collective-permute-start | bytes 147464 | tf_op jit(solution)/shard_map/ppermute | solution.py:29
  125.9 2.7 %collective-permute-start.10 = (bf16[128,192]{1,0:T(8,128)(2,1)S(1)}, bf16[128,192]{1,0:T(8,128)(2,1)S(1)}, u32[]{:S(2)}, u32[]{:S(2)}) collective-permute-start(bf16[128,192]{1,0:T(8,128)(2,1)S(1)} %bitcast.145), channel_id=1, source_target_pairs={{0,3},{1,0},{2,1},{3,2},{4,7},{5,4},{6,5},{7,6},{8,11},{9,8},{10,9... | collective-permute-start | bytes 147464 | tf_op jit(solution)/shard_map/ppermute | solution.py:29
  131.6 6.0 %collective-permute-done.11 = bf16[192,2048]{1,0:T(8,128)(2,1)} collective-permute-done((bf16[192,2048]{1,0:T(8,128)(2,1)}, bf16[192,2048]{1,0:T(8,128)(2,1)}, u32[]{:S(2)}, u32[]{:S(2)}) %collective-permute-start.11) | collective-permute-done | bytes 786464 | tf_op jit(solution)/shard_map/ppermute | solution.py:29
  137.6 2.4 %collective-permute-done.10 = bf16[128,192]{1,0:T(8,128)(2,1)S(1)} collective-permute-done((bf16[128,192]{1,0:T(8,128)(2,1)S(1)}, bf16[128,192]{1,0:T(8,128)(2,1)S(1)}, u32[]{:S(2)}, u32[]{:S(2)}) %collective-permute-start.10) | collective-permute-done | bytes 49184 | tf_op jit(solution)/shard_map/ppermute | solution.py:29
  140.1 1.6 %multiply_reduce_fusion = (f32[128]{0:T(128)S(1)}, f32[128,2048]{1,0:T(8,128)S(1)}) fusion(f32[128,2048]{1,0:T(8,128)S(1)} %fusion.4, f32[128,2048]{1,0:T(8,128)S(1)} %fusion.5, f32[128,2048]{1,0:T(8,128)S(1)} %fusion.6, bf16[128,2048]{1,0:T(8,128)(2,1)S(1)} %constant_dynamic-update-slice_fusion.4, bf16[128,192]{1,0:T(8,128)(2,1)S(1)} %collective-permute-done.10, ...), kind=kOutput, calls=%fused_computation.45 | convolution fusion | flops 103022464 | bytes 5554688 | tf_op jit(solution)/shard_map/dot_general | solution.py:163
  143.3 3.1 %fusion.7 = bf16[128,4,512]{2,0,1:T(8,128)(2,1)S(1)} fusion(bf16[80,4,8,512]{3,2,1,0:T(8,128)(2,1)} %bitcast.150, bf16[2048,640]{1,0:T(8,128)(2,1)S(1)} %copy-done, f32[128,640]{1,0:T(8,128)S(1)} %fusion.55, f32[128,2048]{1,0:T(8,128)} %copy-done.1, f32[2048]{0:T(1024)S(1)} %copy-done.6, f32[128]{0:T(128)S(1)} %add_rsqrt_fusion), kind=kOutput, calls=%fused_computation.17 | convolution fusion | flops 672628736 | bytes 7152128 | tf_op jit(solution)/shard_map/tu,ujd->jtd/dot_general | solution.py:173
  148.4 4.0 %collective-permute-start.13 = (bf16[128,512]{1,0:T(8,128)(2,1)S(1)}, bf16[128,512]{1,0:T(8,128)(2,1)}, u32[]{:S(2)}, u32[]{:S(2)}) collective-permute-start(bf16[128,512]{1,0:T(8,128)(2,1)S(1)} %get-tuple-element.14), channel_id=1, source_target_pairs={{0,2},{1,3},{2,0},{3,1},{4,6},{5,7},{6,4},{7,5},{8,10},{9,11},{10,... | collective-permute-start | bytes 393224 | tf_op jit(solution)/shard_map/ppermute | solution.py:29
  152.4 1.6 fusion.19
  154.0 2.6 %collective-permute-done.13 = bf16[128,512]{1,0:T(8,128)(2,1)} collective-permute-done((bf16[128,512]{1,0:T(8,128)(2,1)S(1)}, bf16[128,512]{1,0:T(8,128)(2,1)}, u32[]{:S(2)}, u32[]{:S(2)}) %collective-permute-start.13) | collective-permute-done | bytes 131104 | tf_op jit(solution)/shard_map/ppermute | solution.py:29
  157.1 1.8 %fusion.37 = bf16[128,512]{1,0:T(8,128)(2,1)} fusion(bf16[128,512]{1,0:T(8,128)(2,1)} %collective-permute-done.14, bf16[128,512]{1,0:T(8,128)(2,1)} %collective-permute-done.13, bf16[128,512]{1,0:T(8,128)(2,1)S(1)} %collective-permute-done.12, f32[128,2048]{1,0:T(8,128)} %copy-done.1, s32[]{:T(128)S(6)} %select_n.138, bf16[128,4,512]{2,0,1:T(8,128)(2,1)S(1)} %fusion.7, ...), kind=kLoop, calls=%fused_computation.62 | loop fusion | flops 589824 | bytes 917512 | tf_op jit(solution)/shard_map/convert_element_type | solution.py:188
  (94 shorter events, 22.8 us)
Async XLA Ops:
  0.6 142.7 %copy-start = (bf16[2048,640]{1,0:T(8,128)(2,1)S(1)}, bf16[2048,640]{1,0:T(8,128)(2,1)}, u32[]{:S(2)}) copy-start(bf16[2048,640]{1,0:T(8,128)(2,1)} %param.26) | copy-start | bytes 7864324
  0.6 18.2 %copy-start.8 = (s32[512]{0:T(512)S(1)}, s32[512]{0:T(512)}, u32[]{:S(2)}) copy-start(s32[512]{0:T(512)} %param.15) | copy-start | bytes 6148
  0.7 18.9 %copy-start.7 = (s32[8,16]{1,0:T(8,128)S(1)}, s32[8,16]{1,0:T(8,128)}, u32[]{:S(2)}) copy-start(s32[8,16]{1,0:T(8,128)} %param.17) | copy-start | bytes 1540
  0.7 49.7 %copy-start.11 = (s32[8]{0:T(128)S(1)}, s32[8]{0:T(128)}, u32[]{:S(2)}) copy-start(s32[8]{0:T(128)} %param.16) | copy-start | bytes 100
  5.5 54.2 %copy-start.13 = (f32[2048]{0:T(1024)S(1)}, f32[2048]{0:T(1024)}, u32[]{:S(2)}) copy-start(f32[2048]{0:T(1024)} %param.20) | copy-start | bytes 24580
  5.5 41.7 %all-to-all-start = ((bf16[64,16,512]{2,1,0:T(8,128)(2,1)}), bf16[64,16,512]{2,1,0:T(8,128)(2,1)}, u32[]{:S(2)}, u32[]{:S(2)}) async-start(bf16[64,16,512]{2,1,0:T(8,128)(2,1)} %scatter_fusion), calls=%async_computation | async-start | bytes 2097152 | tf_op jit(solution)/shard_map/all_to_all | solution.py:86
  49.0 6.4 %collective-permute-start.3 = (bf16[128,512]{1,0:T(8,128)(2,1)S(1)}, bf16[128,512]{1,0:T(8,128)(2,1)S(1)}, u32[]{:S(2)}, u32[]{:S(2)}) collective-permute-start(bf16[128,512]{1,0:T(8,128)(2,1)S(1)} %bitcast.138), channel_id=1, source_target_pairs={{0,1},{1,2},{2,3},{3,0},{4,5},{5,6},{6,7},{7,4},{8,9},{9,10},{10,1... | collective-permute-start | bytes 393224 | tf_op jit(solution)/shard_map/ppermute | solution.py:29
  51.2 8.2 %collective-permute-start.4 = (bf16[128,512]{1,0:T(8,128)(2,1)S(1)}, bf16[128,512]{1,0:T(8,128)(2,1)S(1)}, u32[]{:S(2)}, u32[]{:S(2)}) collective-permute-start(bf16[128,512]{1,0:T(8,128)(2,1)S(1)} %bitcast.139), channel_id=1, source_target_pairs={{0,2},{1,3},{2,0},{3,1},{4,6},{5,7},{6,4},{7,5},{8,10},{9,11},{10,... | collective-permute-start | bytes 393224 | tf_op jit(solution)/shard_map/ppermute | solution.py:29
  53.9 5.5 %collective-permute-start.5 = (bf16[128,512]{1,0:T(8,128)(2,1)S(1)}, bf16[128,512]{1,0:T(8,128)(2,1)S(1)}, u32[]{:S(2)}, u32[]{:S(2)}) collective-permute-start(bf16[128,512]{1,0:T(8,128)(2,1)S(1)} %bitcast.140), channel_id=1, source_target_pairs={{0,3},{1,0},{2,1},{3,2},{4,7},{5,4},{6,5},{7,6},{8,11},{9,8},{10,9... | collective-permute-start | bytes 393224 | tf_op jit(solution)/shard_map/ppermute | solution.py:29
  65.9 14.1 %copy-start.4 = (bf16[8,16,512]{2,1,0:T(8,128)(2,1)S(1)}, bf16[8,16,512]{2,1,0:T(8,128)(2,1)}, u32[]{:S(2)}) copy-start(bf16[8,16,512]{2,1,0:T(8,128)(2,1)} %param.14) | copy-start | bytes 393220
  66.1 18.1 %copy-start.9 = (s32[8]{0:T(128)S(1)}, s32[8]{0:T(128)}, u32[]{:S(2)}) copy-start(s32[8]{0:T(128)} %get-tuple-element.11) | copy-start | bytes 100
  70.0 49.9 %all-to-all-start.1 = ((bf16[64,16,192]{2,1,0:T(8,128)(2,1)}), bf16[64,16,192]{2,1,0:T(8,128)(2,1)}, u32[]{:S(2)}, u32[]{:S(2)}) async-start(bf16[64,16,192]{2,1,0:T(8,128)(2,1)} %scatter_fusion.1), calls=%async_computation.1 | async-start | bytes 1048576 | tf_op jit(solution)/shard_map/all_to_all | solution.py:155
  76.9 49.0 %collective-permute-start.9 = (bf16[192,2048]{1,0:T(8,128)(2,1)}, bf16[192,2048]{1,0:T(8,128)(2,1)}, u32[]{:S(2)}, u32[]{:S(2)}) collective-permute-start(bf16[192,2048]{1,0:T(8,128)(2,1)} %param.23), channel_id=1, source_target_pairs={{0,2},{1,3},{2,0},{3,1},{4,6},{5,7},{6,4},{7,5},{8,10},{9,11},{10,... | collective-permute-start | bytes 2359304 | tf_op jit(solution)/shard_map/ppermute | solution.py:29
  79.9 50.2 %collective-permute-start.7 = (bf16[192,2048]{1,0:T(8,128)(2,1)}, bf16[192,2048]{1,0:T(8,128)(2,1)}, u32[]{:S(2)}, u32[]{:S(2)}) collective-permute-start(bf16[192,2048]{1,0:T(8,128)(2,1)} %param.23), channel_id=1, source_target_pairs={{0,1},{1,2},{2,3},{3,0},{4,5},{5,6},{6,7},{7,4},{8,9},{9,10},{10,1... | collective-permute-start | bytes 2359304 | tf_op jit(solution)/shard_map/ppermute | solution.py:29
  80.0 38.8 %collective-permute-start = (bf16[128,512]{1,0:T(8,128)(2,1)S(1)}, bf16[128,512]{1,0:T(8,128)(2,1)}, u32[]{:S(2)}, u32[]{:S(2)}) collective-permute-start(bf16[128,512]{1,0:T(8,128)(2,1)S(1)} %bitcast.134), channel_id=1, source_target_pairs={{0,1},{1,2},{2,3},{3,0},{4,5},{5,6},{6,7},{7,4},{8,9},{9,10},{10,1... | collective-permute-start | bytes 393224 | tf_op jit(solution)/shard_map/ppermute | solution.py:29
  80.0 39.8 %collective-permute-start.1 = (bf16[128,512]{1,0:T(8,128)(2,1)S(1)}, bf16[128,512]{1,0:T(8,128)(2,1)S(1)}, u32[]{:S(2)}, u32[]{:S(2)}) collective-permute-start(bf16[128,512]{1,0:T(8,128)(2,1)S(1)} %bitcast.135), channel_id=1, source_target_pairs={{0,2},{1,3},{2,0},{3,1},{4,6},{5,7},{6,4},{7,5},{8,10},{9,11},{10,... | collective-permute-start | bytes 393224 | tf_op jit(solution)/shard_map/ppermute | solution.py:29
  83.8 36.1 %collective-permute-start.2 = (bf16[128,512]{1,0:T(8,128)(2,1)S(1)}, bf16[128,512]{1,0:T(8,128)(2,1)S(1)}, u32[]{:S(2)}, u32[]{:S(2)}) collective-permute-start(bf16[128,512]{1,0:T(8,128)(2,1)S(1)} %bitcast.136), channel_id=1, source_target_pairs={{0,3},{1,0},{2,1},{3,2},{4,7},{5,4},{6,5},{7,6},{8,11},{9,8},{10,9... | collective-permute-start | bytes 393224 | tf_op jit(solution)/shard_map/ppermute | solution.py:29
  118.8 18.8 %collective-permute-start.11 = (bf16[192,2048]{1,0:T(8,128)(2,1)}, bf16[192,2048]{1,0:T(8,128)(2,1)}, u32[]{:S(2)}, u32[]{:S(2)}) collective-permute-start(bf16[192,2048]{1,0:T(8,128)(2,1)} %param.23), channel_id=1, source_target_pairs={{0,3},{1,0},{2,1},{3,2},{4,7},{5,4},{6,5},{7,6},{8,11},{9,8},{10,9... | collective-permute-start | bytes 2359304 | tf_op jit(solution)/shard_map/ppermute | solution.py:29
  121.5 7.2 %collective-permute-start.8 = (bf16[128,192]{1,0:T(8,128)(2,1)S(1)}, bf16[128,192]{1,0:T(8,128)(2,1)S(1)}, u32[]{:S(2)}, u32[]{:S(2)}) collective-permute-start(bf16[128,192]{1,0:T(8,128)(2,1)S(1)} %bitcast.142), channel_id=1, source_target_pairs={{0,2},{1,3},{2,0},{3,1},{4,6},{5,7},{6,4},{7,5},{8,10},{9,11},{10,... | collective-permute-start | bytes 147464 | tf_op jit(solution)/shard_map/ppermute | solution.py:29
  124.5 5.6 %collective-permute-start.6 = (bf16[128,192]{1,0:T(8,128)(2,1)S(1)}, bf16[128,192]{1,0:T(8,128)(2,1)S(1)}, u32[]{:S(2)}, u32[]{:S(2)}) collective-permute-start(bf16[128,192]{1,0:T(8,128)(2,1)S(1)} %bitcast.143), channel_id=1, source_target_pairs={{0,1},{1,2},{2,3},{3,0},{4,5},{5,6},{6,7},{7,4},{8,9},{9,10},{10,1... | collective-permute-start | bytes 147464 | tf_op jit(solution)/shard_map/ppermute | solution.py:29
  125.9 14.1 %collective-permute-start.10 = (bf16[128,192]{1,0:T(8,128)(2,1)S(1)}, bf16[128,192]{1,0:T(8,128)(2,1)S(1)}, u32[]{:S(2)}, u32[]{:S(2)}) collective-permute-start(bf16[128,192]{1,0:T(8,128)(2,1)S(1)} %bitcast.145), channel_id=1, source_target_pairs={{0,3},{1,0},{2,1},{3,2},{4,7},{5,4},{6,5},{7,6},{8,11},{9,8},{10,9... | collective-permute-start | bytes 147464 | tf_op jit(solution)/shard_map/ppermute | solution.py:29
  147.2 6.8 %collective-permute-start.12 = (bf16[128,512]{1,0:T(8,128)(2,1)}, bf16[128,512]{1,0:T(8,128)(2,1)S(1)}, u32[]{:S(2)}, u32[]{:S(2)}) collective-permute-start(bf16[128,512]{1,0:T(8,128)(2,1)} %get-tuple-element.12), channel_id=1, source_target_pairs={{0,1},{1,2},{2,3},{3,0},{4,5},{5,6},{6,7},{7,4},{8,9},{9,10},{10,1... | collective-permute-start | bytes 393224 | tf_op jit(solution)/shard_map/ppermute | solution.py:29
  148.4 8.2 %collective-permute-start.13 = (bf16[128,512]{1,0:T(8,128)(2,1)S(1)}, bf16[128,512]{1,0:T(8,128)(2,1)}, u32[]{:S(2)}, u32[]{:S(2)}) collective-permute-start(bf16[128,512]{1,0:T(8,128)(2,1)S(1)} %get-tuple-element.14), channel_id=1, source_target_pairs={{0,2},{1,3},{2,0},{3,1},{4,6},{5,7},{6,4},{7,5},{8,10},{9,11},{10,... | collective-permute-start | bytes 393224 | tf_op jit(solution)/shard_map/ppermute | solution.py:29
  152.4 4.7 %collective-permute-start.14 = (bf16[128,512]{1,0:T(8,128)(2,1)S(1)}, bf16[128,512]{1,0:T(8,128)(2,1)}, u32[]{:S(2)}, u32[]{:S(2)}) collective-permute-start(bf16[128,512]{1,0:T(8,128)(2,1)S(1)} %get-tuple-element.13), channel_id=1, source_target_pairs={{0,3},{1,0},{2,1},{3,2},{4,7},{5,4},{6,5},{7,6},{8,11},{9,8},{10,9... | collective-permute-start | bytes 393224 | tf_op jit(solution)/shard_map/ppermute | solution.py:29
  (8 other events, 60.9 us)

commit v7 on v4

--- a/solution.py
+++ b/solution.py
@@ -171,20 +171,17 @@
     gate_out = jnp.dot(normed_two, w_gate, preferred_element_type=jnp.float32)
     up_out = jnp.dot(normed_two, w_up, preferred_element_type=jnp.float32)
     hidden = (jax.nn.silu(gate_out) * up_out).astype(jnp.bfloat16)
-    unit_part = jnp.einsum(
-        "tu,ujd->jtd",
-        hidden,
-        w_down.reshape(w_down.shape[0], mlp_count, quarter),
-        preferred_element_type=jnp.float32,
-    ).astype(jnp.bfloat16)
-
-    unit_share = lax.dynamic_index_in_dim(unit_part, part_index, 0, keepdims=False).astype(
-        jnp.float32
-    )
+    def unit_block(target):
+        columns = lax.dynamic_slice_in_dim(w_down, target * quarter, quarter, 1)
+        return jnp.dot(hidden, columns, preferred_element_type=jnp.float32).astype(jnp.bfloat16)
+
+    arrived_parts = []
     for k in range(1, mlp_count):
         target = (part_index + k) % mlp_count
-        piece = lax.dynamic_index_in_dim(unit_part, target, 0, keepdims=False)
-        unit_share = unit_share + shift_mlp(piece, k, mlp_count).astype(jnp.float32)
+        arrived_parts.append(shift_mlp(unit_block(target), k, mlp_count))
+    unit_share = unit_block(part_index).astype(jnp.float32)
+    for part in arrived_parts:
+        unit_share = unit_share + part.astype(jnp.float32)
     residual_share = lax.dynamic_slice_in_dim(residual, part_index * quarter, quarter, 1)
     result = (residual_share + unit_share).astype(jnp.bfloat16)
     return (result.reshape(per_owner_rows, tokens, quarter), accepted_rows)

time: 147 us -> 144 us (0.980); the launches traced: 144 us -> 143 us
  other arithmetic: 5.61 us -> 3.81 us
    convert_element_type x1 -> x0, other arithmetic: 1.82 us -> none  [per_device(): result = (residual_share + unit_share).astype(jnp.bfloat16)]
    dot_general x1 -> x5, matrix products: 3.14 us -> 3.5 us  [the longest x4 2.82 us: unit_block(): jnp.dot(hidden, columns, preferred_element_type=jnp.float32)]
  transfers between devices with their start and end apart: 14 -> 14, of which waited for: 10 -> 9; matrix products, arithmetic and copies ran while one was open for 7% -> 7% of each run, Pallas kernels for 0% -> 0%
where the time goes in v7:
time: 144 us; the launch traced here: 143 us
  waiting for transfers between devices  72.6 us (50%)
  starting transfers between devices  37.6 us (26%)
  matrix products  17.8 us (12%)
  local copies, waits for them, and re-layouts  10.1 us (7%)
  other arithmetic  3.81 us (3%)
    ppermute x12, waiting for transfers between devices, shift_mlp(): lax.ppermute(value, 'mlp', [(i, (i + shift) % count) for i in range(count)])  34.3 us
    all_to_all x1, waiting for transfers between devices, per_device(): incoming = lax.all_to_all(outgoing, 'req', 0, 0, tiled=True)  26.8 us
    ppermute x12, starting transfers between devices, shift_mlp(): lax.ppermute(value, 'mlp', [(i, (i + shift) % count) for i in range(count)])  17.4 us
    all_to_all x1, starting transfers between devices, per_device(): incoming = lax.all_to_all(outgoing, 'req', 0, 0, tiled=True)  13.3 us
    all_to_all x1, waiting for transfers between devices, per_device(): arrived = lax.all_to_all(returning, 'req', 0, 0, tiled=True)  11.4 us
    all_to_all x1, starting transfers between devices, per_device(): arrived = lax.all_to_all(returning, 'req', 0, 0, tiled=True)  6.94 us
    dot_general x4, matrix products, per_device(): jnp.dot(piece[:, quarter:], rows_of_group, preferred_element_type=jnp.flo...  6.04 us
  transfers between devices with their start and end apart: 14, of which 9 were waited for; matrix products, arithmetic and copies ran while one was open for 7% of the time, Pallas kernels for 0%

profile of v7, /device:TPU:1, one launch (start us, length us, event | category | flops | bytes accessed | tf_op | source)
XLA Modules:
  0.0 143.0 jit_solution(16142423848713196802)
XLA Ops:
  3.0 2.5 %gather_fusion = bf16[64,16,512]{2,1,0:T(8,128)(2,1)} fusion(bf16[8,16,512]{2,1,0:T(8,128)(2,1)} %param.14, s32[1024]{0:T(1024)S(1)} %pad_clamp_fusion.3), kind=kCustom, calls=%fused_computation | custom fusion | bytes 2097408 | tf_op jit(solution)/shard_map/jit(_take)/gather | solution.py:86
  5.6 13.3 %all-to-all-start = ((bf16[64,16,512]{2,1,0:T(8,128)(2,1)}), bf16[64,16,512]{2,1,0:T(8,128)(2,1)}, u32[]{:S(2)}, u32[]{:S(2)}) async-start(bf16[64,16,512]{2,1,0:T(8,128)(2,1)} %gather_fusion), calls=%async_computation | async-start | bytes 2097152 | tf_op jit(solution)/shard_map/all_to_all | solution.py:87
  20.5 26.8 %all-to-all-done = bf16[64,16,512]{2,1,0:T(8,128)(2,1)} async-done(((bf16[64,16,512]{2,1,0:T(8,128)(2,1)}), bf16[64,16,512]{2,1,0:T(8,128)(2,1)}, u32[]{:S(2)}, u32[]{:S(2)}) %all-to-all-start) | async-done | bytes 1048608 | tf_op jit(solution)/shard_map/all_to_all | solution.py:87
  47.3 1.8 %gather_fusion.1 = bf16[8,16,512]{2,1,0:T(8,128)(2,1)S(1)} fusion(bf16[64,16,512]{2,1,0:T(8,128)(2,1)} %all-to-all-done, s32[1024]{0:T(1024)S(1)} %pad_clamp_fusion.2), kind=kCustom, calls=%fused_computation.1 | custom fusion | bytes 262176 | tf_op jit(solution)/shard_map/jit(_take)/gather | solution.py:88
  51.2 2.7 %collective-permute-start.1 = (bf16[128,512]{1,0:T(8,128)(2,1)S(1)}, bf16[128,512]{1,0:T(8,128)(2,1)S(1)}, u32[]{:S(2)}, u32[]{:S(2)}) collective-permute-start(bf16[128,512]{1,0:T(8,128)(2,1)S(1)} %bitcast.117), channel_id=1, source_target_pairs={{0,2},{1,3},{2,0},{3,1},{4,6},{5,7},{6,4},{7,5},{8,10},{9,11},{10,... | collective-permute-start | bytes 393224 | tf_op jit(solution)/shard_map/ppermute | solution.py:29
  55.5 3.9 %collective-permute-done.1 = bf16[128,512]{1,0:T(8,128)(2,1)S(1)} collective-permute-done((bf16[128,512]{1,0:T(8,128)(2,1)S(1)}, bf16[128,512]{1,0:T(8,128)(2,1)S(1)}, u32[]{:S(2)}, u32[]{:S(2)}) %collective-permute-start.1) | collective-permute-done | bytes 131104 | tf_op jit(solution)/shard_map/ppermute | solution.py:29
  59.7 2.0 %convolution_convert_fusion.8 = bf16[128,128]{1,0:T(8,128)(2,1)} fusion(bf16[2048,128]{1,0:T(8,128)(2,1)} %param.22, bf16[128,2048]{1,0:T(8,128)(2,1)S(1)} %constant_dynamic-update-slice_fusion, f32[2048]{0:T(1024)S(1)} %copy-done.14, f32[128]{0:T(128)S(1)} %add_rsqrt_fusion.1), kind=kOutput, calls=%fused_computation.35 | convolution fusion | flops 68173824 | bytes 1090048 | tf_op jit(solution)/shard_map/dot_general | solution.py:105
  62.3 1.5 %fusion.53 = (f32[8,3,16]{2,1,0:T(4,128)S(1)}, f32[8,1,3,16,16]{3,4,2,0,1:T(8,128)S(1)}) fusion(f32[8,16,3,64]{3,2,1,0:T(4,128)S(1)} %reshape.222, bf16[8,16,1,128]{3,1,0,2:T(8,128)(2,1)} %bitcast.121, pred[8,16,16]{1,2,0:T(8,128)(4,1)S(1)} %copy.35), kind=kOutput, calls=%fused_computation.121 | convolution fusion | flops 4736640 | bytes 159232 | tf_op jit(solution)/shard_map/rtkgd,rjkd->rkgtj/dot_general | solution.py:119
  66.5 1.5 %gather_fusion.2 = bf16[64,16,192]{2,1,0:T(8,128)(2,1)} fusion(bf16[8,16,192]{2,1,0:T(8,128)(2,1)S(1)} %reshape.230, s32[1024]{0:T(1024)} %pad_clamp_fusion.1), kind=kCustom, calls=%fused_computation.2 | custom fusion | bytes 786688 | tf_op jit(solution)/shard_map/jit(_take)/gather | solution.py:152
  68.0 6.9 %all-to-all-start.1 = ((bf16[64,16,192]{2,1,0:T(8,128)(2,1)}), bf16[64,16,192]{2,1,0:T(8,128)(2,1)}, u32[]{:S(2)}, u32[]{:S(2)}) async-start(bf16[64,16,192]{2,1,0:T(8,128)(2,1)} %gather_fusion.2), calls=%async_computation.1 | async-start | bytes 1048576 | tf_op jit(solution)/shard_map/all_to_all | solution.py:153
  74.9 3.0 %collective-permute-start.7 = (bf16[192,2048]{1,0:T(8,128)(2,1)}, bf16[192,2048]{1,0:T(8,128)(2,1)}, u32[]{:S(2)}, u32[]{:S(2)}) collective-permute-start(bf16[192,2048]{1,0:T(8,128)(2,1)} %param.23), channel_id=1, source_target_pairs={{0,2},{1,3},{2,0},{3,1},{4,6},{5,7},{6,4},{7,5},{8,10},{9,11},{10,... | collective-permute-start | bytes 2359304 | tf_op jit(solution)/shard_map/ppermute | solution.py:29
  78.0 2.6 %collective-permute-start.8 = (bf16[192,2048]{1,0:T(8,128)(2,1)}, bf16[192,2048]{1,0:T(8,128)(2,1)}, u32[]{:S(2)}, u32[]{:S(2)}) collective-permute-start(bf16[192,2048]{1,0:T(8,128)(2,1)} %param.23), channel_id=1, source_target_pairs={{0,3},{1,0},{2,1},{3,2},{4,7},{5,4},{6,5},{7,6},{8,11},{9,8},{10,9... | collective-permute-start | bytes 2359304 | tf_op jit(solution)/shard_map/ppermute | solution.py:29
  80.7 11.4 %all-to-all-done.1 = bf16[64,16,192]{2,1,0:T(8,128)(2,1)} async-done(((bf16[64,16,192]{2,1,0:T(8,128)(2,1)}), bf16[64,16,192]{2,1,0:T(8,128)(2,1)}, u32[]{:S(2)}, u32[]{:S(2)}) %all-to-all-start.1) | async-done | bytes 393248 | tf_op jit(solution)/shard_map/all_to_all | solution.py:153
  92.2 1.6 %gather_fusion.3 = bf16[8,16,192]{2,1,0:T(8,128)(2,1)S(1)} fusion(bf16[64,16,192]{2,1,0:T(8,128)(2,1)} %all-to-all-done.1, s32[1024]{0:T(1024)S(1)} %pad_clamp_fusion), kind=kCustom, calls=%fused_computation.3 | custom fusion | bytes 98336 | tf_op jit(solution)/shard_map/jit(_take)/gather | solution.py:154
  93.8 1.5 %collective-permute-start.3 = (bf16[128,704]{1,0:T(8,128)(2,1)S(1)}, bf16[128,704]{1,0:T(8,128)(2,1)S(1)}, u32[]{:S(2)}, u32[]{:S(2)}) collective-permute-start(bf16[128,704]{1,0:T(8,128)(2,1)S(1)} %pad_maximum_fusion), channel_id=1, source_target_pairs={{0,1},{1,2},{2,3},{3,0},{4,5},{5,6},{6,7},{7,4},{8,9},{9,10},{10,1... | collective-permute-start | bytes 540680 | tf_op jit(solution)/shard_map/ppermute | solution.py:29
  95.3 2.1 %collective-permute-start.4 = (bf16[128,704]{1,0:T(8,128)(2,1)S(1)}, bf16[128,704]{1,0:T(8,128)(2,1)S(1)}, u32[]{:S(2)}, u32[]{:S(2)}) collective-permute-start(bf16[128,704]{1,0:T(8,128)(2,1)S(1)} %pad_maximum_fusion), channel_id=1, source_target_pairs={{0,2},{1,3},{2,0},{3,1},{4,6},{5,7},{6,4},{7,5},{8,10},{9,11},{10,... | collective-permute-start | bytes 540680 | tf_op jit(solution)/shard_map/ppermute | solution.py:29
  98.9 19.3 %collective-permute-done.3 = bf16[128,704]{1,0:T(8,128)(2,1)S(1)} collective-permute-done((bf16[128,704]{1,0:T(8,128)(2,1)S(1)}, bf16[128,704]{1,0:T(8,128)(2,1)S(1)}, u32[]{:S(2)}, u32[]{:S(2)}) %collective-permute-start.3) | collective-permute-done | bytes 180256 | tf_op jit(solution)/shard_map/ppermute | solution.py:29
  118.1 2.5 %collective-permute-done.4 = bf16[128,704]{1,0:T(8,128)(2,1)S(1)} collective-permute-done((bf16[128,704]{1,0:T(8,128)(2,1)S(1)}, bf16[128,704]{1,0:T(8,128)(2,1)S(1)}, u32[]{:S(2)}, u32[]{:S(2)}) %collective-permute-start.4) | collective-permute-done | bytes 180256 | tf_op jit(solution)/shard_map/ppermute | solution.py:29
  120.7 3.3 %collective-permute-done.5 = bf16[128,704]{1,0:T(8,128)(2,1)S(1)} collective-permute-done((bf16[128,704]{1,0:T(8,128)(2,1)S(1)}, bf16[128,704]{1,0:T(8,128)(2,1)S(1)}, u32[]{:S(2)}, u32[]{:S(2)}) %collective-permute-start.5) | collective-permute-done | bytes 180256 | tf_op jit(solution)/shard_map/ppermute | solution.py:29
  125.5 1.4 %fusion.2 = f32[128,2048]{1,0:T(8,128)S(1)} fusion(bf16[192,2048]{1,0:T(8,128)(2,1)} %collective-permute-done.6, bf16[128,704]{1,0:T(8,128)(2,1)S(1)} %collective-permute-done.3), kind=kOutput, calls=%fused_computation.9 | convolution fusion | flops 101187584 | bytes 1900544 | tf_op jit(solution)/shard_map/dot_general | solution.py:164
  126.9 1.8 %multiply_reduce_fusion = (f32[128]{0:T(128)S(1)}, f32[128,2048]{1,0:T(8,128)S(1)}) fusion(bf16[192,2048]{1,0:T(8,128)(2,1)} %collective-permute-done.8, bf16[128,704]{1,0:T(8,128)(2,1)S(1)} %collective-permute-done.5, f32[128,2048]{1,0:T(8,128)S(1)} %fusion.1, f32[128,2048]{1,0:T(8,128)S(1)} %fusion.2, f32[128,2048]{1,0:T(8,128)S(1)} %fusion.3, ...), kind=kOutput, calls=%fused_computation.45 | convolution fusion | flops 103022464 | bytes 5571072 | tf_op jit(solution)/shard_map/dot_general | solution.py:164
  132.3 1.5 %collective-permute-start.9 = (bf16[128,512]{1,0:T(8,128)(2,1)S(1)}, bf16[128,512]{1,0:T(8,128)(2,1)S(1)}, u32[]{:S(2)}, u32[]{:S(2)}) collective-permute-start(bf16[128,512]{1,0:T(8,128)(2,1)S(1)} %convolution_convert_fusion.6), channel_id=1, source_target_pairs={{0,1},{1,2},{2,3},{3,0},{4,5},{5,6},{6,7},{7,4},{8,9},{9,10},{10,1... | collective-permute-start | bytes 393224 | tf_op jit(solution)/shard_map/ppermute | solution.py:29
  137.4 3.7 %collective-permute-done.9 = bf16[128,512]{1,0:T(8,128)(2,1)S(1)} collective-permute-done((bf16[128,512]{1,0:T(8,128)(2,1)S(1)}, bf16[128,512]{1,0:T(8,128)(2,1)S(1)}, u32[]{:S(2)}, u32[]{:S(2)}) %collective-permute-start.9) | collective-permute-done | bytes 131104 | tf_op jit(solution)/shard_map/ppermute | solution.py:29
  141.1 2.0 %add_convert_fusion = bf16[128,512]{1,0:T(8,128)(2,1)} fusion(bf16[128,512]{1,0:T(8,128)(2,1)} %collective-permute-done.11, bf16[128,512]{1,0:T(8,128)(2,1)S(1)} %collective-permute-done.10, bf16[128,512]{1,0:T(8,128)(2,1)S(1)} %collective-permute-done.9, f32[128,2048]{1,0:T(8,128)} %copy-done.2, s32[]{:T(128)S(6)} %select_n.132, ...), kind=kOutput, calls=%fused_computation.57 | convolution fusion | flops 84541440 | bytes 1606656 | tf_op jit(solution)/shard_map/dot_general | solution.py:176
  (95 shorter events, 21.3 us)
Async XLA Ops:
  0.6 130.9 %copy-start = (bf16[640,2048]{1,0:T(8,128)(2,1)S(1)}, bf16[640,2048]{1,0:T(8,128)(2,1)}, u32[]{:S(2)}) copy-start(bf16[640,2048]{1,0:T(8,128)(2,1)} %param.27) | copy-start | bytes 7864324
  0.6 18.4 %copy-start.11 = (s32[8]{0:T(128)S(1)}, s32[8]{0:T(128)}, u32[]{:S(2)}) copy-start(s32[8]{0:T(128)} %param.16) | copy-start | bytes 100
  0.7 19.0 %copy-start.8 = (s32[8,16]{1,0:T(8,128)S(1)}, s32[8,16]{1,0:T(8,128)}, u32[]{:S(2)}) copy-start(s32[8,16]{1,0:T(8,128)} %param.17) | copy-start | bytes 1540
  5.6 54.1 %copy-start.14 = (f32[2048]{0:T(1024)S(1)}, f32[2048]{0:T(1024)}, u32[]{:S(2)}) copy-start(f32[2048]{0:T(1024)} %param.20) | copy-start | bytes 24580
  5.6 41.7 %all-to-all-start = ((bf16[64,16,512]{2,1,0:T(8,128)(2,1)}), bf16[64,16,512]{2,1,0:T(8,128)(2,1)}, u32[]{:S(2)}, u32[]{:S(2)}) async-start(bf16[64,16,512]{2,1,0:T(8,128)(2,1)} %gather_fusion), calls=%async_computation | async-start | bytes 2097152 | tf_op jit(solution)/shard_map/all_to_all | solution.py:87
  49.1 6.4 %collective-permute-start = (bf16[128,512]{1,0:T(8,128)(2,1)S(1)}, bf16[128,512]{1,0:T(8,128)(2,1)S(1)}, u32[]{:S(2)}, u32[]{:S(2)}) collective-permute-start(bf16[128,512]{1,0:T(8,128)(2,1)S(1)} %bitcast.116), channel_id=1, source_target_pairs={{0,1},{1,2},{2,3},{3,0},{4,5},{5,6},{6,7},{7,4},{8,9},{9,10},{10,1... | collective-permute-start | bytes 393224 | tf_op jit(solution)/shard_map/ppermute | solution.py:29
  51.2 10.5 %copy-start.13 = (bf16[2048,192]{0,1:T(8,128)(2,1)S(1)}, bf16[2048,192]{0,1:T(8,128)(2,1)}, u32[]{:S(2)}) copy-start(bf16[2048,192]{0,1:T(8,128)(2,1)} %param.21) | copy-start | bytes 2359300
  51.2 8.2 %collective-permute-start.1 = (bf16[128,512]{1,0:T(8,128)(2,1)S(1)}, bf16[128,512]{1,0:T(8,128)(2,1)S(1)}, u32[]{:S(2)}, u32[]{:S(2)}) collective-permute-start(bf16[128,512]{1,0:T(8,128)(2,1)S(1)} %bitcast.117), channel_id=1, source_target_pairs={{0,2},{1,3},{2,0},{3,1},{4,6},{5,7},{6,4},{7,5},{8,10},{9,11},{10,... | collective-permute-start | bytes 393224 | tf_op jit(solution)/shard_map/ppermute | solution.py:29
  53.9 5.5 %collective-permute-start.2 = (bf16[128,512]{1,0:T(8,128)(2,1)S(1)}, bf16[128,512]{1,0:T(8,128)(2,1)S(1)}, u32[]{:S(2)}, u32[]{:S(2)}) collective-permute-start(bf16[128,512]{1,0:T(8,128)(2,1)S(1)} %bitcast.118), channel_id=1, source_target_pairs={{0,3},{1,0},{2,1},{3,2},{4,7},{5,4},{6,5},{7,6},{8,11},{9,8},{10,9... | collective-permute-start | bytes 393224 | tf_op jit(solution)/shard_map/ppermute | solution.py:29
  55.1 8.7 %copy-start.4 = (bf16[8,256,1,128]{3,1,2,0:T(8,128)(2,1)S(1)}, bf16[8,256,1,128]{3,1,2,0:T(8,128)(2,1)}, u32[]{:S(2)}) copy-start(bf16[8,256,1,128]{3,1,2,0:T(8,128)(2,1)} %param.19) | copy-start | bytes 1572868
  65.2 15.4 %copy-start.10 = (s32[8]{0:T(128)S(1)}, s32[8]{0:T(128)}, u32[]{:S(2)}) copy-start(s32[8]{0:T(128)} %copy-done.9) | copy-start | bytes 100
  65.5 15.2 %copy-start.1 = (bf16[8,16,512]{2,1,0:T(8,128)(2,1)S(1)}, bf16[8,16,512]{2,1,0:T(8,128)(2,1)}, u32[]{:S(2)}) copy-start(bf16[8,16,512]{2,1,0:T(8,128)(2,1)} %param.14) | copy-start | bytes 393220
  68.0 24.2 %all-to-all-start.1 = ((bf16[64,16,192]{2,1,0:T(8,128)(2,1)}), bf16[64,16,192]{2,1,0:T(8,128)(2,1)}, u32[]{:S(2)}, u32[]{:S(2)}) async-start(bf16[64,16,192]{2,1,0:T(8,128)(2,1)} %gather_fusion.2), calls=%async_computation.1 | async-start | bytes 1048576 | tf_op jit(solution)/shard_map/all_to_all | solution.py:153
  74.9 49.1 %collective-permute-start.7 = (bf16[192,2048]{1,0:T(8,128)(2,1)}, bf16[192,2048]{1,0:T(8,128)(2,1)}, u32[]{:S(2)}, u32[]{:S(2)}) collective-permute-start(bf16[192,2048]{1,0:T(8,128)(2,1)} %param.23), channel_id=1, source_target_pairs={{0,2},{1,3},{2,0},{3,1},{4,6},{5,7},{6,4},{7,5},{8,10},{9,11},{10,... | collective-permute-start | bytes 2359304 | tf_op jit(solution)/shard_map/ppermute | solution.py:29
  77.9 47.5 %collective-permute-start.6 = (bf16[192,2048]{1,0:T(8,128)(2,1)}, bf16[192,2048]{1,0:T(8,128)(2,1)}, u32[]{:S(2)}, u32[]{:S(2)}) collective-permute-start(bf16[192,2048]{1,0:T(8,128)(2,1)} %param.23), channel_id=1, source_target_pairs={{0,1},{1,2},{2,3},{3,0},{4,5},{5,6},{6,7},{7,4},{8,9},{9,10},{10,1... | collective-permute-start | bytes 2359304 | tf_op jit(solution)/shard_map/ppermute | solution.py:29
  78.0 48.9 %collective-permute-start.8 = (bf16[192,2048]{1,0:T(8,128)(2,1)}, bf16[192,2048]{1,0:T(8,128)(2,1)}, u32[]{:S(2)}, u32[]{:S(2)}) collective-permute-start(bf16[192,2048]{1,0:T(8,128)(2,1)} %param.23), channel_id=1, source_target_pairs={{0,3},{1,0},{2,1},{3,2},{4,7},{5,4},{6,5},{7,6},{8,11},{9,8},{10,9... | collective-permute-start | bytes 2359304 | tf_op jit(solution)/shard_map/ppermute | solution.py:29
  93.8 24.3 %collective-permute-start.3 = (bf16[128,704]{1,0:T(8,128)(2,1)S(1)}, bf16[128,704]{1,0:T(8,128)(2,1)S(1)}, u32[]{:S(2)}, u32[]{:S(2)}) collective-permute-start(bf16[128,704]{1,0:T(8,128)(2,1)S(1)} %pad_maximum_fusion), channel_id=1, source_target_pairs={{0,1},{1,2},{2,3},{3,0},{4,5},{5,6},{6,7},{7,4},{8,9},{9,10},{10,1... | collective-permute-start | bytes 540680 | tf_op jit(solution)/shard_map/ppermute | solution.py:29
  95.3 25.3 %collective-permute-start.4 = (bf16[128,704]{1,0:T(8,128)(2,1)S(1)}, bf16[128,704]{1,0:T(8,128)(2,1)S(1)}, u32[]{:S(2)}, u32[]{:S(2)}) collective-permute-start(bf16[128,704]{1,0:T(8,128)(2,1)S(1)} %pad_maximum_fusion), channel_id=1, source_target_pairs={{0,2},{1,3},{2,0},{3,1},{4,6},{5,7},{6,4},{7,5},{8,10},{9,11},{10,... | collective-permute-start | bytes 540680 | tf_op jit(solution)/shard_map/ppermute | solution.py:29
  118.1 5.9 %collective-permute-start.5 = (bf16[128,704]{1,0:T(8,128)(2,1)S(1)}, bf16[128,704]{1,0:T(8,128)(2,1)S(1)}, u32[]{:S(2)}, u32[]{:S(2)}) collective-permute-start(bf16[128,704]{1,0:T(8,128)(2,1)S(1)} %pad_maximum_fusion), channel_id=1, source_target_pairs={{0,3},{1,0},{2,1},{3,2},{4,7},{5,4},{6,5},{7,6},{8,11},{9,8},{10,9... | collective-permute-start | bytes 540680 | tf_op jit(solution)/shard_map/ppermute | solution.py:29
  130.9 4.5 %copy-start.6 = (bf16[128,128]{1,0:T(8,128)(2,1)S(1)}, bf16[128,128]{1,0:T(8,128)(2,1)}, u32[]{:S(2)}) copy-start(bf16[128,128]{1,0:T(8,128)(2,1)} %convolution_convert_fusion.8) | copy-start | bytes 98308
  130.9 4.5 %copy-start.15 = (s32[8,8]{1,0:T(8,128)S(1)}, s32[8,8]{1,0:T(8,128)}, u32[]{:S(2)}) copy-start(s32[8,8]{1,0:T(8,128)} %param.18) | copy-start | bytes 772
  131.9 5.5 %collective-permute-start.10 = (bf16[128,512]{1,0:T(8,128)(2,1)S(1)}, bf16[128,512]{1,0:T(8,128)(2,1)S(1)}, u32[]{:S(2)}, u32[]{:S(2)}) collective-permute-start(bf16[128,512]{1,0:T(8,128)(2,1)S(1)} %convolution_convert_fusion.5), channel_id=1, source_target_pairs={{0,2},{1,3},{2,0},{3,1},{4,6},{5,7},{6,4},{7,5},{8,10},{9,11},{10,... | collective-permute-start | bytes 393224 | tf_op jit(solution)/shard_map/ppermute | solution.py:29
  132.3 8.8 %collective-permute-start.9 = (bf16[128,512]{1,0:T(8,128)(2,1)S(1)}, bf16[128,512]{1,0:T(8,128)(2,1)S(1)}, u32[]{:S(2)}, u32[]{:S(2)}) collective-permute-start(bf16[128,512]{1,0:T(8,128)(2,1)S(1)} %convolution_convert_fusion.6), channel_id=1, source_target_pairs={{0,1},{1,2},{2,3},{3,0},{4,5},{5,6},{6,7},{7,4},{8,9},{9,10},{10,1... | collective-permute-start | bytes 393224 | tf_op jit(solution)/shard_map/ppermute | solution.py:29
  134.0 7.1 %collective-permute-start.11 = (bf16[128,512]{1,0:T(8,128)(2,1)S(1)}, bf16[128,512]{1,0:T(8,128)(2,1)}, u32[]{:S(2)}, u32[]{:S(2)}) collective-permute-start(bf16[128,512]{1,0:T(8,128)(2,1)S(1)} %convolution_convert_fusion.4), channel_id=1, source_target_pairs={{0,3},{1,0},{2,1},{3,2},{4,7},{5,4},{6,5},{7,6},{8,11},{9,8},{10,9... | collective-permute-start | bytes 393224 | tf_op jit(solution)/shard_map/ppermute | solution.py:29
  (6 other events, 13.2 us)

commit v8 on v7

--- a/solution.py
+++ b/solution.py
@@ -150,19 +150,17 @@
     attended = attended.reshape(per_owner_rows, tokens, head_width)
 
     returning = jnp.take(attended, return_pick, axis=0, mode="clip")
+    owned_pieces = pieces_mlp(drafts.reshape(rows, quarter), mlp_count)
     arrived = lax.all_to_all(returning, "req", 0, 0, tiled=True)
     back_rows = jnp.take(arrived, my_owners, axis=0, mode="clip")
 
-    packed = jnp.concatenate(
-        [drafts.reshape(rows, quarter), back_rows.reshape(rows, head_width)], axis=1
-    )
-    gathered = pieces_mlp(packed, mlp_count)
-    owned_all = place_blocks([piece[:, :quarter] for piece in gathered], mlp_count, part_index)
+    gathered = pieces_mlp(back_rows.reshape(rows, head_width), mlp_count)
+    owned_all = place_blocks(owned_pieces, mlp_count, part_index)
 
     residual = owned_all.astype(jnp.float32)
     for piece, rows_of_group in zip(gathered, w_out_all):
         group_product = jnp.dot(
-            piece[:, quarter:], rows_of_group, preferred_element_type=jnp.float32
+            piece, rows_of_group, preferred_element_type=jnp.float32
         )
         residual = residual + group_product.astype(jnp.bfloat16).astype(jnp.float32)
     normed_two = (

time: 144 us -> 159 us (1.10); the launches traced: 143 us -> 156 us
  starting transfers between devices: 37.6 us -> 44.1 us
  waiting for transfers between devices: 72.6 us -> 78.2 us
    ppermute x12 -> x15, waiting for transfers between devices: 34.3 us -> 51.4 us  [shift_mlp(): lax.ppermute(value, 'mlp', [(i, (i + shift) % count) for i in range(count)])]
    all_to_all x1, waiting for transfers between devices: 11.4 us -> 0.01 us  [per_device(): arrived = lax.all_to_all(returning, 'req', 0, 0, tiled=True)]
    ppermute x12 -> x15, starting transfers between devices: 17.4 us -> 23.8 us  [shift_mlp(): lax.ppermute(value, 'mlp', [(i, (i + shift) % count) for i in range(count)])]
  transfers between devices with their start and end apart: 14 -> 17, of which waited for: 9 -> 9; matrix products, arithmetic and copies ran while one was open for 7% -> 7% of each run, Pallas kernels for 0% -> 0%
where the time goes in v8:
time: 159 us; the launch traced here: 156 us
  waiting for transfers between devices  78.2 us (49%)
  starting transfers between devices  44.1 us (28%)
  matrix products  17.7 us (11%)
  local copies, waits for them, and re-layouts  11 us (7%)
  other arithmetic  3.78 us (2%)
    ppermute x15, waiting for transfers between devices, shift_mlp(): lax.ppermute(value, 'mlp', [(i, (i + shift) % count) for i in range(count)])  51.4 us
    all_to_all x1, waiting for transfers between devices, per_device(): incoming = lax.all_to_all(outgoing, 'req', 0, 0, tiled=True)  26.8 us
    ppermute x15, starting transfers between devices, shift_mlp(): lax.ppermute(value, 'mlp', [(i, (i + shift) % count) for i in range(count)])  23.8 us
    all_to_all x1, starting transfers between devices, per_device(): incoming = lax.all_to_all(outgoing, 'req', 0, 0, tiled=True)  13.3 us
    all_to_all x1, starting transfers between devices, per_device(): arrived = lax.all_to_all(returning, 'req', 0, 0, tiled=True)  6.95 us
    dot_general x4, matrix products, per_device(): jnp.dot(piece, rows_of_group, preferred_element_type=jnp.float32)  5.89 us
  transfers between devices with their start and end apart: 17, of which 9 were waited for; matrix products, arithmetic and copies ran while one was open for 7% of the time, Pallas kernels for 0%

profile of v8, /device:TPU:1, one launch (start us, length us, event | category | flops | bytes accessed | tf_op | source)
XLA Modules:
  0.0 156.0 jit_solution(6487996221315137899)
XLA Ops:
  3.1 2.5 %gather_fusion = bf16[64,16,512]{2,1,0:T(8,128)(2,1)} fusion(bf16[8,16,512]{2,1,0:T(8,128)(2,1)} %param.14, s32[1024]{0:T(1024)S(1)} %pad_clamp_fusion.3), kind=kCustom, calls=%fused_computation | custom fusion | bytes 2097408 | tf_op jit(solution)/shard_map/jit(_take)/gather | solution.py:86
  5.6 13.3 %all-to-all-start = ((bf16[64,16,512]{2,1,0:T(8,128)(2,1)}), bf16[64,16,512]{2,1,0:T(8,128)(2,1)}, u32[]{:S(2)}, u32[]{:S(2)}) async-start(bf16[64,16,512]{2,1,0:T(8,128)(2,1)} %gather_fusion), calls=%async_computation | async-start | bytes 2097152 | tf_op jit(solution)/shard_map/all_to_all | solution.py:87
  20.6 26.8 %all-to-all-done = bf16[64,16,512]{2,1,0:T(8,128)(2,1)} async-done(((bf16[64,16,512]{2,1,0:T(8,128)(2,1)}), bf16[64,16,512]{2,1,0:T(8,128)(2,1)}, u32[]{:S(2)}, u32[]{:S(2)}) %all-to-all-start) | async-done | bytes 1048608 | tf_op jit(solution)/shard_map/all_to_all | solution.py:87
  47.4 1.8 %gather_fusion.1 = bf16[8,16,512]{2,1,0:T(8,128)(2,1)S(1)} fusion(bf16[64,16,512]{2,1,0:T(8,128)(2,1)} %all-to-all-done, s32[1024]{0:T(1024)S(1)} %pad_clamp_fusion.2), kind=kCustom, calls=%fused_computation.1 | custom fusion | bytes 262176 | tf_op jit(solution)/shard_map/jit(_take)/gather | solution.py:88
  51.3 2.7 %collective-permute-start.4 = (bf16[128,512]{1,0:T(8,128)(2,1)S(1)}, bf16[128,512]{1,0:T(8,128)(2,1)S(1)}, u32[]{:S(2)}, u32[]{:S(2)}) collective-permute-start(bf16[128,512]{1,0:T(8,128)(2,1)S(1)} %bitcast.120), channel_id=1, source_target_pairs={{0,2},{1,3},{2,0},{3,1},{4,6},{5,7},{6,4},{7,5},{8,10},{9,11},{10,... | collective-permute-start | bytes 393224 | tf_op jit(solution)/shard_map/ppermute | solution.py:29
  55.5 3.9 %collective-permute-done.4 = bf16[128,512]{1,0:T(8,128)(2,1)S(1)} collective-permute-done((bf16[128,512]{1,0:T(8,128)(2,1)S(1)}, bf16[128,512]{1,0:T(8,128)(2,1)S(1)}, u32[]{:S(2)}, u32[]{:S(2)}) %collective-permute-start.4) | collective-permute-done | bytes 131104 | tf_op jit(solution)/shard_map/ppermute | solution.py:29
  59.7 2.0 %convolution_convert_fusion.8 = bf16[128,128]{1,0:T(8,128)(2,1)} fusion(bf16[2048,128]{1,0:T(8,128)(2,1)} %param.22, bf16[128,2048]{1,0:T(8,128)(2,1)S(1)} %constant_dynamic-update-slice_fusion, f32[2048]{0:T(1024)S(1)} %copy-done.14, f32[128]{0:T(128)S(1)} %add_rsqrt_fusion.1), kind=kOutput, calls=%fused_computation.35 | convolution fusion | flops 68173824 | bytes 1090048 | tf_op jit(solution)/shard_map/dot_general | solution.py:105
  62.3 1.5 fusion.48
  66.5 1.5 gather_fusion.2
  68.0 7.0 %all-to-all-start.1 = ((bf16[64,16,192]{2,1,0:T(8,128)(2,1)}), bf16[64,16,192]{2,1,0:T(8,128)(2,1)}, u32[]{:S(2)}, u32[]{:S(2)}) async-start(bf16[64,16,192]{2,1,0:T(8,128)(2,1)} %gather_fusion.2), calls=%async_computation.1 | async-start | bytes 1048576 | tf_op jit(solution)/shard_map/all_to_all | solution.py:154
  75.0 3.0 %collective-permute-start.9 = (bf16[192,2048]{1,0:T(8,128)(2,1)}, bf16[192,2048]{1,0:T(8,128)(2,1)}, u32[]{:S(2)}, u32[]{:S(2)}) collective-permute-start(bf16[192,2048]{1,0:T(8,128)(2,1)} %param.23), channel_id=1, source_target_pairs={{0,2},{1,3},{2,0},{3,1},{4,6},{5,7},{6,4},{7,5},{8,10},{9,11},{10,... | collective-permute-start | bytes 2359304 | tf_op jit(solution)/shard_map/ppermute | solution.py:29
  78.1 3.8 %collective-permute-start.1 = (bf16[128,512]{1,0:T(8,128)(2,1)S(1)}, bf16[128,512]{1,0:T(8,128)(2,1)S(1)}, u32[]{:S(2)}, u32[]{:S(2)}) collective-permute-start(bf16[128,512]{1,0:T(8,128)(2,1)S(1)} %bitcast.116), channel_id=1, source_target_pairs={{0,2},{1,3},{2,0},{3,1},{4,6},{5,7},{6,4},{7,5},{8,10},{9,11},{10,... | collective-permute-start | bytes 393224 | tf_op jit(solution)/shard_map/ppermute | solution.py:29
  82.4 34.5 %collective-permute-done = bf16[128,512]{1,0:T(8,128)(2,1)} collective-permute-done((bf16[128,512]{1,0:T(8,128)(2,1)S(1)}, bf16[128,512]{1,0:T(8,128)(2,1)}, u32[]{:S(2)}, u32[]{:S(2)}) %collective-permute-start) | collective-permute-done | bytes 131104 | tf_op jit(solution)/shard_map/ppermute | solution.py:29
  118.0 1.6 %gather_fusion.3 = bf16[8,16,192]{2,1,0:T(8,128)(2,1)S(1)} fusion(bf16[64,16,192]{2,1,0:T(8,128)(2,1)} %all-to-all-done.1, s32[1024]{0:T(1024)S(1)} %pad_clamp_fusion), kind=kCustom, calls=%fused_computation.3 | custom fusion | bytes 98336 | tf_op jit(solution)/shard_map/jit(_take)/gather | solution.py:155
  119.6 3.2 %collective-permute-start.8 = (bf16[128,192]{1,0:T(8,128)(2,1)S(1)}, bf16[128,192]{1,0:T(8,128)(2,1)S(1)}, u32[]{:S(2)}, u32[]{:S(2)}) collective-permute-start(bf16[128,192]{1,0:T(8,128)(2,1)S(1)} %bitcast.123), channel_id=1, source_target_pairs={{0,2},{1,3},{2,0},{3,1},{4,6},{5,7},{6,4},{7,5},{8,10},{9,11},{10,... | collective-permute-start | bytes 147464 | tf_op jit(solution)/shard_map/ppermute | solution.py:29
  124.2 2.7 %collective-permute-start.10 = (bf16[128,192]{1,0:T(8,128)(2,1)S(1)}, bf16[128,192]{1,0:T(8,128)(2,1)S(1)}, u32[]{:S(2)}, u32[]{:S(2)}) collective-permute-start(bf16[128,192]{1,0:T(8,128)(2,1)S(1)} %bitcast.126), channel_id=1, source_target_pairs={{0,3},{1,0},{2,1},{3,2},{4,7},{5,4},{6,5},{7,6},{8,11},{9,8},{10,9... | collective-permute-start | bytes 147464 | tf_op jit(solution)/shard_map/ppermute | solution.py:29
  129.9 5.9 %collective-permute-done.11 = bf16[192,2048]{1,0:T(8,128)(2,1)} collective-permute-done((bf16[192,2048]{1,0:T(8,128)(2,1)}, bf16[192,2048]{1,0:T(8,128)(2,1)}, u32[]{:S(2)}, u32[]{:S(2)}) %collective-permute-start.11) | collective-permute-done | bytes 786464 | tf_op jit(solution)/shard_map/ppermute | solution.py:29
  135.7 2.4 %collective-permute-done.10 = bf16[128,192]{1,0:T(8,128)(2,1)S(1)} collective-permute-done((bf16[128,192]{1,0:T(8,128)(2,1)S(1)}, bf16[128,192]{1,0:T(8,128)(2,1)S(1)}, u32[]{:S(2)}, u32[]{:S(2)}) %collective-permute-start.10) | collective-permute-done | bytes 49184 | tf_op jit(solution)/shard_map/ppermute | solution.py:29
  138.1 1.6 %multiply_reduce_fusion = (f32[128]{0:T(128)S(1)}, f32[128,2048]{1,0:T(8,128)S(1)}) fusion(f32[128,2048]{1,0:T(8,128)S(1)} %fusion.1, f32[128,2048]{1,0:T(8,128)S(1)} %fusion.2, f32[128,2048]{1,0:T(8,128)S(1)} %fusion.3, bf16[128,2048]{1,0:T(8,128)(2,1)S(1)} %constant_dynamic-update-slice_fusion.4, bf16[128,192]{1,0:T(8,128)(2,1)S(1)} %collective-permute-done.10, ...), kind=kOutput, calls=%fused_computation.45 | convolution fusion | flops 103022464 | bytes 5554688 | tf_op jit(solution)/shard_map/dot_general | solution.py:162
  140.4 1.4 copy-done.12
  144.5 4.1 %collective-permute-start.13 = (bf16[128,512]{1,0:T(8,128)(2,1)S(1)}, bf16[128,512]{1,0:T(8,128)(2,1)S(1)}, u32[]{:S(2)}, u32[]{:S(2)}) collective-permute-start(bf16[128,512]{1,0:T(8,128)(2,1)S(1)} %convolution_convert_fusion.5), channel_id=1, source_target_pairs={{0,2},{1,3},{2,0},{3,1},{4,6},{5,7},{6,4},{7,5},{8,10},{9,11},{10,... | collective-permute-start | bytes 393224 | tf_op jit(solution)/shard_map/ppermute | solution.py:29
  149.8 2.3 %collective-permute-done.13 = bf16[128,512]{1,0:T(8,128)(2,1)S(1)} collective-permute-done((bf16[128,512]{1,0:T(8,128)(2,1)S(1)}, bf16[128,512]{1,0:T(8,128)(2,1)S(1)}, u32[]{:S(2)}, u32[]{:S(2)}) %collective-permute-start.13) | collective-permute-done | bytes 131104 | tf_op jit(solution)/shard_map/ppermute | solution.py:29
  152.1 1.9 %collective-permute-done.14 = bf16[128,512]{1,0:T(8,128)(2,1)} collective-permute-done((bf16[128,512]{1,0:T(8,128)(2,1)S(1)}, bf16[128,512]{1,0:T(8,128)(2,1)}, u32[]{:S(2)}, u32[]{:S(2)}) %collective-permute-start.14) | collective-permute-done | bytes 131104 | tf_op jit(solution)/shard_map/ppermute | solution.py:29
  154.0 2.0 %add_convert_fusion = bf16[128,512]{1,0:T(8,128)(2,1)} fusion(bf16[128,512]{1,0:T(8,128)(2,1)} %collective-permute-done.14, bf16[128,512]{1,0:T(8,128)(2,1)S(1)} %collective-permute-done.13, bf16[128,512]{1,0:T(8,128)(2,1)S(1)} %collective-permute-done.12, f32[128,2048]{1,0:T(8,128)} %copy-done.2, s32[]{:T(128)S(6)} %select_n.132, ...), kind=kOutput, calls=%fused_computation.57 | convolution fusion | flops 84541440 | bytes 1606656 | tf_op jit(solution)/shard_map/dot_general | solution.py:174
  (100 shorter events, 21.4 us)
Async XLA Ops:
  0.6 141.9 %copy-start = (bf16[640,2048]{1,0:T(8,128)(2,1)S(1)}, bf16[640,2048]{1,0:T(8,128)(2,1)}, u32[]{:S(2)}) copy-start(bf16[640,2048]{1,0:T(8,128)(2,1)} %param.27) | copy-start | bytes 7864324
  0.6 18.4 %copy-start.11 = (s32[8]{0:T(128)S(1)}, s32[8]{0:T(128)}, u32[]{:S(2)}) copy-start(s32[8]{0:T(128)} %param.16) | copy-start | bytes 100
  0.7 19.1 %copy-start.8 = (s32[8,16]{1,0:T(8,128)S(1)}, s32[8,16]{1,0:T(8,128)}, u32[]{:S(2)}) copy-start(s32[8,16]{1,0:T(8,128)} %param.17) | copy-start | bytes 1540
  5.6 54.1 %copy-start.14 = (f32[2048]{0:T(1024)S(1)}, f32[2048]{0:T(1024)}, u32[]{:S(2)}) copy-start(f32[2048]{0:T(1024)} %param.20) | copy-start | bytes 24580
  5.6 41.7 %all-to-all-start = ((bf16[64,16,512]{2,1,0:T(8,128)(2,1)}), bf16[64,16,512]{2,1,0:T(8,128)(2,1)}, u32[]{:S(2)}, u32[]{:S(2)}) async-start(bf16[64,16,512]{2,1,0:T(8,128)(2,1)} %gather_fusion), calls=%async_computation | async-start | bytes 2097152 | tf_op jit(solution)/shard_map/all_to_all | solution.py:87
  49.1 6.4 %collective-permute-start.3 = (bf16[128,512]{1,0:T(8,128)(2,1)S(1)}, bf16[128,512]{1,0:T(8,128)(2,1)S(1)}, u32[]{:S(2)}, u32[]{:S(2)}) collective-permute-start(bf16[128,512]{1,0:T(8,128)(2,1)S(1)} %bitcast.119), channel_id=1, source_target_pairs={{0,1},{1,2},{2,3},{3,0},{4,5},{5,6},{6,7},{7,4},{8,9},{9,10},{10,1... | collective-permute-start | bytes 393224 | tf_op jit(solution)/shard_map/ppermute | solution.py:29
  51.2 10.5 %copy-start.13 = (bf16[2048,192]{0,1:T(8,128)(2,1)S(1)}, bf16[2048,192]{0,1:T(8,128)(2,1)}, u32[]{:S(2)}) copy-start(bf16[2048,192]{0,1:T(8,128)(2,1)} %param.21) | copy-start | bytes 2359300
  51.3 8.2 %collective-permute-start.4 = (bf16[128,512]{1,0:T(8,128)(2,1)S(1)}, bf16[128,512]{1,0:T(8,128)(2,1)S(1)}, u32[]{:S(2)}, u32[]{:S(2)}) collective-permute-start(bf16[128,512]{1,0:T(8,128)(2,1)S(1)} %bitcast.120), channel_id=1, source_target_pairs={{0,2},{1,3},{2,0},{3,1},{4,6},{5,7},{6,4},{7,5},{8,10},{9,11},{10,... | collective-permute-start | bytes 393224 | tf_op jit(solution)/shard_map/ppermute | solution.py:29
  54.0 5.5 %collective-permute-start.5 = (bf16[128,512]{1,0:T(8,128)(2,1)S(1)}, bf16[128,512]{1,0:T(8,128)(2,1)S(1)}, u32[]{:S(2)}, u32[]{:S(2)}) collective-permute-start(bf16[128,512]{1,0:T(8,128)(2,1)S(1)} %bitcast.121), channel_id=1, source_target_pairs={{0,3},{1,0},{2,1},{3,2},{4,7},{5,4},{6,5},{7,6},{8,11},{9,8},{10,9... | collective-permute-start | bytes 393224 | tf_op jit(solution)/shard_map/ppermute | solution.py:29
  65.3 12.8 %copy-start.1 = (bf16[8,16,512]{2,1,0:T(8,128)(2,1)S(1)}, bf16[8,16,512]{2,1,0:T(8,128)(2,1)}, u32[]{:S(2)}) copy-start(bf16[8,16,512]{2,1,0:T(8,128)(2,1)} %param.14) | copy-start | bytes 393220
  65.5 16.8 %copy-start.10 = (s32[8]{0:T(128)S(1)}, s32[8]{0:T(128)}, u32[]{:S(2)}) copy-start(s32[8]{0:T(128)} %copy-done.9) | copy-start | bytes 100
  68.0 49.9 %all-to-all-start.1 = ((bf16[64,16,192]{2,1,0:T(8,128)(2,1)}), bf16[64,16,192]{2,1,0:T(8,128)(2,1)}, u32[]{:S(2)}, u32[]{:S(2)}) async-start(bf16[64,16,192]{2,1,0:T(8,128)(2,1)} %gather_fusion.2), calls=%async_computation.1 | async-start | bytes 1048576 | tf_op jit(solution)/shard_map/all_to_all | solution.py:154
  75.0 49.2 %collective-permute-start.9 = (bf16[192,2048]{1,0:T(8,128)(2,1)}, bf16[192,2048]{1,0:T(8,128)(2,1)}, u32[]{:S(2)}, u32[]{:S(2)}) collective-permute-start(bf16[192,2048]{1,0:T(8,128)(2,1)} %param.23), channel_id=1, source_target_pairs={{0,2},{1,3},{2,0},{3,1},{4,6},{5,7},{6,4},{7,5},{8,10},{9,11},{10,... | collective-permute-start | bytes 2359304 | tf_op jit(solution)/shard_map/ppermute | solution.py:29
  78.0 50.4 %collective-permute-start.7 = (bf16[192,2048]{1,0:T(8,128)(2,1)}, bf16[192,2048]{1,0:T(8,128)(2,1)}, u32[]{:S(2)}, u32[]{:S(2)}) collective-permute-start(bf16[192,2048]{1,0:T(8,128)(2,1)} %param.23), channel_id=1, source_target_pairs={{0,1},{1,2},{2,3},{3,0},{4,5},{5,6},{6,7},{7,4},{8,9},{9,10},{10,1... | collective-permute-start | bytes 2359304 | tf_op jit(solution)/shard_map/ppermute | solution.py:29
  78.1 38.8 %collective-permute-start = (bf16[128,512]{1,0:T(8,128)(2,1)S(1)}, bf16[128,512]{1,0:T(8,128)(2,1)}, u32[]{:S(2)}, u32[]{:S(2)}) collective-permute-start(bf16[128,512]{1,0:T(8,128)(2,1)S(1)} %bitcast.115), channel_id=1, source_target_pairs={{0,1},{1,2},{2,3},{3,0},{4,5},{5,6},{6,7},{7,4},{8,9},{9,10},{10,1... | collective-permute-start | bytes 393224 | tf_op jit(solution)/shard_map/ppermute | solution.py:29
  78.1 39.8 %collective-permute-start.1 = (bf16[128,512]{1,0:T(8,128)(2,1)S(1)}, bf16[128,512]{1,0:T(8,128)(2,1)S(1)}, u32[]{:S(2)}, u32[]{:S(2)}) collective-permute-start(bf16[128,512]{1,0:T(8,128)(2,1)S(1)} %bitcast.116), channel_id=1, source_target_pairs={{0,2},{1,3},{2,0},{3,1},{4,6},{5,7},{6,4},{7,5},{8,10},{9,11},{10,... | collective-permute-start | bytes 393224 | tf_op jit(solution)/shard_map/ppermute | solution.py:29
  81.8 36.1 %collective-permute-start.2 = (bf16[128,512]{1,0:T(8,128)(2,1)S(1)}, bf16[128,512]{1,0:T(8,128)(2,1)S(1)}, u32[]{:S(2)}, u32[]{:S(2)}) collective-permute-start(bf16[128,512]{1,0:T(8,128)(2,1)S(1)} %bitcast.117), channel_id=1, source_target_pairs={{0,3},{1,0},{2,1},{3,2},{4,7},{5,4},{6,5},{7,6},{8,11},{9,8},{10,9... | collective-permute-start | bytes 393224 | tf_op jit(solution)/shard_map/ppermute | solution.py:29
  116.9 18.8 %collective-permute-start.11 = (bf16[192,2048]{1,0:T(8,128)(2,1)}, bf16[192,2048]{1,0:T(8,128)(2,1)}, u32[]{:S(2)}, u32[]{:S(2)}) collective-permute-start(bf16[192,2048]{1,0:T(8,128)(2,1)} %param.23), channel_id=1, source_target_pairs={{0,3},{1,0},{2,1},{3,2},{4,7},{5,4},{6,5},{7,6},{8,11},{9,8},{10,9... | collective-permute-start | bytes 2359304 | tf_op jit(solution)/shard_map/ppermute | solution.py:29
  119.6 7.4 %collective-permute-start.8 = (bf16[128,192]{1,0:T(8,128)(2,1)S(1)}, bf16[128,192]{1,0:T(8,128)(2,1)S(1)}, u32[]{:S(2)}, u32[]{:S(2)}) collective-permute-start(bf16[128,192]{1,0:T(8,128)(2,1)S(1)} %bitcast.123), channel_id=1, source_target_pairs={{0,2},{1,3},{2,0},{3,1},{4,6},{5,7},{6,4},{7,5},{8,10},{9,11},{10,... | collective-permute-start | bytes 147464 | tf_op jit(solution)/shard_map/ppermute | solution.py:29
  122.7 5.6 %collective-permute-start.6 = (bf16[128,192]{1,0:T(8,128)(2,1)S(1)}, bf16[128,192]{1,0:T(8,128)(2,1)S(1)}, u32[]{:S(2)}, u32[]{:S(2)}) collective-permute-start(bf16[128,192]{1,0:T(8,128)(2,1)S(1)} %bitcast.124), channel_id=1, source_target_pairs={{0,1},{1,2},{2,3},{3,0},{4,5},{5,6},{6,7},{7,4},{8,9},{9,10},{10,1... | collective-permute-start | bytes 147464 | tf_op jit(solution)/shard_map/ppermute | solution.py:29
  124.2 13.9 %collective-permute-start.10 = (bf16[128,192]{1,0:T(8,128)(2,1)S(1)}, bf16[128,192]{1,0:T(8,128)(2,1)S(1)}, u32[]{:S(2)}, u32[]{:S(2)}) collective-permute-start(bf16[128,192]{1,0:T(8,128)(2,1)S(1)} %bitcast.126), channel_id=1, source_target_pairs={{0,3},{1,0},{2,1},{3,2},{4,7},{5,4},{6,5},{7,6},{8,11},{9,8},{10,9... | collective-permute-start | bytes 147464 | tf_op jit(solution)/shard_map/ppermute | solution.py:29
  142.9 6.9 %collective-permute-start.12 = (bf16[128,512]{1,0:T(8,128)(2,1)S(1)}, bf16[128,512]{1,0:T(8,128)(2,1)S(1)}, u32[]{:S(2)}, u32[]{:S(2)}) collective-permute-start(bf16[128,512]{1,0:T(8,128)(2,1)S(1)} %convolution_convert_fusion.6), channel_id=1, source_target_pairs={{0,1},{1,2},{2,3},{3,0},{4,5},{5,6},{6,7},{7,4},{8,9},{9,10},{10,1... | collective-permute-start | bytes 393224 | tf_op jit(solution)/shard_map/ppermute | solution.py:29
  144.5 7.6 %collective-permute-start.13 = (bf16[128,512]{1,0:T(8,128)(2,1)S(1)}, bf16[128,512]{1,0:T(8,128)(2,1)S(1)}, u32[]{:S(2)}, u32[]{:S(2)}) collective-permute-start(bf16[128,512]{1,0:T(8,128)(2,1)S(1)} %convolution_convert_fusion.5), channel_id=1, source_target_pairs={{0,2},{1,3},{2,0},{3,1},{4,6},{5,7},{6,4},{7,5},{8,10},{9,11},{10,... | collective-permute-start | bytes 393224 | tf_op jit(solution)/shard_map/ppermute | solution.py:29
  148.9 5.1 %collective-permute-start.14 = (bf16[128,512]{1,0:T(8,128)(2,1)S(1)}, bf16[128,512]{1,0:T(8,128)(2,1)}, u32[]{:S(2)}, u32[]{:S(2)}) collective-permute-start(bf16[128,512]{1,0:T(8,128)(2,1)S(1)} %convolution_convert_fusion.4), channel_id=1, source_target_pairs={{0,3},{1,0},{2,1},{3,2},{4,7},{5,4},{6,5},{7,6},{8,11},{9,8},{10,9... | collective-permute-start | bytes 393224 | tf_op jit(solution)/shard_map/ppermute | solution.py:29
  (9 other events, 52.0 us)

commit v9 on v8

--- a/solution.py
+++ b/solution.py
@@ -83,14 +83,10 @@
         jnp.where(source_of[None, :] == devices[:, None], local_ids[None, :], 0), axis=1
     )
 
-    outgoing = jnp.take(drafts, send_pick, axis=0, mode="clip")
-    incoming = lax.all_to_all(outgoing, "req", 0, 0, tiled=True)
-    local_rows = jnp.take(incoming, source_of, axis=0, mode="clip")
-
     rows = per_owner_rows * tokens
-    owner_pieces = pieces_mlp(local_rows.reshape(rows, quarter), mlp_count)
-    full_rows = place_blocks(owner_pieces, mlp_count, part_index)
-    wide_rows = full_rows.astype(jnp.float32)
+    owned_pieces = pieces_mlp(drafts.reshape(rows, quarter), mlp_count)
+    owned_all = place_blocks(owned_pieces, mlp_count, part_index)
+    wide_rows = owned_all.astype(jnp.float32)
     normalized_rows = (
         wide_rows
         * lax.rsqrt(jnp.mean(wide_rows * wide_rows, axis=1, keepdims=True) + EPS)
@@ -98,13 +94,26 @@
     ).astype(jnp.bfloat16)
     kv_heads = key_value_weight.shape[1] // (2 * HEAD_DIM)
     group_heads = query_weight.shape[1] // (kv_heads * HEAD_DIM)
-    query_rows = jnp.dot(normalized_rows, query_weight, preferred_element_type=jnp.float32).reshape(
-        per_owner_rows, tokens, kv_heads, group_heads, HEAD_DIM
-    )
-    new_key_value = (
-        jnp.dot(normalized_rows, key_value_weight, preferred_element_type=jnp.float32)
-        .astype(jnp.bfloat16)
-        .reshape(per_owner_rows, tokens, kv_heads, 2 * HEAD_DIM)
+    query_width = kv_heads * group_heads * HEAD_DIM
+    queries = jnp.dot(normalized_rows, query_weight, preferred_element_type=jnp.float32)
+    fresh = jnp.dot(normalized_rows, key_value_weight, preferred_element_type=jnp.float32).astype(
+        jnp.bfloat16
+    )
+    query_high = queries.astype(jnp.bfloat16)
+    query_low = (queries - query_high.astype(jnp.float32)).astype(jnp.bfloat16)
+    payload = jnp.concatenate([query_high, query_low, fresh], axis=1).reshape(
+        per_owner_rows, tokens, -1
+    )
+
+    outgoing = jnp.take(payload, send_pick, axis=0, mode="clip")
+    incoming = lax.all_to_all(outgoing, "req", 0, 0, tiled=True)
+    local_rows = jnp.take(incoming, source_of, axis=0, mode="clip")
+    query_rows = (
+        local_rows[..., :query_width].astype(jnp.float32)
+        + local_rows[..., query_width : 2 * query_width].astype(jnp.float32)
+    ).reshape(per_owner_rows, tokens, kv_heads, group_heads, HEAD_DIM)
+    new_key_value = local_rows[..., 2 * query_width :].reshape(
+        per_owner_rows, tokens, kv_heads, 2 * HEAD_DIM
     )
     picker = (
         accepted_tokens[:, :, None] == jnp.arange(tokens, dtype=jnp.int32)[None, None, :]
@@ -150,12 +159,10 @@
     attended = attended.reshape(per_owner_rows, tokens, head_width)
 
     returning = jnp.take(attended, return_pick, axis=0, mode="clip")
-    owned_pieces = pieces_mlp(drafts.reshape(rows, quarter), mlp_count)
     arrived = lax.all_to_all(returning, "req", 0, 0, tiled=True)
     back_rows = jnp.take(arrived, my_owners, axis=0, mode="clip")
 
     gathered = pieces_mlp(back_rows.reshape(rows, head_width), mlp_count)
-    owned_all = place_blocks(owned_pieces, mlp_count, part_index)
 
     residual = owned_all.astype(jnp.float32)
     for piece, rows_of_group in zip(gathered, w_out_all):

time: 159 us -> 135 us (0.85)
  waiting for transfers between devices: 78.2 us -> 61.1 us
  starting transfers between devices: 44.1 us -> 36.9 us
    ppermute x15 -> x12, waiting for transfers between devices: 51.4 us -> 21.1 us  [shift_mlp(): lax.ppermute(value, 'mlp', [(i, (i + shift) % count) for i in range(count)])]
    all_to_all x1, waiting for transfers between devices: 0.01 us -> 14 us  [per_device(): arrived = lax.all_to_all(returning, 'req', 0, 0, tiled=True)]
    ppermute x15 -> x12, starting transfers between devices: 23.8 us -> 17.3 us  [shift_mlp(): lax.ppermute(value, 'mlp', [(i, (i + shift) % count) for i in range(count)])]
    dot_general x1, matrix products: 2.02 us -> 0.4 us  [per_device(): jnp.dot(normalized_rows, key_value_weight, preferred_element_type=jnp.flo...]
  transfers between devices with their start and end apart: 17 -> 14, of which waited for: 9 -> 8; matrix products, arithmetic and copies ran while one was open for 7% -> 8% of each run, Pallas kernels for 0% -> 0%
where the time goes in v9:
time: 135 us; the launch traced here: 133 us
  waiting for transfers between devices  61.1 us (45%)
  starting transfers between devices  36.9 us (27%)
  matrix products  17.5 us (13%)
  local copies, waits for them, and re-layouts  11.9 us (9%)
  other arithmetic  4.83 us (4%)
    all_to_all x1, waiting for transfers between devices, per_device(): incoming = lax.all_to_all(outgoing, 'req', 0, 0, tiled=True)  26.1 us
    ppermute x12, waiting for transfers between devices, shift_mlp(): lax.ppermute(value, 'mlp', [(i, (i + shift) % count) for i in range(count)])  21.1 us
    ppermute x12, starting transfers between devices, shift_mlp(): lax.ppermute(value, 'mlp', [(i, (i + shift) % count) for i in range(count)])  17.3 us
    all_to_all x1, waiting for transfers between devices, per_device(): arrived = lax.all_to_all(returning, 'req', 0, 0, tiled=True)  14 us
    all_to_all x1, starting transfers between devices, per_device(): incoming = lax.all_to_all(outgoing, 'req', 0, 0, tiled=True)  13.2 us
    all_to_all x1, starting transfers between devices, per_device(): arrived = lax.all_to_all(returning, 'req', 0, 0, tiled=True)  6.39 us
    dot_general x4, matrix products, per_device(): jnp.dot(piece, rows_of_group, preferred_element_type=jnp.float32)  4.77 us
    dot_general x4, matrix products, unit_block(): jnp.dot(hidden, columns, preferred_element_type=jnp.float32)  2.87 us
  transfers between devices with their start and end apart: 14, of which 8 were waited for; matrix products, arithmetic and copies ran while one was open for 8% of the time, Pallas kernels for 0%

profile of v9, /device:TPU:1, one launch (start us, length us, event | category | flops | bytes accessed | tf_op | source)
XLA Modules:
  0.0 133.4 jit_solution(1604023908133899345)
XLA Ops:
  0.7 2.2 %collective-permute-start = (bf16[128,512]{1,0:T(8,128)(2,1)}, bf16[128,512]{1,0:T(8,128)(2,1)S(1)}, u32[]{:S(2)}, u32[]{:S(2)}) collective-permute-start(bf16[128,512]{1,0:T(8,128)(2,1)} %bitcast.119), channel_id=1, source_target_pairs={{0,1},{1,2},{2,3},{3,0},{4,5},{5,6},{6,7},{7,4},{8,9},{9,10},{10,1... | collective-permute-start | bytes 393224 | tf_op jit(solution)/shard_map/ppermute | solution.py:29
  2.8 2.6 %collective-permute-start.1 = (bf16[128,512]{1,0:T(8,128)(2,1)}, bf16[128,512]{1,0:T(8,128)(2,1)S(1)}, u32[]{:S(2)}, u32[]{:S(2)}) collective-permute-start(bf16[128,512]{1,0:T(8,128)(2,1)} %bitcast.120), channel_id=1, source_target_pairs={{0,2},{1,3},{2,0},{3,1},{4,6},{5,7},{6,4},{7,5},{8,10},{9,11},{10,... | collective-permute-start | bytes 393224 | tf_op jit(solution)/shard_map/ppermute | solution.py:29
  11.7 1.6 %subtract_convert_fusion = (bf16[128,192]{0,1:T(8,128)(2,1)S(1)}, bf16[128,192]{0,1:T(8,128)(2,1)S(1)}) fusion(bf16[2048,192]{0,1:T(8,128)(2,1)} %param.21, bf16[128,2048]{1,0:T(8,128)(2,1)S(1)} %constant_dynamic-update-slice_fusion, f32[2048]{0:T(1024)} %param.20, f32[128]{0:T(128)S(1)} %add_rsqrt_fusion.1), kind=kOutput, calls=%fused_computation.70 | convolution fusion | flops 101810176 | bytes 1417728 | tf_op jit(solution)/shard_map/dot_general | solution.py:98
  13.9 1.6 %gather_fusion = bf16[64,16,512]{2,1,0:T(8,128)(2,1)} fusion(bf16[8,16,512]{2,1,0:T(8,128)(2,1)S(1)} %bitcast.114, s32[1024]{0:T(1024)S(1)} %pad_clamp_fusion.3), kind=kCustom, calls=%fused_computation | custom fusion | bytes 2097408 | tf_op jit(solution)/shard_map/jit(_take)/gather | solution.py:108
  15.5 13.2 %all-to-all-start = ((bf16[64,16,512]{2,1,0:T(8,128)(2,1)}), bf16[64,16,512]{2,1,0:T(8,128)(2,1)}, u32[]{:S(2)}, u32[]{:S(2)}) async-start(bf16[64,16,512]{2,1,0:T(8,128)(2,1)} %gather_fusion), calls=%async_computation | async-start | bytes 2097152 | tf_op jit(solution)/shard_map/all_to_all | solution.py:109
  31.1 26.1 %all-to-all-done = bf16[64,16,512]{2,1,0:T(8,128)(2,1)} async-done(((bf16[64,16,512]{2,1,0:T(8,128)(2,1)}), bf16[64,16,512]{2,1,0:T(8,128)(2,1)}, u32[]{:S(2)}, u32[]{:S(2)}) %all-to-all-start) | async-done | bytes 1048608 | tf_op jit(solution)/shard_map/all_to_all | solution.py:109
  57.2 1.8 %gather_fusion.1 = bf16[8,16,512]{2,1,0:T(8,128)(2,1)S(1)} fusion(bf16[64,16,512]{2,1,0:T(8,128)(2,1)} %all-to-all-done, s32[1024]{0:T(1024)S(1)} %pad_clamp_fusion.2), kind=kCustom, calls=%fused_computation.1 | custom fusion | bytes 262176 | tf_op jit(solution)/shard_map/jit(_take)/gather | solution.py:110
  61.3 1.5 %fusion.53 = (f32[8,3,16]{2,1,0:T(4,128)S(1)}, f32[8,1,3,16,16]{3,4,2,0,1:T(8,128)S(1)}) fusion(f32[8,16,3,64]{3,2,1,0:T(4,128)S(1)} %reshape.220, bf16[8,16,1,128]{3,1,0,2:T(8,128)(2,1)} %slice_bitcast_fusion.4, pred[8,16,16]{1,2,0:T(8,128)(4,1)S(1)} %copy.35), kind=kOutput, calls=%fused_computation.121 | convolution fusion | flops 4736640 | bytes 159232 | tf_op jit(solution)/shard_map/rtkgd,rjkd->rkgtj/dot_general | solution.py:128
  62.8 1.8 %fusion.54 = (f32[8,3,16]{2,1,0:T(4,128)S(1)}, f32[8,1,3,16,256]{4,3,2,0,1:T(8,128)S(1)}) fusion(bf16[8,256,1,128]{3,1,2,0:T(8,128)(2,1)} %param.19, f32[8,16,3,64]{3,2,1,0:T(4,128)S(1)} %reshape.220, pred[8,256]{1,0:T(8,128)(4,1)} %iota_compare_fusion.5), kind=kOutput, calls=%fused_computation.122 | convolution fusion | flops 75792000 | bytes 1019392 | tf_op jit(solution)/shard_map/rtkgd,rckd->rkgtc/dot_general | solution.py:134
  64.9 1.5 %convolution_bitcast_fusion = f32[8,64,3,16]{1,3,2,0:T(8,128)S(1)} fusion(bf16[8,256,1,128]{3,1,2,0:T(8,128)(2,1)} %param.19, f32[8,1,3,16,256]{4,3,2,0,1:T(8,128)S(1)} %get-tuple-element.13, f32[8,3,16]{2,1,0:T(4,128)S(1)} %max.19), kind=kOutput, calls=%fused_computation.30 | convolution fusion | flops 12779520 | bytes 1017344 | tf_op jit(solution)/shard_map/rkgtc,rckd->rtkgd/dot_general | solution.py:140
  66.9 1.5 %gather_fusion.2 = bf16[64,16,192]{2,1,0:T(8,128)(2,1)} fusion(bf16[8,16,192]{2,1,0:T(8,128)(2,1)S(1)} %reshape.228, s32[1024]{0:T(1024)} %pad_clamp_fusion.1), kind=kCustom, calls=%fused_computation.2 | custom fusion | bytes 786688 | tf_op jit(solution)/shard_map/jit(_take)/gather | solution.py:161
  68.4 6.4 %all-to-all-start.1 = ((bf16[64,16,192]{2,1,0:T(8,128)(2,1)}), bf16[64,16,192]{2,1,0:T(8,128)(2,1)}, u32[]{:S(2)}, u32[]{:S(2)}) async-start(bf16[64,16,192]{2,1,0:T(8,128)(2,1)} %gather_fusion.2), calls=%async_computation.1 | async-start | bytes 1048576 | tf_op jit(solution)/shard_map/all_to_all | solution.py:162
  74.8 1.9 %collective-permute-start.8 = (bf16[192,2048]{1,0:T(8,128)(2,1)}, bf16[192,2048]{1,0:T(8,128)(2,1)}, u32[]{:S(2)}, u32[]{:S(2)}) collective-permute-start(bf16[192,2048]{1,0:T(8,128)(2,1)} %param.23), channel_id=1, source_target_pairs={{0,3},{1,0},{2,1},{3,2},{4,7},{5,4},{6,5},{7,6},{8,11},{9,8},{10,9... | collective-permute-start | bytes 2359304 | tf_op jit(solution)/shard_map/ppermute | solution.py:29
  78.0 14.0 %all-to-all-done.1 = bf16[64,16,192]{2,1,0:T(8,128)(2,1)} async-done(((bf16[64,16,192]{2,1,0:T(8,128)(2,1)}), bf16[64,16,192]{2,1,0:T(8,128)(2,1)}, u32[]{:S(2)}, u32[]{:S(2)}) %all-to-all-start.1) | async-done | bytes 393248 | tf_op jit(solution)/shard_map/all_to_all | solution.py:162
  92.0 1.6 %gather_fusion.3 = bf16[8,16,192]{2,1,0:T(8,128)(2,1)S(1)} fusion(bf16[64,16,192]{2,1,0:T(8,128)(2,1)} %all-to-all-done.1, s32[1024]{0:T(1024)S(1)} %pad_clamp_fusion), kind=kCustom, calls=%fused_computation.3 | custom fusion | bytes 98336 | tf_op jit(solution)/shard_map/jit(_take)/gather | solution.py:163
  93.6 1.9 %collective-permute-start.7 = (bf16[128,192]{1,0:T(8,128)(2,1)S(1)}, bf16[128,192]{1,0:T(8,128)(2,1)S(1)}, u32[]{:S(2)}, u32[]{:S(2)}) collective-permute-start(bf16[128,192]{1,0:T(8,128)(2,1)S(1)} %bitcast.115), channel_id=1, source_target_pairs={{0,3},{1,0},{2,1},{3,2},{4,7},{5,4},{6,5},{7,6},{8,11},{9,8},{10,9... | collective-permute-start | bytes 147464 | tf_op jit(solution)/shard_map/ppermute | solution.py:29
  96.8 15.8 %collective-permute-done.7 = bf16[128,192]{1,0:T(8,128)(2,1)S(1)} collective-permute-done((bf16[128,192]{1,0:T(8,128)(2,1)S(1)}, bf16[128,192]{1,0:T(8,128)(2,1)S(1)}, u32[]{:S(2)}, u32[]{:S(2)}) %collective-permute-start.7) | collective-permute-done | bytes 49184 | tf_op jit(solution)/shard_map/ppermute | solution.py:29
  114.8 1.4 %fusion.1 = f32[128,2048]{1,0:T(8,128)S(1)} fusion(bf16[128,192]{1,0:T(8,128)(2,1)S(1)} %collective-permute-done.5, bf16[192,2048]{1,0:T(8,128)(2,1)} %collective-permute-done.6), kind=kOutput, calls=%fused_computation.7 | convolution fusion | flops 101187584 | bytes 1884160 | tf_op jit(solution)/shard_map/dot_general | solution.py:169
  116.4 1.4 %fusion.2 = f32[128,2048]{1,0:T(8,128)S(1)} fusion(bf16[128,192]{1,0:T(8,128)(2,1)S(1)} %collective-permute-done.3, bf16[192,2048]{1,0:T(8,128)(2,1)} %collective-permute-done.4), kind=kOutput, calls=%fused_computation.9 | convolution fusion | flops 101187584 | bytes 1884160 | tf_op jit(solution)/shard_map/dot_general | solution.py:169
  118.4 1.6 %copy-done.2 = bf16[2048,640]{1,0:T(8,128)(2,1)S(1)} copy-done((bf16[2048,640]{1,0:T(8,128)(2,1)S(1)}, bf16[2048,640]{1,0:T(8,128)(2,1)}, u32[]{:S(2)}) %copy-start.2) | copy-done | bytes 2621464
  121.7 2.2 %collective-permute-start.10 = (bf16[128,512]{1,0:T(8,128)(2,1)S(1)}, bf16[128,512]{1,0:T(8,128)(2,1)S(1)}, u32[]{:S(2)}, u32[]{:S(2)}) collective-permute-start(bf16[128,512]{1,0:T(8,128)(2,1)S(1)} %convolution_convert_fusion.5), channel_id=1, source_target_pairs={{0,2},{1,3},{2,0},{3,1},{4,6},{5,7},{6,4},{7,5},{8,10},{9,11},{10,... | collective-permute-start | bytes 393224 | tf_op jit(solution)/shard_map/ppermute | solution.py:29
  124.2 1.9 %collective-permute-start.9 = (bf16[128,512]{1,0:T(8,128)(2,1)S(1)}, bf16[128,512]{1,0:T(8,128)(2,1)}, u32[]{:S(2)}, u32[]{:S(2)}) collective-permute-start(bf16[128,512]{1,0:T(8,128)(2,1)S(1)} %convolution_convert_fusion.6), channel_id=1, source_target_pairs={{0,1},{1,2},{2,3},{3,0},{4,5},{5,6},{6,7},{7,4},{8,9},{9,10},{10,1... | collective-permute-start | bytes 393224 | tf_op jit(solution)/shard_map/ppermute | solution.py:29
  128.1 2.1 %collective-permute-done.9 = bf16[128,512]{1,0:T(8,128)(2,1)} collective-permute-done((bf16[128,512]{1,0:T(8,128)(2,1)S(1)}, bf16[128,512]{1,0:T(8,128)(2,1)}, u32[]{:S(2)}, u32[]{:S(2)}) %collective-permute-start.9) | collective-permute-done | bytes 131104 | tf_op jit(solution)/shard_map/ppermute | solution.py:29
  131.4 2.0 %add_convert_fusion = bf16[128,512]{1,0:T(8,128)(2,1)} fusion(bf16[128,512]{1,0:T(8,128)(2,1)} %collective-permute-done.11, bf16[128,512]{1,0:T(8,128)(2,1)S(1)} %collective-permute-done.10, bf16[128,512]{1,0:T(8,128)(2,1)} %collective-permute-done.9, f32[128,2048]{1,0:T(8,128)} %copy-done.1, s32[]{:T(128)S(6)} %select_n.120, ...), kind=kOutput, calls=%fused_computation.60 | convolution fusion | flops 84541440 | bytes 1606656 | tf_op jit(solution)/shard_map/dot_general | solution.py:181
  (95 shorter events, 22.7 us)
Async XLA Ops:
  0.6 120.8 %copy-start = (bf16[640,2048]{1,0:T(8,128)(2,1)S(1)}, bf16[640,2048]{1,0:T(8,128)(2,1)}, u32[]{:S(2)}) copy-start(bf16[640,2048]{1,0:T(8,128)(2,1)} %param.27) | copy-start | bytes 7864324
  0.6 12.6 %copy-start.15 = (f32[2048]{0:T(1024)S(1)}, f32[2048]{0:T(1024)}, u32[]{:S(2)}) copy-start(f32[2048]{0:T(1024)} %param.20) | copy-start | bytes 24580
  0.7 9.6 %collective-permute-start = (bf16[128,512]{1,0:T(8,128)(2,1)}, bf16[128,512]{1,0:T(8,128)(2,1)S(1)}, u32[]{:S(2)}, u32[]{:S(2)}) collective-permute-start(bf16[128,512]{1,0:T(8,128)(2,1)} %bitcast.119), channel_id=1, source_target_pairs={{0,1},{1,2},{2,3},{3,0},{4,5},{5,6},{6,7},{7,4},{8,9},{9,10},{10,1... | collective-permute-start | bytes 393224 | tf_op jit(solution)/shard_map/ppermute | solution.py:29
  2.8 8.6 %collective-permute-start.1 = (bf16[128,512]{1,0:T(8,128)(2,1)}, bf16[128,512]{1,0:T(8,128)(2,1)S(1)}, u32[]{:S(2)}, u32[]{:S(2)}) collective-permute-start(bf16[128,512]{1,0:T(8,128)(2,1)} %bitcast.120), channel_id=1, source_target_pairs={{0,2},{1,3},{2,0},{3,1},{4,6},{5,7},{6,4},{7,5},{8,10},{9,11},{10,... | collective-permute-start | bytes 393224 | tf_op jit(solution)/shard_map/ppermute | solution.py:29
  5.5 6.0 %collective-permute-start.2 = (bf16[128,512]{1,0:T(8,128)(2,1)}, bf16[128,512]{1,0:T(8,128)(2,1)S(1)}, u32[]{:S(2)}, u32[]{:S(2)}) collective-permute-start(bf16[128,512]{1,0:T(8,128)(2,1)} %bitcast.121), channel_id=1, source_target_pairs={{0,3},{1,0},{2,1},{3,2},{4,7},{5,4},{6,5},{7,6},{8,11},{9,8},{10,9... | collective-permute-start | bytes 393224 | tf_op jit(solution)/shard_map/ppermute | solution.py:29
  13.7 15.0 %copy-start.6 = (s32[8,16]{1,0:T(8,128)S(1)}, s32[8,16]{1,0:T(8,128)}, u32[]{:S(2)}) copy-start(s32[8,16]{1,0:T(8,128)} %param.17) | copy-start | bytes 1540
  13.7 16.0 %copy-start.10 = (s32[8]{0:T(128)S(1)}, s32[8]{0:T(128)}, u32[]{:S(2)}) copy-start(s32[8]{0:T(128)} %copy-done.9) | copy-start | bytes 100
  13.7 16.0 %copy-start.12 = (s32[8]{0:T(128)S(1)}, s32[8]{0:T(128)}, u32[]{:S(2)}) copy-start(s32[8]{0:T(128)} %get-tuple-element.16) | copy-start | bytes 100
  13.7 16.7 %copy-start.11 = (s32[8]{0:T(128)S(1)}, s32[8]{0:T(128)}, u32[]{:S(2)}) copy-start(s32[8]{0:T(128)} %param.16) | copy-start | bytes 100
  15.5 41.7 %all-to-all-start = ((bf16[64,16,512]{2,1,0:T(8,128)(2,1)}), bf16[64,16,512]{2,1,0:T(8,128)(2,1)}, u32[]{:S(2)}, u32[]{:S(2)}) async-start(bf16[64,16,512]{2,1,0:T(8,128)(2,1)} %gather_fusion), calls=%async_computation | async-start | bytes 2097152 | tf_op jit(solution)/shard_map/all_to_all | solution.py:109
  61.3 5.1 %copy-start.4 = (bf16[8,16,1,128]{3,1,0,2:T(8,128)(2,1)S(1)}, bf16[8,16,1,128]{3,1,0,2:T(8,128)(2,1)}, u32[]{:S(2)}) copy-start(bf16[8,16,1,128]{3,1,0,2:T(8,128)(2,1)} %slice_bitcast_fusion.4) | copy-start | bytes 98308
  64.6 13.4 %copy-start.8 = (s32[8]{0:T(128)S(1)}, s32[8]{0:T(128)}, u32[]{:S(2)}) copy-start(s32[8]{0:T(128)} %copy-done.7) | copy-start | bytes 100
  68.4 23.6 %all-to-all-start.1 = ((bf16[64,16,192]{2,1,0:T(8,128)(2,1)}), bf16[64,16,192]{2,1,0:T(8,128)(2,1)}, u32[]{:S(2)}, u32[]{:S(2)}) async-start(bf16[64,16,192]{2,1,0:T(8,128)(2,1)} %gather_fusion.2), calls=%async_computation.1 | async-start | bytes 1048576 | tf_op jit(solution)/shard_map/all_to_all | solution.py:162
  74.8 21.6 %collective-permute-start.8 = (bf16[192,2048]{1,0:T(8,128)(2,1)}, bf16[192,2048]{1,0:T(8,128)(2,1)}, u32[]{:S(2)}, u32[]{:S(2)}) collective-permute-start(bf16[192,2048]{1,0:T(8,128)(2,1)} %param.23), channel_id=1, source_target_pairs={{0,3},{1,0},{2,1},{3,2},{4,7},{5,4},{6,5},{7,6},{8,11},{9,8},{10,9... | collective-permute-start | bytes 2359304 | tf_op jit(solution)/shard_map/ppermute | solution.py:29
  76.7 37.3 %collective-permute-start.6 = (bf16[192,2048]{1,0:T(8,128)(2,1)}, bf16[192,2048]{1,0:T(8,128)(2,1)}, u32[]{:S(2)}, u32[]{:S(2)}) collective-permute-start(bf16[192,2048]{1,0:T(8,128)(2,1)} %param.23), channel_id=1, source_target_pairs={{0,2},{1,3},{2,0},{3,1},{4,6},{5,7},{6,4},{7,5},{8,10},{9,11},{10,... | collective-permute-start | bytes 2359304 | tf_op jit(solution)/shard_map/ppermute | solution.py:29
  77.6 38.6 %collective-permute-start.4 = (bf16[192,2048]{1,0:T(8,128)(2,1)}, bf16[192,2048]{1,0:T(8,128)(2,1)}, u32[]{:S(2)}, u32[]{:S(2)}) collective-permute-start(bf16[192,2048]{1,0:T(8,128)(2,1)} %param.23), channel_id=1, source_target_pairs={{0,1},{1,2},{2,3},{3,0},{4,5},{5,6},{6,7},{7,4},{8,9},{9,10},{10,1... | collective-permute-start | bytes 2359304 | tf_op jit(solution)/shard_map/ppermute | solution.py:29
  93.6 19.0 %collective-permute-start.7 = (bf16[128,192]{1,0:T(8,128)(2,1)S(1)}, bf16[128,192]{1,0:T(8,128)(2,1)S(1)}, u32[]{:S(2)}, u32[]{:S(2)}) collective-permute-start(bf16[128,192]{1,0:T(8,128)(2,1)S(1)} %bitcast.115), channel_id=1, source_target_pairs={{0,3},{1,0},{2,1},{3,2},{4,7},{5,4},{6,5},{7,6},{8,11},{9,8},{10,9... | collective-permute-start | bytes 147464 | tf_op jit(solution)/shard_map/ppermute | solution.py:29
  95.5 22.3 %copy-start.3 = (bf16[192,2048]{1,0:T(8,128)(2,1)S(1)}, bf16[192,2048]{1,0:T(8,128)(2,1)}, u32[]{:S(2)}) copy-start(bf16[192,2048]{1,0:T(8,128)(2,1)} %param.23) | copy-start | bytes 2359300
  95.5 19.2 %collective-permute-start.5 = (bf16[128,192]{1,0:T(8,128)(2,1)S(1)}, bf16[128,192]{1,0:T(8,128)(2,1)S(1)}, u32[]{:S(2)}, u32[]{:S(2)}) collective-permute-start(bf16[128,192]{1,0:T(8,128)(2,1)S(1)} %bitcast.116), channel_id=1, source_target_pairs={{0,2},{1,3},{2,0},{3,1},{4,6},{5,7},{6,4},{7,5},{8,10},{9,11},{10,... | collective-permute-start | bytes 147464 | tf_op jit(solution)/shard_map/ppermute | solution.py:29
  96.4 20.0 %collective-permute-start.3 = (bf16[128,192]{1,0:T(8,128)(2,1)S(1)}, bf16[128,192]{1,0:T(8,128)(2,1)S(1)}, u32[]{:S(2)}, u32[]{:S(2)}) collective-permute-start(bf16[128,192]{1,0:T(8,128)(2,1)S(1)} %bitcast.117), channel_id=1, source_target_pairs={{0,1},{1,2},{2,3},{3,0},{4,5},{5,6},{6,7},{7,4},{8,9},{9,10},{10,1... | collective-permute-start | bytes 147464 | tf_op jit(solution)/shard_map/ppermute | solution.py:29
  120.8 6.5 %copy-start.16 = (s32[8,8]{1,0:T(8,128)S(1)}, s32[8,8]{1,0:T(8,128)}, u32[]{:S(2)}) copy-start(s32[8,8]{1,0:T(8,128)} %param.18) | copy-start | bytes 772
  121.7 6.4 %collective-permute-start.10 = (bf16[128,512]{1,0:T(8,128)(2,1)S(1)}, bf16[128,512]{1,0:T(8,128)(2,1)S(1)}, u32[]{:S(2)}, u32[]{:S(2)}) collective-permute-start(bf16[128,512]{1,0:T(8,128)(2,1)S(1)} %convolution_convert_fusion.5), channel_id=1, source_target_pairs={{0,2},{1,3},{2,0},{3,1},{4,6},{5,7},{6,4},{7,5},{8,10},{9,11},{10,... | collective-permute-start | bytes 393224 | tf_op jit(solution)/shard_map/ppermute | solution.py:29
  124.2 6.0 %collective-permute-start.9 = (bf16[128,512]{1,0:T(8,128)(2,1)S(1)}, bf16[128,512]{1,0:T(8,128)(2,1)}, u32[]{:S(2)}, u32[]{:S(2)}) collective-permute-start(bf16[128,512]{1,0:T(8,128)(2,1)S(1)} %convolution_convert_fusion.6), channel_id=1, source_target_pairs={{0,1},{1,2},{2,3},{3,0},{4,5},{5,6},{6,7},{7,4},{8,9},{9,10},{10,1... | collective-permute-start | bytes 393224 | tf_op jit(solution)/shard_map/ppermute | solution.py:29
  126.4 5.0 %collective-permute-start.11 = (bf16[128,512]{1,0:T(8,128)(2,1)S(1)}, bf16[128,512]{1,0:T(8,128)(2,1)}, u32[]{:S(2)}, u32[]{:S(2)}) collective-permute-start(bf16[128,512]{1,0:T(8,128)(2,1)S(1)} %convolution_convert_fusion.4), channel_id=1, source_target_pairs={{0,3},{1,0},{2,1},{3,2},{4,7},{5,4},{6,5},{7,6},{8,11},{9,8},{10,9... | collective-permute-start | bytes 393224 | tf_op jit(solution)/shard_map/ppermute | solution.py:29
  (7 other events, 15.1 us)

commit v10 on v9

--- a/solution.py
+++ b/solution.py
@@ -101,18 +101,19 @@
     )
     query_high = queries.astype(jnp.bfloat16)
     query_low = (queries - query_high.astype(jnp.float32)).astype(jnp.bfloat16)
-    payload = jnp.concatenate([query_high, query_low, fresh], axis=1).reshape(
+    payload = jnp.concatenate([fresh, query_high, query_low], axis=1).reshape(
         per_owner_rows, tokens, -1
     )
 
     outgoing = jnp.take(payload, send_pick, axis=0, mode="clip")
     incoming = lax.all_to_all(outgoing, "req", 0, 0, tiled=True)
     local_rows = jnp.take(incoming, source_of, axis=0, mode="clip")
+    fresh_width = fresh.shape[1]
     query_rows = (
-        local_rows[..., :query_width].astype(jnp.float32)
-        + local_rows[..., query_width : 2 * query_width].astype(jnp.float32)
+        local_rows[..., fresh_width : fresh_width + query_width].astype(jnp.float32)
+        + local_rows[..., fresh_width + query_width :].astype(jnp.float32)
     ).reshape(per_owner_rows, tokens, kv_heads, group_heads, HEAD_DIM)
-    new_key_value = local_rows[..., 2 * query_width :].reshape(
+    new_key_value = local_rows[..., :fresh_width].reshape(
         per_owner_rows, tokens, kv_heads, 2 * HEAD_DIM
     )
     picker = (
@@ -164,12 +165,14 @@
 
     gathered = pieces_mlp(back_rows.reshape(rows, head_width), mlp_count)
 
-    residual = owned_all.astype(jnp.float32)
-    for piece, rows_of_group in zip(gathered, w_out_all):
-        group_product = jnp.dot(
-            piece, rows_of_group, preferred_element_type=jnp.float32
-        )
-        residual = residual + group_product.astype(jnp.bfloat16).astype(jnp.float32)
+    group_products = [
+        jnp.dot(piece, rows_of_group, preferred_element_type=jnp.float32).astype(jnp.bfloat16)
+        for piece, rows_of_group in zip(gathered, w_out_all)
+    ]
+    attn_sum = group_products[0].astype(jnp.float32)
+    for product in group_products[1:]:
+        attn_sum = attn_sum + product.astype(jnp.float32)
+    residual = owned_all.astype(jnp.float32) + attn_sum
     normed_two = (
         residual * lax.rsqrt(jnp.mean(residual * residual, axis=1, keepdims=True) + EPS) * mlp_gain
     ).astype(jnp.bfloat16)

time: 135 us -> 137 us (1.015)
  matrix products: 17.5 us -> 19.8 us
  transfers between devices with their start and end apart: 14 -> 14, of which waited for: 8 -> 6; matrix products, arithmetic and copies ran while one was open for 8% -> 9% of each run, Pallas kernels for 0% -> 0%
where the time goes in v10:
time: 137 us; the launch traced here: 136 us
  waiting for transfers between devices  61.5 us (45%)
  starting transfers between devices  36.9 us (27%)
  matrix products  19.8 us (14%)
  local copies, waits for them, and re-layouts  11.6 us (8%)
  other arithmetic  4.84 us (4%)
    all_to_all x1, waiting for transfers between devices, per_device(): incoming = lax.all_to_all(outgoing, 'req', 0, 0, tiled=True)  26 us
    ppermute x12, waiting for transfers between devices, shift_mlp(): lax.ppermute(value, 'mlp', [(i, (i + shift) % count) for i in range(count)])  22.1 us
    ppermute x12, starting transfers between devices, shift_mlp(): lax.ppermute(value, 'mlp', [(i, (i + shift) % count) for i in range(count)])  17.3 us
    all_to_all x1, waiting for transfers between devices, per_device(): arrived = lax.all_to_all(returning, 'req', 0, 0, tiled=True)  13.4 us
    all_to_all x1, starting transfers between devices, per_device(): incoming = lax.all_to_all(outgoing, 'req', 0, 0, tiled=True)  13.2 us
    all_to_all x1, starting transfers between devices, per_device(): arrived = lax.all_to_all(returning, 'req', 0, 0, tiled=True)  6.39 us
    dot_general x4, matrix products, per_device(): jnp.dot(piece, rows_of_group, preferred_element_type=jnp.float32)  6.01 us
    dot_general x4, matrix products, unit_block(): jnp.dot(hidden, columns, preferred_element_type=jnp.float32)  2.87 us
  transfers between devices with their start and end apart: 14, of which 6 were waited for; matrix products, arithmetic and copies ran while one was open for 9% of the time, Pallas kernels for 0%

profile of v10, /device:TPU:1, one launch (start us, length us, event | category | flops | bytes accessed | tf_op | source)
XLA Modules:
  0.0 135.9 jit_solution(9623605267293358934)
XLA Ops:
  0.7 2.2 %collective-permute-start = (bf16[128,512]{1,0:T(8,128)(2,1)}, bf16[128,512]{1,0:T(8,128)(2,1)S(1)}, u32[]{:S(2)}, u32[]{:S(2)}) collective-permute-start(bf16[128,512]{1,0:T(8,128)(2,1)} %bitcast.119), channel_id=1, source_target_pairs={{0,1},{1,2},{2,3},{3,0},{4,5},{5,6},{6,7},{7,4},{8,9},{9,10},{10,1... | collective-permute-start | bytes 393224 | tf_op jit(solution)/shard_map/ppermute | solution.py:29
  2.8 2.6 %collective-permute-start.1 = (bf16[128,512]{1,0:T(8,128)(2,1)}, bf16[128,512]{1,0:T(8,128)(2,1)S(1)}, u32[]{:S(2)}, u32[]{:S(2)}) collective-permute-start(bf16[128,512]{1,0:T(8,128)(2,1)} %bitcast.120), channel_id=1, source_target_pairs={{0,2},{1,3},{2,0},{3,1},{4,6},{5,7},{6,4},{7,5},{8,10},{9,11},{10,... | collective-permute-start | bytes 393224 | tf_op jit(solution)/shard_map/ppermute | solution.py:29
  11.7 1.5 %convolution_convert_fusion.8 = bf16[128,128]{0,1:T(8,128)(2,1)S(1)} fusion(bf16[2048,128]{1,0:T(8,128)(2,1)} %param.22, bf16[128,2048]{1,0:T(8,128)(2,1)S(1)} %constant_dynamic-update-slice_fusion, f32[2048]{0:T(1024)} %param.20, f32[128]{0:T(128)S(1)} %add_rsqrt_fusion.1), kind=kOutput, calls=%fused_computation.39 | convolution fusion | flops 68173824 | bytes 1090048 | tf_op jit(solution)/shard_map/dot_general | solution.py:99
  13.1 1.6 %subtract_convert_fusion = (bf16[128,192]{0,1:T(8,128)(2,1)S(1)}, bf16[128,192]{0,1:T(8,128)(2,1)S(1)}) fusion(bf16[2048,192]{0,1:T(8,128)(2,1)} %param.21, bf16[128,2048]{1,0:T(8,128)(2,1)S(1)} %constant_dynamic-update-slice_fusion, f32[2048]{0:T(1024)S(1)} %copy-done.13, f32[128]{0:T(128)S(1)} %add_rsqrt_fusion.1), kind=kOutput, calls=%fused_computation.70 | convolution fusion | flops 101810176 | bytes 1417728 | tf_op jit(solution)/shard_map/dot_general | solution.py:98
  14.9 1.6 %gather_fusion = bf16[64,16,512]{2,1,0:T(8,128)(2,1)} fusion(bf16[8,16,512]{2,1,0:T(8,128)(2,1)S(1)} %bitcast.114, s32[1024]{0:T(1024)S(1)} %pad_clamp_fusion.3), kind=kCustom, calls=%fused_computation | custom fusion | bytes 2097408 | tf_op jit(solution)/shard_map/jit(_take)/gather | solution.py:108
  16.6 13.2 %all-to-all-start = ((bf16[64,16,512]{2,1,0:T(8,128)(2,1)}), bf16[64,16,512]{2,1,0:T(8,128)(2,1)}, u32[]{:S(2)}, u32[]{:S(2)}) async-start(bf16[64,16,512]{2,1,0:T(8,128)(2,1)} %gather_fusion), calls=%async_computation | async-start | bytes 2097152 | tf_op jit(solution)/shard_map/all_to_all | solution.py:109
  32.2 26.0 %all-to-all-done = bf16[64,16,512]{2,1,0:T(8,128)(2,1)} async-done(((bf16[64,16,512]{2,1,0:T(8,128)(2,1)}), bf16[64,16,512]{2,1,0:T(8,128)(2,1)}, u32[]{:S(2)}, u32[]{:S(2)}) %all-to-all-start) | async-done | bytes 1048608 | tf_op jit(solution)/shard_map/all_to_all | solution.py:109
  58.2 1.8 %gather_fusion.1 = bf16[8,16,512]{2,1,0:T(8,128)(2,1)S(1)} fusion(bf16[64,16,512]{2,1,0:T(8,128)(2,1)} %all-to-all-done, s32[1024]{0:T(1024)S(1)} %pad_clamp_fusion.2), kind=kCustom, calls=%fused_computation.1 | custom fusion | bytes 262176 | tf_op jit(solution)/shard_map/jit(_take)/gather | solution.py:110
  62.4 1.5 %fusion.53 = (f32[8,3,16]{2,1,0:T(4,128)S(1)}, f32[8,1,3,16,16]{3,4,2,0,1:T(8,128)S(1)}) fusion(f32[8,16,3,64]{3,2,1,0:T(4,128)S(1)} %reshape.220, bf16[8,16,1,128]{3,1,0,2:T(8,128)(2,1)} %slice_bitcast_fusion.4, pred[8,16,16]{1,2,0:T(8,128)(4,1)S(1)} %copy.35), kind=kOutput, calls=%fused_computation.121 | convolution fusion | flops 4736640 | bytes 159232 | tf_op jit(solution)/shard_map/rtkgd,rjkd->rkgtj/dot_general | solution.py:129
  63.9 1.8 %fusion.54 = (f32[8,3,16]{2,1,0:T(4,128)S(1)}, f32[8,1,3,16,256]{4,3,2,0,1:T(8,128)S(1)}) fusion(bf16[8,256,1,128]{3,1,2,0:T(8,128)(2,1)} %param.19, f32[8,16,3,64]{3,2,1,0:T(4,128)S(1)} %reshape.220, pred[8,256]{1,0:T(8,128)(4,1)} %iota_compare_fusion.5), kind=kOutput, calls=%fused_computation.122 | convolution fusion | flops 75792000 | bytes 1019392 | tf_op jit(solution)/shard_map/rtkgd,rckd->rkgtc/dot_general | solution.py:135
  65.9 1.5 %convolution_bitcast_fusion = f32[8,64,3,16]{1,3,2,0:T(8,128)S(1)} fusion(bf16[8,256,1,128]{3,1,2,0:T(8,128)(2,1)} %param.19, f32[8,1,3,16,256]{4,3,2,0,1:T(8,128)S(1)} %get-tuple-element.13, f32[8,3,16]{2,1,0:T(4,128)S(1)} %max.19), kind=kOutput, calls=%fused_computation.30 | convolution fusion | flops 12779520 | bytes 1017344 | tf_op jit(solution)/shard_map/rkgtc,rckd->rtkgd/dot_general | solution.py:141
  68.0 1.5 %gather_fusion.2 = bf16[64,16,192]{2,1,0:T(8,128)(2,1)} fusion(bf16[8,16,192]{2,1,0:T(8,128)(2,1)S(1)} %reshape.228, s32[1024]{0:T(1024)} %pad_clamp_fusion.1), kind=kCustom, calls=%fused_computation.2 | custom fusion | bytes 786688 | tf_op jit(solution)/shard_map/jit(_take)/gather | solution.py:162
  69.5 6.4 %all-to-all-start.1 = ((bf16[64,16,192]{2,1,0:T(8,128)(2,1)}), bf16[64,16,192]{2,1,0:T(8,128)(2,1)}, u32[]{:S(2)}, u32[]{:S(2)}) async-start(bf16[64,16,192]{2,1,0:T(8,128)(2,1)} %gather_fusion.2), calls=%async_computation.1 | async-start | bytes 1048576 | tf_op jit(solution)/shard_map/all_to_all | solution.py:163
  76.9 1.7 %collective-permute-start.8 = (bf16[192,2048]{1,0:T(8,128)(2,1)}, bf16[192,2048]{1,0:T(8,128)(2,1)}, u32[]{:S(2)}, u32[]{:S(2)}) collective-permute-start(bf16[192,2048]{1,0:T(8,128)(2,1)} %param.23), channel_id=1, source_target_pairs={{0,3},{1,0},{2,1},{3,2},{4,7},{5,4},{6,5},{7,6},{8,11},{9,8},{10,9... | collective-permute-start | bytes 2359304 | tf_op jit(solution)/shard_map/ppermute | solution.py:29
  79.7 13.4 %all-to-all-done.1 = bf16[64,16,192]{2,1,0:T(8,128)(2,1)} async-done(((bf16[64,16,192]{2,1,0:T(8,128)(2,1)}), bf16[64,16,192]{2,1,0:T(8,128)(2,1)}, u32[]{:S(2)}, u32[]{:S(2)}) %all-to-all-start.1) | async-done | bytes 393248 | tf_op jit(solution)/shard_map/all_to_all | solution.py:163
  93.1 1.6 %gather_fusion.3 = bf16[8,16,192]{2,1,0:T(8,128)(2,1)S(1)} fusion(bf16[64,16,192]{2,1,0:T(8,128)(2,1)} %all-to-all-done.1, s32[1024]{0:T(1024)S(1)} %pad_clamp_fusion), kind=kCustom, calls=%fused_computation.3 | custom fusion | bytes 98336 | tf_op jit(solution)/shard_map/jit(_take)/gather | solution.py:164
  97.1 1.8 %collective-permute-start.7 = (bf16[128,192]{1,0:T(8,128)(2,1)S(1)}, bf16[128,192]{1,0:T(8,128)(2,1)S(1)}, u32[]{:S(2)}, u32[]{:S(2)}) collective-permute-start(bf16[128,192]{1,0:T(8,128)(2,1)S(1)} %bitcast.117), channel_id=1, source_target_pairs={{0,3},{1,0},{2,1},{3,2},{4,7},{5,4},{6,5},{7,6},{8,11},{9,8},{10,9... | collective-permute-start | bytes 147464 | tf_op jit(solution)/shard_map/ppermute | solution.py:29
  100.0 16.2 %collective-permute-done.3 = bf16[128,192]{1,0:T(8,128)(2,1)S(1)} collective-permute-done((bf16[128,192]{1,0:T(8,128)(2,1)S(1)}, bf16[128,192]{1,0:T(8,128)(2,1)S(1)}, u32[]{:S(2)}, u32[]{:S(2)}) %collective-permute-start.3) | collective-permute-done | bytes 49184 | tf_op jit(solution)/shard_map/ppermute | solution.py:29
  116.2 1.4 %fusion.6 = f32[128,2048]{1,0:T(8,128)S(1)} fusion(f32[128,2048]{1,0:T(8,128)S(1)} %fusion.7, bf16[128,192]{1,0:T(8,128)(2,1)S(1)} %collective-permute-done.3, bf16[192,2048]{1,0:T(8,128)(2,1)} %collective-permute-done.4), kind=kOutput, calls=%fused_computation.13 | convolution fusion | flops 101449728 | bytes 2932736 | tf_op jit(solution)/shard_map/dot_general | solution.py:169
  117.7 1.4 %fusion = f32[128,2048]{1,0:T(8,128)S(1)} fusion(bf16[128,192]{1,0:T(8,128)(2,1)S(1)} %collective-permute-done.7, bf16[192,2048]{1,0:T(8,128)(2,1)} %collective-permute-done.8), kind=kOutput, calls=%fused_computation.5 | convolution fusion | flops 101187584 | bytes 1884160 | tf_op jit(solution)/shard_map/dot_general | solution.py:169
  119.1 1.7 %multiply_reduce_fusion = (f32[128]{0:T(128)S(1)}, f32[128,2048]{1,0:T(8,128)S(1)}) fusion(f32[128,2048]{1,0:T(8,128)S(1)} %fusion, f32[128,2048]{1,0:T(8,128)S(1)} %fusion.6, bf16[128,192]{1,0:T(8,128)(2,1)S(1)} %collective-permute-done.5, bf16[192,2048]{1,0:T(8,128)(2,1)} %collective-permute-done.6, ...), kind=kOutput, calls=%fused_computation.49 | convolution fusion | flops 102760320 | bytes 4506112 | tf_op jit(solution)/shard_map/dot_general | solution.py:169
  126.4 1.9 %collective-permute-start.11 = (bf16[128,512]{1,0:T(8,128)(2,1)S(1)}, bf16[128,512]{1,0:T(8,128)(2,1)}, u32[]{:S(2)}, u32[]{:S(2)}) collective-permute-start(bf16[128,512]{1,0:T(8,128)(2,1)S(1)} %convolution_convert_fusion.4), channel_id=1, source_target_pairs={{0,3},{1,0},{2,1},{3,2},{4,7},{5,4},{6,5},{7,6},{8,11},{9,8},{10,9... | collective-permute-start | bytes 393224 | tf_op jit(solution)/shard_map/ppermute | solution.py:29
  130.2 3.7 %collective-permute-done.9 = bf16[128,512]{1,0:T(8,128)(2,1)} collective-permute-done((bf16[128,512]{1,0:T(8,128)(2,1)S(1)}, bf16[128,512]{1,0:T(8,128)(2,1)}, u32[]{:S(2)}, u32[]{:S(2)}) %collective-permute-start.9) | collective-permute-done | bytes 131104 | tf_op jit(solution)/shard_map/ppermute | solution.py:29
  133.9 2.0 %add_convert_fusion = bf16[128,512]{1,0:T(8,128)(2,1)} fusion(bf16[128,512]{1,0:T(8,128)(2,1)} %collective-permute-done.11, bf16[128,512]{1,0:T(8,128)(2,1)S(1)} %collective-permute-done.10, bf16[128,512]{1,0:T(8,128)(2,1)} %collective-permute-done.9, f32[128,2048]{1,0:T(8,128)} %copy-done.1, s32[]{:T(128)S(6)} %select_n.120, ...), kind=kOutput, calls=%fused_computation.60 | convolution fusion | flops 84541440 | bytes 1606656 | tf_op jit(solution)/shard_map/dot_general | solution.py:184
  (91 shorter events, 24.7 us)
Async XLA Ops:
  0.6 123.1 %copy-start = (bf16[640,2048]{1,0:T(8,128)(2,1)S(1)}, bf16[640,2048]{1,0:T(8,128)(2,1)}, u32[]{:S(2)}) copy-start(bf16[640,2048]{1,0:T(8,128)(2,1)} %param.27) | copy-start | bytes 7864324
  0.6 12.5 %copy-start.13 = (f32[2048]{0:T(1024)S(1)}, f32[2048]{0:T(1024)}, u32[]{:S(2)}) copy-start(f32[2048]{0:T(1024)} %param.20) | copy-start | bytes 24580
  0.7 9.6 %collective-permute-start = (bf16[128,512]{1,0:T(8,128)(2,1)}, bf16[128,512]{1,0:T(8,128)(2,1)S(1)}, u32[]{:S(2)}, u32[]{:S(2)}) collective-permute-start(bf16[128,512]{1,0:T(8,128)(2,1)} %bitcast.119), channel_id=1, source_target_pairs={{0,1},{1,2},{2,3},{3,0},{4,5},{5,6},{6,7},{7,4},{8,9},{9,10},{10,1... | collective-permute-start | bytes 393224 | tf_op jit(solution)/shard_map/ppermute | solution.py:29
  2.8 8.6 %collective-permute-start.1 = (bf16[128,512]{1,0:T(8,128)(2,1)}, bf16[128,512]{1,0:T(8,128)(2,1)S(1)}, u32[]{:S(2)}, u32[]{:S(2)}) collective-permute-start(bf16[128,512]{1,0:T(8,128)(2,1)} %bitcast.120), channel_id=1, source_target_pairs={{0,2},{1,3},{2,0},{3,1},{4,6},{5,7},{6,4},{7,5},{8,10},{9,11},{10,... | collective-permute-start | bytes 393224 | tf_op jit(solution)/shard_map/ppermute | solution.py:29
  5.5 6.0 %collective-permute-start.2 = (bf16[128,512]{1,0:T(8,128)(2,1)}, bf16[128,512]{1,0:T(8,128)(2,1)S(1)}, u32[]{:S(2)}, u32[]{:S(2)}) collective-permute-start(bf16[128,512]{1,0:T(8,128)(2,1)} %bitcast.121), channel_id=1, source_target_pairs={{0,3},{1,0},{2,1},{3,2},{4,7},{5,4},{6,5},{7,6},{8,11},{9,8},{10,9... | collective-permute-start | bytes 393224 | tf_op jit(solution)/shard_map/ppermute | solution.py:29
  14.7 15.0 %copy-start.5 = (s32[8,16]{1,0:T(8,128)S(1)}, s32[8,16]{1,0:T(8,128)}, u32[]{:S(2)}) copy-start(s32[8,16]{1,0:T(8,128)} %param.17) | copy-start | bytes 1540
  14.8 16.0 %copy-start.9 = (s32[8]{0:T(128)S(1)}, s32[8]{0:T(128)}, u32[]{:S(2)}) copy-start(s32[8]{0:T(128)} %copy-done.8) | copy-start | bytes 100
  14.8 16.0 %copy-start.11 = (s32[8]{0:T(128)S(1)}, s32[8]{0:T(128)}, u32[]{:S(2)}) copy-start(s32[8]{0:T(128)} %get-tuple-element.16) | copy-start | bytes 100
  14.8 16.7 %copy-start.10 = (s32[8]{0:T(128)S(1)}, s32[8]{0:T(128)}, u32[]{:S(2)}) copy-start(s32[8]{0:T(128)} %param.16) | copy-start | bytes 100
  16.6 41.6 %all-to-all-start = ((bf16[64,16,512]{2,1,0:T(8,128)(2,1)}), bf16[64,16,512]{2,1,0:T(8,128)(2,1)}, u32[]{:S(2)}, u32[]{:S(2)}) async-start(bf16[64,16,512]{2,1,0:T(8,128)(2,1)} %gather_fusion), calls=%async_computation | async-start | bytes 2097152 | tf_op jit(solution)/shard_map/all_to_all | solution.py:109
  62.4 5.1 %copy-start.3 = (bf16[8,16,1,128]{3,1,0,2:T(8,128)(2,1)S(1)}, bf16[8,16,1,128]{3,1,0,2:T(8,128)(2,1)}, u32[]{:S(2)}) copy-start(bf16[8,16,1,128]{3,1,0,2:T(8,128)(2,1)} %slice_bitcast_fusion.4) | copy-start | bytes 98308
  65.7 14.0 %copy-start.7 = (s32[8]{0:T(128)S(1)}, s32[8]{0:T(128)}, u32[]{:S(2)}) copy-start(s32[8]{0:T(128)} %copy-done.6) | copy-start | bytes 100
  69.5 23.6 %all-to-all-start.1 = ((bf16[64,16,192]{2,1,0:T(8,128)(2,1)}), bf16[64,16,192]{2,1,0:T(8,128)(2,1)}, u32[]{:S(2)}, u32[]{:S(2)}) async-start(bf16[64,16,192]{2,1,0:T(8,128)(2,1)} %gather_fusion.2), calls=%async_computation.1 | async-start | bytes 1048576 | tf_op jit(solution)/shard_map/all_to_all | solution.py:163
  75.9 23.1 %collective-permute-start.4 = (bf16[192,2048]{1,0:T(8,128)(2,1)}, bf16[192,2048]{1,0:T(8,128)(2,1)}, u32[]{:S(2)}, u32[]{:S(2)}) collective-permute-start(bf16[192,2048]{1,0:T(8,128)(2,1)} %param.23), channel_id=1, source_target_pairs={{0,1},{1,2},{2,3},{3,0},{4,5},{5,6},{6,7},{7,4},{8,9},{9,10},{10,1... | collective-permute-start | bytes 2359304 | tf_op jit(solution)/shard_map/ppermute | solution.py:29
  76.9 40.8 %collective-permute-start.8 = (bf16[192,2048]{1,0:T(8,128)(2,1)}, bf16[192,2048]{1,0:T(8,128)(2,1)}, u32[]{:S(2)}, u32[]{:S(2)}) collective-permute-start(bf16[192,2048]{1,0:T(8,128)(2,1)} %param.23), channel_id=1, source_target_pairs={{0,3},{1,0},{2,1},{3,2},{4,7},{5,4},{6,5},{7,6},{8,11},{9,8},{10,9... | collective-permute-start | bytes 2359304 | tf_op jit(solution)/shard_map/ppermute | solution.py:29
  78.6 40.5 %collective-permute-start.6 = (bf16[192,2048]{1,0:T(8,128)(2,1)}, bf16[192,2048]{1,0:T(8,128)(2,1)}, u32[]{:S(2)}, u32[]{:S(2)}) collective-permute-start(bf16[192,2048]{1,0:T(8,128)(2,1)} %param.23), channel_id=1, source_target_pairs={{0,2},{1,3},{2,0},{3,1},{4,6},{5,7},{6,4},{7,5},{8,10},{9,11},{10,... | collective-permute-start | bytes 2359304 | tf_op jit(solution)/shard_map/ppermute | solution.py:29
  94.7 21.5 %collective-permute-start.3 = (bf16[128,192]{1,0:T(8,128)(2,1)S(1)}, bf16[128,192]{1,0:T(8,128)(2,1)S(1)}, u32[]{:S(2)}, u32[]{:S(2)}) collective-permute-start(bf16[128,192]{1,0:T(8,128)(2,1)S(1)} %bitcast.115), channel_id=1, source_target_pairs={{0,1},{1,2},{2,3},{3,0},{4,5},{5,6},{6,7},{7,4},{8,9},{9,10},{10,1... | collective-permute-start | bytes 147464 | tf_op jit(solution)/shard_map/ppermute | solution.py:29
  97.1 20.5 %collective-permute-start.7 = (bf16[128,192]{1,0:T(8,128)(2,1)S(1)}, bf16[128,192]{1,0:T(8,128)(2,1)S(1)}, u32[]{:S(2)}, u32[]{:S(2)}) collective-permute-start(bf16[128,192]{1,0:T(8,128)(2,1)S(1)} %bitcast.117), channel_id=1, source_target_pairs={{0,3},{1,0},{2,1},{3,2},{4,7},{5,4},{6,5},{7,6},{8,11},{9,8},{10,9... | collective-permute-start | bytes 147464 | tf_op jit(solution)/shard_map/ppermute | solution.py:29
  98.9 20.2 %collective-permute-start.5 = (bf16[128,192]{1,0:T(8,128)(2,1)S(1)}, bf16[128,192]{1,0:T(8,128)(2,1)S(1)}, u32[]{:S(2)}, u32[]{:S(2)}) collective-permute-start(bf16[128,192]{1,0:T(8,128)(2,1)S(1)} %bitcast.118), channel_id=1, source_target_pairs={{0,2},{1,3},{2,0},{3,1},{4,6},{5,7},{6,4},{7,5},{8,10},{9,11},{10,... | collective-permute-start | bytes 147464 | tf_op jit(solution)/shard_map/ppermute | solution.py:29
  120.9 2.8 %copy-start.1 = (f32[128,2048]{1,0:T(8,128)}, f32[128,2048]{1,0:T(8,128)S(1)}, u32[]{:S(2)}) copy-start(f32[128,2048]{1,0:T(8,128)S(1)} %get-tuple-element.15) | copy-start | bytes 3145732
  123.0 5.3 %copy-start.14 = (s32[8,8]{1,0:T(8,128)S(1)}, s32[8,8]{1,0:T(8,128)}, u32[]{:S(2)}) copy-start(s32[8,8]{1,0:T(8,128)} %param.18) | copy-start | bytes 772
  124.0 6.2 %collective-permute-start.10 = (bf16[128,512]{1,0:T(8,128)(2,1)S(1)}, bf16[128,512]{1,0:T(8,128)(2,1)S(1)}, u32[]{:S(2)}, u32[]{:S(2)}) collective-permute-start(bf16[128,512]{1,0:T(8,128)(2,1)S(1)} %convolution_convert_fusion.5), channel_id=1, source_target_pairs={{0,2},{1,3},{2,0},{3,1},{4,6},{5,7},{6,4},{7,5},{8,10},{9,11},{10,... | collective-permute-start | bytes 393224 | tf_op jit(solution)/shard_map/ppermute | solution.py:29
  125.2 8.7 %collective-permute-start.9 = (bf16[128,512]{1,0:T(8,128)(2,1)S(1)}, bf16[128,512]{1,0:T(8,128)(2,1)}, u32[]{:S(2)}, u32[]{:S(2)}) collective-permute-start(bf16[128,512]{1,0:T(8,128)(2,1)S(1)} %convolution_convert_fusion.6), channel_id=1, source_target_pairs={{0,1},{1,2},{2,3},{3,0},{4,5},{5,6},{6,7},{7,4},{8,9},{9,10},{10,1... | collective-permute-start | bytes 393224 | tf_op jit(solution)/shard_map/ppermute | solution.py:29
  126.4 7.4 %collective-permute-start.11 = (bf16[128,512]{1,0:T(8,128)(2,1)S(1)}, bf16[128,512]{1,0:T(8,128)(2,1)}, u32[]{:S(2)}, u32[]{:S(2)}) collective-permute-start(bf16[128,512]{1,0:T(8,128)(2,1)S(1)} %convolution_convert_fusion.4), channel_id=1, source_target_pairs={{0,3},{1,0},{2,1},{3,2},{4,7},{5,4},{6,5},{7,6},{8,11},{9,8},{10,9... | collective-permute-start | bytes 393224 | tf_op jit(solution)/shard_map/ppermute | solution.py:29
  (5 other events, 8.4 us)

commit v11 on v9

--- a/solution.py
+++ b/solution.py
@@ -108,10 +108,11 @@
     outgoing = jnp.take(payload, send_pick, axis=0, mode="clip")
     incoming = lax.all_to_all(outgoing, "req", 0, 0, tiled=True)
     local_rows = jnp.take(incoming, source_of, axis=0, mode="clip")
-    query_rows = (
-        local_rows[..., :query_width].astype(jnp.float32)
-        + local_rows[..., query_width : 2 * query_width].astype(jnp.float32)
-    ).reshape(per_owner_rows, tokens, kv_heads, group_heads, HEAD_DIM)
+    head_shape = (per_owner_rows, tokens, kv_heads, group_heads, HEAD_DIM)
+    query_parts = (
+        local_rows[..., :query_width].reshape(head_shape),
+        local_rows[..., query_width : 2 * query_width].reshape(head_shape),
+    )
     new_key_value = local_rows[..., 2 * query_width :].reshape(
         per_owner_rows, tokens, kv_heads, 2 * HEAD_DIM
     )
@@ -123,16 +124,18 @@
     ).astype(jnp.bfloat16)
 
     score_scale = 1.0 / math.sqrt(HEAD_DIM)
-    draft_keys = new_key_value[..., :HEAD_DIM].astype(jnp.float32)
-    draft_scores = (
-        jnp.einsum("rtkgd,rjkd->rkgtj", query_rows, draft_keys, precision=HIGH) * score_scale
-    )
+
+    def query_times(keys, spec):
+        high, low = (
+            jnp.einsum(spec, part, keys, preferred_element_type=jnp.float32)
+            for part in query_parts
+        )
+        return (high + low) * score_scale
+
+    draft_scores = query_times(new_key_value[..., :HEAD_DIM], "rtkgd,rjkd->rkgtj")
     draft_scores = jnp.where(ancestry(parents, tokens)[:, None, None], draft_scores, -jnp.inf)
     draft_top = jnp.max(draft_scores, axis=-1)
-    cache_keys = cached_key_value[..., :HEAD_DIM].astype(jnp.float32)
-    scores = (
-        jnp.einsum("rtkgd,rckd->rkgtc", query_rows, cache_keys, precision=HIGH) * score_scale
-    )
+    scores = query_times(cached_key_value[..., :HEAD_DIM], "rtkgd,rckd->rkgtc")
     live_rows = jnp.arange(cached_key_value.shape[1])[None, :] < lengths[:, None]
     scores = jnp.where(live_rows[:, None, None, None, :], scores, -jnp.inf)
     row_top = jnp.maximum(draft_top, jnp.max(scores, axis=-1))
@@ -176,6 +179,7 @@
     gate_out = jnp.dot(normed_two, w_gate, preferred_element_type=jnp.float32)
     up_out = jnp.dot(normed_two, w_up, preferred_element_type=jnp.float32)
     hidden = (jax.nn.silu(gate_out) * up_out).astype(jnp.bfloat16)
+
     def unit_block(target):
         columns = lax.dynamic_slice_in_dim(w_down, target * quarter, quarter, 1)
         return jnp.dot(hidden, columns, preferred_element_type=jnp.float32).astype(jnp.bfloat16)

time: 135 us -> 136 us (level)
    dot_general x2 -> x4, matrix products: 3.24 us -> 4.92 us  [query_times(): jnp.einsum(spec, part, keys, preferred_element_type=jnp.float32)]
where the time goes in v11:
time: 136 us; the launch traced here: 134 us
  waiting for transfers between devices  61.1 us (45%)
  starting transfers between devices  36.9 us (27%)
  matrix products  18.1 us (13%)
  local copies, waits for them, and re-layouts  12.7 us (9%)
  other arithmetic  4.09 us (3%)
    all_to_all x1, waiting for transfers between devices, per_device(): incoming = lax.all_to_all(outgoing, 'req', 0, 0, tiled=True)  26 us
    ppermute x12, waiting for transfers between devices, shift_mlp(): lax.ppermute(value, 'mlp', [(i, (i + shift) % count) for i in range(count)])  21.1 us
    ppermute x12, starting transfers between devices, shift_mlp(): lax.ppermute(value, 'mlp', [(i, (i + shift) % count) for i in range(count)])  17.3 us
    all_to_all x1, waiting for transfers between devices, per_device(): arrived = lax.all_to_all(returning, 'req', 0, 0, tiled=True)  14 us
    all_to_all x1, starting transfers between devices, per_device(): incoming = lax.all_to_all(outgoing, 'req', 0, 0, tiled=True)  13.2 us
    all_to_all x1, starting transfers between devices, per_device(): arrived = lax.all_to_all(returning, 'req', 0, 0, tiled=True)  6.39 us
    dot_general x4, matrix products, query_times(): jnp.einsum(spec, part, keys, preferred_element_type=jnp.float32)  4.92 us
    dot_general x4, matrix products, per_device(): jnp.dot(piece, rows_of_group, preferred_element_type=jnp.float32)  4.77 us
  transfers between devices with their start and end apart: 14, of which 8 were waited for; matrix products, arithmetic and copies ran while one was open for 8% of the time, Pallas kernels for 0%

profile of v11, /device:TPU:1, one launch (start us, length us, event | category | flops | bytes accessed | tf_op | source)
XLA Modules:
  0.0 134.1 jit_solution(15256064388912468165)
XLA Ops:
  0.7 2.2 %collective-permute-start = (bf16[128,512]{1,0:T(8,128)(2,1)}, bf16[128,512]{1,0:T(8,128)(2,1)S(1)}, u32[]{:S(2)}, u32[]{:S(2)}) collective-permute-start(bf16[128,512]{1,0:T(8,128)(2,1)} %bitcast.123), channel_id=1, source_target_pairs={{0,1},{1,2},{2,3},{3,0},{4,5},{5,6},{6,7},{7,4},{8,9},{9,10},{10,1... | collective-permute-start | bytes 393224 | tf_op jit(solution)/shard_map/ppermute | solution.py:29
  2.8 2.6 %collective-permute-start.1 = (bf16[128,512]{1,0:T(8,128)(2,1)}, bf16[128,512]{1,0:T(8,128)(2,1)S(1)}, u32[]{:S(2)}, u32[]{:S(2)}) collective-permute-start(bf16[128,512]{1,0:T(8,128)(2,1)} %bitcast.124), channel_id=1, source_target_pairs={{0,2},{1,3},{2,0},{3,1},{4,6},{5,7},{6,4},{7,5},{8,10},{9,11},{10,... | collective-permute-start | bytes 393224 | tf_op jit(solution)/shard_map/ppermute | solution.py:29
  11.7 1.6 %subtract_convert_fusion = (bf16[128,192]{0,1:T(8,128)(2,1)S(1)}, bf16[128,192]{0,1:T(8,128)(2,1)S(1)}) fusion(bf16[2048,192]{0,1:T(8,128)(2,1)} %param.21, bf16[128,2048]{1,0:T(8,128)(2,1)S(1)} %constant_dynamic-update-slice_fusion, f32[2048]{0:T(1024)} %param.20, f32[128]{0:T(128)S(1)} %add_rsqrt_fusion.1), kind=kOutput, calls=%fused_computation.72 | convolution fusion | flops 101810176 | bytes 1417728 | tf_op jit(solution)/shard_map/dot_general | solution.py:98
  13.9 1.6 %gather_fusion = bf16[64,16,512]{2,1,0:T(8,128)(2,1)} fusion(bf16[8,16,512]{2,1,0:T(8,128)(2,1)S(1)} %bitcast.118, s32[1024]{0:T(1024)S(1)} %pad_clamp_fusion.3), kind=kCustom, calls=%fused_computation | custom fusion | bytes 2097408 | tf_op jit(solution)/shard_map/jit(_take)/gather | solution.py:108
  15.5 13.2 %all-to-all-start = ((bf16[64,16,512]{2,1,0:T(8,128)(2,1)}), bf16[64,16,512]{2,1,0:T(8,128)(2,1)}, u32[]{:S(2)}, u32[]{:S(2)}) async-start(bf16[64,16,512]{2,1,0:T(8,128)(2,1)} %gather_fusion), calls=%async_computation | async-start | bytes 2097152 | tf_op jit(solution)/shard_map/all_to_all | solution.py:109
  31.1 26.0 %all-to-all-done = bf16[64,16,512]{2,1,0:T(8,128)(2,1)} async-done(((bf16[64,16,512]{2,1,0:T(8,128)(2,1)}), bf16[64,16,512]{2,1,0:T(8,128)(2,1)}, u32[]{:S(2)}, u32[]{:S(2)}) %all-to-all-start) | async-done | bytes 1048608 | tf_op jit(solution)/shard_map/all_to_all | solution.py:109
  57.2 1.8 %gather_fusion.1 = bf16[8,16,512]{2,1,0:T(8,128)(2,1)S(1)} fusion(bf16[64,16,512]{2,1,0:T(8,128)(2,1)} %all-to-all-done, s32[1024]{0:T(1024)S(1)} %pad_clamp_fusion.2), kind=kCustom, calls=%fused_computation.1 | custom fusion | bytes 262176 | tf_op jit(solution)/shard_map/jit(_take)/gather | solution.py:110
  62.4 1.3 fusion.31
  64.8 1.4 %fusion.63 = (f32[8,3,16]{2,1,0:T(4,128)S(1)}, f32[8,1,3,16,256]{4,3,2,0,1:T(8,128)S(1)}) fusion(f32[8,16,3,256]{3,1,2,0:T(8,128)S(1)} %fusion.31, bf16[8,256,1,128]{3,1,2,0:T(8,128)(2,1)} %param.19, bf16[8,16,3,64]{3,2,1,0:T(4,128)(2,1)S(1)} %reshape.235, pred[8,256]{1,0:T(8,128)(4,1)} %iota_compare_fusion.5), kind=kOutput, calls=%fused_computation.130 | convolution fusion | flops 12975744 | bytes 1363456 | tf_op jit(solution)/shard_map/rtkgd,rckd->rkgtc/dot_general | solution.py:130
  67.6 1.5 %gather_fusion.2 = bf16[64,16,192]{2,1,0:T(8,128)(2,1)} fusion(bf16[8,16,192]{2,1,0:T(8,128)(2,1)S(1)} %reshape.242, s32[1024]{0:T(1024)} %pad_clamp_fusion.1), kind=kCustom, calls=%fused_computation.2 | custom fusion | bytes 786688 | tf_op jit(solution)/shard_map/jit(_take)/gather | solution.py:164
  69.1 6.4 %all-to-all-start.1 = ((bf16[64,16,192]{2,1,0:T(8,128)(2,1)}), bf16[64,16,192]{2,1,0:T(8,128)(2,1)}, u32[]{:S(2)}, u32[]{:S(2)}) async-start(bf16[64,16,192]{2,1,0:T(8,128)(2,1)} %gather_fusion.2), calls=%async_computation.1 | async-start | bytes 1048576 | tf_op jit(solution)/shard_map/all_to_all | solution.py:165
  75.5 1.9 %collective-permute-start.8 = (bf16[192,2048]{1,0:T(8,128)(2,1)}, bf16[192,2048]{1,0:T(8,128)(2,1)}, u32[]{:S(2)}, u32[]{:S(2)}) collective-permute-start(bf16[192,2048]{1,0:T(8,128)(2,1)} %param.23), channel_id=1, source_target_pairs={{0,3},{1,0},{2,1},{3,2},{4,7},{5,4},{6,5},{7,6},{8,11},{9,8},{10,9... | collective-permute-start | bytes 2359304 | tf_op jit(solution)/shard_map/ppermute | solution.py:29
  78.7 14.0 %all-to-all-done.1 = bf16[64,16,192]{2,1,0:T(8,128)(2,1)} async-done(((bf16[64,16,192]{2,1,0:T(8,128)(2,1)}), bf16[64,16,192]{2,1,0:T(8,128)(2,1)}, u32[]{:S(2)}, u32[]{:S(2)}) %all-to-all-start.1) | async-done | bytes 393248 | tf_op jit(solution)/shard_map/all_to_all | solution.py:165
  92.7 1.6 %gather_fusion.3 = bf16[8,16,192]{2,1,0:T(8,128)(2,1)S(1)} fusion(bf16[64,16,192]{2,1,0:T(8,128)(2,1)} %all-to-all-done.1, s32[1024]{0:T(1024)S(1)} %pad_clamp_fusion), kind=kCustom, calls=%fused_computation.3 | custom fusion | bytes 98336 | tf_op jit(solution)/shard_map/jit(_take)/gather | solution.py:166
  94.3 1.9 %collective-permute-start.7 = (bf16[128,192]{1,0:T(8,128)(2,1)S(1)}, bf16[128,192]{1,0:T(8,128)(2,1)S(1)}, u32[]{:S(2)}, u32[]{:S(2)}) collective-permute-start(bf16[128,192]{1,0:T(8,128)(2,1)S(1)} %bitcast.119), channel_id=1, source_target_pairs={{0,3},{1,0},{2,1},{3,2},{4,7},{5,4},{6,5},{7,6},{8,11},{9,8},{10,9... | collective-permute-start | bytes 147464 | tf_op jit(solution)/shard_map/ppermute | solution.py:29
  97.5 15.8 %collective-permute-done.7 = bf16[128,192]{1,0:T(8,128)(2,1)S(1)} collective-permute-done((bf16[128,192]{1,0:T(8,128)(2,1)S(1)}, bf16[128,192]{1,0:T(8,128)(2,1)S(1)}, u32[]{:S(2)}, u32[]{:S(2)}) %collective-permute-start.7) | collective-permute-done | bytes 49184 | tf_op jit(solution)/shard_map/ppermute | solution.py:29
  113.2 1.4 %fusion = f32[128,2048]{1,0:T(8,128)S(1)} fusion(bf16[128,192]{1,0:T(8,128)(2,1)S(1)} %collective-permute-done.7, bf16[192,2048]{1,0:T(8,128)(2,1)} %collective-permute-done.8), kind=kOutput, calls=%fused_computation.5 | convolution fusion | flops 101187584 | bytes 1884160 | tf_op jit(solution)/shard_map/dot_general | solution.py:172
  115.4 1.4 %fusion.1 = f32[128,2048]{1,0:T(8,128)S(1)} fusion(bf16[128,192]{1,0:T(8,128)(2,1)S(1)} %collective-permute-done.5, bf16[192,2048]{1,0:T(8,128)(2,1)} %collective-permute-done.6), kind=kOutput, calls=%fused_computation.7 | convolution fusion | flops 101187584 | bytes 1884160 | tf_op jit(solution)/shard_map/dot_general | solution.py:172
  117.0 1.4 %fusion.2 = f32[128,2048]{1,0:T(8,128)S(1)} fusion(bf16[128,192]{1,0:T(8,128)(2,1)S(1)} %collective-permute-done.3, bf16[192,2048]{1,0:T(8,128)(2,1)} %collective-permute-done.4), kind=kOutput, calls=%fused_computation.9 | convolution fusion | flops 101187584 | bytes 1884160 | tf_op jit(solution)/shard_map/dot_general | solution.py:172
  119.0 1.6 %copy-done.3 = bf16[2048,640]{1,0:T(8,128)(2,1)S(1)} copy-done((bf16[2048,640]{1,0:T(8,128)(2,1)S(1)}, bf16[2048,640]{1,0:T(8,128)(2,1)}, u32[]{:S(2)}) %copy-start.3) | copy-done | bytes 2621464
  122.3 2.2 %collective-permute-start.10 = (bf16[128,512]{1,0:T(8,128)(2,1)S(1)}, bf16[128,512]{1,0:T(8,128)(2,1)S(1)}, u32[]{:S(2)}, u32[]{:S(2)}) collective-permute-start(bf16[128,512]{1,0:T(8,128)(2,1)S(1)} %convolution_convert_fusion.5), channel_id=1, source_target_pairs={{0,2},{1,3},{2,0},{3,1},{4,6},{5,7},{6,4},{7,5},{8,10},{9,11},{10,... | collective-permute-start | bytes 393224 | tf_op jit(solution)/shard_map/ppermute | solution.py:29
  124.8 1.9 %collective-permute-start.9 = (bf16[128,512]{1,0:T(8,128)(2,1)S(1)}, bf16[128,512]{1,0:T(8,128)(2,1)}, u32[]{:S(2)}, u32[]{:S(2)}) collective-permute-start(bf16[128,512]{1,0:T(8,128)(2,1)S(1)} %convolution_convert_fusion.6), channel_id=1, source_target_pairs={{0,1},{1,2},{2,3},{3,0},{4,5},{5,6},{6,7},{7,4},{8,9},{9,10},{10,1... | collective-permute-start | bytes 393224 | tf_op jit(solution)/shard_map/ppermute | solution.py:29
  128.7 2.1 %collective-permute-done.9 = bf16[128,512]{1,0:T(8,128)(2,1)} collective-permute-done((bf16[128,512]{1,0:T(8,128)(2,1)S(1)}, bf16[128,512]{1,0:T(8,128)(2,1)}, u32[]{:S(2)}, u32[]{:S(2)}) %collective-permute-start.9) | collective-permute-done | bytes 131104 | tf_op jit(solution)/shard_map/ppermute | solution.py:29
  132.0 2.0 %add_convert_fusion = bf16[128,512]{1,0:T(8,128)(2,1)} fusion(bf16[128,512]{1,0:T(8,128)(2,1)} %collective-permute-done.11, bf16[128,512]{1,0:T(8,128)(2,1)S(1)} %collective-permute-done.10, bf16[128,512]{1,0:T(8,128)(2,1)} %collective-permute-done.9, f32[128,2048]{1,0:T(8,128)} %copy-done.1, s32[]{:T(128)S(6)} %select_n.120, ...), kind=kOutput, calls=%fused_computation.65 | convolution fusion | flops 84541440 | bytes 1606656 | tf_op jit(solution)/shard_map/dot_general | solution.py:185
  (100 shorter events, 23.8 us)
Async XLA Ops:
  0.6 121.4 %copy-start = (bf16[640,2048]{1,0:T(8,128)(2,1)S(1)}, bf16[640,2048]{1,0:T(8,128)(2,1)}, u32[]{:S(2)}) copy-start(bf16[640,2048]{1,0:T(8,128)(2,1)} %param.27) | copy-start | bytes 7864324
  0.6 12.6 %copy-start.16 = (f32[2048]{0:T(1024)S(1)}, f32[2048]{0:T(1024)}, u32[]{:S(2)}) copy-start(f32[2048]{0:T(1024)} %param.20) | copy-start | bytes 24580
  0.7 9.6 %collective-permute-start = (bf16[128,512]{1,0:T(8,128)(2,1)}, bf16[128,512]{1,0:T(8,128)(2,1)S(1)}, u32[]{:S(2)}, u32[]{:S(2)}) collective-permute-start(bf16[128,512]{1,0:T(8,128)(2,1)} %bitcast.123), channel_id=1, source_target_pairs={{0,1},{1,2},{2,3},{3,0},{4,5},{5,6},{6,7},{7,4},{8,9},{9,10},{10,1... | collective-permute-start | bytes 393224 | tf_op jit(solution)/shard_map/ppermute | solution.py:29
  2.8 8.6 %collective-permute-start.1 = (bf16[128,512]{1,0:T(8,128)(2,1)}, bf16[128,512]{1,0:T(8,128)(2,1)S(1)}, u32[]{:S(2)}, u32[]{:S(2)}) collective-permute-start(bf16[128,512]{1,0:T(8,128)(2,1)} %bitcast.124), channel_id=1, source_target_pairs={{0,2},{1,3},{2,0},{3,1},{4,6},{5,7},{6,4},{7,5},{8,10},{9,11},{10,... | collective-permute-start | bytes 393224 | tf_op jit(solution)/shard_map/ppermute | solution.py:29
  5.5 6.0 %collective-permute-start.2 = (bf16[128,512]{1,0:T(8,128)(2,1)}, bf16[128,512]{1,0:T(8,128)(2,1)S(1)}, u32[]{:S(2)}, u32[]{:S(2)}) collective-permute-start(bf16[128,512]{1,0:T(8,128)(2,1)} %bitcast.125), channel_id=1, source_target_pairs={{0,3},{1,0},{2,1},{3,2},{4,7},{5,4},{6,5},{7,6},{8,11},{9,8},{10,9... | collective-permute-start | bytes 393224 | tf_op jit(solution)/shard_map/ppermute | solution.py:29
  13.7 15.0 %copy-start.7 = (s32[8,16]{1,0:T(8,128)S(1)}, s32[8,16]{1,0:T(8,128)}, u32[]{:S(2)}) copy-start(s32[8,16]{1,0:T(8,128)} %param.17) | copy-start | bytes 1540
  13.7 16.0 %copy-start.11 = (s32[8]{0:T(128)S(1)}, s32[8]{0:T(128)}, u32[]{:S(2)}) copy-start(s32[8]{0:T(128)} %copy-done.10) | copy-start | bytes 100
  13.7 16.0 %copy-start.13 = (s32[8]{0:T(128)S(1)}, s32[8]{0:T(128)}, u32[]{:S(2)}) copy-start(s32[8]{0:T(128)} %get-tuple-element.18) | copy-start | bytes 100
  13.7 16.7 %copy-start.12 = (s32[8]{0:T(128)S(1)}, s32[8]{0:T(128)}, u32[]{:S(2)}) copy-start(s32[8]{0:T(128)} %param.16) | copy-start | bytes 100
  15.5 41.7 %all-to-all-start = ((bf16[64,16,512]{2,1,0:T(8,128)(2,1)}), bf16[64,16,512]{2,1,0:T(8,128)(2,1)}, u32[]{:S(2)}, u32[]{:S(2)}) async-start(bf16[64,16,512]{2,1,0:T(8,128)(2,1)} %gather_fusion), calls=%async_computation | async-start | bytes 2097152 | tf_op jit(solution)/shard_map/all_to_all | solution.py:109
  61.3 5.7 %copy-start.5 = (bf16[8,16,1,128]{3,1,0,2:T(8,128)(2,1)S(1)}, bf16[8,16,1,128]{3,1,0,2:T(8,128)(2,1)}, u32[]{:S(2)}) copy-start(bf16[8,16,1,128]{3,1,0,2:T(8,128)(2,1)} %slice_bitcast_fusion.5) | copy-start | bytes 98308
  66.3 12.4 %copy-start.9 = (s32[8]{0:T(128)S(1)}, s32[8]{0:T(128)}, u32[]{:S(2)}) copy-start(s32[8]{0:T(128)} %copy-done.8) | copy-start | bytes 100
  69.1 23.6 %all-to-all-start.1 = ((bf16[64,16,192]{2,1,0:T(8,128)(2,1)}), bf16[64,16,192]{2,1,0:T(8,128)(2,1)}, u32[]{:S(2)}, u32[]{:S(2)}) async-start(bf16[64,16,192]{2,1,0:T(8,128)(2,1)} %gather_fusion.2), calls=%async_computation.1 | async-start | bytes 1048576 | tf_op jit(solution)/shard_map/all_to_all | solution.py:165
  75.5 21.6 %collective-permute-start.8 = (bf16[192,2048]{1,0:T(8,128)(2,1)}, bf16[192,2048]{1,0:T(8,128)(2,1)}, u32[]{:S(2)}, u32[]{:S(2)}) collective-permute-start(bf16[192,2048]{1,0:T(8,128)(2,1)} %param.23), channel_id=1, source_target_pairs={{0,3},{1,0},{2,1},{3,2},{4,7},{5,4},{6,5},{7,6},{8,11},{9,8},{10,9... | collective-permute-start | bytes 2359304 | tf_op jit(solution)/shard_map/ppermute | solution.py:29
  77.4 37.3 %collective-permute-start.6 = (bf16[192,2048]{1,0:T(8,128)(2,1)}, bf16[192,2048]{1,0:T(8,128)(2,1)}, u32[]{:S(2)}, u32[]{:S(2)}) collective-permute-start(bf16[192,2048]{1,0:T(8,128)(2,1)} %param.23), channel_id=1, source_target_pairs={{0,2},{1,3},{2,0},{3,1},{4,6},{5,7},{6,4},{7,5},{8,10},{9,11},{10,... | collective-permute-start | bytes 2359304 | tf_op jit(solution)/shard_map/ppermute | solution.py:29
  78.2 38.6 %collective-permute-start.4 = (bf16[192,2048]{1,0:T(8,128)(2,1)}, bf16[192,2048]{1,0:T(8,128)(2,1)}, u32[]{:S(2)}, u32[]{:S(2)}) collective-permute-start(bf16[192,2048]{1,0:T(8,128)(2,1)} %param.23), channel_id=1, source_target_pairs={{0,1},{1,2},{2,3},{3,0},{4,5},{5,6},{6,7},{7,4},{8,9},{9,10},{10,1... | collective-permute-start | bytes 2359304 | tf_op jit(solution)/shard_map/ppermute | solution.py:29
  94.3 19.0 %collective-permute-start.7 = (bf16[128,192]{1,0:T(8,128)(2,1)S(1)}, bf16[128,192]{1,0:T(8,128)(2,1)S(1)}, u32[]{:S(2)}, u32[]{:S(2)}) collective-permute-start(bf16[128,192]{1,0:T(8,128)(2,1)S(1)} %bitcast.119), channel_id=1, source_target_pairs={{0,3},{1,0},{2,1},{3,2},{4,7},{5,4},{6,5},{7,6},{8,11},{9,8},{10,9... | collective-permute-start | bytes 147464 | tf_op jit(solution)/shard_map/ppermute | solution.py:29
  96.2 22.3 %copy-start.4 = (bf16[192,2048]{1,0:T(8,128)(2,1)S(1)}, bf16[192,2048]{1,0:T(8,128)(2,1)}, u32[]{:S(2)}) copy-start(bf16[192,2048]{1,0:T(8,128)(2,1)} %param.23) | copy-start | bytes 2359300
  96.2 19.2 %collective-permute-start.5 = (bf16[128,192]{1,0:T(8,128)(2,1)S(1)}, bf16[128,192]{1,0:T(8,128)(2,1)S(1)}, u32[]{:S(2)}, u32[]{:S(2)}) collective-permute-start(bf16[128,192]{1,0:T(8,128)(2,1)S(1)} %bitcast.120), channel_id=1, source_target_pairs={{0,2},{1,3},{2,0},{3,1},{4,6},{5,7},{6,4},{7,5},{8,10},{9,11},{10,... | collective-permute-start | bytes 147464 | tf_op jit(solution)/shard_map/ppermute | solution.py:29
  97.0 20.0 %collective-permute-start.3 = (bf16[128,192]{1,0:T(8,128)(2,1)S(1)}, bf16[128,192]{1,0:T(8,128)(2,1)S(1)}, u32[]{:S(2)}, u32[]{:S(2)}) collective-permute-start(bf16[128,192]{1,0:T(8,128)(2,1)S(1)} %bitcast.121), channel_id=1, source_target_pairs={{0,1},{1,2},{2,3},{3,0},{4,5},{5,6},{6,7},{7,4},{8,9},{9,10},{10,1... | collective-permute-start | bytes 147464 | tf_op jit(solution)/shard_map/ppermute | solution.py:29
  121.4 6.5 %copy-start.17 = (s32[8,8]{1,0:T(8,128)S(1)}, s32[8,8]{1,0:T(8,128)}, u32[]{:S(2)}) copy-start(s32[8,8]{1,0:T(8,128)} %param.18) | copy-start | bytes 772
  122.3 6.4 %collective-permute-start.10 = (bf16[128,512]{1,0:T(8,128)(2,1)S(1)}, bf16[128,512]{1,0:T(8,128)(2,1)S(1)}, u32[]{:S(2)}, u32[]{:S(2)}) collective-permute-start(bf16[128,512]{1,0:T(8,128)(2,1)S(1)} %convolution_convert_fusion.5), channel_id=1, source_target_pairs={{0,2},{1,3},{2,0},{3,1},{4,6},{5,7},{6,4},{7,5},{8,10},{9,11},{10,... | collective-permute-start | bytes 393224 | tf_op jit(solution)/shard_map/ppermute | solution.py:29
  124.8 6.0 %collective-permute-start.9 = (bf16[128,512]{1,0:T(8,128)(2,1)S(1)}, bf16[128,512]{1,0:T(8,128)(2,1)}, u32[]{:S(2)}, u32[]{:S(2)}) collective-permute-start(bf16[128,512]{1,0:T(8,128)(2,1)S(1)} %convolution_convert_fusion.6), channel_id=1, source_target_pairs={{0,1},{1,2},{2,3},{3,0},{4,5},{5,6},{6,7},{7,4},{8,9},{9,10},{10,1... | collective-permute-start | bytes 393224 | tf_op jit(solution)/shard_map/ppermute | solution.py:29
  127.0 5.0 %collective-permute-start.11 = (bf16[128,512]{1,0:T(8,128)(2,1)S(1)}, bf16[128,512]{1,0:T(8,128)(2,1)}, u32[]{:S(2)}, u32[]{:S(2)}) collective-permute-start(bf16[128,512]{1,0:T(8,128)(2,1)S(1)} %convolution_convert_fusion.4), channel_id=1, source_target_pairs={{0,3},{1,0},{2,1},{3,2},{4,7},{5,4},{6,5},{7,6},{8,11},{9,8},{10,9... | collective-permute-start | bytes 393224 | tf_op jit(solution)/shard_map/ppermute | solution.py:29
  (8 other events, 20.3 us)

commit v12 on v9

--- a/solution.py
+++ b/solution.py
@@ -1,9 +1,13 @@
+import functools
 import math
 
 import jax
 import jax.numpy as jnp
 from jax import lax
 from jax.sharding import PartitionSpec as P
+
+from jax.experimental import pallas as pl
+from jax.experimental.pallas import tpu as pltpu
 
 
 HEAD_DIM = 64
@@ -40,6 +44,45 @@
         offset = ((part_index - k) % count) * width
         full = lax.dynamic_update_slice_in_dim(full, piece, offset, full.ndim - 1)
     return full
+
+
+def attend_kernel(source_ref, length_ref, row_ref, cache_ref, mask_ref, out_ref, *, widths):
+    query_width, group_heads = widths
+    slot = pl.program_id(0)
+    row = row_ref[0]
+    cache = cache_ref[0, :, 0, :]
+    keys_cache, values_cache = cache[:, :HEAD_DIM], cache[:, HEAD_DIM:]
+    fresh = row[:, 2 * query_width :]
+    keys_draft, values_draft = fresh[:, :HEAD_DIM], fresh[:, HEAD_DIM:]
+    live = lax.broadcasted_iota(jnp.int32, (1, cache.shape[0]), 1) < length_ref[slot]
+    visible = mask_ref[0] > 0.5
+    scale = 1.0 / math.sqrt(HEAD_DIM)
+    contract = (((1,), (1,)), ((), ()))
+
+    def times(part, keys):
+        return lax.dot_general(part, keys, contract, preferred_element_type=jnp.float32)
+
+    outs = []
+    for g in range(group_heads):
+        high = row[:, g * HEAD_DIM : (g + 1) * HEAD_DIM]
+        low = row[:, query_width + g * HEAD_DIM : query_width + (g + 1) * HEAD_DIM]
+        score_cache = (times(high, keys_cache) + times(low, keys_cache)) * scale
+        score_cache = jnp.where(live, score_cache, -jnp.inf)
+        score_draft = (times(high, keys_draft) + times(low, keys_draft)) * scale
+        score_draft = jnp.where(visible, score_draft, -jnp.inf)
+        top = jnp.maximum(
+            jnp.max(score_cache, axis=1, keepdims=True), jnp.max(score_draft, axis=1, keepdims=True)
+        )
+        weight_cache = jnp.exp(score_cache - top).astype(jnp.bfloat16)
+        weight_draft = jnp.exp(score_draft - top).astype(jnp.bfloat16)
+        numerator = jnp.dot(
+            weight_cache, values_cache, preferred_element_type=jnp.float32
+        ) + jnp.dot(weight_draft, values_draft, preferred_element_type=jnp.float32)
+        denominator = jnp.sum(weight_cache.astype(jnp.float32), axis=1, keepdims=True) + jnp.sum(
+            weight_draft.astype(jnp.float32), axis=1, keepdims=True
+        )
+        outs.append((numerator / denominator).astype(jnp.bfloat16))
+    out_ref[0] = jnp.concatenate(outs, axis=1)
 
 
 def per_device(
@@ -79,9 +122,6 @@
         jnp.where(slot_of[None, :] == owned_slots[:, None], requests[None, :], 0), axis=1
     )
     source_of = request_of // per_owner_rows
-    return_pick = jnp.sum(
-        jnp.where(source_of[None, :] == devices[:, None], local_ids[None, :], 0), axis=1
-    )
 
     rows = per_owner_rows * tokens
     owned_pieces = pieces_mlp(drafts.reshape(rows, quarter), mlp_count)
@@ -108,10 +148,6 @@
     outgoing = jnp.take(payload, send_pick, axis=0, mode="clip")
     incoming = lax.all_to_all(outgoing, "req", 0, 0, tiled=True)
     local_rows = jnp.take(incoming, source_of, axis=0, mode="clip")
-    query_rows = (
-        local_rows[..., :query_width].astype(jnp.float32)
-        + local_rows[..., query_width : 2 * query_width].astype(jnp.float32)
-    ).reshape(per_owner_rows, tokens, kv_heads, group_heads, HEAD_DIM)
     new_key_value = local_rows[..., 2 * query_width :].reshape(
         per_owner_rows, tokens, kv_heads, 2 * HEAD_DIM
     )
@@ -122,43 +158,25 @@
         "rat,rtkd->rakd", picker, new_key_value, preferred_element_type=jnp.float32
     ).astype(jnp.bfloat16)
 
-    score_scale = 1.0 / math.sqrt(HEAD_DIM)
-    draft_keys = new_key_value[..., :HEAD_DIM].astype(jnp.float32)
-    draft_scores = (
-        jnp.einsum("rtkgd,rjkd->rkgtj", query_rows, draft_keys, precision=HIGH) * score_scale
-    )
-    draft_scores = jnp.where(ancestry(parents, tokens)[:, None, None], draft_scores, -jnp.inf)
-    draft_top = jnp.max(draft_scores, axis=-1)
-    cache_keys = cached_key_value[..., :HEAD_DIM].astype(jnp.float32)
-    scores = (
-        jnp.einsum("rtkgd,rckd->rkgtc", query_rows, cache_keys, precision=HIGH) * score_scale
-    )
-    live_rows = jnp.arange(cached_key_value.shape[1])[None, :] < lengths[:, None]
-    scores = jnp.where(live_rows[:, None, None, None, :], scores, -jnp.inf)
-    row_top = jnp.maximum(draft_top, jnp.max(scores, axis=-1))
-    weights = jnp.exp(scores - row_top[..., None]).astype(jnp.bfloat16)
-    numerator = jnp.einsum(
-        "rkgtc,rckd->rtkgd",
-        weights,
-        cached_key_value[..., HEAD_DIM:],
-        preferred_element_type=jnp.float32,
-    )
-    denominator = jnp.sum(weights.astype(jnp.float32), axis=-1)
-    draft_weights = jnp.exp(draft_scores - row_top[..., None]).astype(jnp.bfloat16)
-    numerator = numerator + jnp.einsum(
-        "rkgtj,rjkd->rtkgd",
-        draft_weights,
-        new_key_value[..., HEAD_DIM:],
-        preferred_element_type=jnp.float32,
-    )
-    denominator = denominator + jnp.sum(draft_weights.astype(jnp.float32), axis=-1)
-    attended = (numerator / jnp.transpose(denominator, (0, 3, 1, 2))[..., None]).astype(
-        jnp.bfloat16
-    )
+    visible = ancestry(parents, tokens).astype(jnp.float32)
     head_width = kv_heads * group_heads * HEAD_DIM
-    attended = attended.reshape(per_owner_rows, tokens, head_width)
-
-    returning = jnp.take(attended, return_pick, axis=0, mode="clip")
+    cache_len = cached_key_value.shape[1]
+    grid_spec = pltpu.PrefetchScalarGridSpec(
+        num_scalar_prefetch=2,
+        grid=(per_owner_rows,),
+        in_specs=[
+            pl.BlockSpec((1, tokens, incoming.shape[2]), lambda j, src, lens: (src[j], 0, 0)),
+            pl.BlockSpec((1, cache_len, 1, 2 * HEAD_DIM), lambda j, src, lens: (j, 0, 0, 0)),
+            pl.BlockSpec((1, tokens, tokens), lambda j, src, lens: (j, 0, 0)),
+        ],
+        out_specs=pl.BlockSpec((1, tokens, head_width), lambda j, src, lens: (src[j], 0, 0)),
+    )
+    returning = pl.pallas_call(
+        functools.partial(attend_kernel, widths=(query_width, group_heads)),
+        grid_spec=grid_spec,
+        out_shape=jax.ShapeDtypeStruct((req_count, tokens, head_width), jnp.bfloat16),
+    )(source_of, lengths, incoming, cached_key_value, visible)
+
     arrived = lax.all_to_all(returning, "req", 0, 0, tiled=True)
     back_rows = jnp.take(arrived, my_owners, axis=0, mode="clip")
 
@@ -176,6 +194,7 @@
     gate_out = jnp.dot(normed_two, w_gate, preferred_element_type=jnp.float32)
     up_out = jnp.dot(normed_two, w_up, preferred_element_type=jnp.float32)
     hidden = (jax.nn.silu(gate_out) * up_out).astype(jnp.bfloat16)
+
     def unit_block(target):
         columns = lax.dynamic_slice_in_dim(w_down, target * quarter, quarter, 1)
         return jnp.dot(hidden, columns, preferred_element_type=jnp.float32).astype(jnp.bfloat16)

time: 135 us -> 140 us (1.037)
  the two profiles are of different devices: /device:TPU:1 before, /device:TPU:6 now
where the time goes in v12:
time: 140 us
  waiting for transfers between devices  64.9 us (46%)
  starting transfers between devices  35.3 us (25%)
  matrix products  14.2 us (10%)
  Pallas kernels  11.3 us (8%)
  local copies, waits for them, and re-layouts  10.8 us (8%)
  other arithmetic  1.8 us (1%)
    ppermute x12, waiting for transfers between devices, shift_mlp(): lax.ppermute(value, 'mlp', [(i, (i + shift) % count) for i in range(count)])  30.2 us
    all_to_all x1, waiting for transfers between devices, per_device(): incoming = lax.all_to_all(outgoing, 'req', 0, 0, tiled=True)  21.4 us
    ppermute x12, starting transfers between devices, shift_mlp(): lax.ppermute(value, 'mlp', [(i, (i + shift) % count) for i in range(count)])  14.7 us
    all_to_all x1, waiting for transfers between devices, per_device(): arrived = lax.all_to_all(returning, 'req', 0, 0, tiled=True)  13.3 us
    all_to_all x1, starting transfers between devices, per_device(): incoming = lax.all_to_all(outgoing, 'req', 0, 0, tiled=True)  12.4 us
    pallas_call x1, Pallas kernels, per_device(): pl.pallas_call(functools.partial(attend_kernel, widths=(query_width, grou...  11.3 us
    all_to_all x1, starting transfers between devices, per_device(): arrived = lax.all_to_all(returning, 'req', 0, 0, tiled=True)  8.28 us
    dot_general x4, matrix products, per_device(): jnp.dot(piece, rows_of_group, preferred_element_type=jnp.float32)  4.77 us
  transfers between devices with their start and end apart: 14, of which 8 were waited for; matrix products, arithmetic and copies ran while one was open for 10% of the time, Pallas kernels for 0%

profile of v12, /device:TPU:6, one launch (start us, length us, event | category | flops | bytes accessed | tf_op | source)
XLA Modules:
  0.0 139.5 jit_solution(11433892746354713157)
XLA Ops:
  0.7 3.1 %collective-permute-start.2 = (bf16[128,512]{1,0:T(8,128)(2,1)}, bf16[128,512]{1,0:T(8,128)(2,1)S(1)}, u32[]{:S(2)}, u32[]{:S(2)}) collective-permute-start(bf16[128,512]{1,0:T(8,128)(2,1)} %bitcast.47), channel_id=1, source_target_pairs={{0,3},{1,0},{2,1},{3,2},{4,7},{5,4},{6,5},{7,6},{8,11},{9,8},{10,9... | collective-permute-start | bytes 393224 | tf_op jit(solution)/shard_map/ppermute | solution.py:33
  7.2 6.0 %collective-permute-done = bf16[128,512]{1,0:T(8,128)(2,1)S(1)} collective-permute-done((bf16[128,512]{1,0:T(8,128)(2,1)}, bf16[128,512]{1,0:T(8,128)(2,1)S(1)}, u32[]{:S(2)}, u32[]{:S(2)}) %collective-permute-start) | collective-permute-done | bytes 131104 | tf_op jit(solution)/shard_map/ppermute | solution.py:33
  13.5 1.5 %convolution_convert_fusion.8 = bf16[128,128]{0,1:T(8,128)(2,1)S(1)} fusion(bf16[2048,128]{1,0:T(8,128)(2,1)} %param.22, bf16[128,2048]{1,0:T(8,128)(2,1)S(1)} %constant_dynamic-update-slice_fusion, f32[2048]{0:T(1024)} %param.20, f32[128]{0:T(128)S(1)} %add_rsqrt_fusion.1), kind=kOutput, calls=%fused_computation.28 | convolution fusion | flops 68173824 | bytes 1090048 | tf_op jit(solution)/shard_map/dot_general | solution.py:139
  15.0 1.6 %subtract_convert_fusion = (bf16[128,192]{0,1:T(8,128)(2,1)S(1)}, bf16[128,192]{0,1:T(8,128)(2,1)S(1)}) fusion(bf16[2048,192]{0,1:T(8,128)(2,1)} %param.21, bf16[128,2048]{1,0:T(8,128)(2,1)S(1)} %constant_dynamic-update-slice_fusion, f32[2048]{0:T(1024)S(1)} %copy-done.8, f32[128]{0:T(128)S(1)} %add_rsqrt_fusion.1), kind=kOutput, calls=%fused_computation.45 | convolution fusion | flops 101810176 | bytes 1417728 | tf_op jit(solution)/shard_map/dot_general | solution.py:138
  16.8 1.6 %gather_fusion = bf16[64,16,512]{2,1,0:T(8,128)(2,1)} fusion(bf16[8,16,512]{2,1,0:T(8,128)(2,1)S(1)} %bitcast.42, s32[1024]{0:T(1024)S(1)} %pad_clamp_fusion.2), kind=kCustom, calls=%fused_computation | custom fusion | bytes 2097408 | tf_op jit(solution)/shard_map/jit(_take)/gather | solution.py:148
  18.4 12.4 %all-to-all-start = ((bf16[64,16,512]{2,1,0:T(8,128)(2,1)}), bf16[64,16,512]{2,1,0:T(8,128)(2,1)}, u32[]{:S(2)}, u32[]{:S(2)}) async-start(bf16[64,16,512]{2,1,0:T(8,128)(2,1)} %gather_fusion), calls=%async_computation | async-start | bytes 2097152 | tf_op jit(solution)/shard_map/all_to_all | solution.py:149
  30.7 2.9 %copy.22.cache_ref = bf16[8,256,1,128]{3,2,1,0:T(2,128)(2,1)} copy(bf16[8,256,1,128]{3,1,2,0:T(8,128)(2,1)} %param.19) | data formatting | bytes 1048576 | tf_op args[5]
  35.8 21.4 %all-to-all-done.row_ref = bf16[64,16,512]{2,1,0:T(8,128)(2,1)} async-done(((bf16[64,16,512]{2,1,0:T(8,128)(2,1)}), bf16[64,16,512]{2,1,0:T(8,128)(2,1)}, u32[]{:S(2)}, u32[]{:S(2)}) %all-to-all-start) | async-done | bytes 1048608 | tf_op jit(solution)/shard_map/all_to_all | solution.py:149
  57.3 11.3 %shard_map.149 = bf16[64,16,192]{2,1,0:T(8,128)(2,1)} custom-call(s32[8]{0:T(128)} %and_select_fusion.2.source_ref, s32[8]{0:T(128)} %length_ref.1, bf16[64,16,512]{2,1,0:T(8,128)(2,1)} %all-to-all-done.row_ref, bf16[8,256,1,128]{3,2,1,0:T(2,128)(2,1)} %copy.22.cache_ref, f32[8,16,16]{2,1,0:T(8,128)} %fusion.11.mask_ref), custom_call_target="tpu_custom_call" | custom-call | tf_op jit(solution)/shard_map/pallas_call | solution.py:174
  68.6 8.3 %all-to-all-start.1 = ((bf16[64,16,192]{2,1,0:T(8,128)(2,1)}), bf16[64,16,192]{2,1,0:T(8,128)(2,1)}, u32[]{:S(2)}, u32[]{:S(2)}) async-start(bf16[64,16,192]{2,1,0:T(8,128)(2,1)} %shard_map.149), calls=%async_computation.1 | async-start | bytes 1048576 | tf_op jit(solution)/shard_map/all_to_all | solution.py:180
  77.0 2.0 %collective-permute-start.6 = (bf16[192,2048]{1,0:T(8,128)(2,1)}, bf16[192,2048]{1,0:T(8,128)(2,1)}, u32[]{:S(2)}, u32[]{:S(2)}) collective-permute-start(bf16[192,2048]{1,0:T(8,128)(2,1)} %param.23), channel_id=1, source_target_pairs={{0,2},{1,3},{2,0},{3,1},{4,6},{5,7},{6,4},{7,5},{8,10},{9,11},{10,... | collective-permute-start | bytes 2359304 | tf_op jit(solution)/shard_map/ppermute | solution.py:33
  80.2 13.3 %all-to-all-done.1 = bf16[64,16,192]{2,1,0:T(8,128)(2,1)} async-done(((bf16[64,16,192]{2,1,0:T(8,128)(2,1)}), bf16[64,16,192]{2,1,0:T(8,128)(2,1)}, u32[]{:S(2)}, u32[]{:S(2)}) %all-to-all-start.1) | async-done | bytes 393248 | tf_op jit(solution)/shard_map/all_to_all | solution.py:180
  93.5 1.6 %gather_fusion.1 = bf16[8,16,192]{2,1,0:T(8,128)(2,1)S(1)} fusion(bf16[64,16,192]{2,1,0:T(8,128)(2,1)} %all-to-all-done.1, s32[1024]{0:T(1024)S(1)} %pad_clamp_fusion.1), kind=kCustom, calls=%fused_computation.1 | custom fusion | bytes 98336 | tf_op jit(solution)/shard_map/jit(_take)/gather | solution.py:181
  95.3 3.2 %collective-permute-start.7 = (bf16[128,192]{1,0:T(8,128)(2,1)S(1)}, bf16[128,192]{1,0:T(8,128)(2,1)S(1)}, u32[]{:S(2)}, u32[]{:S(2)}) collective-permute-start(bf16[128,192]{1,0:T(8,128)(2,1)S(1)} %bitcast.44), channel_id=1, source_target_pairs={{0,3},{1,0},{2,1},{3,2},{4,7},{5,4},{6,5},{7,6},{8,11},{9,8},{10,9... | collective-permute-start | bytes 147464 | tf_op jit(solution)/shard_map/ppermute | solution.py:33
  98.5 17.1 %collective-permute-done.4 = bf16[192,2048]{1,0:T(8,128)(2,1)} collective-permute-done((bf16[192,2048]{1,0:T(8,128)(2,1)}, bf16[192,2048]{1,0:T(8,128)(2,1)}, u32[]{:S(2)}, u32[]{:S(2)}) %collective-permute-start.4) | collective-permute-done | bytes 786464 | tf_op jit(solution)/shard_map/ppermute | solution.py:33
  116.2 1.4 %fusion.2 = f32[128,2048]{1,0:T(8,128)S(1)} fusion(bf16[128,192]{1,0:T(8,128)(2,1)S(1)} %collective-permute-done.3, bf16[192,2048]{1,0:T(8,128)(2,1)} %collective-permute-done.4), kind=kOutput, calls=%fused_computation.8 | convolution fusion | flops 101187584 | bytes 1884160 | tf_op jit(solution)/shard_map/dot_general | solution.py:187
  117.7 3.7 %collective-permute-done.5 = bf16[128,192]{1,0:T(8,128)(2,1)S(1)} collective-permute-done((bf16[128,192]{1,0:T(8,128)(2,1)S(1)}, bf16[128,192]{1,0:T(8,128)(2,1)S(1)}, u32[]{:S(2)}, u32[]{:S(2)}) %collective-permute-start.5) | collective-permute-done | bytes 49184 | tf_op jit(solution)/shard_map/ppermute | solution.py:33
  121.4 1.4 %fusion.1 = f32[128,2048]{1,0:T(8,128)S(1)} fusion(bf16[128,192]{1,0:T(8,128)(2,1)S(1)} %collective-permute-done.5, bf16[192,2048]{1,0:T(8,128)(2,1)} %collective-permute-done.6), kind=kOutput, calls=%fused_computation.6 | convolution fusion | flops 101187584 | bytes 1884160 | tf_op jit(solution)/shard_map/dot_general | solution.py:187
  122.9 1.4 %fusion = f32[128,2048]{1,0:T(8,128)S(1)} fusion(bf16[128,192]{1,0:T(8,128)(2,1)S(1)} %collective-permute-done.7, bf16[192,2048]{1,0:T(8,128)(2,1)} %collective-permute-done.8), kind=kOutput, calls=%fused_computation.4 | convolution fusion | flops 101187584 | bytes 1884160 | tf_op jit(solution)/shard_map/dot_general | solution.py:187
  124.8 1.6 %copy-done.2 = bf16[2048,640]{1,0:T(8,128)(2,1)S(1)} copy-done((bf16[2048,640]{1,0:T(8,128)(2,1)S(1)}, bf16[2048,640]{1,0:T(8,128)(2,1)}, u32[]{:S(2)}) %copy-start.2) | copy-done | bytes 2621464
  129.9 2.2 %collective-permute-start.11 = (bf16[128,512]{1,0:T(8,128)(2,1)S(1)}, bf16[128,512]{1,0:T(8,128)(2,1)}, u32[]{:S(2)}, u32[]{:S(2)}) collective-permute-start(bf16[128,512]{1,0:T(8,128)(2,1)S(1)} %convolution_convert_fusion.4), channel_id=1, source_target_pairs={{0,3},{1,0},{2,1},{3,2},{4,7},{5,4},{6,5},{7,6},{8,11},{9,8},{10,9... | collective-permute-start | bytes 393224 | tf_op jit(solution)/shard_map/ppermute | solution.py:33
  132.1 1.8 %gather_fusion.2 = bf16[8,16,512]{2,1,0:T(8,128)(2,1)S(1)} fusion(bf16[64,16,512]{2,1,0:T(8,128)(2,1)} %all-to-all-done.row_ref, s32[1024]{0:T(1024)S(1)} %pad_clamp_fusion), kind=kCustom, calls=%fused_computation.2 | custom fusion | bytes 262176 | tf_op jit(solution)/shard_map/jit(_take)/gather | solution.py:150
  134.7 1.7 %collective-permute-done.9 = bf16[128,512]{1,0:T(8,128)(2,1)S(1)} collective-permute-done((bf16[128,512]{1,0:T(8,128)(2,1)S(1)}, bf16[128,512]{1,0:T(8,128)(2,1)S(1)}, u32[]{:S(2)}, u32[]{:S(2)}) %collective-permute-start.9) | collective-permute-done | bytes 131104 | tf_op jit(solution)/shard_map/ppermute | solution.py:33
  137.5 2.0 %add_convert_fusion = bf16[128,512]{1,0:T(8,128)(2,1)} fusion(bf16[128,512]{1,0:T(8,128)(2,1)} %collective-permute-done.11, bf16[128,512]{1,0:T(8,128)(2,1)} %collective-permute-done.10, bf16[128,512]{1,0:T(8,128)(2,1)S(1)} %collective-permute-done.9, f32[128,2048]{1,0:T(8,128)} %copy-done.1, s32[]{:T(128)S(6)} %select_n.90, ...), kind=kOutput, calls=%fused_computation.42 | convolution fusion | flops 84541440 | bytes 1606656 | tf_op jit(solution)/shard_map/dot_general | solution.py:200
  (66 shorter events, 13.7 us)
Async XLA Ops:
  0.6 127.3 %copy-start = (bf16[640,2048]{1,0:T(8,128)(2,1)S(1)}, bf16[640,2048]{1,0:T(8,128)(2,1)}, u32[]{:S(2)}) copy-start(bf16[640,2048]{1,0:T(8,128)(2,1)} %param.27) | copy-start | bytes 7864324
  0.6 14.3 %copy-start.8 = (f32[2048]{0:T(1024)S(1)}, f32[2048]{0:T(1024)}, u32[]{:S(2)}) copy-start(f32[2048]{0:T(1024)} %param.20) | copy-start | bytes 24580
  0.7 12.6 %collective-permute-start.2 = (bf16[128,512]{1,0:T(8,128)(2,1)}, bf16[128,512]{1,0:T(8,128)(2,1)S(1)}, u32[]{:S(2)}, u32[]{:S(2)}) collective-permute-start(bf16[128,512]{1,0:T(8,128)(2,1)} %bitcast.47), channel_id=1, source_target_pairs={{0,3},{1,0},{2,1},{3,2},{4,7},{5,4},{6,5},{7,6},{8,11},{9,8},{10,9... | collective-permute-start | bytes 393224 | tf_op jit(solution)/shard_map/ppermute | solution.py:33
  3.7 9.5 %collective-permute-start.1 = (bf16[128,512]{1,0:T(8,128)(2,1)}, bf16[128,512]{1,0:T(8,128)(2,1)S(1)}, u32[]{:S(2)}, u32[]{:S(2)}) collective-permute-start(bf16[128,512]{1,0:T(8,128)(2,1)} %bitcast.48), channel_id=1, source_target_pairs={{0,2},{1,3},{2,0},{3,1},{4,6},{5,7},{6,4},{7,5},{8,10},{9,11},{10,... | collective-permute-start | bytes 393224 | tf_op jit(solution)/shard_map/ppermute | solution.py:33
  4.4 8.9 %collective-permute-start = (bf16[128,512]{1,0:T(8,128)(2,1)}, bf16[128,512]{1,0:T(8,128)(2,1)S(1)}, u32[]{:S(2)}, u32[]{:S(2)}) collective-permute-start(bf16[128,512]{1,0:T(8,128)(2,1)} %bitcast.49), channel_id=1, source_target_pairs={{0,1},{1,2},{2,3},{3,0},{4,5},{5,6},{6,7},{7,4},{8,9},{9,10},{10,1... | collective-permute-start | bytes 393224 | tf_op jit(solution)/shard_map/ppermute | solution.py:33
  16.7 16.9 %copy-start.6 = (s32[512]{0:T(512)S(1)}, s32[512]{0:T(512)}, u32[]{:S(2)}) copy-start(s32[512]{0:T(512)} %param.15) | copy-start | bytes 6148
  16.7 17.6 %copy-start.5 = (s32[8,16]{1,0:T(8,128)S(1)}, s32[8,16]{1,0:T(8,128)}, u32[]{:S(2)}) copy-start(s32[8,16]{1,0:T(8,128)} %param.17) | copy-start | bytes 1540
  18.4 38.9 %all-to-all-start = ((bf16[64,16,512]{2,1,0:T(8,128)(2,1)}), bf16[64,16,512]{2,1,0:T(8,128)(2,1)}, u32[]{:S(2)}, u32[]{:S(2)}) async-start(bf16[64,16,512]{2,1,0:T(8,128)(2,1)} %gather_fusion), calls=%async_computation | async-start | bytes 2097152 | tf_op jit(solution)/shard_map/all_to_all | solution.py:149
  68.6 24.9 %all-to-all-start.1 = ((bf16[64,16,192]{2,1,0:T(8,128)(2,1)}), bf16[64,16,192]{2,1,0:T(8,128)(2,1)}, u32[]{:S(2)}, u32[]{:S(2)}) async-start(bf16[64,16,192]{2,1,0:T(8,128)(2,1)} %shard_map.149), calls=%async_computation.1 | async-start | bytes 1048576 | tf_op jit(solution)/shard_map/all_to_all | solution.py:180
  76.9 38.7 %collective-permute-start.4 = (bf16[192,2048]{1,0:T(8,128)(2,1)}, bf16[192,2048]{1,0:T(8,128)(2,1)}, u32[]{:S(2)}, u32[]{:S(2)}) collective-permute-start(bf16[192,2048]{1,0:T(8,128)(2,1)} %param.23), channel_id=1, source_target_pairs={{0,1},{1,2},{2,3},{3,0},{4,5},{5,6},{6,7},{7,4},{8,9},{9,10},{10,1... | collective-permute-start | bytes 2359304 | tf_op jit(solution)/shard_map/ppermute | solution.py:33
  77.0 40.7 %collective-permute-start.6 = (bf16[192,2048]{1,0:T(8,128)(2,1)}, bf16[192,2048]{1,0:T(8,128)(2,1)}, u32[]{:S(2)}, u32[]{:S(2)}) collective-permute-start(bf16[192,2048]{1,0:T(8,128)(2,1)} %param.23), channel_id=1, source_target_pairs={{0,2},{1,3},{2,0},{3,1},{4,6},{5,7},{6,4},{7,5},{8,10},{9,11},{10,... | collective-permute-start | bytes 2359304 | tf_op jit(solution)/shard_map/ppermute | solution.py:33
  79.0 43.8 %collective-permute-start.8 = (bf16[192,2048]{1,0:T(8,128)(2,1)}, bf16[192,2048]{1,0:T(8,128)(2,1)}, u32[]{:S(2)}, u32[]{:S(2)}) collective-permute-start(bf16[192,2048]{1,0:T(8,128)(2,1)} %param.23), channel_id=1, source_target_pairs={{0,3},{1,0},{2,1},{3,2},{4,7},{5,4},{6,5},{7,6},{8,11},{9,8},{10,9... | collective-permute-start | bytes 2359304 | tf_op jit(solution)/shard_map/ppermute | solution.py:33
  95.1 21.1 %collective-permute-start.3 = (bf16[128,192]{1,0:T(8,128)(2,1)S(1)}, bf16[128,192]{1,0:T(8,128)(2,1)S(1)}, u32[]{:S(2)}, u32[]{:S(2)}) collective-permute-start(bf16[128,192]{1,0:T(8,128)(2,1)S(1)} %bitcast.43), channel_id=1, source_target_pairs={{0,1},{1,2},{2,3},{3,0},{4,5},{5,6},{6,7},{7,4},{8,9},{9,10},{10,1... | collective-permute-start | bytes 147464 | tf_op jit(solution)/shard_map/ppermute | solution.py:33
  95.2 29.0 %copy-start.3 = (bf16[192,2048]{1,0:T(8,128)(2,1)S(1)}, bf16[192,2048]{1,0:T(8,128)(2,1)}, u32[]{:S(2)}) copy-start(bf16[192,2048]{1,0:T(8,128)(2,1)} %param.23) | copy-start | bytes 2359300
  95.3 27.6 %collective-permute-start.7 = (bf16[128,192]{1,0:T(8,128)(2,1)S(1)}, bf16[128,192]{1,0:T(8,128)(2,1)S(1)}, u32[]{:S(2)}, u32[]{:S(2)}) collective-permute-start(bf16[128,192]{1,0:T(8,128)(2,1)S(1)} %bitcast.44), channel_id=1, source_target_pairs={{0,3},{1,0},{2,1},{3,2},{4,7},{5,4},{6,5},{7,6},{8,11},{9,8},{10,9... | collective-permute-start | bytes 147464 | tf_op jit(solution)/shard_map/ppermute | solution.py:33
  115.6 5.8 %collective-permute-start.5 = (bf16[128,192]{1,0:T(8,128)(2,1)S(1)}, bf16[128,192]{1,0:T(8,128)(2,1)S(1)}, u32[]{:S(2)}, u32[]{:S(2)}) collective-permute-start(bf16[128,192]{1,0:T(8,128)(2,1)S(1)} %bitcast.45), channel_id=1, source_target_pairs={{0,2},{1,3},{2,0},{3,1},{4,6},{5,7},{6,4},{7,5},{8,10},{9,11},{10,... | collective-permute-start | bytes 147464 | tf_op jit(solution)/shard_map/ppermute | solution.py:33
  124.3 2.1 %copy-start.2 = (bf16[2048,640]{1,0:T(8,128)(2,1)S(1)}, bf16[2048,640]{1,0:T(8,128)(2,1)}, u32[]{:S(2)}) copy-start(bf16[2048,640]{1,0:T(8,128)(2,1)} %param.25) | copy-start | bytes 7864324
  124.3 2.1 %copy-start.4 = (f32[2048]{0:T(1024)S(1)}, f32[2048]{0:T(1024)}, u32[]{:S(2)}) copy-start(f32[2048]{0:T(1024)} %param.24) | copy-start | bytes 24580
  124.8 3.1 %copy-start.1 = (f32[128,2048]{1,0:T(8,128)}, f32[128,2048]{1,0:T(8,128)S(1)}, u32[]{:S(2)}) copy-start(f32[128,2048]{1,0:T(8,128)S(1)} %get-tuple-element.11) | copy-start | bytes 3145732
  124.8 2.4 %copy-start.7 = (bf16[2048,640]{1,0:T(8,128)(2,1)S(1)}, bf16[2048,640]{1,0:T(8,128)(2,1)}, u32[]{:S(2)}) copy-start(bf16[2048,640]{1,0:T(8,128)(2,1)} %param.26) | copy-start | bytes 7864324
  127.9 6.0 %copy-start.9 = (s32[8,8]{1,0:T(8,128)S(1)}, s32[8,8]{1,0:T(8,128)}, u32[]{:S(2)}) copy-start(s32[8,8]{1,0:T(8,128)} %param.18) | copy-start | bytes 772
  128.8 7.7 %collective-permute-start.9 = (bf16[128,512]{1,0:T(8,128)(2,1)S(1)}, bf16[128,512]{1,0:T(8,128)(2,1)S(1)}, u32[]{:S(2)}, u32[]{:S(2)}) collective-permute-start(bf16[128,512]{1,0:T(8,128)(2,1)S(1)} %convolution_convert_fusion.6), channel_id=1, source_target_pairs={{0,1},{1,2},{2,3},{3,0},{4,5},{5,6},{6,7},{7,4},{8,9},{9,10},{10,1... | collective-permute-start | bytes 393224 | tf_op jit(solution)/shard_map/ppermute | solution.py:33
  128.9 7.6 %collective-permute-start.10 = (bf16[128,512]{1,0:T(8,128)(2,1)S(1)}, bf16[128,512]{1,0:T(8,128)(2,1)}, u32[]{:S(2)}, u32[]{:S(2)}) collective-permute-start(bf16[128,512]{1,0:T(8,128)(2,1)S(1)} %convolution_convert_fusion.5), channel_id=1, source_target_pairs={{0,2},{1,3},{2,0},{3,1},{4,6},{5,7},{6,4},{7,5},{8,10},{9,11},{10,... | collective-permute-start | bytes 393224 | tf_op jit(solution)/shard_map/ppermute | solution.py:33
  129.9 7.6 %collective-permute-start.11 = (bf16[128,512]{1,0:T(8,128)(2,1)S(1)}, bf16[128,512]{1,0:T(8,128)(2,1)}, u32[]{:S(2)}, u32[]{:S(2)}) collective-permute-start(bf16[128,512]{1,0:T(8,128)(2,1)S(1)} %convolution_convert_fusion.4), channel_id=1, source_target_pairs={{0,3},{1,0},{2,1},{3,2},{4,7},{5,4},{6,5},{7,6},{8,11},{9,8},{10,9... | collective-permute-start | bytes 393224 | tf_op jit(solution)/shard_map/ppermute | solution.py:33

commit v13 on v12

--- a/solution.py
+++ b/solution.py
@@ -50,7 +50,7 @@
     query_width, group_heads = widths
     slot = pl.program_id(0)
     row = row_ref[0]
-    cache = cache_ref[0, :, 0, :]
+    cache = cache_ref[0]
     keys_cache, values_cache = cache[:, :HEAD_DIM], cache[:, HEAD_DIM:]
     fresh = row[:, 2 * query_width :]
     keys_draft, values_draft = fresh[:, :HEAD_DIM], fresh[:, HEAD_DIM:]
@@ -166,7 +166,7 @@
         grid=(per_owner_rows,),
         in_specs=[
             pl.BlockSpec((1, tokens, incoming.shape[2]), lambda j, src, lens: (src[j], 0, 0)),
-            pl.BlockSpec((1, cache_len, 1, 2 * HEAD_DIM), lambda j, src, lens: (j, 0, 0, 0)),
+            pl.BlockSpec((1, cache_len, 2 * HEAD_DIM), lambda j, src, lens: (j, 0, 0)),
             pl.BlockSpec((1, tokens, tokens), lambda j, src, lens: (j, 0, 0)),
         ],
         out_specs=pl.BlockSpec((1, tokens, head_width), lambda j, src, lens: (src[j], 0, 0)),
@@ -175,7 +175,13 @@
         functools.partial(attend_kernel, widths=(query_width, group_heads)),
         grid_spec=grid_spec,
         out_shape=jax.ShapeDtypeStruct((req_count, tokens, head_width), jnp.bfloat16),
-    )(source_of, lengths, incoming, cached_key_value, visible)
+    )(
+        source_of,
+        lengths,
+        incoming,
+        cached_key_value.reshape(per_owner_rows, cache_len, 2 * HEAD_DIM),
+        visible,
+    )
 
     arrived = lax.all_to_all(returning, "req", 0, 0, tiled=True)
     back_rows = jnp.take(arrived, my_owners, axis=0, mode="clip")

time: 140 us -> 139 us (level)
  waiting for transfers between devices: 64.9 us -> 67.8 us
  local copies, waits for them, and re-layouts: 10.8 us -> 7.94 us
    unnamed x21 -> x20, local copies, waits for them, and re-layouts: 4.73 us -> 1.84 us
    all_to_all x1, waiting for transfers between devices: 21.4 us -> 24.3 us  [per_device(): incoming = lax.all_to_all(outgoing, 'req', 0, 0, tiled=True)]
  transfers between devices with their start and end apart: 14 -> 14, of which waited for: 8 -> 8; matrix products, arithmetic and copies ran while one was open for 10% -> 8% of each run, Pallas kernels for 0% -> 0%
where the time goes in v13:
time: 139 us; the launch traced here: 138 us
  waiting for transfers between devices  67.8 us (49%)
  starting transfers between devices  35.3 us (25%)
  matrix products  14.2 us (10%)
  Pallas kernels  10.3 us (7%)
  local copies, waits for them, and re-layouts  7.94 us (6%)
  other arithmetic  1.8 us (1%)
    ppermute x12, waiting for transfers between devices, shift_mlp(): lax.ppermute(value, 'mlp', [(i, (i + shift) % count) for i in range(count)])  30.2 us
    all_to_all x1, waiting for transfers between devices, per_device(): incoming = lax.all_to_all(outgoing, 'req', 0, 0, tiled=True)  24.3 us
    ppermute x12, starting transfers between devices, shift_mlp(): lax.ppermute(value, 'mlp', [(i, (i + shift) % count) for i in range(count)])  14.7 us
    all_to_all x1, waiting for transfers between devices, per_device(): arrived = lax.all_to_all(returning, 'req', 0, 0, tiled=True)  13.3 us
    all_to_all x1, starting transfers between devices, per_device(): incoming = lax.all_to_all(outgoing, 'req', 0, 0, tiled=True)  12.4 us
    pallas_call x1, Pallas kernels, per_device(): pl.pallas_call(functools.partial(attend_kernel, widths=(query_width, grou...  10.3 us
    all_to_all x1, starting transfers between devices, per_device(): arrived = lax.all_to_all(returning, 'req', 0, 0, tiled=True)  8.29 us
    dot_general x4, matrix products, per_device(): jnp.dot(piece, rows_of_group, preferred_element_type=jnp.float32)  4.77 us
  transfers between devices with their start and end apart: 14, of which 8 were waited for; matrix products, arithmetic and copies ran while one was open for 8% of the time, Pallas kernels for 0%

profile of v13, /device:TPU:6, one launch (start us, length us, event | category | flops | bytes accessed | tf_op | source)
XLA Modules:
  0.0 138.5 jit_solution(17739517570846191718)
XLA Ops:
  0.7 3.1 %collective-permute-start.2 = (bf16[128,512]{1,0:T(8,128)(2,1)}, bf16[128,512]{1,0:T(8,128)(2,1)S(1)}, u32[]{:S(2)}, u32[]{:S(2)}) collective-permute-start(bf16[128,512]{1,0:T(8,128)(2,1)} %bitcast.49), channel_id=1, source_target_pairs={{0,3},{1,0},{2,1},{3,2},{4,7},{5,4},{6,5},{7,6},{8,11},{9,8},{10,9... | collective-permute-start | bytes 393224 | tf_op jit(solution)/shard_map/ppermute | solution.py:33
  7.2 6.0 %collective-permute-done = bf16[128,512]{1,0:T(8,128)(2,1)S(1)} collective-permute-done((bf16[128,512]{1,0:T(8,128)(2,1)}, bf16[128,512]{1,0:T(8,128)(2,1)S(1)}, u32[]{:S(2)}, u32[]{:S(2)}) %collective-permute-start) | collective-permute-done | bytes 131104 | tf_op jit(solution)/shard_map/ppermute | solution.py:33
  13.5 1.5 %convolution_convert_fusion.8 = bf16[128,128]{0,1:T(8,128)(2,1)S(1)} fusion(bf16[2048,128]{1,0:T(8,128)(2,1)} %param.22, bf16[128,2048]{1,0:T(8,128)(2,1)S(1)} %constant_dynamic-update-slice_fusion, f32[2048]{0:T(1024)} %param.20, f32[128]{0:T(128)S(1)} %add_rsqrt_fusion.1), kind=kOutput, calls=%fused_computation.28 | convolution fusion | flops 68173824 | bytes 1090048 | tf_op jit(solution)/shard_map/dot_general | solution.py:139
  15.0 1.6 %subtract_convert_fusion = (bf16[128,192]{0,1:T(8,128)(2,1)S(1)}, bf16[128,192]{0,1:T(8,128)(2,1)S(1)}) fusion(bf16[2048,192]{0,1:T(8,128)(2,1)} %param.21, bf16[128,2048]{1,0:T(8,128)(2,1)S(1)} %constant_dynamic-update-slice_fusion, f32[2048]{0:T(1024)S(1)} %copy-done.8, f32[128]{0:T(128)S(1)} %add_rsqrt_fusion.1), kind=kOutput, calls=%fused_computation.45 | convolution fusion | flops 101810176 | bytes 1417728 | tf_op jit(solution)/shard_map/dot_general | solution.py:138
  16.8 1.6 %gather_fusion = bf16[64,16,512]{2,1,0:T(8,128)(2,1)} fusion(bf16[8,16,512]{2,1,0:T(8,128)(2,1)S(1)} %bitcast.43, s32[1024]{0:T(1024)S(1)} %pad_clamp_fusion.2), kind=kCustom, calls=%fused_computation | custom fusion | bytes 2097408 | tf_op jit(solution)/shard_map/jit(_take)/gather | solution.py:148
  18.4 12.4 %all-to-all-start = ((bf16[64,16,512]{2,1,0:T(8,128)(2,1)}), bf16[64,16,512]{2,1,0:T(8,128)(2,1)}, u32[]{:S(2)}, u32[]{:S(2)}) async-start(bf16[64,16,512]{2,1,0:T(8,128)(2,1)} %gather_fusion), calls=%async_computation | async-start | bytes 2097152 | tf_op jit(solution)/shard_map/all_to_all | solution.py:149
  33.0 24.3 %all-to-all-done.row_ref = bf16[64,16,512]{2,1,0:T(8,128)(2,1)} async-done(((bf16[64,16,512]{2,1,0:T(8,128)(2,1)}), bf16[64,16,512]{2,1,0:T(8,128)(2,1)}, u32[]{:S(2)}, u32[]{:S(2)}) %all-to-all-start) | async-done | bytes 1048608 | tf_op jit(solution)/shard_map/all_to_all | solution.py:149
  57.3 10.3 %shard_map.149 = bf16[64,16,192]{2,1,0:T(8,128)(2,1)} custom-call(s32[8]{0:T(128)} %and_select_fusion.2.source_ref, s32[8]{0:T(128)} %length_ref.1, bf16[64,16,512]{2,1,0:T(8,128)(2,1)} %all-to-all-done.row_ref, bf16[8,256,128]{2,1,0:T(8,128)(2,1)} %bitcast.44, f32[8,16,16]{2,1,0:T(8,128)} %fusion.11.mask_ref), custom_call_target="tpu_custom_call" | custom-call | tf_op jit(solution)/shard_map/pallas_call | solution.py:174
  67.6 8.3 %all-to-all-start.1 = ((bf16[64,16,192]{2,1,0:T(8,128)(2,1)}), bf16[64,16,192]{2,1,0:T(8,128)(2,1)}, u32[]{:S(2)}, u32[]{:S(2)}) async-start(bf16[64,16,192]{2,1,0:T(8,128)(2,1)} %shard_map.149), calls=%async_computation.1 | async-start | bytes 1048576 | tf_op jit(solution)/shard_map/all_to_all | solution.py:186
  76.0 2.0 %collective-permute-start.6 = (bf16[192,2048]{1,0:T(8,128)(2,1)}, bf16[192,2048]{1,0:T(8,128)(2,1)}, u32[]{:S(2)}, u32[]{:S(2)}) collective-permute-start(bf16[192,2048]{1,0:T(8,128)(2,1)} %param.23), channel_id=1, source_target_pairs={{0,2},{1,3},{2,0},{3,1},{4,6},{5,7},{6,4},{7,5},{8,10},{9,11},{10,... | collective-permute-start | bytes 2359304 | tf_op jit(solution)/shard_map/ppermute | solution.py:33
  78.0 1.2 collective-permute-start.8
  79.2 13.3 %all-to-all-done.1 = bf16[64,16,192]{2,1,0:T(8,128)(2,1)} async-done(((bf16[64,16,192]{2,1,0:T(8,128)(2,1)}), bf16[64,16,192]{2,1,0:T(8,128)(2,1)}, u32[]{:S(2)}, u32[]{:S(2)}) %all-to-all-start.1) | async-done | bytes 393248 | tf_op jit(solution)/shard_map/all_to_all | solution.py:186
  92.5 1.6 %gather_fusion.1 = bf16[8,16,192]{2,1,0:T(8,128)(2,1)S(1)} fusion(bf16[64,16,192]{2,1,0:T(8,128)(2,1)} %all-to-all-done.1, s32[1024]{0:T(1024)S(1)} %pad_clamp_fusion.1), kind=kCustom, calls=%fused_computation.1 | custom fusion | bytes 98336 | tf_op jit(solution)/shard_map/jit(_take)/gather | solution.py:187
  94.2 3.2 %collective-permute-start.7 = (bf16[128,192]{1,0:T(8,128)(2,1)S(1)}, bf16[128,192]{1,0:T(8,128)(2,1)S(1)}, u32[]{:S(2)}, u32[]{:S(2)}) collective-permute-start(bf16[128,192]{1,0:T(8,128)(2,1)S(1)} %bitcast.46), channel_id=1, source_target_pairs={{0,3},{1,0},{2,1},{3,2},{4,7},{5,4},{6,5},{7,6},{8,11},{9,8},{10,9... | collective-permute-start | bytes 147464 | tf_op jit(solution)/shard_map/ppermute | solution.py:33
  97.5 17.1 %collective-permute-done.4 = bf16[192,2048]{1,0:T(8,128)(2,1)} collective-permute-done((bf16[192,2048]{1,0:T(8,128)(2,1)}, bf16[192,2048]{1,0:T(8,128)(2,1)}, u32[]{:S(2)}, u32[]{:S(2)}) %collective-permute-start.4) | collective-permute-done | bytes 786464 | tf_op jit(solution)/shard_map/ppermute | solution.py:33
  115.2 1.4 %fusion.2 = f32[128,2048]{1,0:T(8,128)S(1)} fusion(bf16[128,192]{1,0:T(8,128)(2,1)S(1)} %collective-permute-done.3, bf16[192,2048]{1,0:T(8,128)(2,1)} %collective-permute-done.4), kind=kOutput, calls=%fused_computation.8 | convolution fusion | flops 101187584 | bytes 1884160 | tf_op jit(solution)/shard_map/dot_general | solution.py:193
  116.6 3.7 %collective-permute-done.5 = bf16[128,192]{1,0:T(8,128)(2,1)S(1)} collective-permute-done((bf16[128,192]{1,0:T(8,128)(2,1)S(1)}, bf16[128,192]{1,0:T(8,128)(2,1)S(1)}, u32[]{:S(2)}, u32[]{:S(2)}) %collective-permute-start.5) | collective-permute-done | bytes 49184 | tf_op jit(solution)/shard_map/ppermute | solution.py:33
  120.4 1.4 %fusion.1 = f32[128,2048]{1,0:T(8,128)S(1)} fusion(bf16[128,192]{1,0:T(8,128)(2,1)S(1)} %collective-permute-done.5, bf16[192,2048]{1,0:T(8,128)(2,1)} %collective-permute-done.6), kind=kOutput, calls=%fused_computation.6 | convolution fusion | flops 101187584 | bytes 1884160 | tf_op jit(solution)/shard_map/dot_general | solution.py:193
  121.8 1.4 %fusion = f32[128,2048]{1,0:T(8,128)S(1)} fusion(bf16[128,192]{1,0:T(8,128)(2,1)S(1)} %collective-permute-done.7, bf16[192,2048]{1,0:T(8,128)(2,1)} %collective-permute-done.8), kind=kOutput, calls=%fused_computation.4 | convolution fusion | flops 101187584 | bytes 1884160 | tf_op jit(solution)/shard_map/dot_general | solution.py:193
  123.8 1.6 %copy-done.2 = bf16[2048,640]{1,0:T(8,128)(2,1)S(1)} copy-done((bf16[2048,640]{1,0:T(8,128)(2,1)S(1)}, bf16[2048,640]{1,0:T(8,128)(2,1)}, u32[]{:S(2)}) %copy-start.2) | copy-done | bytes 2621464
  128.8 2.2 %collective-permute-start.11 = (bf16[128,512]{1,0:T(8,128)(2,1)S(1)}, bf16[128,512]{1,0:T(8,128)(2,1)}, u32[]{:S(2)}, u32[]{:S(2)}) collective-permute-start(bf16[128,512]{1,0:T(8,128)(2,1)S(1)} %convolution_convert_fusion.4), channel_id=1, source_target_pairs={{0,3},{1,0},{2,1},{3,2},{4,7},{5,4},{6,5},{7,6},{8,11},{9,8},{10,9... | collective-permute-start | bytes 393224 | tf_op jit(solution)/shard_map/ppermute | solution.py:33
  131.1 1.8 %gather_fusion.2 = bf16[8,16,512]{2,1,0:T(8,128)(2,1)S(1)} fusion(bf16[64,16,512]{2,1,0:T(8,128)(2,1)} %all-to-all-done.row_ref, s32[1024]{0:T(1024)S(1)} %pad_clamp_fusion), kind=kCustom, calls=%fused_computation.2 | custom fusion | bytes 262176 | tf_op jit(solution)/shard_map/jit(_take)/gather | solution.py:150
  133.7 1.7 %collective-permute-done.9 = bf16[128,512]{1,0:T(8,128)(2,1)S(1)} collective-permute-done((bf16[128,512]{1,0:T(8,128)(2,1)S(1)}, bf16[128,512]{1,0:T(8,128)(2,1)S(1)}, u32[]{:S(2)}, u32[]{:S(2)}) %collective-permute-start.9) | collective-permute-done | bytes 131104 | tf_op jit(solution)/shard_map/ppermute | solution.py:33
  136.4 2.0 %add_convert_fusion = bf16[128,512]{1,0:T(8,128)(2,1)} fusion(bf16[128,512]{1,0:T(8,128)(2,1)} %collective-permute-done.11, bf16[128,512]{1,0:T(8,128)(2,1)} %collective-permute-done.10, bf16[128,512]{1,0:T(8,128)(2,1)S(1)} %collective-permute-done.9, f32[128,2048]{1,0:T(8,128)} %copy-done.1, s32[]{:T(128)S(6)} %select_n.90, ...), kind=kOutput, calls=%fused_computation.42 | convolution fusion | flops 84541440 | bytes 1606656 | tf_op jit(solution)/shard_map/dot_general | solution.py:206
  (65 shorter events, 12.5 us)
Async XLA Ops:
  0.6 126.2 %copy-start = (bf16[640,2048]{1,0:T(8,128)(2,1)S(1)}, bf16[640,2048]{1,0:T(8,128)(2,1)}, u32[]{:S(2)}) copy-start(bf16[640,2048]{1,0:T(8,128)(2,1)} %param.27) | copy-start | bytes 7864324
  0.6 14.3 %copy-start.8 = (f32[2048]{0:T(1024)S(1)}, f32[2048]{0:T(1024)}, u32[]{:S(2)}) copy-start(f32[2048]{0:T(1024)} %param.20) | copy-start | bytes 24580
  0.7 12.6 %collective-permute-start.2 = (bf16[128,512]{1,0:T(8,128)(2,1)}, bf16[128,512]{1,0:T(8,128)(2,1)S(1)}, u32[]{:S(2)}, u32[]{:S(2)}) collective-permute-start(bf16[128,512]{1,0:T(8,128)(2,1)} %bitcast.49), channel_id=1, source_target_pairs={{0,3},{1,0},{2,1},{3,2},{4,7},{5,4},{6,5},{7,6},{8,11},{9,8},{10,9... | collective-permute-start | bytes 393224 | tf_op jit(solution)/shard_map/ppermute | solution.py:33
  3.7 9.5 %collective-permute-start.1 = (bf16[128,512]{1,0:T(8,128)(2,1)}, bf16[128,512]{1,0:T(8,128)(2,1)S(1)}, u32[]{:S(2)}, u32[]{:S(2)}) collective-permute-start(bf16[128,512]{1,0:T(8,128)(2,1)} %bitcast.50), channel_id=1, source_target_pairs={{0,2},{1,3},{2,0},{3,1},{4,6},{5,7},{6,4},{7,5},{8,10},{9,11},{10,... | collective-permute-start | bytes 393224 | tf_op jit(solution)/shard_map/ppermute | solution.py:33
  4.4 8.9 %collective-permute-start = (bf16[128,512]{1,0:T(8,128)(2,1)}, bf16[128,512]{1,0:T(8,128)(2,1)S(1)}, u32[]{:S(2)}, u32[]{:S(2)}) collective-permute-start(bf16[128,512]{1,0:T(8,128)(2,1)} %bitcast.51), channel_id=1, source_target_pairs={{0,1},{1,2},{2,3},{3,0},{4,5},{5,6},{6,7},{7,4},{8,9},{9,10},{10,1... | collective-permute-start | bytes 393224 | tf_op jit(solution)/shard_map/ppermute | solution.py:33
  16.6 14.2 %copy-start.6 = (s32[512]{0:T(512)S(1)}, s32[512]{0:T(512)}, u32[]{:S(2)}) copy-start(s32[512]{0:T(512)} %param.15) | copy-start | bytes 6148
  16.6 14.9 %copy-start.5 = (s32[8,16]{1,0:T(8,128)S(1)}, s32[8,16]{1,0:T(8,128)}, u32[]{:S(2)}) copy-start(s32[8,16]{1,0:T(8,128)} %param.17) | copy-start | bytes 1540
  18.4 38.9 %all-to-all-start = ((bf16[64,16,512]{2,1,0:T(8,128)(2,1)}), bf16[64,16,512]{2,1,0:T(8,128)(2,1)}, u32[]{:S(2)}, u32[]{:S(2)}) async-start(bf16[64,16,512]{2,1,0:T(8,128)(2,1)} %gather_fusion), calls=%async_computation | async-start | bytes 2097152 | tf_op jit(solution)/shard_map/all_to_all | solution.py:149
  67.6 24.9 %all-to-all-start.1 = ((bf16[64,16,192]{2,1,0:T(8,128)(2,1)}), bf16[64,16,192]{2,1,0:T(8,128)(2,1)}, u32[]{:S(2)}, u32[]{:S(2)}) async-start(bf16[64,16,192]{2,1,0:T(8,128)(2,1)} %shard_map.149), calls=%async_computation.1 | async-start | bytes 1048576 | tf_op jit(solution)/shard_map/all_to_all | solution.py:186
  75.9 38.7 %collective-permute-start.4 = (bf16[192,2048]{1,0:T(8,128)(2,1)}, bf16[192,2048]{1,0:T(8,128)(2,1)}, u32[]{:S(2)}, u32[]{:S(2)}) collective-permute-start(bf16[192,2048]{1,0:T(8,128)(2,1)} %param.23), channel_id=1, source_target_pairs={{0,1},{1,2},{2,3},{3,0},{4,5},{5,6},{6,7},{7,4},{8,9},{9,10},{10,1... | collective-permute-start | bytes 2359304 | tf_op jit(solution)/shard_map/ppermute | solution.py:33
  76.0 40.7 %collective-permute-start.6 = (bf16[192,2048]{1,0:T(8,128)(2,1)}, bf16[192,2048]{1,0:T(8,128)(2,1)}, u32[]{:S(2)}, u32[]{:S(2)}) collective-permute-start(bf16[192,2048]{1,0:T(8,128)(2,1)} %param.23), channel_id=1, source_target_pairs={{0,2},{1,3},{2,0},{3,1},{4,6},{5,7},{6,4},{7,5},{8,10},{9,11},{10,... | collective-permute-start | bytes 2359304 | tf_op jit(solution)/shard_map/ppermute | solution.py:33
  78.0 43.8 %collective-permute-start.8 = (bf16[192,2048]{1,0:T(8,128)(2,1)}, bf16[192,2048]{1,0:T(8,128)(2,1)}, u32[]{:S(2)}, u32[]{:S(2)}) collective-permute-start(bf16[192,2048]{1,0:T(8,128)(2,1)} %param.23), channel_id=1, source_target_pairs={{0,3},{1,0},{2,1},{3,2},{4,7},{5,4},{6,5},{7,6},{8,11},{9,8},{10,9... | collective-permute-start | bytes 2359304 | tf_op jit(solution)/shard_map/ppermute | solution.py:33
  94.1 21.1 %collective-permute-start.3 = (bf16[128,192]{1,0:T(8,128)(2,1)S(1)}, bf16[128,192]{1,0:T(8,128)(2,1)S(1)}, u32[]{:S(2)}, u32[]{:S(2)}) collective-permute-start(bf16[128,192]{1,0:T(8,128)(2,1)S(1)} %bitcast.45), channel_id=1, source_target_pairs={{0,1},{1,2},{2,3},{3,0},{4,5},{5,6},{6,7},{7,4},{8,9},{9,10},{10,1... | collective-permute-start | bytes 147464 | tf_op jit(solution)/shard_map/ppermute | solution.py:33
  94.2 29.0 %copy-start.3 = (bf16[192,2048]{1,0:T(8,128)(2,1)S(1)}, bf16[192,2048]{1,0:T(8,128)(2,1)}, u32[]{:S(2)}) copy-start(bf16[192,2048]{1,0:T(8,128)(2,1)} %param.23) | copy-start | bytes 2359300
  94.2 27.6 %collective-permute-start.7 = (bf16[128,192]{1,0:T(8,128)(2,1)S(1)}, bf16[128,192]{1,0:T(8,128)(2,1)S(1)}, u32[]{:S(2)}, u32[]{:S(2)}) collective-permute-start(bf16[128,192]{1,0:T(8,128)(2,1)S(1)} %bitcast.46), channel_id=1, source_target_pairs={{0,3},{1,0},{2,1},{3,2},{4,7},{5,4},{6,5},{7,6},{8,11},{9,8},{10,9... | collective-permute-start | bytes 147464 | tf_op jit(solution)/shard_map/ppermute | solution.py:33
  114.6 5.8 %collective-permute-start.5 = (bf16[128,192]{1,0:T(8,128)(2,1)S(1)}, bf16[128,192]{1,0:T(8,128)(2,1)S(1)}, u32[]{:S(2)}, u32[]{:S(2)}) collective-permute-start(bf16[128,192]{1,0:T(8,128)(2,1)S(1)} %bitcast.47), channel_id=1, source_target_pairs={{0,2},{1,3},{2,0},{3,1},{4,6},{5,7},{6,4},{7,5},{8,10},{9,11},{10,... | collective-permute-start | bytes 147464 | tf_op jit(solution)/shard_map/ppermute | solution.py:33
  123.3 2.1 %copy-start.2 = (bf16[2048,640]{1,0:T(8,128)(2,1)S(1)}, bf16[2048,640]{1,0:T(8,128)(2,1)}, u32[]{:S(2)}) copy-start(bf16[2048,640]{1,0:T(8,128)(2,1)} %param.25) | copy-start | bytes 7864324
  123.3 2.1 %copy-start.4 = (f32[2048]{0:T(1024)S(1)}, f32[2048]{0:T(1024)}, u32[]{:S(2)}) copy-start(f32[2048]{0:T(1024)} %param.24) | copy-start | bytes 24580
  123.8 3.1 %copy-start.1 = (f32[128,2048]{1,0:T(8,128)}, f32[128,2048]{1,0:T(8,128)S(1)}, u32[]{:S(2)}) copy-start(f32[128,2048]{1,0:T(8,128)S(1)} %get-tuple-element.11) | copy-start | bytes 3145732
  123.8 2.4 %copy-start.7 = (bf16[2048,640]{1,0:T(8,128)(2,1)S(1)}, bf16[2048,640]{1,0:T(8,128)(2,1)}, u32[]{:S(2)}) copy-start(bf16[2048,640]{1,0:T(8,128)(2,1)} %param.26) | copy-start | bytes 7864324
  126.9 6.0 %copy-start.9 = (s32[8,8]{1,0:T(8,128)S(1)}, s32[8,8]{1,0:T(8,128)}, u32[]{:S(2)}) copy-start(s32[8,8]{1,0:T(8,128)} %param.18) | copy-start | bytes 772
  127.8 7.7 %collective-permute-start.9 = (bf16[128,512]{1,0:T(8,128)(2,1)S(1)}, bf16[128,512]{1,0:T(8,128)(2,1)S(1)}, u32[]{:S(2)}, u32[]{:S(2)}) collective-permute-start(bf16[128,512]{1,0:T(8,128)(2,1)S(1)} %convolution_convert_fusion.6), channel_id=1, source_target_pairs={{0,1},{1,2},{2,3},{3,0},{4,5},{5,6},{6,7},{7,4},{8,9},{9,10},{10,1... | collective-permute-start | bytes 393224 | tf_op jit(solution)/shard_map/ppermute | solution.py:33
  127.9 7.6 %collective-permute-start.10 = (bf16[128,512]{1,0:T(8,128)(2,1)S(1)}, bf16[128,512]{1,0:T(8,128)(2,1)}, u32[]{:S(2)}, u32[]{:S(2)}) collective-permute-start(bf16[128,512]{1,0:T(8,128)(2,1)S(1)} %convolution_convert_fusion.5), channel_id=1, source_target_pairs={{0,2},{1,3},{2,0},{3,1},{4,6},{5,7},{6,4},{7,5},{8,10},{9,11},{10,... | collective-permute-start | bytes 393224 | tf_op jit(solution)/shard_map/ppermute | solution.py:33
  128.8 7.6 %collective-permute-start.11 = (bf16[128,512]{1,0:T(8,128)(2,1)S(1)}, bf16[128,512]{1,0:T(8,128)(2,1)}, u32[]{:S(2)}, u32[]{:S(2)}) collective-permute-start(bf16[128,512]{1,0:T(8,128)(2,1)S(1)} %convolution_convert_fusion.4), channel_id=1, source_target_pairs={{0,3},{1,0},{2,1},{3,2},{4,7},{5,4},{6,5},{7,6},{8,11},{9,8},{10,9... | collective-permute-start | bytes 393224 | tf_op jit(solution)/shard_map/ppermute | solution.py:33

commit v14 on v13

--- a/solution.py
+++ b/solution.py
@@ -50,39 +50,48 @@
     query_width, group_heads = widths
     slot = pl.program_id(0)
     row = row_ref[0]
+    tokens = row.shape[0]
     cache = cache_ref[0]
-    keys_cache, values_cache = cache[:, :HEAD_DIM], cache[:, HEAD_DIM:]
+    keys_cache = cache[:, :HEAD_DIM].T
+    values_cache = cache[:, HEAD_DIM:]
     fresh = row[:, 2 * query_width :]
-    keys_draft, values_draft = fresh[:, :HEAD_DIM], fresh[:, HEAD_DIM:]
+    keys_draft = fresh[:, :HEAD_DIM].T
+    values_draft = fresh[:, HEAD_DIM:]
     live = lax.broadcasted_iota(jnp.int32, (1, cache.shape[0]), 1) < length_ref[slot]
-    visible = mask_ref[0] > 0.5
+    visible = jnp.concatenate([mask_ref[0]] * group_heads, axis=0) > 0.5
     scale = 1.0 / math.sqrt(HEAD_DIM)
-    contract = (((1,), (1,)), ((), ()))
-
-    def times(part, keys):
-        return lax.dot_general(part, keys, contract, preferred_element_type=jnp.float32)
-
-    outs = []
-    for g in range(group_heads):
-        high = row[:, g * HEAD_DIM : (g + 1) * HEAD_DIM]
-        low = row[:, query_width + g * HEAD_DIM : query_width + (g + 1) * HEAD_DIM]
-        score_cache = (times(high, keys_cache) + times(low, keys_cache)) * scale
-        score_cache = jnp.where(live, score_cache, -jnp.inf)
-        score_draft = (times(high, keys_draft) + times(low, keys_draft)) * scale
-        score_draft = jnp.where(visible, score_draft, -jnp.inf)
-        top = jnp.maximum(
-            jnp.max(score_cache, axis=1, keepdims=True), jnp.max(score_draft, axis=1, keepdims=True)
+
+    def stacked(offset):
+        return jnp.concatenate(
+            [row[:, offset + g * HEAD_DIM : offset + (g + 1) * HEAD_DIM] for g in range(group_heads)],
+            axis=0,
         )
-        weight_cache = jnp.exp(score_cache - top).astype(jnp.bfloat16)
-        weight_draft = jnp.exp(score_draft - top).astype(jnp.bfloat16)
-        numerator = jnp.dot(
-            weight_cache, values_cache, preferred_element_type=jnp.float32
-        ) + jnp.dot(weight_draft, values_draft, preferred_element_type=jnp.float32)
-        denominator = jnp.sum(weight_cache.astype(jnp.float32), axis=1, keepdims=True) + jnp.sum(
-            weight_draft.astype(jnp.float32), axis=1, keepdims=True
-        )
-        outs.append((numerator / denominator).astype(jnp.bfloat16))
-    out_ref[0] = jnp.concatenate(outs, axis=1)
+
+    high, low = stacked(0), stacked(query_width)
+
+    def times(keys):
+        return (
+            jnp.dot(high, keys, preferred_element_type=jnp.float32)
+            + jnp.dot(low, keys, preferred_element_type=jnp.float32)
+        ) * scale
+
+    score_cache = jnp.where(live, times(keys_cache), -jnp.inf)
+    score_draft = jnp.where(visible, times(keys_draft), -jnp.inf)
+    top = jnp.maximum(
+        jnp.max(score_cache, axis=1, keepdims=True), jnp.max(score_draft, axis=1, keepdims=True)
+    )
+    weight_cache = jnp.exp(score_cache - top).astype(jnp.bfloat16)
+    weight_draft = jnp.exp(score_draft - top).astype(jnp.bfloat16)
+    numerator = jnp.dot(weight_cache, values_cache, preferred_element_type=jnp.float32) + jnp.dot(
+        weight_draft, values_draft, preferred_element_type=jnp.float32
+    )
+    denominator = jnp.sum(weight_cache.astype(jnp.float32), axis=1, keepdims=True) + jnp.sum(
+        weight_draft.astype(jnp.float32), axis=1, keepdims=True
+    )
+    attended = (numerator / denominator).astype(jnp.bfloat16)
+    out_ref[0] = jnp.concatenate(
+        [attended[g * tokens : (g + 1) * tokens] for g in range(group_heads)], axis=1
+    )
 
 
 def per_device(

time: 139 us -> 137 us (0.986)
  Pallas kernels: 10.3 us -> 7.46 us
    pallas_call x1, Pallas kernels: 10.3 us -> 7.46 us  [per_device(): pl.pallas_call(functools.partial(attend_kernel, widths=(query_width, grou...]
where the time goes in v14:
time: 137 us; the launch traced here: 136 us
  waiting for transfers between devices  67.8 us (49%)
  starting transfers between devices  35.3 us (26%)
  matrix products  14.2 us (10%)
  local copies, waits for them, and re-layouts  7.94 us (6%)
  Pallas kernels  7.46 us (5%)
  other arithmetic  1.8 us (1%)
    ppermute x12, waiting for transfers between devices, shift_mlp(): lax.ppermute(value, 'mlp', [(i, (i + shift) % count) for i in range(count)])  30.2 us
    all_to_all x1, waiting for transfers between devices, per_device(): incoming = lax.all_to_all(outgoing, 'req', 0, 0, tiled=True)  24.3 us
    ppermute x12, starting transfers between devices, shift_mlp(): lax.ppermute(value, 'mlp', [(i, (i + shift) % count) for i in range(count)])  14.7 us
    all_to_all x1, waiting for transfers between devices, per_device(): arrived = lax.all_to_all(returning, 'req', 0, 0, tiled=True)  13.3 us
    all_to_all x1, starting transfers between devices, per_device(): incoming = lax.all_to_all(outgoing, 'req', 0, 0, tiled=True)  12.4 us
    all_to_all x1, starting transfers between devices, per_device(): arrived = lax.all_to_all(returning, 'req', 0, 0, tiled=True)  8.29 us
    pallas_call x1, Pallas kernels, per_device(): pl.pallas_call(functools.partial(attend_kernel, widths=(query_width, grou...  7.46 us
    dot_general x4, matrix products, per_device(): jnp.dot(piece, rows_of_group, preferred_element_type=jnp.float32)  4.78 us
  transfers between devices with their start and end apart: 14, of which 8 were waited for; matrix products, arithmetic and copies ran while one was open for 8% of the time, Pallas kernels for 0%

profile of v14, /device:TPU:6, one launch (start us, length us, event | category | flops | bytes accessed | tf_op | source)
XLA Modules:
  0.0 135.6 jit_solution(10735711901341440676)
XLA Ops:
  0.7 3.1 %collective-permute-start.2 = (bf16[128,512]{1,0:T(8,128)(2,1)}, bf16[128,512]{1,0:T(8,128)(2,1)S(1)}, u32[]{:S(2)}, u32[]{:S(2)}) collective-permute-start(bf16[128,512]{1,0:T(8,128)(2,1)} %bitcast.49), channel_id=1, source_target_pairs={{0,3},{1,0},{2,1},{3,2},{4,7},{5,4},{6,5},{7,6},{8,11},{9,8},{10,9... | collective-permute-start | bytes 393224 | tf_op jit(solution)/shard_map/ppermute | solution.py:33
  7.2 6.0 %collective-permute-done = bf16[128,512]{1,0:T(8,128)(2,1)S(1)} collective-permute-done((bf16[128,512]{1,0:T(8,128)(2,1)}, bf16[128,512]{1,0:T(8,128)(2,1)S(1)}, u32[]{:S(2)}, u32[]{:S(2)}) %collective-permute-start) | collective-permute-done | bytes 131104 | tf_op jit(solution)/shard_map/ppermute | solution.py:33
  13.5 1.5 %convolution_convert_fusion.8 = bf16[128,128]{0,1:T(8,128)(2,1)S(1)} fusion(bf16[2048,128]{1,0:T(8,128)(2,1)} %param.22, bf16[128,2048]{1,0:T(8,128)(2,1)S(1)} %constant_dynamic-update-slice_fusion, f32[2048]{0:T(1024)} %param.20, f32[128]{0:T(128)S(1)} %add_rsqrt_fusion.1), kind=kOutput, calls=%fused_computation.28 | convolution fusion | flops 68173824 | bytes 1090048 | tf_op jit(solution)/shard_map/dot_general | solution.py:148
  15.0 1.6 %subtract_convert_fusion = (bf16[128,192]{0,1:T(8,128)(2,1)S(1)}, bf16[128,192]{0,1:T(8,128)(2,1)S(1)}) fusion(bf16[2048,192]{0,1:T(8,128)(2,1)} %param.21, bf16[128,2048]{1,0:T(8,128)(2,1)S(1)} %constant_dynamic-update-slice_fusion, f32[2048]{0:T(1024)S(1)} %copy-done.8, f32[128]{0:T(128)S(1)} %add_rsqrt_fusion.1), kind=kOutput, calls=%fused_computation.45 | convolution fusion | flops 101810176 | bytes 1417728 | tf_op jit(solution)/shard_map/dot_general | solution.py:147
  16.8 1.6 %gather_fusion = bf16[64,16,512]{2,1,0:T(8,128)(2,1)} fusion(bf16[8,16,512]{2,1,0:T(8,128)(2,1)S(1)} %bitcast.43, s32[1024]{0:T(1024)S(1)} %pad_clamp_fusion.2), kind=kCustom, calls=%fused_computation | custom fusion | bytes 2097408 | tf_op jit(solution)/shard_map/jit(_take)/gather | solution.py:157
  18.4 12.4 %all-to-all-start = ((bf16[64,16,512]{2,1,0:T(8,128)(2,1)}), bf16[64,16,512]{2,1,0:T(8,128)(2,1)}, u32[]{:S(2)}, u32[]{:S(2)}) async-start(bf16[64,16,512]{2,1,0:T(8,128)(2,1)} %gather_fusion), calls=%async_computation | async-start | bytes 2097152 | tf_op jit(solution)/shard_map/all_to_all | solution.py:158
  33.0 24.3 %all-to-all-done.row_ref = bf16[64,16,512]{2,1,0:T(8,128)(2,1)} async-done(((bf16[64,16,512]{2,1,0:T(8,128)(2,1)}), bf16[64,16,512]{2,1,0:T(8,128)(2,1)}, u32[]{:S(2)}, u32[]{:S(2)}) %all-to-all-start) | async-done | bytes 1048608 | tf_op jit(solution)/shard_map/all_to_all | solution.py:158
  57.3 7.5 %shard_map.149 = bf16[64,16,192]{2,1,0:T(8,128)(2,1)} custom-call(s32[8]{0:T(128)} %and_select_fusion.2.source_ref, s32[8]{0:T(128)} %length_ref.1, bf16[64,16,512]{2,1,0:T(8,128)(2,1)} %all-to-all-done.row_ref, bf16[8,256,128]{2,1,0:T(8,128)(2,1)} %bitcast.44, f32[8,16,16]{2,1,0:T(8,128)} %fusion.11.mask_ref), custom_call_target="tpu_custom_call" | custom-call | tf_op jit(solution)/shard_map/pallas_call | solution.py:183
  64.7 8.3 %all-to-all-start.1 = ((bf16[64,16,192]{2,1,0:T(8,128)(2,1)}), bf16[64,16,192]{2,1,0:T(8,128)(2,1)}, u32[]{:S(2)}, u32[]{:S(2)}) async-start(bf16[64,16,192]{2,1,0:T(8,128)(2,1)} %shard_map.149), calls=%async_computation.1 | async-start | bytes 1048576 | tf_op jit(solution)/shard_map/all_to_all | solution.py:195
  73.1 2.0 %collective-permute-start.6 = (bf16[192,2048]{1,0:T(8,128)(2,1)}, bf16[192,2048]{1,0:T(8,128)(2,1)}, u32[]{:S(2)}, u32[]{:S(2)}) collective-permute-start(bf16[192,2048]{1,0:T(8,128)(2,1)} %param.23), channel_id=1, source_target_pairs={{0,2},{1,3},{2,0},{3,1},{4,6},{5,7},{6,4},{7,5},{8,10},{9,11},{10,... | collective-permute-start | bytes 2359304 | tf_op jit(solution)/shard_map/ppermute | solution.py:33
  75.1 1.2 collective-permute-start.8
  76.4 13.3 %all-to-all-done.1 = bf16[64,16,192]{2,1,0:T(8,128)(2,1)} async-done(((bf16[64,16,192]{2,1,0:T(8,128)(2,1)}), bf16[64,16,192]{2,1,0:T(8,128)(2,1)}, u32[]{:S(2)}, u32[]{:S(2)}) %all-to-all-start.1) | async-done | bytes 393248 | tf_op jit(solution)/shard_map/all_to_all | solution.py:195
  89.6 1.6 %gather_fusion.1 = bf16[8,16,192]{2,1,0:T(8,128)(2,1)S(1)} fusion(bf16[64,16,192]{2,1,0:T(8,128)(2,1)} %all-to-all-done.1, s32[1024]{0:T(1024)S(1)} %pad_clamp_fusion.1), kind=kCustom, calls=%fused_computation.1 | custom fusion | bytes 98336 | tf_op jit(solution)/shard_map/jit(_take)/gather | solution.py:196
  91.4 3.2 %collective-permute-start.7 = (bf16[128,192]{1,0:T(8,128)(2,1)S(1)}, bf16[128,192]{1,0:T(8,128)(2,1)S(1)}, u32[]{:S(2)}, u32[]{:S(2)}) collective-permute-start(bf16[128,192]{1,0:T(8,128)(2,1)S(1)} %bitcast.46), channel_id=1, source_target_pairs={{0,3},{1,0},{2,1},{3,2},{4,7},{5,4},{6,5},{7,6},{8,11},{9,8},{10,9... | collective-permute-start | bytes 147464 | tf_op jit(solution)/shard_map/ppermute | solution.py:33
  94.6 17.1 %collective-permute-done.4 = bf16[192,2048]{1,0:T(8,128)(2,1)} collective-permute-done((bf16[192,2048]{1,0:T(8,128)(2,1)}, bf16[192,2048]{1,0:T(8,128)(2,1)}, u32[]{:S(2)}, u32[]{:S(2)}) %collective-permute-start.4) | collective-permute-done | bytes 786464 | tf_op jit(solution)/shard_map/ppermute | solution.py:33
  112.3 1.4 %fusion.2 = f32[128,2048]{1,0:T(8,128)S(1)} fusion(bf16[128,192]{1,0:T(8,128)(2,1)S(1)} %collective-permute-done.3, bf16[192,2048]{1,0:T(8,128)(2,1)} %collective-permute-done.4), kind=kOutput, calls=%fused_computation.8 | convolution fusion | flops 101187584 | bytes 1884160 | tf_op jit(solution)/shard_map/dot_general | solution.py:202
  113.8 3.7 %collective-permute-done.5 = bf16[128,192]{1,0:T(8,128)(2,1)S(1)} collective-permute-done((bf16[128,192]{1,0:T(8,128)(2,1)S(1)}, bf16[128,192]{1,0:T(8,128)(2,1)S(1)}, u32[]{:S(2)}, u32[]{:S(2)}) %collective-permute-start.5) | collective-permute-done | bytes 49184 | tf_op jit(solution)/shard_map/ppermute | solution.py:33
  117.5 1.4 %fusion.1 = f32[128,2048]{1,0:T(8,128)S(1)} fusion(bf16[128,192]{1,0:T(8,128)(2,1)S(1)} %collective-permute-done.5, bf16[192,2048]{1,0:T(8,128)(2,1)} %collective-permute-done.6), kind=kOutput, calls=%fused_computation.6 | convolution fusion | flops 101187584 | bytes 1884160 | tf_op jit(solution)/shard_map/dot_general | solution.py:202
  119.0 1.4 %fusion = f32[128,2048]{1,0:T(8,128)S(1)} fusion(bf16[128,192]{1,0:T(8,128)(2,1)S(1)} %collective-permute-done.7, bf16[192,2048]{1,0:T(8,128)(2,1)} %collective-permute-done.8), kind=kOutput, calls=%fused_computation.4 | convolution fusion | flops 101187584 | bytes 1884160 | tf_op jit(solution)/shard_map/dot_general | solution.py:202
  121.0 1.6 %copy-done.2 = bf16[2048,640]{1,0:T(8,128)(2,1)S(1)} copy-done((bf16[2048,640]{1,0:T(8,128)(2,1)S(1)}, bf16[2048,640]{1,0:T(8,128)(2,1)}, u32[]{:S(2)}) %copy-start.2) | copy-done | bytes 2621464
  126.0 2.2 %collective-permute-start.11 = (bf16[128,512]{1,0:T(8,128)(2,1)S(1)}, bf16[128,512]{1,0:T(8,128)(2,1)}, u32[]{:S(2)}, u32[]{:S(2)}) collective-permute-start(bf16[128,512]{1,0:T(8,128)(2,1)S(1)} %convolution_convert_fusion.4), channel_id=1, source_target_pairs={{0,3},{1,0},{2,1},{3,2},{4,7},{5,4},{6,5},{7,6},{8,11},{9,8},{10,9... | collective-permute-start | bytes 393224 | tf_op jit(solution)/shard_map/ppermute | solution.py:33
  128.2 1.8 %gather_fusion.2 = bf16[8,16,512]{2,1,0:T(8,128)(2,1)S(1)} fusion(bf16[64,16,512]{2,1,0:T(8,128)(2,1)} %all-to-all-done.row_ref, s32[1024]{0:T(1024)S(1)} %pad_clamp_fusion), kind=kCustom, calls=%fused_computation.2 | custom fusion | bytes 262176 | tf_op jit(solution)/shard_map/jit(_take)/gather | solution.py:159
  130.8 1.7 %collective-permute-done.9 = bf16[128,512]{1,0:T(8,128)(2,1)S(1)} collective-permute-done((bf16[128,512]{1,0:T(8,128)(2,1)S(1)}, bf16[128,512]{1,0:T(8,128)(2,1)S(1)}, u32[]{:S(2)}, u32[]{:S(2)}) %collective-permute-start.9) | collective-permute-done | bytes 131104 | tf_op jit(solution)/shard_map/ppermute | solution.py:33
  133.6 2.0 %add_convert_fusion = bf16[128,512]{1,0:T(8,128)(2,1)} fusion(bf16[128,512]{1,0:T(8,128)(2,1)} %collective-permute-done.11, bf16[128,512]{1,0:T(8,128)(2,1)} %collective-permute-done.10, bf16[128,512]{1,0:T(8,128)(2,1)S(1)} %collective-permute-done.9, f32[128,2048]{1,0:T(8,128)} %copy-done.1, s32[]{:T(128)S(6)} %select_n.90, ...), kind=kOutput, calls=%fused_computation.42 | convolution fusion | flops 84541440 | bytes 1606656 | tf_op jit(solution)/shard_map/dot_general | solution.py:215
  (65 shorter events, 12.5 us)
Async XLA Ops:
  0.6 123.4 %copy-start = (bf16[640,2048]{1,0:T(8,128)(2,1)S(1)}, bf16[640,2048]{1,0:T(8,128)(2,1)}, u32[]{:S(2)}) copy-start(bf16[640,2048]{1,0:T(8,128)(2,1)} %param.27) | copy-start | bytes 7864324
  0.6 14.3 %copy-start.8 = (f32[2048]{0:T(1024)S(1)}, f32[2048]{0:T(1024)}, u32[]{:S(2)}) copy-start(f32[2048]{0:T(1024)} %param.20) | copy-start | bytes 24580
  0.7 12.6 %collective-permute-start.2 = (bf16[128,512]{1,0:T(8,128)(2,1)}, bf16[128,512]{1,0:T(8,128)(2,1)S(1)}, u32[]{:S(2)}, u32[]{:S(2)}) collective-permute-start(bf16[128,512]{1,0:T(8,128)(2,1)} %bitcast.49), channel_id=1, source_target_pairs={{0,3},{1,0},{2,1},{3,2},{4,7},{5,4},{6,5},{7,6},{8,11},{9,8},{10,9... | collective-permute-start | bytes 393224 | tf_op jit(solution)/shard_map/ppermute | solution.py:33
  3.7 9.5 %collective-permute-start.1 = (bf16[128,512]{1,0:T(8,128)(2,1)}, bf16[128,512]{1,0:T(8,128)(2,1)S(1)}, u32[]{:S(2)}, u32[]{:S(2)}) collective-permute-start(bf16[128,512]{1,0:T(8,128)(2,1)} %bitcast.50), channel_id=1, source_target_pairs={{0,2},{1,3},{2,0},{3,1},{4,6},{5,7},{6,4},{7,5},{8,10},{9,11},{10,... | collective-permute-start | bytes 393224 | tf_op jit(solution)/shard_map/ppermute | solution.py:33
  4.4 8.9 %collective-permute-start = (bf16[128,512]{1,0:T(8,128)(2,1)}, bf16[128,512]{1,0:T(8,128)(2,1)S(1)}, u32[]{:S(2)}, u32[]{:S(2)}) collective-permute-start(bf16[128,512]{1,0:T(8,128)(2,1)} %bitcast.51), channel_id=1, source_target_pairs={{0,1},{1,2},{2,3},{3,0},{4,5},{5,6},{6,7},{7,4},{8,9},{9,10},{10,1... | collective-permute-start | bytes 393224 | tf_op jit(solution)/shard_map/ppermute | solution.py:33
  16.6 14.2 %copy-start.6 = (s32[512]{0:T(512)S(1)}, s32[512]{0:T(512)}, u32[]{:S(2)}) copy-start(s32[512]{0:T(512)} %param.15) | copy-start | bytes 6148
  16.6 14.9 %copy-start.5 = (s32[8,16]{1,0:T(8,128)S(1)}, s32[8,16]{1,0:T(8,128)}, u32[]{:S(2)}) copy-start(s32[8,16]{1,0:T(8,128)} %param.17) | copy-start | bytes 1540
  18.4 38.9 %all-to-all-start = ((bf16[64,16,512]{2,1,0:T(8,128)(2,1)}), bf16[64,16,512]{2,1,0:T(8,128)(2,1)}, u32[]{:S(2)}, u32[]{:S(2)}) async-start(bf16[64,16,512]{2,1,0:T(8,128)(2,1)} %gather_fusion), calls=%async_computation | async-start | bytes 2097152 | tf_op jit(solution)/shard_map/all_to_all | solution.py:158
  64.7 24.9 %all-to-all-start.1 = ((bf16[64,16,192]{2,1,0:T(8,128)(2,1)}), bf16[64,16,192]{2,1,0:T(8,128)(2,1)}, u32[]{:S(2)}, u32[]{:S(2)}) async-start(bf16[64,16,192]{2,1,0:T(8,128)(2,1)} %shard_map.149), calls=%async_computation.1 | async-start | bytes 1048576 | tf_op jit(solution)/shard_map/all_to_all | solution.py:195
  73.0 38.7 %collective-permute-start.4 = (bf16[192,2048]{1,0:T(8,128)(2,1)}, bf16[192,2048]{1,0:T(8,128)(2,1)}, u32[]{:S(2)}, u32[]{:S(2)}) collective-permute-start(bf16[192,2048]{1,0:T(8,128)(2,1)} %param.23), channel_id=1, source_target_pairs={{0,1},{1,2},{2,3},{3,0},{4,5},{5,6},{6,7},{7,4},{8,9},{9,10},{10,1... | collective-permute-start | bytes 2359304 | tf_op jit(solution)/shard_map/ppermute | solution.py:33
  73.1 40.7 %collective-permute-start.6 = (bf16[192,2048]{1,0:T(8,128)(2,1)}, bf16[192,2048]{1,0:T(8,128)(2,1)}, u32[]{:S(2)}, u32[]{:S(2)}) collective-permute-start(bf16[192,2048]{1,0:T(8,128)(2,1)} %param.23), channel_id=1, source_target_pairs={{0,2},{1,3},{2,0},{3,1},{4,6},{5,7},{6,4},{7,5},{8,10},{9,11},{10,... | collective-permute-start | bytes 2359304 | tf_op jit(solution)/shard_map/ppermute | solution.py:33
  75.1 43.8 %collective-permute-start.8 = (bf16[192,2048]{1,0:T(8,128)(2,1)}, bf16[192,2048]{1,0:T(8,128)(2,1)}, u32[]{:S(2)}, u32[]{:S(2)}) collective-permute-start(bf16[192,2048]{1,0:T(8,128)(2,1)} %param.23), channel_id=1, source_target_pairs={{0,3},{1,0},{2,1},{3,2},{4,7},{5,4},{6,5},{7,6},{8,11},{9,8},{10,9... | collective-permute-start | bytes 2359304 | tf_op jit(solution)/shard_map/ppermute | solution.py:33
  91.2 21.1 %collective-permute-start.3 = (bf16[128,192]{1,0:T(8,128)(2,1)S(1)}, bf16[128,192]{1,0:T(8,128)(2,1)S(1)}, u32[]{:S(2)}, u32[]{:S(2)}) collective-permute-start(bf16[128,192]{1,0:T(8,128)(2,1)S(1)} %bitcast.45), channel_id=1, source_target_pairs={{0,1},{1,2},{2,3},{3,0},{4,5},{5,6},{6,7},{7,4},{8,9},{9,10},{10,1... | collective-permute-start | bytes 147464 | tf_op jit(solution)/shard_map/ppermute | solution.py:33
  91.4 29.0 %copy-start.3 = (bf16[192,2048]{1,0:T(8,128)(2,1)S(1)}, bf16[192,2048]{1,0:T(8,128)(2,1)}, u32[]{:S(2)}) copy-start(bf16[192,2048]{1,0:T(8,128)(2,1)} %param.23) | copy-start | bytes 2359300
  91.4 27.6 %collective-permute-start.7 = (bf16[128,192]{1,0:T(8,128)(2,1)S(1)}, bf16[128,192]{1,0:T(8,128)(2,1)S(1)}, u32[]{:S(2)}, u32[]{:S(2)}) collective-permute-start(bf16[128,192]{1,0:T(8,128)(2,1)S(1)} %bitcast.46), channel_id=1, source_target_pairs={{0,3},{1,0},{2,1},{3,2},{4,7},{5,4},{6,5},{7,6},{8,11},{9,8},{10,9... | collective-permute-start | bytes 147464 | tf_op jit(solution)/shard_map/ppermute | solution.py:33
  111.8 5.8 %collective-permute-start.5 = (bf16[128,192]{1,0:T(8,128)(2,1)S(1)}, bf16[128,192]{1,0:T(8,128)(2,1)S(1)}, u32[]{:S(2)}, u32[]{:S(2)}) collective-permute-start(bf16[128,192]{1,0:T(8,128)(2,1)S(1)} %bitcast.47), channel_id=1, source_target_pairs={{0,2},{1,3},{2,0},{3,1},{4,6},{5,7},{6,4},{7,5},{8,10},{9,11},{10,... | collective-permute-start | bytes 147464 | tf_op jit(solution)/shard_map/ppermute | solution.py:33
  120.4 2.1 %copy-start.2 = (bf16[2048,640]{1,0:T(8,128)(2,1)S(1)}, bf16[2048,640]{1,0:T(8,128)(2,1)}, u32[]{:S(2)}) copy-start(bf16[2048,640]{1,0:T(8,128)(2,1)} %param.25) | copy-start | bytes 7864324
  120.4 2.1 %copy-start.4 = (f32[2048]{0:T(1024)S(1)}, f32[2048]{0:T(1024)}, u32[]{:S(2)}) copy-start(f32[2048]{0:T(1024)} %param.24) | copy-start | bytes 24580
  120.9 3.1 %copy-start.1 = (f32[128,2048]{1,0:T(8,128)}, f32[128,2048]{1,0:T(8,128)S(1)}, u32[]{:S(2)}) copy-start(f32[128,2048]{1,0:T(8,128)S(1)} %get-tuple-element.11) | copy-start | bytes 3145732
  121.0 2.4 %copy-start.7 = (bf16[2048,640]{1,0:T(8,128)(2,1)S(1)}, bf16[2048,640]{1,0:T(8,128)(2,1)}, u32[]{:S(2)}) copy-start(bf16[2048,640]{1,0:T(8,128)(2,1)} %param.26) | copy-start | bytes 7864324
  124.0 6.0 %copy-start.9 = (s32[8,8]{1,0:T(8,128)S(1)}, s32[8,8]{1,0:T(8,128)}, u32[]{:S(2)}) copy-start(s32[8,8]{1,0:T(8,128)} %param.18) | copy-start | bytes 772
  124.9 7.7 %collective-permute-start.9 = (bf16[128,512]{1,0:T(8,128)(2,1)S(1)}, bf16[128,512]{1,0:T(8,128)(2,1)S(1)}, u32[]{:S(2)}, u32[]{:S(2)}) collective-permute-start(bf16[128,512]{1,0:T(8,128)(2,1)S(1)} %convolution_convert_fusion.6), channel_id=1, source_target_pairs={{0,1},{1,2},{2,3},{3,0},{4,5},{5,6},{6,7},{7,4},{8,9},{9,10},{10,1... | collective-permute-start | bytes 393224 | tf_op jit(solution)/shard_map/ppermute | solution.py:33
  125.0 7.6 %collective-permute-start.10 = (bf16[128,512]{1,0:T(8,128)(2,1)S(1)}, bf16[128,512]{1,0:T(8,128)(2,1)}, u32[]{:S(2)}, u32[]{:S(2)}) collective-permute-start(bf16[128,512]{1,0:T(8,128)(2,1)S(1)} %convolution_convert_fusion.5), channel_id=1, source_target_pairs={{0,2},{1,3},{2,0},{3,1},{4,6},{5,7},{6,4},{7,5},{8,10},{9,11},{10,... | collective-permute-start | bytes 393224 | tf_op jit(solution)/shard_map/ppermute | solution.py:33
  126.0 7.6 %collective-permute-start.11 = (bf16[128,512]{1,0:T(8,128)(2,1)S(1)}, bf16[128,512]{1,0:T(8,128)(2,1)}, u32[]{:S(2)}, u32[]{:S(2)}) collective-permute-start(bf16[128,512]{1,0:T(8,128)(2,1)S(1)} %convolution_convert_fusion.4), channel_id=1, source_target_pairs={{0,3},{1,0},{2,1},{3,2},{4,7},{5,4},{6,5},{7,6},{8,11},{9,8},{10,9... | collective-permute-start | bytes 393224 | tf_op jit(solution)/shard_map/ppermute | solution.py:33

commit v15 on v14

--- a/solution.py
+++ b/solution.py
@@ -47,18 +47,23 @@
 
 
 def attend_kernel(source_ref, length_ref, row_ref, cache_ref, mask_ref, out_ref, *, widths):
+    for slot in range(cache_ref.shape[0]):
+        attend_slot(source_ref, length_ref, row_ref, cache_ref, mask_ref, out_ref, slot, widths)
+
+
+def attend_slot(source_ref, length_ref, row_ref, cache_ref, mask_ref, out_ref, slot, widths):
     query_width, group_heads = widths
-    slot = pl.program_id(0)
-    row = row_ref[0]
+    source = source_ref[slot]
+    row = row_ref[source]
     tokens = row.shape[0]
-    cache = cache_ref[0]
+    cache = cache_ref[slot]
     keys_cache = cache[:, :HEAD_DIM].T
     values_cache = cache[:, HEAD_DIM:]
     fresh = row[:, 2 * query_width :]
     keys_draft = fresh[:, :HEAD_DIM].T
     values_draft = fresh[:, HEAD_DIM:]
     live = lax.broadcasted_iota(jnp.int32, (1, cache.shape[0]), 1) < length_ref[slot]
-    visible = jnp.concatenate([mask_ref[0]] * group_heads, axis=0) > 0.5
+    visible = jnp.concatenate([mask_ref[slot]] * group_heads, axis=0) > 0.5
     scale = 1.0 / math.sqrt(HEAD_DIM)
 
     def stacked(offset):
@@ -89,7 +94,7 @@
         weight_draft.astype(jnp.float32), axis=1, keepdims=True
     )
     attended = (numerator / denominator).astype(jnp.bfloat16)
-    out_ref[0] = jnp.concatenate(
+    out_ref[source] = jnp.concatenate(
         [attended[g * tokens : (g + 1) * tokens] for g in range(group_heads)], axis=1
     )
 
@@ -172,13 +177,13 @@
     cache_len = cached_key_value.shape[1]
     grid_spec = pltpu.PrefetchScalarGridSpec(
         num_scalar_prefetch=2,
-        grid=(per_owner_rows,),
+        grid=(1,),
         in_specs=[
-            pl.BlockSpec((1, tokens, incoming.shape[2]), lambda j, src, lens: (src[j], 0, 0)),
-            pl.BlockSpec((1, cache_len, 2 * HEAD_DIM), lambda j, src, lens: (j, 0, 0)),
-            pl.BlockSpec((1, tokens, tokens), lambda j, src, lens: (j, 0, 0)),
+            pl.BlockSpec(incoming.shape, lambda j, src, lens: (0, 0, 0)),
+            pl.BlockSpec((per_owner_rows, cache_len, 2 * HEAD_DIM), lambda j, src, lens: (0, 0, 0)),
+            pl.BlockSpec((per_owner_rows, tokens, tokens), lambda j, src, lens: (0, 0, 0)),
         ],
-        out_specs=pl.BlockSpec((1, tokens, head_width), lambda j, src, lens: (src[j], 0, 0)),
+        out_specs=pl.BlockSpec((req_count, tokens, head_width), lambda j, src, lens: (0, 0, 0)),
     )
     returning = pl.pallas_call(
         functools.partial(attend_kernel, widths=(query_width, group_heads)),

time: 137 us -> 134 us (0.978)
  Pallas kernels: 7.46 us -> 5.66 us
    pallas_call x1, Pallas kernels: 7.46 us -> 5.66 us  [per_device(): pl.pallas_call(functools.partial(attend_kernel, widths=(query_width, grou...]
where the time goes in v15:
time: 134 us
  waiting for transfers between devices  67.8 us (51%)
  starting transfers between devices  35.3 us (26%)
  matrix products  14.2 us (11%)
  local copies, waits for them, and re-layouts  7.93 us (6%)
  Pallas kernels  5.66 us (4%)
  other arithmetic  1.8 us (1%)
    ppermute x12, waiting for transfers between devices, shift_mlp(): lax.ppermute(value, 'mlp', [(i, (i + shift) % count) for i in range(count)])  30.2 us
    all_to_all x1, waiting for transfers between devices, per_device(): incoming = lax.all_to_all(outgoing, 'req', 0, 0, tiled=True)  24.3 us
    ppermute x12, starting transfers between devices, shift_mlp(): lax.ppermute(value, 'mlp', [(i, (i + shift) % count) for i in range(count)])  14.7 us
    all_to_all x1, waiting for transfers between devices, per_device(): arrived = lax.all_to_all(returning, 'req', 0, 0, tiled=True)  13.3 us
    all_to_all x1, starting transfers between devices, per_device(): incoming = lax.all_to_all(outgoing, 'req', 0, 0, tiled=True)  12.4 us
    all_to_all x1, starting transfers between devices, per_device(): arrived = lax.all_to_all(returning, 'req', 0, 0, tiled=True)  8.28 us
    pallas_call x1, Pallas kernels, per_device(): pl.pallas_call(functools.partial(attend_kernel, widths=(query_width, grou...  5.66 us
    dot_general x4, matrix products, per_device(): jnp.dot(piece, rows_of_group, preferred_element_type=jnp.float32)  4.78 us
  transfers between devices with their start and end apart: 14, of which 8 were waited for; matrix products, arithmetic and copies ran while one was open for 8% of the time, Pallas kernels for 0%

profile of v15, /device:TPU:6, one launch (start us, length us, event | category | flops | bytes accessed | tf_op | source)
XLA Modules:
  0.0 133.8 jit_solution(3542812573820917861)
XLA Ops:
  0.7 3.1 %collective-permute-start.2 = (bf16[128,512]{1,0:T(8,128)(2,1)}, bf16[128,512]{1,0:T(8,128)(2,1)S(1)}, u32[]{:S(2)}, u32[]{:S(2)}) collective-permute-start(bf16[128,512]{1,0:T(8,128)(2,1)} %bitcast.49), channel_id=1, source_target_pairs={{0,3},{1,0},{2,1},{3,2},{4,7},{5,4},{6,5},{7,6},{8,11},{9,8},{10,9... | collective-permute-start | bytes 393224 | tf_op jit(solution)/shard_map/ppermute | solution.py:33
  7.2 6.0 %collective-permute-done = bf16[128,512]{1,0:T(8,128)(2,1)S(1)} collective-permute-done((bf16[128,512]{1,0:T(8,128)(2,1)}, bf16[128,512]{1,0:T(8,128)(2,1)S(1)}, u32[]{:S(2)}, u32[]{:S(2)}) %collective-permute-start) | collective-permute-done | bytes 131104 | tf_op jit(solution)/shard_map/ppermute | solution.py:33
  13.5 1.5 %convolution_convert_fusion.8 = bf16[128,128]{0,1:T(8,128)(2,1)S(1)} fusion(bf16[2048,128]{1,0:T(8,128)(2,1)} %param.22, bf16[128,2048]{1,0:T(8,128)(2,1)S(1)} %constant_dynamic-update-slice_fusion, f32[2048]{0:T(1024)} %param.20, f32[128]{0:T(128)S(1)} %add_rsqrt_fusion.1), kind=kOutput, calls=%fused_computation.28 | convolution fusion | flops 68173824 | bytes 1090048 | tf_op jit(solution)/shard_map/dot_general | solution.py:153
  15.0 1.6 %subtract_convert_fusion = (bf16[128,192]{0,1:T(8,128)(2,1)S(1)}, bf16[128,192]{0,1:T(8,128)(2,1)S(1)}) fusion(bf16[2048,192]{0,1:T(8,128)(2,1)} %param.21, bf16[128,2048]{1,0:T(8,128)(2,1)S(1)} %constant_dynamic-update-slice_fusion, f32[2048]{0:T(1024)S(1)} %copy-done.8, f32[128]{0:T(128)S(1)} %add_rsqrt_fusion.1), kind=kOutput, calls=%fused_computation.45 | convolution fusion | flops 101810176 | bytes 1417728 | tf_op jit(solution)/shard_map/dot_general | solution.py:152
  16.8 1.6 %gather_fusion = bf16[64,16,512]{2,1,0:T(8,128)(2,1)} fusion(bf16[8,16,512]{2,1,0:T(8,128)(2,1)S(1)} %bitcast.43, s32[1024]{0:T(1024)S(1)} %pad_clamp_fusion.2), kind=kCustom, calls=%fused_computation | custom fusion | bytes 2097408 | tf_op jit(solution)/shard_map/jit(_take)/gather | solution.py:162
  18.4 12.4 %all-to-all-start = ((bf16[64,16,512]{2,1,0:T(8,128)(2,1)}), bf16[64,16,512]{2,1,0:T(8,128)(2,1)}, u32[]{:S(2)}, u32[]{:S(2)}) async-start(bf16[64,16,512]{2,1,0:T(8,128)(2,1)} %gather_fusion), calls=%async_computation | async-start | bytes 2097152 | tf_op jit(solution)/shard_map/all_to_all | solution.py:163
  33.0 24.3 %all-to-all-done.row_ref = bf16[64,16,512]{2,1,0:T(8,128)(2,1)} async-done(((bf16[64,16,512]{2,1,0:T(8,128)(2,1)}), bf16[64,16,512]{2,1,0:T(8,128)(2,1)}, u32[]{:S(2)}, u32[]{:S(2)}) %all-to-all-start) | async-done | bytes 1048608 | tf_op jit(solution)/shard_map/all_to_all | solution.py:163
  57.3 5.7 %shard_map.149 = bf16[64,16,192]{2,1,0:T(8,128)(2,1)} custom-call(s32[8]{0:T(128)} %and_select_fusion.2.source_ref, s32[8]{0:T(128)} %length_ref.1, bf16[64,16,512]{2,1,0:T(8,128)(2,1)} %all-to-all-done.row_ref, bf16[8,256,128]{2,1,0:T(8,128)(2,1)} %bitcast.44, f32[8,16,16]{2,1,0:T(8,128)} %fusion.11.mask_ref), custom_call_target="tpu_custom_call" | custom-call | tf_op jit(solution)/shard_map/pallas_call | solution.py:188
  62.9 8.3 %all-to-all-start.1 = ((bf16[64,16,192]{2,1,0:T(8,128)(2,1)}), bf16[64,16,192]{2,1,0:T(8,128)(2,1)}, u32[]{:S(2)}, u32[]{:S(2)}) async-start(bf16[64,16,192]{2,1,0:T(8,128)(2,1)} %shard_map.149), calls=%async_computation.1 | async-start | bytes 1048576 | tf_op jit(solution)/shard_map/all_to_all | solution.py:200
  71.3 2.0 %collective-permute-start.6 = (bf16[192,2048]{1,0:T(8,128)(2,1)}, bf16[192,2048]{1,0:T(8,128)(2,1)}, u32[]{:S(2)}, u32[]{:S(2)}) collective-permute-start(bf16[192,2048]{1,0:T(8,128)(2,1)} %param.23), channel_id=1, source_target_pairs={{0,2},{1,3},{2,0},{3,1},{4,6},{5,7},{6,4},{7,5},{8,10},{9,11},{10,... | collective-permute-start | bytes 2359304 | tf_op jit(solution)/shard_map/ppermute | solution.py:33
  73.3 1.2 collective-permute-start.8
  74.6 13.3 %all-to-all-done.1 = bf16[64,16,192]{2,1,0:T(8,128)(2,1)} async-done(((bf16[64,16,192]{2,1,0:T(8,128)(2,1)}), bf16[64,16,192]{2,1,0:T(8,128)(2,1)}, u32[]{:S(2)}, u32[]{:S(2)}) %all-to-all-start.1) | async-done | bytes 393248 | tf_op jit(solution)/shard_map/all_to_all | solution.py:200
  87.8 1.6 %gather_fusion.1 = bf16[8,16,192]{2,1,0:T(8,128)(2,1)S(1)} fusion(bf16[64,16,192]{2,1,0:T(8,128)(2,1)} %all-to-all-done.1, s32[1024]{0:T(1024)S(1)} %pad_clamp_fusion.1), kind=kCustom, calls=%fused_computation.1 | custom fusion | bytes 98336 | tf_op jit(solution)/shard_map/jit(_take)/gather | solution.py:201
  89.6 3.2 %collective-permute-start.7 = (bf16[128,192]{1,0:T(8,128)(2,1)S(1)}, bf16[128,192]{1,0:T(8,128)(2,1)S(1)}, u32[]{:S(2)}, u32[]{:S(2)}) collective-permute-start(bf16[128,192]{1,0:T(8,128)(2,1)S(1)} %bitcast.46), channel_id=1, source_target_pairs={{0,3},{1,0},{2,1},{3,2},{4,7},{5,4},{6,5},{7,6},{8,11},{9,8},{10,9... | collective-permute-start | bytes 147464 | tf_op jit(solution)/shard_map/ppermute | solution.py:33
  92.8 17.1 %collective-permute-done.4 = bf16[192,2048]{1,0:T(8,128)(2,1)} collective-permute-done((bf16[192,2048]{1,0:T(8,128)(2,1)}, bf16[192,2048]{1,0:T(8,128)(2,1)}, u32[]{:S(2)}, u32[]{:S(2)}) %collective-permute-start.4) | collective-permute-done | bytes 786464 | tf_op jit(solution)/shard_map/ppermute | solution.py:33
  110.5 1.4 %fusion.2 = f32[128,2048]{1,0:T(8,128)S(1)} fusion(bf16[128,192]{1,0:T(8,128)(2,1)S(1)} %collective-permute-done.3, bf16[192,2048]{1,0:T(8,128)(2,1)} %collective-permute-done.4), kind=kOutput, calls=%fused_computation.8 | convolution fusion | flops 101187584 | bytes 1884160 | tf_op jit(solution)/shard_map/dot_general | solution.py:207
  112.0 3.7 %collective-permute-done.5 = bf16[128,192]{1,0:T(8,128)(2,1)S(1)} collective-permute-done((bf16[128,192]{1,0:T(8,128)(2,1)S(1)}, bf16[128,192]{1,0:T(8,128)(2,1)S(1)}, u32[]{:S(2)}, u32[]{:S(2)}) %collective-permute-start.5) | collective-permute-done | bytes 49184 | tf_op jit(solution)/shard_map/ppermute | solution.py:33
  115.7 1.4 %fusion.1 = f32[128,2048]{1,0:T(8,128)S(1)} fusion(bf16[128,192]{1,0:T(8,128)(2,1)S(1)} %collective-permute-done.5, bf16[192,2048]{1,0:T(8,128)(2,1)} %collective-permute-done.6), kind=kOutput, calls=%fused_computation.6 | convolution fusion | flops 101187584 | bytes 1884160 | tf_op jit(solution)/shard_map/dot_general | solution.py:207
  117.2 1.4 %fusion = f32[128,2048]{1,0:T(8,128)S(1)} fusion(bf16[128,192]{1,0:T(8,128)(2,1)S(1)} %collective-permute-done.7, bf16[192,2048]{1,0:T(8,128)(2,1)} %collective-permute-done.8), kind=kOutput, calls=%fused_computation.4 | convolution fusion | flops 101187584 | bytes 1884160 | tf_op jit(solution)/shard_map/dot_general | solution.py:207
  119.2 1.6 %copy-done.2 = bf16[2048,640]{1,0:T(8,128)(2,1)S(1)} copy-done((bf16[2048,640]{1,0:T(8,128)(2,1)S(1)}, bf16[2048,640]{1,0:T(8,128)(2,1)}, u32[]{:S(2)}) %copy-start.2) | copy-done | bytes 2621464
  124.2 2.2 %collective-permute-start.11 = (bf16[128,512]{1,0:T(8,128)(2,1)S(1)}, bf16[128,512]{1,0:T(8,128)(2,1)}, u32[]{:S(2)}, u32[]{:S(2)}) collective-permute-start(bf16[128,512]{1,0:T(8,128)(2,1)S(1)} %convolution_convert_fusion.4), channel_id=1, source_target_pairs={{0,3},{1,0},{2,1},{3,2},{4,7},{5,4},{6,5},{7,6},{8,11},{9,8},{10,9... | collective-permute-start | bytes 393224 | tf_op jit(solution)/shard_map/ppermute | solution.py:33
  126.4 1.8 %gather_fusion.2 = bf16[8,16,512]{2,1,0:T(8,128)(2,1)S(1)} fusion(bf16[64,16,512]{2,1,0:T(8,128)(2,1)} %all-to-all-done.row_ref, s32[1024]{0:T(1024)S(1)} %pad_clamp_fusion), kind=kCustom, calls=%fused_computation.2 | custom fusion | bytes 262176 | tf_op jit(solution)/shard_map/jit(_take)/gather | solution.py:164
  129.0 1.7 %collective-permute-done.9 = bf16[128,512]{1,0:T(8,128)(2,1)S(1)} collective-permute-done((bf16[128,512]{1,0:T(8,128)(2,1)S(1)}, bf16[128,512]{1,0:T(8,128)(2,1)S(1)}, u32[]{:S(2)}, u32[]{:S(2)}) %collective-permute-start.9) | collective-permute-done | bytes 131104 | tf_op jit(solution)/shard_map/ppermute | solution.py:33
  131.8 2.0 %add_convert_fusion = bf16[128,512]{1,0:T(8,128)(2,1)} fusion(bf16[128,512]{1,0:T(8,128)(2,1)} %collective-permute-done.11, bf16[128,512]{1,0:T(8,128)(2,1)} %collective-permute-done.10, bf16[128,512]{1,0:T(8,128)(2,1)S(1)} %collective-permute-done.9, f32[128,2048]{1,0:T(8,128)} %copy-done.1, s32[]{:T(128)S(6)} %select_n.90, ...), kind=kOutput, calls=%fused_computation.42 | convolution fusion | flops 84541440 | bytes 1606656 | tf_op jit(solution)/shard_map/dot_general | solution.py:220
  (65 shorter events, 12.5 us)
Async XLA Ops:
  0.6 121.6 %copy-start = (bf16[640,2048]{1,0:T(8,128)(2,1)S(1)}, bf16[640,2048]{1,0:T(8,128)(2,1)}, u32[]{:S(2)}) copy-start(bf16[640,2048]{1,0:T(8,128)(2,1)} %param.27) | copy-start | bytes 7864324
  0.6 14.3 %copy-start.8 = (f32[2048]{0:T(1024)S(1)}, f32[2048]{0:T(1024)}, u32[]{:S(2)}) copy-start(f32[2048]{0:T(1024)} %param.20) | copy-start | bytes 24580
  0.7 12.6 %collective-permute-start.2 = (bf16[128,512]{1,0:T(8,128)(2,1)}, bf16[128,512]{1,0:T(8,128)(2,1)S(1)}, u32[]{:S(2)}, u32[]{:S(2)}) collective-permute-start(bf16[128,512]{1,0:T(8,128)(2,1)} %bitcast.49), channel_id=1, source_target_pairs={{0,3},{1,0},{2,1},{3,2},{4,7},{5,4},{6,5},{7,6},{8,11},{9,8},{10,9... | collective-permute-start | bytes 393224 | tf_op jit(solution)/shard_map/ppermute | solution.py:33
  3.7 9.5 %collective-permute-start.1 = (bf16[128,512]{1,0:T(8,128)(2,1)}, bf16[128,512]{1,0:T(8,128)(2,1)S(1)}, u32[]{:S(2)}, u32[]{:S(2)}) collective-permute-start(bf16[128,512]{1,0:T(8,128)(2,1)} %bitcast.50), channel_id=1, source_target_pairs={{0,2},{1,3},{2,0},{3,1},{4,6},{5,7},{6,4},{7,5},{8,10},{9,11},{10,... | collective-permute-start | bytes 393224 | tf_op jit(solution)/shard_map/ppermute | solution.py:33
  4.4 8.9 %collective-permute-start = (bf16[128,512]{1,0:T(8,128)(2,1)}, bf16[128,512]{1,0:T(8,128)(2,1)S(1)}, u32[]{:S(2)}, u32[]{:S(2)}) collective-permute-start(bf16[128,512]{1,0:T(8,128)(2,1)} %bitcast.51), channel_id=1, source_target_pairs={{0,1},{1,2},{2,3},{3,0},{4,5},{5,6},{6,7},{7,4},{8,9},{9,10},{10,1... | collective-permute-start | bytes 393224 | tf_op jit(solution)/shard_map/ppermute | solution.py:33
  16.6 14.2 %copy-start.6 = (s32[512]{0:T(512)S(1)}, s32[512]{0:T(512)}, u32[]{:S(2)}) copy-start(s32[512]{0:T(512)} %param.15) | copy-start | bytes 6148
  16.6 14.9 %copy-start.5 = (s32[8,16]{1,0:T(8,128)S(1)}, s32[8,16]{1,0:T(8,128)}, u32[]{:S(2)}) copy-start(s32[8,16]{1,0:T(8,128)} %param.17) | copy-start | bytes 1540
  18.4 38.9 %all-to-all-start = ((bf16[64,16,512]{2,1,0:T(8,128)(2,1)}), bf16[64,16,512]{2,1,0:T(8,128)(2,1)}, u32[]{:S(2)}, u32[]{:S(2)}) async-start(bf16[64,16,512]{2,1,0:T(8,128)(2,1)} %gather_fusion), calls=%async_computation | async-start | bytes 2097152 | tf_op jit(solution)/shard_map/all_to_all | solution.py:163
  62.9 24.9 %all-to-all-start.1 = ((bf16[64,16,192]{2,1,0:T(8,128)(2,1)}), bf16[64,16,192]{2,1,0:T(8,128)(2,1)}, u32[]{:S(2)}, u32[]{:S(2)}) async-start(bf16[64,16,192]{2,1,0:T(8,128)(2,1)} %shard_map.149), calls=%async_computation.1 | async-start | bytes 1048576 | tf_op jit(solution)/shard_map/all_to_all | solution.py:200
  71.2 38.7 %collective-permute-start.4 = (bf16[192,2048]{1,0:T(8,128)(2,1)}, bf16[192,2048]{1,0:T(8,128)(2,1)}, u32[]{:S(2)}, u32[]{:S(2)}) collective-permute-start(bf16[192,2048]{1,0:T(8,128)(2,1)} %param.23), channel_id=1, source_target_pairs={{0,1},{1,2},{2,3},{3,0},{4,5},{5,6},{6,7},{7,4},{8,9},{9,10},{10,1... | collective-permute-start | bytes 2359304 | tf_op jit(solution)/shard_map/ppermute | solution.py:33
  71.3 40.7 %collective-permute-start.6 = (bf16[192,2048]{1,0:T(8,128)(2,1)}, bf16[192,2048]{1,0:T(8,128)(2,1)}, u32[]{:S(2)}, u32[]{:S(2)}) collective-permute-start(bf16[192,2048]{1,0:T(8,128)(2,1)} %param.23), channel_id=1, source_target_pairs={{0,2},{1,3},{2,0},{3,1},{4,6},{5,7},{6,4},{7,5},{8,10},{9,11},{10,... | collective-permute-start | bytes 2359304 | tf_op jit(solution)/shard_map/ppermute | solution.py:33
  73.3 43.8 %collective-permute-start.8 = (bf16[192,2048]{1,0:T(8,128)(2,1)}, bf16[192,2048]{1,0:T(8,128)(2,1)}, u32[]{:S(2)}, u32[]{:S(2)}) collective-permute-start(bf16[192,2048]{1,0:T(8,128)(2,1)} %param.23), channel_id=1, source_target_pairs={{0,3},{1,0},{2,1},{3,2},{4,7},{5,4},{6,5},{7,6},{8,11},{9,8},{10,9... | collective-permute-start | bytes 2359304 | tf_op jit(solution)/shard_map/ppermute | solution.py:33
  89.4 21.1 %collective-permute-start.3 = (bf16[128,192]{1,0:T(8,128)(2,1)S(1)}, bf16[128,192]{1,0:T(8,128)(2,1)S(1)}, u32[]{:S(2)}, u32[]{:S(2)}) collective-permute-start(bf16[128,192]{1,0:T(8,128)(2,1)S(1)} %bitcast.45), channel_id=1, source_target_pairs={{0,1},{1,2},{2,3},{3,0},{4,5},{5,6},{6,7},{7,4},{8,9},{9,10},{10,1... | collective-permute-start | bytes 147464 | tf_op jit(solution)/shard_map/ppermute | solution.py:33
  89.6 29.0 %copy-start.3 = (bf16[192,2048]{1,0:T(8,128)(2,1)S(1)}, bf16[192,2048]{1,0:T(8,128)(2,1)}, u32[]{:S(2)}) copy-start(bf16[192,2048]{1,0:T(8,128)(2,1)} %param.23) | copy-start | bytes 2359300
  89.6 27.6 %collective-permute-start.7 = (bf16[128,192]{1,0:T(8,128)(2,1)S(1)}, bf16[128,192]{1,0:T(8,128)(2,1)S(1)}, u32[]{:S(2)}, u32[]{:S(2)}) collective-permute-start(bf16[128,192]{1,0:T(8,128)(2,1)S(1)} %bitcast.46), channel_id=1, source_target_pairs={{0,3},{1,0},{2,1},{3,2},{4,7},{5,4},{6,5},{7,6},{8,11},{9,8},{10,9... | collective-permute-start | bytes 147464 | tf_op jit(solution)/shard_map/ppermute | solution.py:33
  109.9 5.8 %collective-permute-start.5 = (bf16[128,192]{1,0:T(8,128)(2,1)S(1)}, bf16[128,192]{1,0:T(8,128)(2,1)S(1)}, u32[]{:S(2)}, u32[]{:S(2)}) collective-permute-start(bf16[128,192]{1,0:T(8,128)(2,1)S(1)} %bitcast.47), channel_id=1, source_target_pairs={{0,2},{1,3},{2,0},{3,1},{4,6},{5,7},{6,4},{7,5},{8,10},{9,11},{10,... | collective-permute-start | bytes 147464 | tf_op jit(solution)/shard_map/ppermute | solution.py:33
  118.6 2.1 %copy-start.2 = (bf16[2048,640]{1,0:T(8,128)(2,1)S(1)}, bf16[2048,640]{1,0:T(8,128)(2,1)}, u32[]{:S(2)}) copy-start(bf16[2048,640]{1,0:T(8,128)(2,1)} %param.25) | copy-start | bytes 7864324
  118.6 2.1 %copy-start.4 = (f32[2048]{0:T(1024)S(1)}, f32[2048]{0:T(1024)}, u32[]{:S(2)}) copy-start(f32[2048]{0:T(1024)} %param.24) | copy-start | bytes 24580
  119.1 3.1 %copy-start.1 = (f32[128,2048]{1,0:T(8,128)}, f32[128,2048]{1,0:T(8,128)S(1)}, u32[]{:S(2)}) copy-start(f32[128,2048]{1,0:T(8,128)S(1)} %get-tuple-element.11) | copy-start | bytes 3145732
  119.2 2.4 %copy-start.7 = (bf16[2048,640]{1,0:T(8,128)(2,1)S(1)}, bf16[2048,640]{1,0:T(8,128)(2,1)}, u32[]{:S(2)}) copy-start(bf16[2048,640]{1,0:T(8,128)(2,1)} %param.26) | copy-start | bytes 7864324
  122.2 6.0 %copy-start.9 = (s32[8,8]{1,0:T(8,128)S(1)}, s32[8,8]{1,0:T(8,128)}, u32[]{:S(2)}) copy-start(s32[8,8]{1,0:T(8,128)} %param.18) | copy-start | bytes 772
  123.1 7.7 %collective-permute-start.9 = (bf16[128,512]{1,0:T(8,128)(2,1)S(1)}, bf16[128,512]{1,0:T(8,128)(2,1)S(1)}, u32[]{:S(2)}, u32[]{:S(2)}) collective-permute-start(bf16[128,512]{1,0:T(8,128)(2,1)S(1)} %convolution_convert_fusion.6), channel_id=1, source_target_pairs={{0,1},{1,2},{2,3},{3,0},{4,5},{5,6},{6,7},{7,4},{8,9},{9,10},{10,1... | collective-permute-start | bytes 393224 | tf_op jit(solution)/shard_map/ppermute | solution.py:33
  123.2 7.6 %collective-permute-start.10 = (bf16[128,512]{1,0:T(8,128)(2,1)S(1)}, bf16[128,512]{1,0:T(8,128)(2,1)}, u32[]{:S(2)}, u32[]{:S(2)}) collective-permute-start(bf16[128,512]{1,0:T(8,128)(2,1)S(1)} %convolution_convert_fusion.5), channel_id=1, source_target_pairs={{0,2},{1,3},{2,0},{3,1},{4,6},{5,7},{6,4},{7,5},{8,10},{9,11},{10,... | collective-permute-start | bytes 393224 | tf_op jit(solution)/shard_map/ppermute | solution.py:33
  124.2 7.6 %collective-permute-start.11 = (bf16[128,512]{1,0:T(8,128)(2,1)S(1)}, bf16[128,512]{1,0:T(8,128)(2,1)}, u32[]{:S(2)}, u32[]{:S(2)}) collective-permute-start(bf16[128,512]{1,0:T(8,128)(2,1)S(1)} %convolution_convert_fusion.4), channel_id=1, source_target_pairs={{0,3},{1,0},{2,1},{3,2},{4,7},{5,4},{6,5},{7,6},{8,11},{9,8},{10,9... | collective-permute-start | bytes 393224 | tf_op jit(solution)/shard_map/ppermute | solution.py:33

commit v16 on v15

--- a/solution.py
+++ b/solution.py
@@ -72,13 +72,12 @@
             axis=0,
         )
 
-    high, low = stacked(0), stacked(query_width)
+    parts = jnp.concatenate([stacked(0), stacked(query_width)], axis=0)
+    rows = parts.shape[0] // 2
 
     def times(keys):
-        return (
-            jnp.dot(high, keys, preferred_element_type=jnp.float32)
-            + jnp.dot(low, keys, preferred_element_type=jnp.float32)
-        ) * scale
+        both = jnp.dot(parts, keys, preferred_element_type=jnp.float32)
+        return (both[:rows] + both[rows:]) * scale
 
     score_cache = jnp.where(live, times(keys_cache), -jnp.inf)
     score_draft = jnp.where(visible, times(keys_draft), -jnp.inf)

time: 134 us -> 134 us (level)
  no operation moved by 1% of the time
where the time goes in v16:
time: 134 us
  waiting for transfers between devices  67.8 us (51%)
  starting transfers between devices  35.3 us (26%)
  matrix products  14.2 us (11%)
  local copies, waits for them, and re-layouts  7.94 us (6%)
  Pallas kernels  5.35 us (4%)
  other arithmetic  1.8 us (1%)
    ppermute x12, waiting for transfers between devices, shift_mlp(): lax.ppermute(value, 'mlp', [(i, (i + shift) % count) for i in range(count)])  30.2 us
    all_to_all x1, waiting for transfers between devices, per_device(): incoming = lax.all_to_all(outgoing, 'req', 0, 0, tiled=True)  24.3 us
    ppermute x12, starting transfers between devices, shift_mlp(): lax.ppermute(value, 'mlp', [(i, (i + shift) % count) for i in range(count)])  14.7 us
    all_to_all x1, waiting for transfers between devices, per_device(): arrived = lax.all_to_all(returning, 'req', 0, 0, tiled=True)  13.3 us
    all_to_all x1, starting transfers between devices, per_device(): incoming = lax.all_to_all(outgoing, 'req', 0, 0, tiled=True)  12.4 us
    all_to_all x1, starting transfers between devices, per_device(): arrived = lax.all_to_all(returning, 'req', 0, 0, tiled=True)  8.29 us
    pallas_call x1, Pallas kernels, per_device(): pl.pallas_call(functools.partial(attend_kernel, widths=(query_width, grou...  5.35 us
    dot_general x4, matrix products, per_device(): jnp.dot(piece, rows_of_group, preferred_element_type=jnp.float32)  4.78 us
  transfers between devices with their start and end apart: 14, of which 8 were waited for; matrix products, arithmetic and copies ran while one was open for 8% of the time, Pallas kernels for 0%

profile of v16, /device:TPU:6, one launch (start us, length us, event | category | flops | bytes accessed | tf_op | source)
XLA Modules:
  0.0 133.5 jit_solution(13156240572666921679)
XLA Ops:
  0.7 3.1 %collective-permute-start.2 = (bf16[128,512]{1,0:T(8,128)(2,1)}, bf16[128,512]{1,0:T(8,128)(2,1)S(1)}, u32[]{:S(2)}, u32[]{:S(2)}) collective-permute-start(bf16[128,512]{1,0:T(8,128)(2,1)} %bitcast.49), channel_id=1, source_target_pairs={{0,3},{1,0},{2,1},{3,2},{4,7},{5,4},{6,5},{7,6},{8,11},{9,8},{10,9... | collective-permute-start | bytes 393224 | tf_op jit(solution)/shard_map/ppermute | solution.py:33
  7.2 6.0 %collective-permute-done = bf16[128,512]{1,0:T(8,128)(2,1)S(1)} collective-permute-done((bf16[128,512]{1,0:T(8,128)(2,1)}, bf16[128,512]{1,0:T(8,128)(2,1)S(1)}, u32[]{:S(2)}, u32[]{:S(2)}) %collective-permute-start) | collective-permute-done | bytes 131104 | tf_op jit(solution)/shard_map/ppermute | solution.py:33
  13.5 1.5 %convolution_convert_fusion.8 = bf16[128,128]{0,1:T(8,128)(2,1)S(1)} fusion(bf16[2048,128]{1,0:T(8,128)(2,1)} %param.22, bf16[128,2048]{1,0:T(8,128)(2,1)S(1)} %constant_dynamic-update-slice_fusion, f32[2048]{0:T(1024)} %param.20, f32[128]{0:T(128)S(1)} %add_rsqrt_fusion.1), kind=kOutput, calls=%fused_computation.28 | convolution fusion | flops 68173824 | bytes 1090048 | tf_op jit(solution)/shard_map/dot_general | solution.py:152
  15.0 1.6 %subtract_convert_fusion = (bf16[128,192]{0,1:T(8,128)(2,1)S(1)}, bf16[128,192]{0,1:T(8,128)(2,1)S(1)}) fusion(bf16[2048,192]{0,1:T(8,128)(2,1)} %param.21, bf16[128,2048]{1,0:T(8,128)(2,1)S(1)} %constant_dynamic-update-slice_fusion, f32[2048]{0:T(1024)S(1)} %copy-done.8, f32[128]{0:T(128)S(1)} %add_rsqrt_fusion.1), kind=kOutput, calls=%fused_computation.45 | convolution fusion | flops 101810176 | bytes 1417728 | tf_op jit(solution)/shard_map/dot_general | solution.py:151
  16.8 1.6 %gather_fusion = bf16[64,16,512]{2,1,0:T(8,128)(2,1)} fusion(bf16[8,16,512]{2,1,0:T(8,128)(2,1)S(1)} %bitcast.43, s32[1024]{0:T(1024)S(1)} %pad_clamp_fusion.2), kind=kCustom, calls=%fused_computation | custom fusion | bytes 2097408 | tf_op jit(solution)/shard_map/jit(_take)/gather | solution.py:161
  18.4 12.4 %all-to-all-start = ((bf16[64,16,512]{2,1,0:T(8,128)(2,1)}), bf16[64,16,512]{2,1,0:T(8,128)(2,1)}, u32[]{:S(2)}, u32[]{:S(2)}) async-start(bf16[64,16,512]{2,1,0:T(8,128)(2,1)} %gather_fusion), calls=%async_computation | async-start | bytes 2097152 | tf_op jit(solution)/shard_map/all_to_all | solution.py:162
  33.0 24.3 %all-to-all-done.row_ref = bf16[64,16,512]{2,1,0:T(8,128)(2,1)} async-done(((bf16[64,16,512]{2,1,0:T(8,128)(2,1)}), bf16[64,16,512]{2,1,0:T(8,128)(2,1)}, u32[]{:S(2)}, u32[]{:S(2)}) %all-to-all-start) | async-done | bytes 1048608 | tf_op jit(solution)/shard_map/all_to_all | solution.py:162
  57.3 5.3 %shard_map.149 = bf16[64,16,192]{2,1,0:T(8,128)(2,1)} custom-call(s32[8]{0:T(128)} %and_select_fusion.2.source_ref, s32[8]{0:T(128)} %length_ref.1, bf16[64,16,512]{2,1,0:T(8,128)(2,1)} %all-to-all-done.row_ref, bf16[8,256,128]{2,1,0:T(8,128)(2,1)} %bitcast.44, f32[8,16,16]{2,1,0:T(8,128)} %fusion.11.mask_ref), custom_call_target="tpu_custom_call" | custom-call | tf_op jit(solution)/shard_map/pallas_call | solution.py:187
  62.6 8.3 %all-to-all-start.1 = ((bf16[64,16,192]{2,1,0:T(8,128)(2,1)}), bf16[64,16,192]{2,1,0:T(8,128)(2,1)}, u32[]{:S(2)}, u32[]{:S(2)}) async-start(bf16[64,16,192]{2,1,0:T(8,128)(2,1)} %shard_map.149), calls=%async_computation.1 | async-start | bytes 1048576 | tf_op jit(solution)/shard_map/all_to_all | solution.py:199
  71.0 2.0 %collective-permute-start.6 = (bf16[192,2048]{1,0:T(8,128)(2,1)}, bf16[192,2048]{1,0:T(8,128)(2,1)}, u32[]{:S(2)}, u32[]{:S(2)}) collective-permute-start(bf16[192,2048]{1,0:T(8,128)(2,1)} %param.23), channel_id=1, source_target_pairs={{0,2},{1,3},{2,0},{3,1},{4,6},{5,7},{6,4},{7,5},{8,10},{9,11},{10,... | collective-permute-start | bytes 2359304 | tf_op jit(solution)/shard_map/ppermute | solution.py:33
  73.0 1.2 collective-permute-start.8
  74.3 13.3 %all-to-all-done.1 = bf16[64,16,192]{2,1,0:T(8,128)(2,1)} async-done(((bf16[64,16,192]{2,1,0:T(8,128)(2,1)}), bf16[64,16,192]{2,1,0:T(8,128)(2,1)}, u32[]{:S(2)}, u32[]{:S(2)}) %all-to-all-start.1) | async-done | bytes 393248 | tf_op jit(solution)/shard_map/all_to_all | solution.py:199
  87.5 1.6 %gather_fusion.1 = bf16[8,16,192]{2,1,0:T(8,128)(2,1)S(1)} fusion(bf16[64,16,192]{2,1,0:T(8,128)(2,1)} %all-to-all-done.1, s32[1024]{0:T(1024)S(1)} %pad_clamp_fusion.1), kind=kCustom, calls=%fused_computation.1 | custom fusion | bytes 98336 | tf_op jit(solution)/shard_map/jit(_take)/gather | solution.py:200
  89.3 3.2 %collective-permute-start.7 = (bf16[128,192]{1,0:T(8,128)(2,1)S(1)}, bf16[128,192]{1,0:T(8,128)(2,1)S(1)}, u32[]{:S(2)}, u32[]{:S(2)}) collective-permute-start(bf16[128,192]{1,0:T(8,128)(2,1)S(1)} %bitcast.46), channel_id=1, source_target_pairs={{0,3},{1,0},{2,1},{3,2},{4,7},{5,4},{6,5},{7,6},{8,11},{9,8},{10,9... | collective-permute-start | bytes 147464 | tf_op jit(solution)/shard_map/ppermute | solution.py:33
  92.5 17.1 %collective-permute-done.4 = bf16[192,2048]{1,0:T(8,128)(2,1)} collective-permute-done((bf16[192,2048]{1,0:T(8,128)(2,1)}, bf16[192,2048]{1,0:T(8,128)(2,1)}, u32[]{:S(2)}, u32[]{:S(2)}) %collective-permute-start.4) | collective-permute-done | bytes 786464 | tf_op jit(solution)/shard_map/ppermute | solution.py:33
  110.2 1.4 %fusion.2 = f32[128,2048]{1,0:T(8,128)S(1)} fusion(bf16[128,192]{1,0:T(8,128)(2,1)S(1)} %collective-permute-done.3, bf16[192,2048]{1,0:T(8,128)(2,1)} %collective-permute-done.4), kind=kOutput, calls=%fused_computation.8 | convolution fusion | flops 101187584 | bytes 1884160 | tf_op jit(solution)/shard_map/dot_general | solution.py:206
  111.7 3.7 %collective-permute-done.5 = bf16[128,192]{1,0:T(8,128)(2,1)S(1)} collective-permute-done((bf16[128,192]{1,0:T(8,128)(2,1)S(1)}, bf16[128,192]{1,0:T(8,128)(2,1)S(1)}, u32[]{:S(2)}, u32[]{:S(2)}) %collective-permute-start.5) | collective-permute-done | bytes 49184 | tf_op jit(solution)/shard_map/ppermute | solution.py:33
  115.4 1.4 %fusion.1 = f32[128,2048]{1,0:T(8,128)S(1)} fusion(bf16[128,192]{1,0:T(8,128)(2,1)S(1)} %collective-permute-done.5, bf16[192,2048]{1,0:T(8,128)(2,1)} %collective-permute-done.6), kind=kOutput, calls=%fused_computation.6 | convolution fusion | flops 101187584 | bytes 1884160 | tf_op jit(solution)/shard_map/dot_general | solution.py:206
  116.9 1.4 %fusion = f32[128,2048]{1,0:T(8,128)S(1)} fusion(bf16[128,192]{1,0:T(8,128)(2,1)S(1)} %collective-permute-done.7, bf16[192,2048]{1,0:T(8,128)(2,1)} %collective-permute-done.8), kind=kOutput, calls=%fused_computation.4 | convolution fusion | flops 101187584 | bytes 1884160 | tf_op jit(solution)/shard_map/dot_general | solution.py:206
  118.9 1.6 %copy-done.2 = bf16[2048,640]{1,0:T(8,128)(2,1)S(1)} copy-done((bf16[2048,640]{1,0:T(8,128)(2,1)S(1)}, bf16[2048,640]{1,0:T(8,128)(2,1)}, u32[]{:S(2)}) %copy-start.2) | copy-done | bytes 2621464
  123.9 2.2 %collective-permute-start.11 = (bf16[128,512]{1,0:T(8,128)(2,1)S(1)}, bf16[128,512]{1,0:T(8,128)(2,1)}, u32[]{:S(2)}, u32[]{:S(2)}) collective-permute-start(bf16[128,512]{1,0:T(8,128)(2,1)S(1)} %convolution_convert_fusion.4), channel_id=1, source_target_pairs={{0,3},{1,0},{2,1},{3,2},{4,7},{5,4},{6,5},{7,6},{8,11},{9,8},{10,9... | collective-permute-start | bytes 393224 | tf_op jit(solution)/shard_map/ppermute | solution.py:33
  126.1 1.8 %gather_fusion.2 = bf16[8,16,512]{2,1,0:T(8,128)(2,1)S(1)} fusion(bf16[64,16,512]{2,1,0:T(8,128)(2,1)} %all-to-all-done.row_ref, s32[1024]{0:T(1024)S(1)} %pad_clamp_fusion), kind=kCustom, calls=%fused_computation.2 | custom fusion | bytes 262176 | tf_op jit(solution)/shard_map/jit(_take)/gather | solution.py:163
  128.7 1.7 %collective-permute-done.9 = bf16[128,512]{1,0:T(8,128)(2,1)S(1)} collective-permute-done((bf16[128,512]{1,0:T(8,128)(2,1)S(1)}, bf16[128,512]{1,0:T(8,128)(2,1)S(1)}, u32[]{:S(2)}, u32[]{:S(2)}) %collective-permute-start.9) | collective-permute-done | bytes 131104 | tf_op jit(solution)/shard_map/ppermute | solution.py:33
  131.5 2.0 %add_convert_fusion = bf16[128,512]{1,0:T(8,128)(2,1)} fusion(bf16[128,512]{1,0:T(8,128)(2,1)} %collective-permute-done.11, bf16[128,512]{1,0:T(8,128)(2,1)} %collective-permute-done.10, bf16[128,512]{1,0:T(8,128)(2,1)S(1)} %collective-permute-done.9, f32[128,2048]{1,0:T(8,128)} %copy-done.1, s32[]{:T(128)S(6)} %select_n.90, ...), kind=kOutput, calls=%fused_computation.42 | convolution fusion | flops 84541440 | bytes 1606656 | tf_op jit(solution)/shard_map/dot_general | solution.py:219
  (65 shorter events, 12.5 us)
Async XLA Ops:
  0.6 121.3 %copy-start = (bf16[640,2048]{1,0:T(8,128)(2,1)S(1)}, bf16[640,2048]{1,0:T(8,128)(2,1)}, u32[]{:S(2)}) copy-start(bf16[640,2048]{1,0:T(8,128)(2,1)} %param.27) | copy-start | bytes 7864324
  0.6 14.3 %copy-start.8 = (f32[2048]{0:T(1024)S(1)}, f32[2048]{0:T(1024)}, u32[]{:S(2)}) copy-start(f32[2048]{0:T(1024)} %param.20) | copy-start | bytes 24580
  0.7 12.6 %collective-permute-start.2 = (bf16[128,512]{1,0:T(8,128)(2,1)}, bf16[128,512]{1,0:T(8,128)(2,1)S(1)}, u32[]{:S(2)}, u32[]{:S(2)}) collective-permute-start(bf16[128,512]{1,0:T(8,128)(2,1)} %bitcast.49), channel_id=1, source_target_pairs={{0,3},{1,0},{2,1},{3,2},{4,7},{5,4},{6,5},{7,6},{8,11},{9,8},{10,9... | collective-permute-start | bytes 393224 | tf_op jit(solution)/shard_map/ppermute | solution.py:33
  3.7 9.5 %collective-permute-start.1 = (bf16[128,512]{1,0:T(8,128)(2,1)}, bf16[128,512]{1,0:T(8,128)(2,1)S(1)}, u32[]{:S(2)}, u32[]{:S(2)}) collective-permute-start(bf16[128,512]{1,0:T(8,128)(2,1)} %bitcast.50), channel_id=1, source_target_pairs={{0,2},{1,3},{2,0},{3,1},{4,6},{5,7},{6,4},{7,5},{8,10},{9,11},{10,... | collective-permute-start | bytes 393224 | tf_op jit(solution)/shard_map/ppermute | solution.py:33
  4.4 8.9 %collective-permute-start = (bf16[128,512]{1,0:T(8,128)(2,1)}, bf16[128,512]{1,0:T(8,128)(2,1)S(1)}, u32[]{:S(2)}, u32[]{:S(2)}) collective-permute-start(bf16[128,512]{1,0:T(8,128)(2,1)} %bitcast.51), channel_id=1, source_target_pairs={{0,1},{1,2},{2,3},{3,0},{4,5},{5,6},{6,7},{7,4},{8,9},{9,10},{10,1... | collective-permute-start | bytes 393224 | tf_op jit(solution)/shard_map/ppermute | solution.py:33
  16.6 14.2 %copy-start.6 = (s32[512]{0:T(512)S(1)}, s32[512]{0:T(512)}, u32[]{:S(2)}) copy-start(s32[512]{0:T(512)} %param.15) | copy-start | bytes 6148
  16.6 14.9 %copy-start.5 = (s32[8,16]{1,0:T(8,128)S(1)}, s32[8,16]{1,0:T(8,128)}, u32[]{:S(2)}) copy-start(s32[8,16]{1,0:T(8,128)} %param.17) | copy-start | bytes 1540
  18.4 38.9 %all-to-all-start = ((bf16[64,16,512]{2,1,0:T(8,128)(2,1)}), bf16[64,16,512]{2,1,0:T(8,128)(2,1)}, u32[]{:S(2)}, u32[]{:S(2)}) async-start(bf16[64,16,512]{2,1,0:T(8,128)(2,1)} %gather_fusion), calls=%async_computation | async-start | bytes 2097152 | tf_op jit(solution)/shard_map/all_to_all | solution.py:162
  62.6 24.9 %all-to-all-start.1 = ((bf16[64,16,192]{2,1,0:T(8,128)(2,1)}), bf16[64,16,192]{2,1,0:T(8,128)(2,1)}, u32[]{:S(2)}, u32[]{:S(2)}) async-start(bf16[64,16,192]{2,1,0:T(8,128)(2,1)} %shard_map.149), calls=%async_computation.1 | async-start | bytes 1048576 | tf_op jit(solution)/shard_map/all_to_all | solution.py:199
  70.9 38.7 %collective-permute-start.4 = (bf16[192,2048]{1,0:T(8,128)(2,1)}, bf16[192,2048]{1,0:T(8,128)(2,1)}, u32[]{:S(2)}, u32[]{:S(2)}) collective-permute-start(bf16[192,2048]{1,0:T(8,128)(2,1)} %param.23), channel_id=1, source_target_pairs={{0,1},{1,2},{2,3},{3,0},{4,5},{5,6},{6,7},{7,4},{8,9},{9,10},{10,1... | collective-permute-start | bytes 2359304 | tf_op jit(solution)/shard_map/ppermute | solution.py:33
  71.0 40.7 %collective-permute-start.6 = (bf16[192,2048]{1,0:T(8,128)(2,1)}, bf16[192,2048]{1,0:T(8,128)(2,1)}, u32[]{:S(2)}, u32[]{:S(2)}) collective-permute-start(bf16[192,2048]{1,0:T(8,128)(2,1)} %param.23), channel_id=1, source_target_pairs={{0,2},{1,3},{2,0},{3,1},{4,6},{5,7},{6,4},{7,5},{8,10},{9,11},{10,... | collective-permute-start | bytes 2359304 | tf_op jit(solution)/shard_map/ppermute | solution.py:33
  73.0 43.8 %collective-permute-start.8 = (bf16[192,2048]{1,0:T(8,128)(2,1)}, bf16[192,2048]{1,0:T(8,128)(2,1)}, u32[]{:S(2)}, u32[]{:S(2)}) collective-permute-start(bf16[192,2048]{1,0:T(8,128)(2,1)} %param.23), channel_id=1, source_target_pairs={{0,3},{1,0},{2,1},{3,2},{4,7},{5,4},{6,5},{7,6},{8,11},{9,8},{10,9... | collective-permute-start | bytes 2359304 | tf_op jit(solution)/shard_map/ppermute | solution.py:33
  89.1 21.1 %collective-permute-start.3 = (bf16[128,192]{1,0:T(8,128)(2,1)S(1)}, bf16[128,192]{1,0:T(8,128)(2,1)S(1)}, u32[]{:S(2)}, u32[]{:S(2)}) collective-permute-start(bf16[128,192]{1,0:T(8,128)(2,1)S(1)} %bitcast.45), channel_id=1, source_target_pairs={{0,1},{1,2},{2,3},{3,0},{4,5},{5,6},{6,7},{7,4},{8,9},{9,10},{10,1... | collective-permute-start | bytes 147464 | tf_op jit(solution)/shard_map/ppermute | solution.py:33
  89.3 29.0 %copy-start.3 = (bf16[192,2048]{1,0:T(8,128)(2,1)S(1)}, bf16[192,2048]{1,0:T(8,128)(2,1)}, u32[]{:S(2)}) copy-start(bf16[192,2048]{1,0:T(8,128)(2,1)} %param.23) | copy-start | bytes 2359300
  89.3 27.6 %collective-permute-start.7 = (bf16[128,192]{1,0:T(8,128)(2,1)S(1)}, bf16[128,192]{1,0:T(8,128)(2,1)S(1)}, u32[]{:S(2)}, u32[]{:S(2)}) collective-permute-start(bf16[128,192]{1,0:T(8,128)(2,1)S(1)} %bitcast.46), channel_id=1, source_target_pairs={{0,3},{1,0},{2,1},{3,2},{4,7},{5,4},{6,5},{7,6},{8,11},{9,8},{10,9... | collective-permute-start | bytes 147464 | tf_op jit(solution)/shard_map/ppermute | solution.py:33
  109.6 5.8 %collective-permute-start.5 = (bf16[128,192]{1,0:T(8,128)(2,1)S(1)}, bf16[128,192]{1,0:T(8,128)(2,1)S(1)}, u32[]{:S(2)}, u32[]{:S(2)}) collective-permute-start(bf16[128,192]{1,0:T(8,128)(2,1)S(1)} %bitcast.47), channel_id=1, source_target_pairs={{0,2},{1,3},{2,0},{3,1},{4,6},{5,7},{6,4},{7,5},{8,10},{9,11},{10,... | collective-permute-start | bytes 147464 | tf_op jit(solution)/shard_map/ppermute | solution.py:33
  118.3 2.1 %copy-start.2 = (bf16[2048,640]{1,0:T(8,128)(2,1)S(1)}, bf16[2048,640]{1,0:T(8,128)(2,1)}, u32[]{:S(2)}) copy-start(bf16[2048,640]{1,0:T(8,128)(2,1)} %param.25) | copy-start | bytes 7864324
  118.3 2.1 %copy-start.4 = (f32[2048]{0:T(1024)S(1)}, f32[2048]{0:T(1024)}, u32[]{:S(2)}) copy-start(f32[2048]{0:T(1024)} %param.24) | copy-start | bytes 24580
  118.8 3.1 %copy-start.1 = (f32[128,2048]{1,0:T(8,128)}, f32[128,2048]{1,0:T(8,128)S(1)}, u32[]{:S(2)}) copy-start(f32[128,2048]{1,0:T(8,128)S(1)} %get-tuple-element.11) | copy-start | bytes 3145732
  118.8 2.4 %copy-start.7 = (bf16[2048,640]{1,0:T(8,128)(2,1)S(1)}, bf16[2048,640]{1,0:T(8,128)(2,1)}, u32[]{:S(2)}) copy-start(bf16[2048,640]{1,0:T(8,128)(2,1)} %param.26) | copy-start | bytes 7864324
  121.9 6.0 %copy-start.9 = (s32[8,8]{1,0:T(8,128)S(1)}, s32[8,8]{1,0:T(8,128)}, u32[]{:S(2)}) copy-start(s32[8,8]{1,0:T(8,128)} %param.18) | copy-start | bytes 772
  122.8 7.7 %collective-permute-start.9 = (bf16[128,512]{1,0:T(8,128)(2,1)S(1)}, bf16[128,512]{1,0:T(8,128)(2,1)S(1)}, u32[]{:S(2)}, u32[]{:S(2)}) collective-permute-start(bf16[128,512]{1,0:T(8,128)(2,1)S(1)} %convolution_convert_fusion.6), channel_id=1, source_target_pairs={{0,1},{1,2},{2,3},{3,0},{4,5},{5,6},{6,7},{7,4},{8,9},{9,10},{10,1... | collective-permute-start | bytes 393224 | tf_op jit(solution)/shard_map/ppermute | solution.py:33
  122.9 7.6 %collective-permute-start.10 = (bf16[128,512]{1,0:T(8,128)(2,1)S(1)}, bf16[128,512]{1,0:T(8,128)(2,1)}, u32[]{:S(2)}, u32[]{:S(2)}) collective-permute-start(bf16[128,512]{1,0:T(8,128)(2,1)S(1)} %convolution_convert_fusion.5), channel_id=1, source_target_pairs={{0,2},{1,3},{2,0},{3,1},{4,6},{5,7},{6,4},{7,5},{8,10},{9,11},{10,... | collective-permute-start | bytes 393224 | tf_op jit(solution)/shard_map/ppermute | solution.py:33
  123.9 7.6 %collective-permute-start.11 = (bf16[128,512]{1,0:T(8,128)(2,1)S(1)}, bf16[128,512]{1,0:T(8,128)(2,1)}, u32[]{:S(2)}, u32[]{:S(2)}) collective-permute-start(bf16[128,512]{1,0:T(8,128)(2,1)S(1)} %convolution_convert_fusion.4), channel_id=1, source_target_pairs={{0,3},{1,0},{2,1},{3,2},{4,7},{5,4},{6,5},{7,6},{8,11},{9,8},{10,9... | collective-permute-start | bytes 393224 | tf_op jit(solution)/shard_map/ppermute | solution.py:33
